TPU v7x, 32 devices: a whole 2x2x4 slice. The times are simulated.
32 devices in a mesh: groups: 2 (over y), gx: 4 (over z), gy: 2 (over x), gz: 2 (over core).
Axes of the slice: x: 2, y: 2, z: 4, core: 2. Of those that a mesh axis runs over, the one named last changes fastest.
Arguments:
- parent: bfloat16 [160, 32, 1024], P('groups', 'gx', ('gy', 'gz')), parts along dimension 0, may hold values from -6 to 6
- nest: bfloat16 [160, 24, 1536], P('groups', 'gx', ('gy', 'gz')), parts along dimension 0, may hold values from -6 to 6
- nu_parent: float32 [80], replicated, may hold values from 0.03 to 0.24
- nu_nest: float32 [80], replicated, may hold values from 0.03 to 0.24
- relax: float32 [80], replicated, may hold values from 0.1 to 0.5
- feedback: float32 [80], replicated, may hold values from 0.3 to 1
- vert_mix: float32 [80, 80], replicated, may hold values from -1 to 1
- fp_owner: int32 [4, 4, 256, 1], P('gx', ('gy', 'gz')), may hold values from 0 to 3; in each aligned block of 256 rows (0 to 255, 256 to 511, ..., all dimensions but the last counted through in order) at most 256 rows name the same one
- fp_cell: int32 [4, 4, 256], P('gx', ('gy', 'gz')), may hold values from 0 to 2047
- nest_of: int32 [24], replicated, may hold values from 0 to 2, as said below
Outputs:
- parent_out: bfloat16 [160, 32, 1024], P('groups', 'gx', ('gy', 'gz')), parts along dimension 0
- nest_out: bfloat16 [160, 24, 1536], P('groups', 'gx', ('gy', 'gz')), parts along dimension 0
There are 2 independent parts, one for each index of `groups`. A program takes and returns all parts, laid end to end along the dimension named above; an argument that names none is the same for every part. Nothing has to cross between parts.
Inputs may be any that keep to these rules, and one draw needn't show every extreme that they name: `fp_owner`: within the 256 blocks of one nest tile no parent tile is named more than 256 times; in some nest tiles one is named exactly 256 times. `nest_of`: never falls along the rows; every nest holds one or more rows; nest 1 holds rows 11 and 12.
All inputs are finite; a program needn't handle non-finite values.
Results may differ from a plain program's by a relative error of at most 0.0033.
Values may be sent and summed in bfloat16 or wider, within the bound.
No kernel may reach another device: no remote copies, remote signals or barrier semaphores. Data moves between devices by JAX's collectives and lax.ppermute only.
A program may use at most 64 MiB of HBM per device.

v0:
```python
import jax
import jax.numpy as jnp
from jax import lax
from jax.sharding import PartitionSpec as P


def extended(block, sides, width):
    for axis, dim in sides:
        count = lax.axis_size(axis)
        forward = [(i, i + 1) for i in range(count - 1)]
        backward = [(target, source) for source, target in forward]
        low = lax.ppermute(
            lax.slice_in_dim(block, block.shape[dim] - width, None, axis=dim), axis, forward
        )
        high = lax.ppermute(lax.slice_in_dim(block, 0, width, axis=dim), axis, backward)
        block = jnp.concatenate([low, block, high], axis=dim)
    return block


def mix_levels(matrix, values):
    flat_values = values.reshape(values.shape[0], -1)
    mixed = jnp.dot(
        matrix, flat_values, precision=lax.Precision.HIGHEST, preferred_element_type=jnp.float32
    )
    return mixed.reshape(values.shape)


def stencil(padded, centre):
    return (
        padded[:, 2:, 1:-1]
        + padded[:, :-2, 1:-1]
        + padded[:, 1:-1, 2:]
        + padded[:, 1:-1, :-2]
        - 4.0 * centre
    )


def nest_stencil(padded, centre, left_w, right_w):
    return (
        padded[:, 2:, 1:-1] * right_w[None, :, None]
        + padded[:, :-2, 1:-1] * left_w[None, :, None]
        + padded[:, 1:-1, 2:]
        + padded[:, 1:-1, :-2]
        - 4.0 * centre
    )


def advance(padded, centre, target, nu_nest, relax, vert_mix, left_w, right_w):
    moved = centre + nu_nest[:, None, None] * nest_stencil(padded, centre, left_w, right_w)
    moved = moved + relax[:, None, None] * (target - moved)
    return mix_levels(vert_mix, moved)


def nest_segments(nest_of, first, count):
    index_rows = first + jnp.arange(count, dtype=jnp.int32)
    inside = (index_rows >= 0) & (index_rows < nest_of.shape[0])
    return jnp.where(inside, nest_of[jnp.clip(index_rows, 0, nest_of.shape[0] - 1)], -1)


def row_weights(segments):
    left_w = (segments[:-2] == segments[1:-1]).astype(jnp.float32)
    right_w = (segments[2:] == segments[1:-1]).astype(jnp.float32)
    return (left_w, right_w)


def body(parent, nest, nu_parent, nu_nest, relax, feedback, vert_mix, fp_owner, fp_cell, nest_of):
    levels = parent.shape[0]
    tiles_x = lax.axis_size("gx")
    here_x = lax.axis_index("gx")
    coarse_rim = extended(parent, (("gx", 1), (("gy", "gz"), 2)), 1).astype(jnp.float32)
    centre = coarse_rim[:, 1:-1, 1:-1]
    stepped = mix_levels(vert_mix, centre + nu_parent[:, None, None] * stencil(coarse_rim, centre))
    flat_parent = stepped.reshape(levels, -1)
    owners = fp_owner.reshape(-1)
    cells = fp_cell.reshape(-1)
    requests = owners.shape[0]
    slots = 4 * requests // tiles_x
    onehot = (owners[:, None] == jnp.arange(tiles_x, dtype=jnp.int32)[None, :]).astype(jnp.int32)
    before = jnp.cumsum(onehot, axis=0) - onehot
    order_in = jnp.sum(before * onehot, axis=1)
    places = owners * slots + order_in
    wanted = jnp.zeros((tiles_x * slots,), jnp.int32).at[places].set(cells)
    served_ids = lax.all_to_all(wanted, "gx", split_axis=0, concat_axis=0, tiled=True)
    answers = lax.all_to_all(
        jnp.take(flat_parent, served_ids, axis=1), "gx", split_axis=1, concat_axis=1, tiled=True
    )
    forcing_flat = jnp.take(answers, places, axis=1)
    nest_rows = nest.shape[1]
    nest_cols = nest.shape[2]
    block_rows = nest_rows // 3
    block_cols = nest_cols // 3
    forcing_block = forcing_flat.reshape(levels, block_rows, block_cols)
    row_start = here_x * nest_rows
    forcing_full = jnp.repeat(jnp.repeat(forcing_block, 3, axis=1), 3, axis=2)
    left_w, right_w = row_weights(nest_segments(nest_of, row_start - 1, nest_rows + 2))
    nest_state = nest.astype(jnp.float32)
    for turn_no in range(3):
        padded = extended(
            nest_state.astype(jnp.bfloat16), (("gx", 1), (("gy", "gz"), 2)), 1
        ).astype(nest_state.dtype)
        nest_state = advance(
            padded, nest_state, forcing_full, nu_nest, relax, vert_mix, left_w, right_w
        )
    blocks = nest_state.reshape(levels, block_rows, 3, block_cols, 3).mean(axis=(2, 4))
    nudge_gap = (blocks - forcing_block).reshape(levels, -1)
    outgoing = jnp.zeros((levels, tiles_x * slots), jnp.float32).at[:, places].set(nudge_gap)
    incoming = lax.all_to_all(outgoing, "gx", split_axis=1, concat_axis=1, tiled=True)
    summed = jnp.zeros_like(flat_parent).at[:, served_ids].add(incoming)
    parent_out = (stepped + feedback[:, None, None] * summed.reshape(stepped.shape)).astype(
        jnp.bfloat16
    )
    return (parent_out, nest_state.astype(jnp.bfloat16))


def solution(mesh):
    placed = (
        P("groups", "gx", ("gy", "gz")),
        P("groups", "gx", ("gy", "gz")),
        P(),
        P(),
        P(),
        P(),
        P(),
        P("gx", ("gy", "gz"), None, None),
        P("gx", ("gy", "gz"), None),
        P(),
    )
    return jax.shard_map(
        body,
        mesh=mesh,
        in_specs=placed,
        out_specs=(P("groups", "gx", ("gy", "gz")), P("groups", "gx", ("gy", "gz"))),
        check_vma=False,
    )
```

profile of v0, /device:TPU:0, one launch (start us, length us, event | category | flops | bytes accessed | tf_op | source)
XLA Modules:
  0.0 137.2 jit_solution(6008696607934461132)
XLA Ops:
  4.4 2.1 %scatter_custom_fusion = s32[1024]{0:T(1024)} fusion(s32[256]{0:T(256)S(1)} %bitcast.129, s32[256]{0:T(256)} %bitcast.133, s32[]{:T(128)} %constant.22.clone.1), kind=kCustom, calls=%fused_computation.87 | custom fusion | bytes 4608 | tf_op jit(solution)/shard_map/scatter | solution.py:82
  6.5 6.3 %all-to-all-start = ((s32[4,256,1]{1,2,0:T(1,128)}), s32[4,256,1]{1,2,0:T(1,128)S(1)}, u32[]{:S(2)}, u32[]{:S(2)}) async-start(s32[4,256,1]{1,2,0:T(1,128)} %bitcast.9), calls=%async_computation | async-start | bytes 8192 | tf_op jit(solution)/shard_map/all_to_all | solution.py:83
  14.1 3.9 %collective-permute-start = (bf16[80,1,256]{2,1,0:T(2,128)(2,1)S(1)}, bf16[80,1,256]{2,1,0:T(2,128)(2,1)S(1)}, u32[]{:S(2)}, u32[]{:S(2)}) collective-permute-start(bf16[80,1,256]{2,1,0:T(2,128)(2,1)S(1)} %get-tuple-element.24), channel_id=1, source_target_pairs={{0,4},{4,8},{8,12},{1,5},{5,9},{9,13},{2,6},{6,10},{10,14},{3,7},{... | collective-permute-start | bytes 122888 | tf_op jit(solution)/shard_map/ppermute | solution.py:12
  19.3 1.3 copy.67
  21.3 4.5 %collective-permute-start.4 = (bf16[80,1,384]{0,2,1:T(8,128)(2,1)}, bf16[80,1,384]{0,2,1:T(8,128)(2,1)S(1)}, u32[]{:S(2)}, u32[]{:S(2)}) collective-permute-start(bf16[80,1,384]{0,2,1:T(8,128)(2,1)} %get-tuple-element.22), channel_id=1, source_target_pairs={{0,4},{4,8},{8,12},{1,5},{5,9},{9,13},{2,6},{6,10},{10,14},{3,7},{... | collective-permute-start | bytes 184328 | tf_op jit(solution)/shard_map/ppermute | solution.py:12
  29.1 1.3 collective-permute-start.2
  31.7 3.9 %collective-permute-done.3 = bf16[80,10,1]{2,1,0:T(8,128)(2,1)S(1)} collective-permute-done((bf16[80,10,1]{2,1,0:T(8,128)(2,1)S(1)}, bf16[80,10,1]{2,1,0:T(8,128)(2,1)S(1)}, u32[]{:S(2)}, u32[]{:S(2)}) %collective-permute-start.3) | collective-permute-done | bytes 1632 | tf_op jit(solution)/shard_map/ppermute | solution.py:15
  38.9 2.8 %gather_fusion.1 = f32[1024,80]{1,0:T(8,128)S(1)} fusion(f32[80,2048]{0,1:T(8,128)S(1)} %copy.71, s32[1024]{0:T(1024)S(1)} %broadcast_clamp_fusion), kind=kCustom, calls=%fused_computation.1 | custom fusion | bytes 659456 | tf_op jit(solution)/shard_map/jit(_take)/gather | solution.py:85
  42.7 5.7 %all-to-all-start.1 = ((f32[80,4,256]{2,0,1:T(8,128)}), f32[80,4,256]{2,0,1:T(8,128)S(1)}, u32[]{:S(2)}, u32[]{:S(2)}) async-start(f32[80,4,256]{2,0,1:T(8,128)} %broadcast_select_fusion), calls=%async_computation.1 | async-start | bytes 655360 | tf_op jit(solution)/shard_map/all_to_all | solution.py:84
  49.1 7.0 %collective-permute-start.6 = (bf16[80,8,1]{0,2,1:T(2,128)(2,1)S(1)}, bf16[80,8,1]{0,2,1:T(2,128)(2,1)S(1)}, u32[]{:S(2)}, u32[]{:S(2)}) collective-permute-start(bf16[80,8,1]{0,2,1:T(2,128)(2,1)S(1)} %get-tuple-element.14), channel_id=1, source_target_pairs={{0,1},{1,2},{2,3},{4,5},{5,6},{6,7},{8,9},{9,10},{10,11},{12,13},{... | collective-permute-start | bytes 3848 | tf_op jit(solution)/shard_map/ppermute | solution.py:12
  57.4 1.7 %collective-permute-done.7 = bf16[80,8,1]{0,2,1:T(2,128)(2,1)S(1)} collective-permute-done((bf16[80,8,1]{0,2,1:T(2,128)(2,1)S(1)}, bf16[80,8,1]{0,2,1:T(2,128)(2,1)S(1)}, u32[]{:S(2)}, u32[]{:S(2)}) %collective-permute-start.7) | collective-permute-done | bytes 1312 | tf_op jit(solution)/shard_map/ppermute | solution.py:15
  61.4 1.5 %broadcast_in_dim.67 = f32[80,6,128,3]{0,3,2,1:T(4,128)} broadcast(f32[80,6,128]{0,2,1:T(8,128)S(1)} %bitcast.114), dimensions={0,1,2} | broadcast | bytes 983040 | tf_op jit(solution)/shard_map/broadcast_in_dim | solution.py:94
  62.9 2.2 %reshape.183 = f32[80,6,384]{0,2,1:T(8,128)S(1)} reshape(f32[80,6,128,3]{0,3,2,1:T(4,128)} %broadcast_in_dim.67) | data formatting | bytes 1474560 | tf_op jit(solution)/shard_map/reshape | solution.py:94
  65.1 1.4 %multiply_add_fusion.2 = f32[80,6,384]{0,2,1:T(8,128)S(1)} fusion(f32[80,6,384]{0,2,1:T(8,128)S(1)} %reshape.183, f32[80,8,386]{0,2,1:T(8,128)S(1)} %maximum_convert_fusion.1, bf16[80,6,384]{0,2,1:T(8,128)(2,1)S(1)} %copy.67, f32[80]{0:T(128)} %param.14, f32[6]{0:T(128)} %get-tuple-element.27, f32[6]{0:T(128)} %get-tuple-element.26, f32[80]{0:T(128)} %param.13), kind=kLoop, calls=%fused_computation.36 | loop fusion | flops 2396160 | bytes 4793008 | tf_op jit(solution)/shard_map/add | solution.py:50
  66.5 2.3 %convolution_bitcast_fusion.2 = f32[80,2304]{1,0:T(8,128)} fusion(f32[80,2304]{0,1:T(8,128)S(1)} %bitcast.108, f32[80,80]{1,0:T(8,128)S(1)} %copy-done), kind=kOutput, calls=%fused_computation.8 | convolution fusion | flops 176947200 | bytes 1500160 | tf_op jit(solution)/shard_map/dot_general | solution.py:22
  68.8 1.5 %copy.92 = f32[80,2304]{0,1:T(8,128)S(1)} copy(f32[80,2304]{1,0:T(8,128)} %convolution_bitcast_fusion.2) | data formatting | bytes 1474560 | tf_op jit(solution)/shard_map/reshape | solution.py:25
  70.4 3.7 %collective-permute-start.8 = (bf16[80,1,384]{0,2,1:T(8,128)(2,1)S(1)}, bf16[80,1,384]{0,2,1:T(8,128)(2,1)S(1)}, u32[]{:S(2)}, u32[]{:S(2)}) collective-permute-start(bf16[80,1,384]{0,2,1:T(8,128)(2,1)S(1)} %get-tuple-element.20), channel_id=1, source_target_pairs={{0,4},{4,8},{8,12},{1,5},{5,9},{9,13},{2,6},{6,10},{10,14},{3,7},{... | collective-permute-start | bytes 184328 | tf_op jit(solution)/shard_map/ppermute | solution.py:12
  76.2 4.4 %collective-permute-done.9 = bf16[80,1,384]{0,2,1:T(8,128)(2,1)S(1)} collective-permute-done((bf16[80,1,384]{0,2,1:T(8,128)(2,1)S(1)}, bf16[80,1,384]{0,2,1:T(8,128)(2,1)S(1)}, u32[]{:S(2)}, u32[]{:S(2)}) %collective-permute-start.9) | collective-permute-done | bytes 61472 | tf_op jit(solution)/shard_map/ppermute | solution.py:15
  80.6 2.7 %collective-permute-start.10 = (bf16[80,8,1]{0,2,1:T(2,128)(2,1)S(1)}, bf16[80,8,1]{0,2,1:T(2,128)(2,1)S(1)}, u32[]{:S(2)}, u32[]{:S(2)}) collective-permute-start(bf16[80,8,1]{0,2,1:T(2,128)(2,1)S(1)} %get-tuple-element.12), channel_id=1, source_target_pairs={{0,1},{1,2},{2,3},{4,5},{5,6},{6,7},{8,9},{9,10},{10,11},{12,13},{... | collective-permute-start | bytes 3848 | tf_op jit(solution)/shard_map/ppermute | solution.py:12
  83.4 1.5 %collective-permute-start.11 = (bf16[80,8,1]{0,2,1:T(2,128)(2,1)S(1)}, bf16[80,8,1]{0,2,1:T(2,128)(2,1)S(1)}, u32[]{:S(2)}, u32[]{:S(2)}) collective-permute-start(bf16[80,8,1]{0,2,1:T(2,128)(2,1)S(1)} %get-tuple-element.13), channel_id=1, source_target_pairs={{1,0},{2,1},{3,2},{5,4},{6,5},{7,6},{9,8},{10,9},{11,10},{13,12},{... | collective-permute-start | bytes 3848 | tf_op jit(solution)/shard_map/ppermute | solution.py:15
  84.9 2.5 %collective-permute-done.11 = bf16[80,8,1]{0,2,1:T(2,128)(2,1)S(1)} collective-permute-done((bf16[80,8,1]{0,2,1:T(2,128)(2,1)S(1)}, bf16[80,8,1]{0,2,1:T(2,128)(2,1)S(1)}, u32[]{:S(2)}, u32[]{:S(2)}) %collective-permute-start.11) | collective-permute-done | bytes 1312 | tf_op jit(solution)/shard_map/ppermute | solution.py:15
  88.4 2.3 %convolution_bitcast_fusion.1 = f32[80,2304]{1,0:T(8,128)} fusion(f32[80,2304]{0,1:T(8,128)S(1)} %bitcast.107, f32[80,80]{1,0:T(8,128)S(1)} %copy-done), kind=kOutput, calls=%fused_computation.7 | convolution fusion | flops 176947200 | bytes 1500160 | tf_op jit(solution)/shard_map/dot_general | solution.py:22
  90.7 1.5 %copy.93 = f32[80,2304]{0,1:T(8,128)S(1)} copy(f32[80,2304]{1,0:T(8,128)} %convolution_bitcast_fusion.1) | data formatting | bytes 1474560 | tf_op jit(solution)/shard_map/reshape | solution.py:25
  92.3 3.4 %collective-permute-start.12 = (bf16[80,1,384]{0,2,1:T(8,128)(2,1)S(1)}, bf16[80,1,384]{0,2,1:T(8,128)(2,1)S(1)}, u32[]{:S(2)}, u32[]{:S(2)}) collective-permute-start(bf16[80,1,384]{0,2,1:T(8,128)(2,1)S(1)} %get-tuple-element.18), channel_id=1, source_target_pairs={{0,4},{4,8},{8,12},{1,5},{5,9},{9,13},{2,6},{6,10},{10,14},{3,7},{... | collective-permute-start | bytes 184328 | tf_op jit(solution)/shard_map/ppermute | solution.py:12
  97.8 4.3 %collective-permute-done.13 = bf16[80,1,384]{0,2,1:T(8,128)(2,1)S(1)} collective-permute-done((bf16[80,1,384]{0,2,1:T(8,128)(2,1)S(1)}, bf16[80,1,384]{0,2,1:T(8,128)(2,1)S(1)}, u32[]{:S(2)}, u32[]{:S(2)}) %collective-permute-start.13) | collective-permute-done | bytes 61472 | tf_op jit(solution)/shard_map/ppermute | solution.py:15
  102.2 2.8 %collective-permute-start.14 = (bf16[80,8,1]{0,2,1:T(2,128)(2,1)S(1)}, bf16[80,8,1]{0,2,1:T(2,128)(2,1)S(1)}, u32[]{:S(2)}, u32[]{:S(2)}) collective-permute-start(bf16[80,8,1]{0,2,1:T(2,128)(2,1)S(1)} %get-tuple-element.10), channel_id=1, source_target_pairs={{0,1},{1,2},{2,3},{4,5},{5,6},{6,7},{8,9},{9,10},{10,11},{12,13},{... | collective-permute-start | bytes 3848 | tf_op jit(solution)/shard_map/ppermute | solution.py:12
  106.3 2.7 %collective-permute-done.15 = bf16[80,8,1]{0,2,1:T(2,128)(2,1)S(1)} collective-permute-done((bf16[80,8,1]{0,2,1:T(2,128)(2,1)S(1)}, bf16[80,8,1]{0,2,1:T(2,128)(2,1)S(1)}, u32[]{:S(2)}, u32[]{:S(2)}) %collective-permute-start.15) | collective-permute-done | bytes 1312 | tf_op jit(solution)/shard_map/ppermute | solution.py:15
  110.0 1.4 %fusion.31 = (bf16[80,2304]{1,0:T(8,128)(2,1)S(1)}, f32[80,2304]{1,0:T(8,128)S(1)}) fusion(f32[80,2304]{0,1:T(8,128)S(1)} %bitcast.106, f32[80,80]{1,0:T(8,128)S(1)} %copy-done), kind=kOutput, calls=%fused_computation.102 | convolution fusion | flops 177131520 | bytes 1868800 | tf_op jit(solution)/shard_map/dot_general | solution.py:22
  113.0 1.6 %scatter_custom_fusion.1 = f32[80,1024]{0,1:T(8,128)S(1)} fusion(s32[256]{0:T(256)} %bitcast.131, f32[]{:T(128)} %constant.21.clone.1, f32[80,256]{0,1:T(8,128)S(1)} %bitcast_subtract_fusion), kind=kCustom, calls=%fused_computation.53 | custom fusion | bytes 410112 | tf_op jit(solution)/shard_map/scatter | solution.py:106
  115.5 3.5 %all-to-all-start.2 = ((f32[80,4,256]{2,0,1:T(8,128)}), f32[80,4,256]{2,0,1:T(8,128)S(1)}, u32[]{:S(2)}, u32[]{:S(2)}) async-start(f32[80,4,256]{2,0,1:T(8,128)} %copy.84), calls=%async_computation.2 | async-start | bytes 655360 | tf_op jit(solution)/shard_map/all_to_all | solution.py:107
  119.9 8.8 %all-to-all-done.2 = f32[80,4,256]{2,0,1:T(8,128)S(1)} async-done(((f32[80,4,256]{2,0,1:T(8,128)}), f32[80,4,256]{2,0,1:T(8,128)S(1)}, u32[]{:S(2)}, u32[]{:S(2)}) %all-to-all-start.2) | async-done | bytes 327712 | tf_op jit(solution)/shard_map/all_to_all | solution.py:107
  129.0 6.9 %scatter_custom_fusion.2 = f32[80,2048]{0,1:T(8,128)S(1)} fusion(s32[1024]{0:T(1024)S(1)} %bitcast.127, f32[1024,80]{1,0:T(8,128)S(1)} %copy.86, f32[]{:T(128)} %constant.21.clone.1), kind=kCustom, calls=%fused_computation.50 | custom fusion | flops 81920 | bytes 655364 | tf_op jit(solution)/shard_map/scatter-add | solution.py:108
  (113 shorter events, 32.4 us)
Async XLA Ops:
  0.6 37.2 %copy-start = (f32[80,80]{1,0:T(8,128)S(1)}, f32[80,80]{1,0:T(8,128)}, u32[]{:S(2)}) copy-start(f32[80,80]{1,0:T(8,128)} %param.16) | copy-start | bytes 76804
  0.6 26.5 %copy-start.6 = (s32[1,1,256,1]{2,3,1,0:T(1,128)S(1)}, s32[1,1,256,1]{2,3,1,0:T(1,128)}, u32[]{:S(2)}) copy-start(s32[1,1,256,1]{2,3,1,0:T(1,128)} %param.17) | copy-start | bytes 3076
  0.7 27.8 %copy-start.4 = (bf16[80,8,256]{2,1,0:T(8,128)(2,1)S(1)}, bf16[80,8,256]{2,1,0:T(8,128)(2,1)}, u32[]{:S(2)}) copy-start(bf16[80,8,256]{2,1,0:T(8,128)(2,1)} %param.10) | copy-start | bytes 983044
  0.7 27.1 %copy-start.1 = (s32[24]{0:T(128)S(1)}, s32[24]{0:T(128)}, u32[]{:S(2)}) copy-start(s32[24]{0:T(128)} %param.19) | copy-start | bytes 292
  3.7 24.7 %copy-start.7 = (s32[256]{0:T(256)}, s32[256]{0:T(256)S(1)}, u32[]{:S(2)}) copy-start(s32[256]{0:T(256)S(1)} %fusion.22) | copy-start | bytes 3076
  4.4 53.0 %copy-start.13 = (s32[256,1]{0,1:T(1,128)}, s32[256,1]{0,1:T(1,128)S(1)}, u32[]{:S(2)}) copy-start(s32[256,1]{0,1:T(1,128)S(1)} %compare_select_fusion.2) | copy-start | bytes 3076
  6.5 21.9 %all-to-all-start = ((s32[4,256,1]{1,2,0:T(1,128)}), s32[4,256,1]{1,2,0:T(1,128)S(1)}, u32[]{:S(2)}, u32[]{:S(2)}) async-start(s32[4,256,1]{1,2,0:T(1,128)} %bitcast.9), calls=%async_computation | async-start | bytes 8192 | tf_op jit(solution)/shard_map/all_to_all | solution.py:83
  14.1 14.4 %collective-permute-start = (bf16[80,1,256]{2,1,0:T(2,128)(2,1)S(1)}, bf16[80,1,256]{2,1,0:T(2,128)(2,1)S(1)}, u32[]{:S(2)}, u32[]{:S(2)}) collective-permute-start(bf16[80,1,256]{2,1,0:T(2,128)(2,1)S(1)} %get-tuple-element.24), channel_id=1, source_target_pairs={{0,4},{4,8},{8,12},{1,5},{5,9},{9,13},{2,6},{6,10},{10,14},{3,7},{... | collective-permute-start | bytes 122888 | tf_op jit(solution)/shard_map/ppermute | solution.py:12
  18.0 10.4 %collective-permute-start.1 = (bf16[80,1,256]{2,1,0:T(2,128)(2,1)S(1)}, bf16[80,1,256]{2,1,0:T(2,128)(2,1)S(1)}, u32[]{:S(2)}, u32[]{:S(2)}) collective-permute-start(bf16[80,1,256]{2,1,0:T(2,128)(2,1)S(1)} %get-tuple-element.25), channel_id=1, source_target_pairs={{4,0},{8,4},{12,8},{5,1},{9,5},{13,9},{6,2},{10,6},{14,10},{7,3},{... | collective-permute-start | bytes 122888 | tf_op jit(solution)/shard_map/ppermute | solution.py:15
  21.3 27.8 %collective-permute-start.4 = (bf16[80,1,384]{0,2,1:T(8,128)(2,1)}, bf16[80,1,384]{0,2,1:T(8,128)(2,1)S(1)}, u32[]{:S(2)}, u32[]{:S(2)}) collective-permute-start(bf16[80,1,384]{0,2,1:T(8,128)(2,1)} %get-tuple-element.22), channel_id=1, source_target_pairs={{0,4},{4,8},{8,12},{1,5},{5,9},{9,13},{2,6},{6,10},{10,14},{3,7},{... | collective-permute-start | bytes 184328 | tf_op jit(solution)/shard_map/ppermute | solution.py:12
  25.9 23.2 %collective-permute-start.5 = (bf16[80,1,384]{0,2,1:T(8,128)(2,1)S(1)}, bf16[80,1,384]{0,2,1:T(8,128)(2,1)S(1)}, u32[]{:S(2)}, u32[]{:S(2)}) collective-permute-start(bf16[80,1,384]{0,2,1:T(8,128)(2,1)S(1)} %get-tuple-element.23), channel_id=1, source_target_pairs={{4,0},{8,4},{12,8},{5,1},{9,5},{13,9},{6,2},{10,6},{14,10},{7,3},{... | collective-permute-start | bytes 184328 | tf_op jit(solution)/shard_map/ppermute | solution.py:15
  29.1 2.6 %collective-permute-start.2 = (bf16[80,10,1]{2,1,0:T(8,128)(2,1)S(1)}, bf16[80,10,1]{2,1,0:T(8,128)(2,1)S(1)}, u32[]{:S(2)}, u32[]{:S(2)}) collective-permute-start(bf16[80,10,1]{2,1,0:T(8,128)(2,1)S(1)} %get-tuple-element.16), channel_id=1, source_target_pairs={{0,1},{1,2},{2,3},{4,5},{5,6},{6,7},{8,9},{9,10},{10,11},{12,13},{... | collective-permute-start | bytes 4808 | tf_op jit(solution)/shard_map/ppermute | solution.py:12
  30.4 5.2 %collective-permute-start.3 = (bf16[80,10,1]{2,1,0:T(8,128)(2,1)S(1)}, bf16[80,10,1]{2,1,0:T(8,128)(2,1)S(1)}, u32[]{:S(2)}, u32[]{:S(2)}) collective-permute-start(bf16[80,10,1]{2,1,0:T(8,128)(2,1)S(1)} %get-tuple-element.17), channel_id=1, source_target_pairs={{1,0},{2,1},{3,2},{5,4},{6,5},{7,6},{9,8},{10,9},{11,10},{13,12},{... | collective-permute-start | bytes 4808 | tf_op jit(solution)/shard_map/ppermute | solution.py:15
  31.7 5.0 %copy-start.15 = (f32[80]{0:T(128)S(1)}, f32[80]{0:T(128)}, u32[]{:S(2)}) copy-start(f32[80]{0:T(128)} %param.12) | copy-start | bytes 964
  42.7 17.6 %all-to-all-start.1 = ((f32[80,4,256]{2,0,1:T(8,128)}), f32[80,4,256]{2,0,1:T(8,128)S(1)}, u32[]{:S(2)}, u32[]{:S(2)}) async-start(f32[80,4,256]{2,0,1:T(8,128)} %broadcast_select_fusion), calls=%async_computation.1 | async-start | bytes 655360 | tf_op jit(solution)/shard_map/all_to_all | solution.py:84
  49.1 8.4 %copy-start.5 = (bf16[80,1,384]{0,2,1:T(8,128)(2,1)}, bf16[80,1,384]{0,2,1:T(8,128)(2,1)S(1)}, u32[]{:S(2)}) copy-start(bf16[80,1,384]{0,2,1:T(8,128)(2,1)S(1)} %collective-permute-done.5) | copy-start | bytes 184324
  49.1 8.3 %collective-permute-start.6 = (bf16[80,8,1]{0,2,1:T(2,128)(2,1)S(1)}, bf16[80,8,1]{0,2,1:T(2,128)(2,1)S(1)}, u32[]{:S(2)}, u32[]{:S(2)}) collective-permute-start(bf16[80,8,1]{0,2,1:T(2,128)(2,1)S(1)} %get-tuple-element.14), channel_id=1, source_target_pairs={{0,1},{1,2},{2,3},{4,5},{5,6},{6,7},{8,9},{9,10},{10,11},{12,13},{... | collective-permute-start | bytes 3848 | tf_op jit(solution)/shard_map/ppermute | solution.py:12
  56.1 3.1 %collective-permute-start.7 = (bf16[80,8,1]{0,2,1:T(2,128)(2,1)S(1)}, bf16[80,8,1]{0,2,1:T(2,128)(2,1)S(1)}, u32[]{:S(2)}, u32[]{:S(2)}) collective-permute-start(bf16[80,8,1]{0,2,1:T(2,128)(2,1)S(1)} %get-tuple-element.15), channel_id=1, source_target_pairs={{1,0},{2,1},{3,2},{5,4},{6,5},{7,6},{9,8},{10,9},{11,10},{13,12},{... | collective-permute-start | bytes 3848 | tf_op jit(solution)/shard_map/ppermute | solution.py:15
  70.4 5.8 %collective-permute-start.8 = (bf16[80,1,384]{0,2,1:T(8,128)(2,1)S(1)}, bf16[80,1,384]{0,2,1:T(8,128)(2,1)S(1)}, u32[]{:S(2)}, u32[]{:S(2)}) collective-permute-start(bf16[80,1,384]{0,2,1:T(8,128)(2,1)S(1)} %get-tuple-element.20), channel_id=1, source_target_pairs={{0,4},{4,8},{8,12},{1,5},{5,9},{9,13},{2,6},{6,10},{10,14},{3,7},{... | collective-permute-start | bytes 184328 | tf_op jit(solution)/shard_map/ppermute | solution.py:12
  74.0 6.5 %collective-permute-start.9 = (bf16[80,1,384]{0,2,1:T(8,128)(2,1)S(1)}, bf16[80,1,384]{0,2,1:T(8,128)(2,1)S(1)}, u32[]{:S(2)}, u32[]{:S(2)}) collective-permute-start(bf16[80,1,384]{0,2,1:T(8,128)(2,1)S(1)} %get-tuple-element.21), channel_id=1, source_target_pairs={{4,0},{8,4},{12,8},{5,1},{9,5},{13,9},{6,2},{10,6},{14,10},{7,3},{... | collective-permute-start | bytes 184328 | tf_op jit(solution)/shard_map/ppermute | solution.py:15
  80.6 4.3 %collective-permute-start.10 = (bf16[80,8,1]{0,2,1:T(2,128)(2,1)S(1)}, bf16[80,8,1]{0,2,1:T(2,128)(2,1)S(1)}, u32[]{:S(2)}, u32[]{:S(2)}) collective-permute-start(bf16[80,8,1]{0,2,1:T(2,128)(2,1)S(1)} %get-tuple-element.12), channel_id=1, source_target_pairs={{0,1},{1,2},{2,3},{4,5},{5,6},{6,7},{8,9},{9,10},{10,11},{12,13},{... | collective-permute-start | bytes 3848 | tf_op jit(solution)/shard_map/ppermute | solution.py:12
  83.4 4.3 %copy-start.9 = (f32[6]{0:T(128)S(1)}, f32[6]{0:T(128)}, u32[]{:S(2)}) copy-start(f32[6]{0:T(128)} %get-tuple-element.26) | copy-start | bytes 76
  83.4 4.3 %copy-start.10 = (f32[6]{0:T(128)S(1)}, f32[6]{0:T(128)}, u32[]{:S(2)}) copy-start(f32[6]{0:T(128)} %get-tuple-element.27) | copy-start | bytes 76
  83.4 4.0 %collective-permute-start.11 = (bf16[80,8,1]{0,2,1:T(2,128)(2,1)S(1)}, bf16[80,8,1]{0,2,1:T(2,128)(2,1)S(1)}, u32[]{:S(2)}, u32[]{:S(2)}) collective-permute-start(bf16[80,8,1]{0,2,1:T(2,128)(2,1)S(1)} %get-tuple-element.13), channel_id=1, source_target_pairs={{1,0},{2,1},{3,2},{5,4},{6,5},{7,6},{9,8},{10,9},{11,10},{13,12},{... | collective-permute-start | bytes 3848 | tf_op jit(solution)/shard_map/ppermute | solution.py:15
  92.1 14.2 %copy-start.8 = (s32[256]{0:T(256)S(1)}, s32[256]{0:T(256)}, u32[]{:S(2)}) copy-start(s32[256]{0:T(256)} %copy-done.7) | copy-start | bytes 3076
  92.3 5.6 %collective-permute-start.12 = (bf16[80,1,384]{0,2,1:T(8,128)(2,1)S(1)}, bf16[80,1,384]{0,2,1:T(8,128)(2,1)S(1)}, u32[]{:S(2)}, u32[]{:S(2)}) collective-permute-start(bf16[80,1,384]{0,2,1:T(8,128)(2,1)S(1)} %get-tuple-element.18), channel_id=1, source_target_pairs={{0,4},{4,8},{8,12},{1,5},{5,9},{9,13},{2,6},{6,10},{10,14},{3,7},{... | collective-permute-start | bytes 184328 | tf_op jit(solution)/shard_map/ppermute | solution.py:12
  95.6 6.5 %collective-permute-start.13 = (bf16[80,1,384]{0,2,1:T(8,128)(2,1)S(1)}, bf16[80,1,384]{0,2,1:T(8,128)(2,1)S(1)}, u32[]{:S(2)}, u32[]{:S(2)}) collective-permute-start(bf16[80,1,384]{0,2,1:T(8,128)(2,1)S(1)} %get-tuple-element.19), channel_id=1, source_target_pairs={{4,0},{8,4},{12,8},{5,1},{9,5},{13,9},{6,2},{10,6},{14,10},{7,3},{... | collective-permute-start | bytes 184328 | tf_op jit(solution)/shard_map/ppermute | solution.py:15
  102.2 4.2 %collective-permute-start.14 = (bf16[80,8,1]{0,2,1:T(2,128)(2,1)S(1)}, bf16[80,8,1]{0,2,1:T(2,128)(2,1)S(1)}, u32[]{:S(2)}, u32[]{:S(2)}) collective-permute-start(bf16[80,8,1]{0,2,1:T(2,128)(2,1)S(1)} %get-tuple-element.10), channel_id=1, source_target_pairs={{0,1},{1,2},{2,3},{4,5},{5,6},{6,7},{8,9},{9,10},{10,11},{12,13},{... | collective-permute-start | bytes 3848 | tf_op jit(solution)/shard_map/ppermute | solution.py:12
  105.0 4.0 %collective-permute-start.15 = (bf16[80,8,1]{0,2,1:T(2,128)(2,1)S(1)}, bf16[80,8,1]{0,2,1:T(2,128)(2,1)S(1)}, u32[]{:S(2)}, u32[]{:S(2)}) collective-permute-start(bf16[80,8,1]{0,2,1:T(2,128)(2,1)S(1)} %get-tuple-element.11), channel_id=1, source_target_pairs={{1,0},{2,1},{3,2},{5,4},{6,5},{7,6},{9,8},{10,9},{11,10},{13,12},{... | collective-permute-start | bytes 3848 | tf_op jit(solution)/shard_map/ppermute | solution.py:15
  113.0 6.0 %copy-start.3 = (f32[2048,80]{0,1:T(8,128)S(1)}, f32[2048,80]{0,1:T(8,128)}, u32[]{:S(2)}) copy-start(f32[2048,80]{0,1:T(8,128)} %copy-done.2) | copy-start | bytes 1966084
  115.5 13.3 %all-to-all-start.2 = ((f32[80,4,256]{2,0,1:T(8,128)}), f32[80,4,256]{2,0,1:T(8,128)S(1)}, u32[]{:S(2)}, u32[]{:S(2)}) async-start(f32[80,4,256]{2,0,1:T(8,128)} %copy.84), calls=%async_computation.2 | async-start | bytes 655360 | tf_op jit(solution)/shard_map/all_to_all | solution.py:107
  129.0 7.3 %copy-start.16 = (f32[80]{0:T(128)S(1)}, f32[80]{0:T(128)}, u32[]{:S(2)}) copy-start(f32[80]{0:T(128)} %param.15) | copy-start | bytes 964
  (4 other events, 12.7 us)
where the time goes:
time: 140 us; the launch traced here: 137 us
  starting transfers between devices  55.4 us (40%)
  waiting for transfers between devices  30.1 us (22%)
  local copies, waits for them, and re-layouts  22.6 us (16%)
  other arithmetic  21 us (15%)
  matrix products  6.7 us (5%)
    ppermute x8, starting transfers between devices, extended(): lax.ppermute(lax.slice_in_dim(block, block.shape[dim] - width, None, axis...  29.4 us
    ppermute x8, waiting for transfers between devices, extended(): lax.ppermute(lax.slice_in_dim(block, 0, width, axis=dim), axis, backward)  19.5 us
    ppermute x8, starting transfers between devices, extended(): lax.ppermute(lax.slice_in_dim(block, 0, width, axis=dim), axis, backward)  10.5 us
    all_to_all x1, waiting for transfers between devices, body(): lax.all_to_all(outgoing, 'gx', split_axis=1, concat_axis=1, tiled=True)  8.82 us
    scatter-add x1, other arithmetic, body(): summed = jnp.zeros_like(flat_parent).at[:, served_ids].add(incoming)  6.87 us
    dot_general x4, matrix products, mix_levels(): jnp.dot(matrix, flat_values, precision=lax.Precision.HIGHEST, preferred_e...  6.7 us
    all_to_all x1, starting transfers between devices, body(): lax.all_to_all(wanted, 'gx', split_axis=0, concat_axis=0, tiled=True)  6.35 us
    all_to_all x1, starting transfers between devices, body(): lax.all_to_all(jnp.take(flat_parent, served_ids, axis=1), 'gx', split_axi...  5.71 us
  transfers between devices with their start and end apart: 19, of which 9 were waited for; matrix products, arithmetic and copies ran while one was open for 11% of the time, Pallas kernels for 0%

commit v1 on v0

v1 whole, which is shorter than its diff:
```python
import jax
import jax.numpy as jnp
from jax import lax
from jax.sharding import PartitionSpec as P

Y_AXES = ("gy", "gz")


def shift_pairs(count):
    forward = [(i, i + 1) for i in range(count - 1)]
    backward = [(i + 1, i) for i in range(count - 1)]
    return forward, backward


def exchange(blocks):
    fwd_x, bwd_x = shift_pairs(lax.axis_size("gx"))
    fwd_y, bwd_y = shift_pairs(lax.axis_size(Y_AXES))
    widths = [b.shape[2] for b in blocks]
    heights = [b.shape[1] for b in blocks]
    last_rows = jnp.concatenate([b[:, -1, :] for b in blocks], axis=1)
    first_rows = jnp.concatenate([b[:, 0, :] for b in blocks], axis=1)
    last_cols = jnp.concatenate([b[:, :, -1] for b in blocks], axis=1)
    first_cols = jnp.concatenate([b[:, :, 0] for b in blocks], axis=1)
    above = lax.ppermute(last_rows, "gx", fwd_x)
    below = lax.ppermute(first_rows, "gx", bwd_x)
    left = lax.ppermute(last_cols, Y_AXES, fwd_y)
    right = lax.ppermute(first_cols, Y_AXES, bwd_y)
    out = []
    xo = 0
    yo = 0
    for w, h in zip(widths, heights):
        out.append(
            (
                above[:, xo : xo + w],
                below[:, xo : xo + w],
                left[:, yo : yo + h],
                right[:, yo : yo + h],
            )
        )
        xo += w
        yo += h
    return out


def neighbours(centre, halo):
    above, below, left, right = (h.astype(centre.dtype) for h in halo)
    up = jnp.concatenate([above[:, None, :], centre[:, :-1, :]], axis=1)
    down = jnp.concatenate([centre[:, 1:, :], below[:, None, :]], axis=1)
    west = jnp.concatenate([left[:, :, None], centre[:, :, :-1]], axis=2)
    east = jnp.concatenate([centre[:, :, 1:], right[:, :, None]], axis=2)
    return up, down, west, east


def mix_levels(matrix, values):
    return jnp.einsum(
        "kl,lrc->krc",
        matrix,
        values,
        precision=lax.Precision.HIGHEST,
        preferred_element_type=jnp.float32,
    )


def nest_segments(nest_of, first, count):
    index_rows = first + jnp.arange(count, dtype=jnp.int32)
    inside = (index_rows >= 0) & (index_rows < nest_of.shape[0])
    return jnp.where(inside, nest_of[jnp.clip(index_rows, 0, nest_of.shape[0] - 1)], -1)


def row_weights(segments):
    left_w = (segments[:-2] == segments[1:-1]).astype(jnp.float32)
    right_w = (segments[2:] == segments[1:-1]).astype(jnp.float32)
    return (left_w, right_w)


def nest_advance(state, halo, target, nu_nest, relax, vert_mix, left_w, right_w):
    up, down, west, east = neighbours(state, halo)
    stencil_sum = (
        down * right_w[None, :, None] + up * left_w[None, :, None] + east + west - 4.0 * state
    )
    moved = state + nu_nest[:, None, None] * stencil_sum
    moved = moved + relax[:, None, None] * (target - moved)
    return mix_levels(vert_mix, moved)


def body(parent, nest, nu_parent, nu_nest, relax, feedback, vert_mix, fp_owner, fp_cell, nest_of):
    levels = parent.shape[0]
    tiles_x = lax.axis_size("gx")
    here_x = lax.axis_index("gx")

    parent_halo, nest_halo = exchange([parent, nest])
    centre = parent.astype(jnp.float32)
    up, down, west, east = neighbours(centre, parent_halo)
    stencil = down + up + east + west - 4.0 * centre
    stepped = mix_levels(vert_mix, centre + nu_parent[:, None, None] * stencil)
    flat_parent = stepped.reshape(levels, -1)

    owners = fp_owner.reshape(-1)
    cells = fp_cell.reshape(-1)
    requests = owners.shape[0]
    slots = 4 * requests // tiles_x
    onehot = (owners[:, None] == jnp.arange(tiles_x, dtype=jnp.int32)[None, :]).astype(jnp.int32)
    before = jnp.cumsum(onehot, axis=0) - onehot
    order_in = jnp.sum(before * onehot, axis=1)
    places = owners * slots + order_in
    wanted = jnp.zeros((tiles_x * slots,), jnp.int32).at[places].set(cells)
    served_ids = lax.all_to_all(wanted, "gx", split_axis=0, concat_axis=0, tiled=True)
    answers = lax.all_to_all(
        jnp.take(flat_parent, served_ids, axis=1), "gx", split_axis=1, concat_axis=1, tiled=True
    )
    forcing_flat = jnp.take(answers, places, axis=1)

    nest_rows = nest.shape[1]
    nest_cols = nest.shape[2]
    block_rows = nest_rows // 3
    block_cols = nest_cols // 3
    forcing_block = forcing_flat.reshape(levels, block_rows, block_cols)
    row_start = here_x * nest_rows
    forcing_full = jnp.repeat(jnp.repeat(forcing_block, 3, axis=1), 3, axis=2)
    left_w, right_w = row_weights(nest_segments(nest_of, row_start - 1, nest_rows + 2))

    nest_state = nest.astype(jnp.float32)
    halo = nest_halo
    for turn_no in range(3):
        if turn_no > 0:
            (halo,) = exchange([nest_state.astype(jnp.bfloat16)])
        nest_state = nest_advance(
            nest_state, halo, forcing_full, nu_nest, relax, vert_mix, left_w, right_w
        )

    blocks = nest_state.reshape(levels, block_rows, 3, block_cols, 3).mean(axis=(2, 4))
    nudge_gap = (blocks - forcing_block).reshape(levels, -1)
    outgoing = jnp.zeros((levels, tiles_x * slots), jnp.float32).at[:, places].set(nudge_gap)
    incoming = lax.all_to_all(outgoing, "gx", split_axis=1, concat_axis=1, tiled=True)
    summed = jnp.zeros_like(flat_parent).at[:, served_ids].add(incoming)
    parent_out = (stepped + feedback[:, None, None] * summed.reshape(stepped.shape)).astype(
        jnp.bfloat16
    )
    return (parent_out, nest_state.astype(jnp.bfloat16))


def solution(mesh):
    placed = (
        P("groups", "gx", Y_AXES),
        P("groups", "gx", Y_AXES),
        P(),
        P(),
        P(),
        P(),
        P(),
        P("gx", Y_AXES, None, None),
        P("gx", Y_AXES, None),
        P(),
    )
    return jax.shard_map(
        body,
        mesh=mesh,
        in_specs=placed,
        out_specs=(P("groups", "gx", Y_AXES), P("groups", "gx", Y_AXES)),
        check_vma=False,
    )
```

time: 140 us -> 136 us (0.971)
  starting transfers between devices: 55.4 us -> 35.5 us
  waiting for transfers between devices: 30.1 us -> 15.7 us
  blocking collectives: 0 us -> 14.1 us
  local copies, waits for them, and re-layouts: 22.6 us -> 35.8 us
  matrix products: 6.7 us -> 10.6 us
    ppermute x16 -> x12, starting transfers between devices: 39.9 us -> 25 us  [the longest x3 10.3 us: exchange(): above = lax.ppermute(last_rows, 'gx', fwd_x)]
    all_to_all x0 -> x1, blocking collectives: none -> 14.1 us  [body(): lax.all_to_all(outgoing, 'gx', split_axis=1, concat_axis=1, tiled=True)]
    ppermute x16 -> x12, waiting for transfers between devices: 21.3 us -> 8.07 us  [the longest x3 8.05 us: exchange(): below = lax.ppermute(first_rows, 'gx', bwd_x)]
    all_to_all x1 -> x0, waiting for transfers between devices: 8.82 us -> none  [body(): lax.all_to_all(outgoing, 'gx', split_axis=1, concat_axis=1, tiled=True)]
    slice x7 -> x15, local copies, waits for them, and re-layouts: 2.25 us -> 10.5 us  [the longest x4 3.96 us: neighbours(): west = jnp.concatenate([left[:, :, None], centre[:, :, :-1]], axis=2)]
    all_to_all x1, waiting for transfers between devices: 0.01 us -> 7.59 us  [body(): lax.all_to_all(jnp.take(flat_parent, served_ids, axis=1), 'gx', split_axi...]
    broadcast_in_dim x0 -> x16, other arithmetic: none -> 6.26 us  [the longest x4 3.12 us: neighbours(): up = jnp.concatenate([above[:, None, :], centre[:, :-1, :]], axis=1)]
    broadcast_in_dim x0 -> x10, local copies, waits for them, and re-layouts: none -> 4.25 us  [the longest x4 2.05 us: neighbours(): west = jnp.concatenate([left[:, :, None], centre[:, :, :-1]], axis=2)]
  transfers between devices with their start and end apart: 19 -> 14, of which waited for: 9 -> 3; matrix products, arithmetic and copies ran while one was open for 11% -> 13% of each run, Pallas kernels for 0% -> 0%
where the time goes in v1:
time: 136 us; the launch traced here: 135 us
  local copies, waits for them, and re-layouts  35.8 us (26%)
  starting transfers between devices  35.5 us (26%)
  other arithmetic  21.5 us (16%)
  waiting for transfers between devices  15.7 us (12%)
  blocking collectives  14.1 us (10%)
  matrix products  10.6 us (8%)
    all_to_all x1, blocking collectives, body(): lax.all_to_all(outgoing, 'gx', split_axis=1, concat_axis=1, tiled=True)  14.1 us
    dot_general x4, matrix products, mix_levels(): jnp.einsum('kl,lrc->krc', matrix, values, precision=lax.Precision.HIGHEST...  10.6 us
    ppermute x3, starting transfers between devices, exchange(): above = lax.ppermute(last_rows, 'gx', fwd_x)  10.3 us
    ppermute x3, waiting for transfers between devices, exchange(): below = lax.ppermute(first_rows, 'gx', bwd_x)  8.05 us
    scatter-add x1, other arithmetic, body(): summed = jnp.zeros_like(flat_parent).at[:, served_ids].add(incoming)  7.61 us
    all_to_all x1, waiting for transfers between devices, body(): lax.all_to_all(jnp.take(flat_parent, served_ids, axis=1), 'gx', split_axi...  7.59 us
    ppermute x3, starting transfers between devices, exchange(): left = lax.ppermute(last_cols, Y_AXES, fwd_y)  6.8 us
    all_to_all x1, starting transfers between devices, body(): lax.all_to_all(wanted, 'gx', split_axis=0, concat_axis=0, tiled=True)  6.35 us
  transfers between devices with their start and end apart: 14, of which 3 were waited for; matrix products, arithmetic and copies ran while one was open for 13% of the time, Pallas kernels for 0%

profile of v1, /device:TPU:0, one launch (start us, length us, event | category | flops | bytes accessed | tf_op | source)
XLA Modules:
  0.0 134.5 jit_solution(8841769482351864123)
XLA Ops:
  4.4 2.1 %scatter_custom_fusion = s32[1024]{0:T(1024)} fusion(s32[256]{0:T(256)S(1)} %bitcast.202, s32[256]{0:T(256)} %bitcast.206, s32[]{:T(128)} %constant.22.clone.1), kind=kCustom, calls=%fused_computation.141 | custom fusion | bytes 4608 | tf_op jit(solution)/shard_map/scatter | solution.py:106
  6.5 6.3 %all-to-all-start = ((s32[4,256,1]{1,2,0:T(1,128)}), s32[4,256,1]{1,2,0:T(1,128)S(1)}, u32[]{:S(2)}, u32[]{:S(2)}) async-start(s32[4,256,1]{1,2,0:T(1,128)} %bitcast.22), calls=%async_computation | async-start | bytes 8192 | tf_op jit(solution)/shard_map/all_to_all | solution.py:107
  15.0 1.3 collective-permute-start
  17.0 5.2 %collective-permute-start.1 = (bf16[80,640]{1,0:T(8,128)(2,1)}, bf16[80,640]{1,0:T(8,128)(2,1)}, u32[]{:S(2)}, u32[]{:S(2)}) collective-permute-start(bf16[80,640]{1,0:T(8,128)(2,1)} %pad_maximum_fusion.1), channel_id=1, source_target_pairs={{0,4},{4,8},{8,12},{1,5},{5,9},{9,13},{2,6},{6,10},{10,14},{3,7},{... | collective-permute-start | bytes 307208 | tf_op jit(solution)/shard_map/ppermute | solution.py:24
  23.7 1.3 collective-permute-start.2
  25.3 3.0 %collective-permute-start.3 = (bf16[80,14]{0,1:T(8,128)(2,1)S(1)}, bf16[80,14]{0,1:T(8,128)(2,1)S(1)}, u32[]{:S(2)}, u32[]{:S(2)}) collective-permute-start(bf16[80,14]{0,1:T(8,128)(2,1)S(1)} %pad_maximum_fusion.3), channel_id=1, source_target_pairs={{0,1},{1,2},{2,3},{4,5},{5,6},{6,7},{8,9},{9,10},{10,11},{12,13},{... | collective-permute-start | bytes 6728 | tf_op jit(solution)/shard_map/ppermute | solution.py:26
  35.6 1.7 %fusion.37 = f32[80,8,256]{2,1,0:T(8,128)S(1)} fusion(f32[80,1,256]{2,1,0:T(1,128)S(1)} %copy.152, f32[80,7,256]{2,1,0:T(8,128)S(1)} %get-tuple-element.45, f32[80,7,256]{2,1,0:T(8,128)S(1)} %get-tuple-element.44, f32[80,1,256]{2,1,0:T(1,128)S(1)} %copy.154, f32[80,8,1]{2,1,0:T(8,128)} %copy.157, f32[80,8,255]{2,1,0:T(8,128)S(1)} %get-tuple-element.41, ...), kind=kLoop, calls=%fused_computation.51 | loop fusion | flops 1966080 | bytes 3604800 | tf_op jit(solution)/shard_map/add | solution.py:95
  38.5 2.8 %gather_fusion.1 = f32[1024,80]{1,0:T(8,128)S(1)} fusion(f32[80,2048]{0,1:T(8,128)S(1)} %bitcast.179, s32[1024]{0:T(1024)S(1)} %broadcast_clamp_fusion), kind=kCustom, calls=%fused_computation.1 | custom fusion | bytes 659456 | tf_op jit(solution)/shard_map/jit(_take)/gather | solution.py:109
  42.3 4.2 %all-to-all-start.1 = ((f32[80,4,256]{2,0,1:T(8,128)}), f32[80,4,256]{2,0,1:T(8,128)S(1)}, u32[]{:S(2)}, u32[]{:S(2)}) async-start(f32[80,4,256]{2,0,1:T(8,128)} %broadcast_select_fusion), calls=%async_computation.1 | async-start | bytes 655360 | tf_op jit(solution)/shard_map/all_to_all | solution.py:108
  47.5 1.5 %fusion.61 = f32[80,1,384]{2,0,1:T(8,128)} fusion(bf16[80,640]{1,0:T(8,128)(2,1)} %collective-permute-done), kind=kLoop, calls=%fused_computation.93 | loop fusion | flops 30720 | bytes 184320 | tf_op jit(solution)/shard_map/broadcast_in_dim | solution.py:48
  48.9 1.5 %fusion.60 = f32[80,1,384]{2,0,1:T(8,128)} fusion(bf16[80,640]{1,0:T(8,128)(2,1)} %collective-permute-done.1), kind=kLoop, calls=%fused_computation.91 | loop fusion | flops 30720 | bytes 184320 | tf_op jit(solution)/shard_map/broadcast_in_dim | solution.py:47
  50.4 7.6 %all-to-all-done.1 = f32[80,4,256]{2,0,1:T(8,128)S(1)} async-done(((f32[80,4,256]{2,0,1:T(8,128)}), f32[80,4,256]{2,0,1:T(8,128)S(1)}, u32[]{:S(2)}, u32[]{:S(2)}) %all-to-all-start.1) | async-done | bytes 327712 | tf_op jit(solution)/shard_map/all_to_all | solution.py:108
  59.9 1.4 %reshape.165 = f32[80,6,384]{0,2,1:T(8,128)} reshape(f32[80,6,128,3]{0,3,2,1:T(4,128)S(1)} %broadcast_in_dim.179) | data formatting | bytes 1474560 | tf_op jit(solution)/shard_map/reshape | solution.py:119
  61.3 1.7 %copy.170 = f32[80,6,384]{2,0,1:T(8,128)S(1)} copy(f32[80,6,384]{0,2,1:T(8,128)} %reshape.165) | data formatting | bytes 1474560 | tf_op jit(solution)/shard_map/reshape | solution.py:119
  63.0 3.0 %fusion.95 = (bf16[80,6,384]{2,0,1:T(8,128)(2,1)S(1)}, f32[80,6,384]{2,0,1:T(8,128)S(1)}) fusion(f32[80,80]{1,0:T(8,128)S(1)} %copy-done, f32[80,6,384]{2,0,1:T(8,128)S(1)} %copy.170, f32[80,6,383]{2,0,1:T(8,128)S(1)} %copy-done.4, f32[80,6,1]{2,0,1:T(8,128)S(1)} %copy.165, f32[80,6,1]{2,0,1:T(8,128)} %copy.164, f32[80,6,383]{2,0,1:T(8,128)} %get-tuple-element.31, ...), kind=kOutput, calls=%fused_computation.168 | convolution fusion | flops 180264960 | bytes 5187248 | tf_op jit(solution)/shard_map/kl,lrc->krc/dot_general | solution.py:55
  67.1 1.3 fusion.86
  68.7 1.9 %collective-permute-start.7 = (bf16[80,6]{0,1:T(8,128)(2,1)S(1)}, bf16[80,6]{0,1:T(8,128)(2,1)S(1)}, u32[]{:S(2)}, u32[]{:S(2)}) collective-permute-start(bf16[80,6]{0,1:T(8,128)(2,1)S(1)} %get-tuple-element.16), channel_id=1, source_target_pairs={{0,1},{1,2},{2,3},{4,5},{5,6},{6,7},{8,9},{9,10},{10,11},{12,13},{... | collective-permute-start | bytes 2888 | tf_op jit(solution)/shard_map/ppermute | solution.py:26
  70.6 1.3 collective-permute-start.6
  71.9 1.7 %collective-permute-start.5 = (bf16[80,384]{1,0:T(8,128)(2,1)S(1)}, bf16[80,384]{1,0:T(8,128)(2,1)S(1)}, u32[]{:S(2)}, u32[]{:S(2)}) collective-permute-start(bf16[80,384]{1,0:T(8,128)(2,1)S(1)} %get-tuple-element.28), channel_id=1, source_target_pairs={{0,4},{4,8},{8,12},{1,5},{5,9},{9,13},{2,6},{6,10},{10,14},{3,7},{... | collective-permute-start | bytes 184328 | tf_op jit(solution)/shard_map/ppermute | solution.py:24
  73.6 1.3 collective-permute-start.4
  76.0 4.3 %collective-permute-done.4 = bf16[80,384]{1,0:T(8,128)(2,1)S(1)} collective-permute-done((bf16[80,384]{1,0:T(8,128)(2,1)S(1)}, bf16[80,384]{1,0:T(8,128)(2,1)S(1)}, u32[]{:S(2)}, u32[]{:S(2)}) %collective-permute-start.4) | collective-permute-done | bytes 61472 | tf_op jit(solution)/shard_map/ppermute | solution.py:25
  80.3 3.1 %fusion.96 = (bf16[80,6,384]{2,0,1:T(8,128)(2,1)S(1)}, f32[80,6,384]{2,0,1:T(8,128)S(1)}) fusion(f32[80,80]{1,0:T(8,128)S(1)} %copy-done, f32[80,6,384]{2,0,1:T(8,128)S(1)} %copy.170, f32[80,6,384]{2,0,1:T(8,128)S(1)} %get-tuple-element.49, f32[80,6,383]{2,0,1:T(8,128)} %get-tuple-element.22, f32[80,6,1]{2,0,1:T(8,128)} %copy.172, ...), kind=kOutput, calls=%fused_computation.169 | convolution fusion | flops 180080640 | bytes 5555888 | tf_op jit(solution)/shard_map/kl,lrc->krc/dot_general | solution.py:55
  85.9 1.9 %collective-permute-start.11 = (bf16[80,6]{0,1:T(8,128)(2,1)S(1)}, bf16[80,6]{0,1:T(8,128)(2,1)S(1)}, u32[]{:S(2)}, u32[]{:S(2)}) collective-permute-start(bf16[80,6]{0,1:T(8,128)(2,1)S(1)} %get-tuple-element.14), channel_id=1, source_target_pairs={{0,1},{1,2},{2,3},{4,5},{5,6},{6,7},{8,9},{9,10},{10,11},{12,13},{... | collective-permute-start | bytes 2888 | tf_op jit(solution)/shard_map/ppermute | solution.py:26
  89.7 3.4 %collective-permute-start.9 = (bf16[80,384]{1,0:T(8,128)(2,1)}, bf16[80,384]{1,0:T(8,128)(2,1)}, u32[]{:S(2)}, u32[]{:S(2)}) collective-permute-start(bf16[80,384]{1,0:T(8,128)(2,1)} %get-tuple-element.26), channel_id=1, source_target_pairs={{0,4},{4,8},{8,12},{1,5},{5,9},{9,13},{2,6},{6,10},{10,14},{3,7},{... | collective-permute-start | bytes 184328 | tf_op jit(solution)/shard_map/ppermute | solution.py:24
  93.2 1.5 %collective-permute-start.8 = (bf16[80,384]{1,0:T(8,128)(2,1)}, bf16[80,384]{1,0:T(8,128)(2,1)}, u32[]{:S(2)}, u32[]{:S(2)}) collective-permute-start(bf16[80,384]{1,0:T(8,128)(2,1)} %get-tuple-element.27), channel_id=1, source_target_pairs={{4,0},{8,4},{12,8},{5,1},{9,5},{13,9},{6,2},{10,6},{14,10},{7,3},{... | collective-permute-start | bytes 184328 | tf_op jit(solution)/shard_map/ppermute | solution.py:25
  95.8 3.8 %collective-permute-done.8 = bf16[80,384]{1,0:T(8,128)(2,1)} collective-permute-done((bf16[80,384]{1,0:T(8,128)(2,1)}, bf16[80,384]{1,0:T(8,128)(2,1)}, u32[]{:S(2)}, u32[]{:S(2)}) %collective-permute-start.8) | collective-permute-done | bytes 61472 | tf_op jit(solution)/shard_map/ppermute | solution.py:25
  100.4 3.7 %fusion.97 = (bf16[80,6,384]{2,0,1:T(8,128)(2,1)}, f32[80,6,384]{2,0,1:T(8,128)}) fusion(f32[80,80]{1,0:T(8,128)S(1)} %copy-done, f32[80,6,384]{2,0,1:T(8,128)S(1)} %copy.170, f32[80,6,384]{2,0,1:T(8,128)S(1)} %get-tuple-element.51, f32[80,6,383]{2,0,1:T(8,128)S(1)} %get-tuple-element.18, f32[80,6,1]{2,0,1:T(8,128)S(1)} %copy.175, ...), kind=kOutput, calls=%fused_computation.170 | convolution fusion | flops 180080640 | bytes 5555888 | tf_op jit(solution)/shard_map/kl,lrc->krc/dot_general | solution.py:55
  104.1 2.5 %copy.177 = f32[80,6,384]{0,2,1:T(8,128)} copy(f32[80,6,384]{2,0,1:T(8,128)} %get-tuple-element.53) | data formatting | bytes 1474560 | tf_op jit(solution)/shard_map/kl,lrc->krc/dot_general | solution.py:55
  106.6 2.1 %reshape.166 = f32[80,2,3,128,3]{0,4,3,2,1:T(4,128)S(1)} reshape(f32[80,6,384]{0,2,1:T(8,128)} %copy.177) | data formatting | bytes 1474560 | tf_op jit(solution)/shard_map/reshape | solution.py:131
  109.8 1.3 scatter_custom_fusion.1
  111.3 14.1 %all_to_all.36 = f32[80,4,256]{2,0,1:T(8,128)S(1)} all-to-all(f32[80,4,256]{2,0,1:T(8,128)S(1)} %copy.178), channel_id=1, replica_groups=mesh['groups'=2,'gx'=4,'gy'=2,'gz'=2] {'gx'}, dimensions={1} | all-to-all | bytes 655360 | tf_op jit(solution)/shard_map/all_to_all | solution.py:134
  125.6 7.6 %scatter_custom_fusion.2 = f32[80,2048]{0,1:T(8,128)S(1)} fusion(s32[1024]{0:T(1024)S(1)} %bitcast.196, f32[1024,80]{1,0:T(8,128)S(1)} %copy.180, f32[]{:T(128)} %constant.21.clone.1), kind=kCustom, calls=%fused_computation.54 | custom fusion | flops 81920 | bytes 655364 | tf_op jit(solution)/shard_map/scatter-add | solution.py:135
  (124 shorter events, 31.9 us)
Async XLA Ops:
  0.6 36.6 %copy-start = (f32[80,80]{1,0:T(8,128)S(1)}, f32[80,80]{1,0:T(8,128)}, u32[]{:S(2)}) copy-start(f32[80,80]{1,0:T(8,128)} %param.16) | copy-start | bytes 76804
  0.6 27.7 %copy-start.7 = (s32[1,1,256,1]{2,3,1,0:T(1,128)S(1)}, s32[1,1,256,1]{2,3,1,0:T(1,128)}, u32[]{:S(2)}) copy-start(s32[1,1,256,1]{2,3,1,0:T(1,128)} %param.17) | copy-start | bytes 3076
  0.7 27.7 %copy-start.3 = (bf16[80,6,384]{2,0,1:T(8,128)(2,1)S(1)}, bf16[80,6,384]{2,0,1:T(8,128)(2,1)}, u32[]{:S(2)}) copy-start(bf16[80,6,384]{2,0,1:T(8,128)(2,1)} %param.11) | copy-start | bytes 1105924
  0.7 22.6 %copy-start.2 = (bf16[80,8,256]{2,1,0:T(8,128)(2,1)S(1)}, bf16[80,8,256]{2,1,0:T(8,128)(2,1)}, u32[]{:S(2)}) copy-start(bf16[80,8,256]{2,1,0:T(8,128)(2,1)} %param.10) | copy-start | bytes 983044
  6.5 27.2 %all-to-all-start = ((s32[4,256,1]{1,2,0:T(1,128)}), s32[4,256,1]{1,2,0:T(1,128)S(1)}, u32[]{:S(2)}, u32[]{:S(2)}) async-start(s32[4,256,1]{1,2,0:T(1,128)} %bitcast.22), calls=%async_computation | async-start | bytes 8192 | tf_op jit(solution)/shard_map/all_to_all | solution.py:107
  15.0 18.8 %collective-permute-start = (bf16[80,640]{1,0:T(8,128)(2,1)S(1)}, bf16[80,640]{1,0:T(8,128)(2,1)}, u32[]{:S(2)}, u32[]{:S(2)}) collective-permute-start(bf16[80,640]{1,0:T(8,128)(2,1)S(1)} %pad_maximum_fusion), channel_id=1, source_target_pairs={{4,0},{8,4},{12,8},{5,1},{9,5},{13,9},{6,2},{10,6},{14,10},{7,3},{... | collective-permute-start | bytes 307208 | tf_op jit(solution)/shard_map/ppermute | solution.py:25
  17.0 17.7 %collective-permute-start.1 = (bf16[80,640]{1,0:T(8,128)(2,1)}, bf16[80,640]{1,0:T(8,128)(2,1)}, u32[]{:S(2)}, u32[]{:S(2)}) collective-permute-start(bf16[80,640]{1,0:T(8,128)(2,1)} %pad_maximum_fusion.1), channel_id=1, source_target_pairs={{0,4},{4,8},{8,12},{1,5},{5,9},{9,13},{2,6},{6,10},{10,14},{3,7},{... | collective-permute-start | bytes 307208 | tf_op jit(solution)/shard_map/ppermute | solution.py:24
  23.7 8.2 %collective-permute-start.2 = (bf16[80,14]{0,1:T(8,128)(2,1)S(1)}, bf16[80,14]{0,1:T(8,128)(2,1)S(1)}, u32[]{:S(2)}, u32[]{:S(2)}) collective-permute-start(bf16[80,14]{0,1:T(8,128)(2,1)S(1)} %pad_maximum_fusion.2), channel_id=1, source_target_pairs={{1,0},{2,1},{3,2},{5,4},{6,5},{7,6},{9,8},{10,9},{11,10},{13,12},{... | collective-permute-start | bytes 6728 | tf_op jit(solution)/shard_map/ppermute | solution.py:27
  25.3 6.6 %collective-permute-start.3 = (bf16[80,14]{0,1:T(8,128)(2,1)S(1)}, bf16[80,14]{0,1:T(8,128)(2,1)S(1)}, u32[]{:S(2)}, u32[]{:S(2)}) collective-permute-start(bf16[80,14]{0,1:T(8,128)(2,1)S(1)} %pad_maximum_fusion.3), channel_id=1, source_target_pairs={{0,1},{1,2},{2,3},{4,5},{5,6},{6,7},{8,9},{9,10},{10,11},{12,13},{... | collective-permute-start | bytes 6728 | tf_op jit(solution)/shard_map/ppermute | solution.py:26
  29.8 1.3 copy-start.1
  31.1 4.5 %copy-start.10 = (f32[80]{0:T(128)S(1)}, f32[80]{0:T(128)}, u32[]{:S(2)}) copy-start(f32[80]{0:T(128)} %param.12) | copy-start | bytes 964
  42.3 15.7 %all-to-all-start.1 = ((f32[80,4,256]{2,0,1:T(8,128)}), f32[80,4,256]{2,0,1:T(8,128)S(1)}, u32[]{:S(2)}, u32[]{:S(2)}) async-start(f32[80,4,256]{2,0,1:T(8,128)} %broadcast_select_fusion), calls=%async_computation.1 | async-start | bytes 655360 | tf_op jit(solution)/shard_map/all_to_all | solution.py:108
  58.9 0.6 copy-start.5
  61.3 1.7 %copy-start.4 = (f32[80,6,383]{2,0,1:T(8,128)S(1)}, f32[80,6,383]{2,0,1:T(8,128)}, u32[]{:S(2)}) copy-start(f32[80,6,383]{2,0,1:T(8,128)} %get-tuple-element.30) | copy-start | bytes 2206084
  61.3 1.7 %copy-start.8 = (f32[80]{0:T(128)S(1)}, f32[80]{0:T(128)}, u32[]{:S(2)}) copy-start(f32[80]{0:T(128)} %param.14) | copy-start | bytes 964
  61.3 1.7 %copy-start.9 = (f32[80]{0:T(128)S(1)}, f32[80]{0:T(128)}, u32[]{:S(2)}) copy-start(f32[80]{0:T(128)} %param.13) | copy-start | bytes 964
  68.7 6.2 %collective-permute-start.7 = (bf16[80,6]{0,1:T(8,128)(2,1)S(1)}, bf16[80,6]{0,1:T(8,128)(2,1)S(1)}, u32[]{:S(2)}, u32[]{:S(2)}) collective-permute-start(bf16[80,6]{0,1:T(8,128)(2,1)S(1)} %get-tuple-element.16), channel_id=1, source_target_pairs={{0,1},{1,2},{2,3},{4,5},{5,6},{6,7},{8,9},{9,10},{10,11},{12,13},{... | collective-permute-start | bytes 2888 | tf_op jit(solution)/shard_map/ppermute | solution.py:26
  70.6 4.3 %collective-permute-start.6 = (bf16[80,6]{0,1:T(8,128)(2,1)S(1)}, bf16[80,6]{0,1:T(8,128)(2,1)S(1)}, u32[]{:S(2)}, u32[]{:S(2)}) collective-permute-start(bf16[80,6]{0,1:T(8,128)(2,1)S(1)} %get-tuple-element.17), channel_id=1, source_target_pairs={{1,0},{2,1},{3,2},{5,4},{6,5},{7,6},{9,8},{10,9},{11,10},{13,12},{... | collective-permute-start | bytes 2888 | tf_op jit(solution)/shard_map/ppermute | solution.py:27
  71.9 4.1 %collective-permute-start.5 = (bf16[80,384]{1,0:T(8,128)(2,1)S(1)}, bf16[80,384]{1,0:T(8,128)(2,1)S(1)}, u32[]{:S(2)}, u32[]{:S(2)}) collective-permute-start(bf16[80,384]{1,0:T(8,128)(2,1)S(1)} %get-tuple-element.28), channel_id=1, source_target_pairs={{0,4},{4,8},{8,12},{1,5},{5,9},{9,13},{2,6},{6,10},{10,14},{3,7},{... | collective-permute-start | bytes 184328 | tf_op jit(solution)/shard_map/ppermute | solution.py:24
  73.6 6.7 %collective-permute-start.4 = (bf16[80,384]{1,0:T(8,128)(2,1)S(1)}, bf16[80,384]{1,0:T(8,128)(2,1)S(1)}, u32[]{:S(2)}, u32[]{:S(2)}) collective-permute-start(bf16[80,384]{1,0:T(8,128)(2,1)S(1)} %get-tuple-element.29), channel_id=1, source_target_pairs={{4,0},{8,4},{12,8},{5,1},{9,5},{13,9},{6,2},{10,6},{14,10},{7,3},{... | collective-permute-start | bytes 184328 | tf_op jit(solution)/shard_map/ppermute | solution.py:25
  85.9 8.7 %collective-permute-start.11 = (bf16[80,6]{0,1:T(8,128)(2,1)S(1)}, bf16[80,6]{0,1:T(8,128)(2,1)S(1)}, u32[]{:S(2)}, u32[]{:S(2)}) collective-permute-start(bf16[80,6]{0,1:T(8,128)(2,1)S(1)} %get-tuple-element.14), channel_id=1, source_target_pairs={{0,1},{1,2},{2,3},{4,5},{5,6},{6,7},{8,9},{9,10},{10,11},{12,13},{... | collective-permute-start | bytes 2888 | tf_op jit(solution)/shard_map/ppermute | solution.py:26
  88.4 6.2 %collective-permute-start.10 = (bf16[80,6]{0,1:T(8,128)(2,1)S(1)}, bf16[80,6]{0,1:T(8,128)(2,1)S(1)}, u32[]{:S(2)}, u32[]{:S(2)}) collective-permute-start(bf16[80,6]{0,1:T(8,128)(2,1)S(1)} %get-tuple-element.15), channel_id=1, source_target_pairs={{1,0},{2,1},{3,2},{5,4},{6,5},{7,6},{9,8},{10,9},{11,10},{13,12},{... | collective-permute-start | bytes 2888 | tf_op jit(solution)/shard_map/ppermute | solution.py:27
  89.7 5.2 %collective-permute-start.9 = (bf16[80,384]{1,0:T(8,128)(2,1)}, bf16[80,384]{1,0:T(8,128)(2,1)}, u32[]{:S(2)}, u32[]{:S(2)}) collective-permute-start(bf16[80,384]{1,0:T(8,128)(2,1)} %get-tuple-element.26), channel_id=1, source_target_pairs={{0,4},{4,8},{8,12},{1,5},{5,9},{9,13},{2,6},{6,10},{10,14},{3,7},{... | collective-permute-start | bytes 184328 | tf_op jit(solution)/shard_map/ppermute | solution.py:24
  93.2 6.4 %collective-permute-start.8 = (bf16[80,384]{1,0:T(8,128)(2,1)}, bf16[80,384]{1,0:T(8,128)(2,1)}, u32[]{:S(2)}, u32[]{:S(2)}) collective-permute-start(bf16[80,384]{1,0:T(8,128)(2,1)} %get-tuple-element.27), channel_id=1, source_target_pairs={{4,0},{8,4},{12,8},{5,1},{9,5},{13,9},{6,2},{10,6},{14,10},{7,3},{... | collective-permute-start | bytes 184328 | tf_op jit(solution)/shard_map/ppermute | solution.py:25
  108.8 0.9 copy-start.6
  125.6 8.0 %copy-start.11 = (f32[80]{0:T(128)S(1)}, f32[80]{0:T(128)}, u32[]{:S(2)}) copy-start(f32[80]{0:T(128)} %param.15) | copy-start | bytes 964

commit v2 on v1

v2 whole, which is shorter than its diff:
```python
import jax
import jax.numpy as jnp
from jax import lax
from jax.sharding import PartitionSpec as P

Y_AXES = ("gy", "gz")
HI = lax.Precision.HIGHEST


def shift_pairs(count):
    forward = [(i, i + 1) for i in range(count - 1)]
    backward = [(i + 1, i) for i in range(count - 1)]
    return forward, backward


def exchange(blocks):
    fwd_x, bwd_x = shift_pairs(lax.axis_size("gx"))
    fwd_y, bwd_y = shift_pairs(lax.axis_size(Y_AXES))
    last_rows = jnp.concatenate([b[:, -1, :] for b in blocks], axis=1)
    first_rows = jnp.concatenate([b[:, 0, :] for b in blocks], axis=1)
    last_cols = jnp.concatenate([b[:, :, -1] for b in blocks], axis=1)
    first_cols = jnp.concatenate([b[:, :, 0] for b in blocks], axis=1)
    above = lax.ppermute(last_rows, "gx", fwd_x)
    below = lax.ppermute(first_rows, "gx", bwd_x)
    left = lax.ppermute(last_cols, Y_AXES, fwd_y)
    right = lax.ppermute(first_cols, Y_AXES, bwd_y)
    out = []
    xo = 0
    yo = 0
    for b in blocks:
        w, h = b.shape[2], b.shape[1]
        out.append(
            (above[:, xo : xo + w], below[:, xo : xo + w], left[:, yo : yo + h], right[:, yo : yo + h])
        )
        xo += w
        yo += h
    return out


def per_row(values, rows, cols):
    if values.ndim == 1:
        return jnp.broadcast_to(values[:, None], (rows, cols)).reshape(rows * cols)
    return jnp.broadcast_to(values[:, :, None], values.shape + (cols,)).reshape(
        values.shape[0], rows * cols
    )


def flat_stencil(flat, rows, cols, halo, up_w=None, down_w=None):
    above, below, left, right = (h.astype(flat.dtype) for h in halo)
    levels = flat.shape[0]
    up = jnp.concatenate([above, flat[:, :-cols]], axis=1)
    down = jnp.concatenate([flat[:, cols:], below], axis=1)
    col = lax.broadcasted_iota(jnp.int32, (1, rows * cols), 1) % cols
    zero = jnp.zeros((levels, 1), flat.dtype)
    west = jnp.where(col == 0, per_row(left, rows, cols), jnp.concatenate([zero, flat[:, :-1]], axis=1))
    east = jnp.where(
        col == cols - 1, per_row(right, rows, cols), jnp.concatenate([flat[:, 1:], zero], axis=1)
    )
    if down_w is not None:
        down = down * down_w[None, :]
        up = up * up_w[None, :]
    return down + up + east + west - 4.0 * flat


def mix_levels(matrix, flat):
    return jnp.dot(matrix, flat, precision=HI, preferred_element_type=jnp.float32)


def nest_segments(nest_of, first, count):
    index_rows = first + jnp.arange(count, dtype=jnp.int32)
    inside = (index_rows >= 0) & (index_rows < nest_of.shape[0])
    return jnp.where(inside, nest_of[jnp.clip(index_rows, 0, nest_of.shape[0] - 1)], -1)


def row_weights(segments):
    left_w = (segments[:-2] == segments[1:-1]).astype(jnp.float32)
    right_w = (segments[2:] == segments[1:-1]).astype(jnp.float32)
    return (left_w, right_w)


def block_expansion(block_rows, block_cols, rows, cols, zero):
    r = lax.broadcasted_iota(jnp.int32, (block_rows * block_cols, rows * cols), 0) + zero
    p = lax.broadcasted_iota(jnp.int32, (block_rows * block_cols, rows * cols), 1)
    hit = ((p // cols) // 3 == r // block_cols) & ((p % cols) // 3 == r % block_cols)
    return hit.astype(jnp.float32)


def body(parent, nest, nu_parent, nu_nest, relax, feedback, vert_mix, fp_owner, fp_cell, nest_of):
    levels, p_rows, p_cols = parent.shape
    _, n_rows, n_cols = nest.shape
    tiles_x = lax.axis_size("gx")
    here_x = lax.axis_index("gx")
    zero = jnp.minimum(here_x, 0)

    parent_halo, nest_halo = exchange([parent, nest])
    centre = parent.astype(jnp.float32).reshape(levels, p_rows * p_cols)
    stencil = flat_stencil(centre, p_rows, p_cols, parent_halo)
    flat_parent = mix_levels(vert_mix, centre + nu_parent[:, None] * stencil)

    owners = fp_owner.reshape(-1)
    cells = fp_cell.reshape(-1)
    requests = owners.shape[0]
    slots = 4 * requests // tiles_x
    owner_ids = jnp.arange(tiles_x, dtype=jnp.int32)
    if slots >= requests:
        chosen = owners[None, :] == owner_ids[:, None]
        wanted = jnp.where(chosen, cells[None, :], 0)
        wanted = jnp.pad(wanted, ((0, 0), (0, slots - requests))).reshape(-1)
    else:
        onehot = (owners[:, None] == owner_ids[None, :]).astype(jnp.int32)
        before = jnp.cumsum(onehot, axis=0) - onehot
        order_in = jnp.sum(before * onehot, axis=1)
        places = owners * slots + order_in
        wanted = jnp.zeros((tiles_x * slots,), jnp.int32).at[places].set(cells)
    served_ids = lax.all_to_all(wanted, "gx", split_axis=0, concat_axis=0, tiled=True)
    answers = lax.all_to_all(
        jnp.take(flat_parent, served_ids, axis=1), "gx", split_axis=1, concat_axis=1, tiled=True
    )
    if slots >= requests:
        answers = answers.reshape(levels, tiles_x, slots)[:, :, :requests]
        forcing_flat = answers[:, 0, :]
        for o in range(1, tiles_x):
            forcing_flat = jnp.where(chosen[o][None, :], answers[:, o, :], forcing_flat)
    else:
        forcing_flat = jnp.take(answers, places, axis=1)

    block_rows = n_rows // 3
    block_cols = n_cols // 3
    expand = block_expansion(block_rows, block_cols, n_rows, n_cols, zero)
    forcing_full = jnp.dot(forcing_flat, expand, precision=HI, preferred_element_type=jnp.float32)
    row_start = here_x * n_rows
    left_w, right_w = row_weights(nest_segments(nest_of, row_start - 1, n_rows + 2))
    up_w = per_row(left_w, n_rows, n_cols)
    down_w = per_row(right_w, n_rows, n_cols)

    nest_state = nest.astype(jnp.float32).reshape(levels, n_rows * n_cols)
    halo = nest_halo
    for turn_no in range(3):
        if turn_no > 0:
            shaped = nest_state.astype(jnp.bfloat16).reshape(levels, n_rows, n_cols)
            (halo,) = exchange([shaped])
        stencil_sum = flat_stencil(nest_state, n_rows, n_cols, halo, up_w, down_w)
        moved = nest_state + nu_nest[:, None] * stencil_sum
        moved = moved + relax[:, None] * (forcing_full - moved)
        nest_state = mix_levels(vert_mix, moved)

    block_sum = lax.dot_general(
        nest_state, expand, (((1,), (1,)), ((), ())), precision=HI, preferred_element_type=jnp.float32
    )
    nudge_gap = block_sum / 9.0 - forcing_flat
    if slots >= requests:
        outgoing = jnp.where(chosen[None, :, :], nudge_gap[:, None, :], 0.0)
        outgoing = jnp.pad(outgoing, ((0, 0), (0, 0), (0, slots - requests)))
        outgoing = outgoing.reshape(levels, tiles_x * slots)
    else:
        outgoing = jnp.zeros((levels, tiles_x * slots), jnp.float32).at[:, places].set(nudge_gap)
    incoming = lax.all_to_all(outgoing, "gx", split_axis=1, concat_axis=1, tiled=True)
    summed = jnp.zeros_like(flat_parent).at[:, served_ids].add(incoming)
    parent_out = (flat_parent + feedback[:, None] * summed).astype(jnp.bfloat16)
    return (
        parent_out.reshape(levels, p_rows, p_cols),
        nest_state.astype(jnp.bfloat16).reshape(levels, n_rows, n_cols),
    )


def solution(mesh):
    placed = (
        P("groups", "gx", Y_AXES),
        P("groups", "gx", Y_AXES),
        P(),
        P(),
        P(),
        P(),
        P(),
        P("gx", Y_AXES, None, None),
        P("gx", Y_AXES, None),
        P(),
    )
    return jax.shard_map(
        body,
        mesh=mesh,
        in_specs=placed,
        out_specs=(P("groups", "gx", Y_AXES), P("groups", "gx", Y_AXES)),
        check_vma=False,
    )
```

time: 136 us -> 122 us (0.90)
  blocking collectives: 14.1 us -> 0 us
  starting transfers between devices: 35.5 us -> 43.9 us
  local copies, waits for them, and re-layouts: 35.8 us -> 30.1 us
  other arithmetic: 21.5 us -> 18.9 us
    all_to_all x1 -> x0, blocking collectives: 14.1 us -> none  [body(): lax.all_to_all(outgoing, 'gx', split_axis=1, concat_axis=1, tiled=True)]
    all_to_all x0 -> x1, waiting for transfers between devices: none -> 9.08 us  [body(): lax.all_to_all(outgoing, 'gx', split_axis=1, concat_axis=1, tiled=True)]
    unnamed x31 -> x68, local copies, waits for them, and re-layouts: 2.34 us -> 10.8 us
    ppermute x3, waiting for transfers between devices: 8.05 us -> 0.01 us  [exchange(): below = lax.ppermute(first_rows, 'gx', bwd_x)]
    broadcast_in_dim x16 -> x0, other arithmetic: 6.26 us -> none  [the longest x4 3.12 us: neighbours(): up = jnp.concatenate([above[:, None, :], centre[:, :-1, :]], axis=1)]
    convert_element_type x2 -> x13, other arithmetic: 0.88 us -> 6.56 us  [the longest x12 6.43 us: flat_stencil(): above, below, left, right = (h.astype(flat.dtype) for h in halo)]
    all_to_all x0 -> x1, starting transfers between devices: none -> 4.98 us  [body(): lax.all_to_all(outgoing, 'gx', split_axis=1, concat_axis=1, tiled=True)]
    reshape x5 -> x4, local copies, waits for them, and re-layouts: 5.83 us -> 1.64 us  [the longest x2 0.82 us: body(): shaped = nest_state.astype(jnp.bfloat16).reshape(levels, n_rows, n_cols)]
  transfers between devices with their start and end apart: 14 -> 15, of which waited for: 3 -> 4; matrix products, arithmetic and copies ran while one was open for 13% -> 23% of each run, Pallas kernels for 0% -> 0%
where the time goes in v2:
time: 122 us; the launch traced here: 120 us
  starting transfers between devices  43.9 us (36%)
  local copies, waits for them, and re-layouts  30.1 us (25%)
  other arithmetic  18.9 us (15%)
  waiting for transfers between devices  15.1 us (12%)
  matrix products  10.8 us (9%)
  between operations  1.45 us (1%)
    ppermute x3, starting transfers between devices, exchange(): above = lax.ppermute(last_rows, 'gx', fwd_x)  13.8 us
    unnamed x68, local copies, waits for them, and re-layouts  10.8 us
    all_to_all x1, waiting for transfers between devices, body(): lax.all_to_all(outgoing, 'gx', split_axis=1, concat_axis=1, tiled=True)  9.08 us
    dot_general x4, matrix products, mix_levels(): jnp.dot(matrix, flat, precision=HI, preferred_element_type=jnp.float32)  8.71 us
    ppermute x3, starting transfers between devices, exchange(): left = lax.ppermute(last_cols, Y_AXES, fwd_y)  7.92 us
    scatter-add x1, other arithmetic, body(): summed = jnp.zeros_like(flat_parent).at[:, served_ids].add(incoming)  6.46 us
    convert_element_type x12, other arithmetic, flat_stencil(): above, below, left, right = (h.astype(flat.dtype) for h in halo)  6.43 us
    all_to_all x1, starting transfers between devices, body(): lax.all_to_all(jnp.take(flat_parent, served_ids, axis=1), 'gx', split_axi...  5.09 us
  transfers between devices with their start and end apart: 15, of which 4 were waited for; matrix products, arithmetic and copies ran while one was open for 23% of the time, Pallas kernels for 0%

profile of v2, /device:TPU:0, one launch (start us, length us, event | category | flops | bytes accessed | tf_op | source)
XLA Modules:
  0.0 120.2 jit_solution(3893287503478127455)
XLA Ops:
  1.6 1.2 %fusion.144 = (bf16[80,1,256]{2,1,0:T(2,128)(2,1)S(1)}, bf16[80,1,256]{2,1,0:T(2,128)(2,1)S(1)}) fusion(bf16[80,8,256]{2,1,0:T(8,128)(2,1)} %param.10), kind=kLoop, calls=%fused_computation.220 | loop fusion | bytes 163840 | tf_op jit(solution)/shard_map/slice | solution.py:19
  3.5 1.4 %collective-permute-start = (bf16[80,640]{1,0:T(8,128)(2,1)}, bf16[80,640]{1,0:T(8,128)(2,1)}, u32[]{:S(2)}, u32[]{:S(2)}) collective-permute-start(bf16[80,640]{1,0:T(8,128)(2,1)} %pad_maximum_fusion), channel_id=1, source_target_pairs={{4,0},{8,4},{12,8},{5,1},{9,5},{13,9},{6,2},{10,6},{14,10},{7,3},{... | collective-permute-start | bytes 307208 | tf_op jit(solution)/shard_map/ppermute | solution.py:24
  5.6 6.2 %collective-permute-start.1 = (bf16[80,640]{1,0:T(8,128)(2,1)}, bf16[80,640]{1,0:T(8,128)(2,1)}, u32[]{:S(2)}, u32[]{:S(2)}) collective-permute-start(bf16[80,640]{1,0:T(8,128)(2,1)} %pad_maximum_fusion.1), channel_id=1, source_target_pairs={{0,4},{4,8},{8,12},{1,5},{5,9},{9,13},{2,6},{6,10},{10,14},{3,7},{... | collective-permute-start | bytes 307208 | tf_op jit(solution)/shard_map/ppermute | solution.py:23
  12.4 1.5 %collective-permute-start.3 = (bf16[80,14]{0,1:T(8,128)(2,1)S(1)}, bf16[80,14]{0,1:T(8,128)(2,1)S(1)}, u32[]{:S(2)}, u32[]{:S(2)}) collective-permute-start(bf16[80,14]{0,1:T(8,128)(2,1)S(1)} %pad_maximum_fusion.3), channel_id=1, source_target_pairs={{0,1},{1,2},{2,3},{4,5},{5,6},{6,7},{8,9},{9,10},{10,11},{12,13},{... | collective-permute-start | bytes 6728 | tf_op jit(solution)/shard_map/ppermute | solution.py:25
  14.1 1.3 %collective-permute-start.2 = (bf16[80,14]{0,1:T(8,128)(2,1)S(1)}, bf16[80,14]{0,1:T(8,128)(2,1)S(1)}, u32[]{:S(2)}, u32[]{:S(2)}) collective-permute-start(bf16[80,14]{0,1:T(8,128)(2,1)S(1)} %pad_maximum_fusion.2), channel_id=1, source_target_pairs={{1,0},{2,1},{3,2},{5,4},{6,5},{7,6},{9,8},{10,9},{11,10},{13,12},{... | collective-permute-start | bytes 6728 | tf_op jit(solution)/shard_map/ppermute | solution.py:26
  16.0 4.1 %all-to-all-start = ((s32[4,256,1]{1,2,0:T(1,128)}), s32[4,256,1]{1,2,0:T(1,128)S(1)}, u32[]{:S(2)}, u32[]{:S(2)}) async-start(s32[4,256,1]{1,2,0:T(1,128)} %compare_select_fusion.1), calls=%async_computation | async-start | bytes 8192 | tf_op jit(solution)/shard_map/all_to_all | solution.py:115
  21.8 1.1 fusion.135
  22.9 1.4 %fusion.134 = (f32[80,2303]{1,0:T(8,128)}, f32[80,2303]{1,0:T(8,128)}) fusion(f32[80,2304]{1,0:T(8,128)S(1)} %bitcast.111), kind=kLoop, calls=%fused_computation.210 | loop fusion | bytes 2947840 | tf_op jit(solution)/shard_map/slice | solution.py:57
  25.1 2.2 %fusion.6 = pred[256,2304]{1,0:T(32,128)(4,1)} fusion(s32[256]{0:T(256)S(1)} %get-tuple-element.58, s32[256]{0:T(256)S(1)} %get-tuple-element.59, s32[2304]{0:T(1024)S(1)} %get-tuple-element.62, s32[2304]{0:T(1024)S(1)} %get-tuple-element.63, s32[256]{0:T(256)S(1)} %get-tuple-element.57, s32[256]{0:T(256)S(1)} %get-tuple-element.60, ...), kind=kLoop, calls=%fused_computation.20 | loop fusion | flops 13565952 | bytes 635904 | tf_op jit(solution)/shard_map/and | solution.py:84
  31.7 2.8 %convolution_bitcast_fusion.2 = f32[80,2048]{1,0:T(8,128)S(1)} fusion(f32[80,80]{1,0:T(8,128)S(1)} %copy-done, f32[80,2048]{1,0:T(8,128)S(1)} %bitcast.115, f32[80,256]{1,0:T(8,128)S(1)} %slice_convert_fusion.3, f32[80,1792]{1,0:T(8,128)} %get-tuple-element.28, f32[80,1792]{1,0:T(8,128)} %get-tuple-element.27, f32[80,256]{1,0:T(8,128)S(1)} %slice_convert_fusion.2, ...), kind=kOutput, calls=%fused_computation.13 | convolution fusion | flops 159088640 | bytes 5272256 | tf_op jit(solution)/shard_map/dot_general | solution.py:66
  34.8 2.8 %gather_fusion.1 = f32[1024,80]{1,0:T(8,128)S(1)} fusion(f32[80,2048]{0,1:T(8,128)S(1)} %copy.93, s32[1024]{0:T(1024)S(1)} %broadcast_clamp_fusion), kind=kCustom, calls=%fused_computation.1 | custom fusion | bytes 659456 | tf_op jit(solution)/shard_map/jit(_take)/gather | solution.py:117
  38.6 5.1 %all-to-all-start.1 = ((f32[80,4,256]{2,0,1:T(8,128)}), f32[80,4,256]{2,0,1:T(8,128)S(1)}, u32[]{:S(2)}, u32[]{:S(2)}) async-start(f32[80,4,256]{2,0,1:T(8,128)} %broadcast_select_fusion.1), calls=%async_computation.1 | async-start | bytes 655360 | tf_op jit(solution)/shard_map/all_to_all | solution.py:116
  46.2 1.5 %slice_convert_fusion = f32[80,384]{1,0:T(8,128)} fusion(bf16[80,640]{1,0:T(8,128)(2,1)} %collective-permute-done.1), kind=kLoop, calls=%fused_computation.131 | loop fusion | flops 30720 | bytes 184320 | tf_op jit(solution)/shard_map/convert_element_type | solution.py:49
  47.7 1.6 %slice_convert_fusion.1 = f32[80,384]{1,0:T(8,128)} fusion(bf16[80,640]{1,0:T(8,128)(2,1)} %collective-permute-done), kind=kLoop, calls=%fused_computation.132 | loop fusion | flops 30720 | bytes 184320 | tf_op jit(solution)/shard_map/convert_element_type | solution.py:49
  49.3 4.3 %all-to-all-done.1 = f32[80,4,256]{2,0,1:T(8,128)S(1)} async-done(((f32[80,4,256]{2,0,1:T(8,128)}), f32[80,4,256]{2,0,1:T(8,128)S(1)}, u32[]{:S(2)}, u32[]{:S(2)}) %all-to-all-start.1) | async-done | bytes 327712 | tf_op jit(solution)/shard_map/all_to_all | solution.py:116
  54.5 3.3 %fusion.145 = (bf16[80,2304]{1,0:T(8,128)(2,1)S(1)}, f32[80,2304]{1,0:T(8,128)S(1)}) fusion(f32[80,80]{1,0:T(8,128)S(1)} %copy-done, f32[80,2304]{1,0:T(8,128)S(1)} %fusion.148, f32[80,2304]{1,0:T(8,128)S(1)} %bitcast.112, f32[80,1920]{1,0:T(8,128)} %get-tuple-element.23, f32[80,384]{1,0:T(8,128)S(1)} %copy-done.16, f32[80,384]{1,0:T(8,128)S(1)} %copy-done.17, ...), kind=kOutput, calls=%fused_computation.221 | convolution fusion | flops 180080640 | bytes 7052800 | tf_op jit(solution)/shard_map/dot_general | solution.py:66
  58.5 2.4 %collective-permute-start.5 = (bf16[80,384]{1,0:T(8,128)(2,1)S(1)}, bf16[80,384]{1,0:T(8,128)(2,1)S(1)}, u32[]{:S(2)}, u32[]{:S(2)}) collective-permute-start(bf16[80,384]{1,0:T(8,128)(2,1)S(1)} %bitcast.142), channel_id=1, source_target_pairs={{0,4},{4,8},{8,12},{1,5},{5,9},{9,13},{2,6},{6,10},{10,14},{3,7},{... | collective-permute-start | bytes 184328 | tf_op jit(solution)/shard_map/ppermute | solution.py:23
  61.0 1.3 %collective-permute-start.4 = (bf16[80,384]{1,0:T(8,128)(2,1)S(1)}, bf16[80,384]{1,0:T(8,128)(2,1)S(1)}, u32[]{:S(2)}, u32[]{:S(2)}) collective-permute-start(bf16[80,384]{1,0:T(8,128)(2,1)S(1)} %bitcast.144), channel_id=1, source_target_pairs={{4,0},{8,4},{12,8},{5,1},{9,5},{13,9},{6,2},{10,6},{14,10},{7,3},{... | collective-permute-start | bytes 184328 | tf_op jit(solution)/shard_map/ppermute | solution.py:24
  62.4 2.5 %collective-permute-start.7 = (bf16[80,6]{0,1:T(8,128)(2,1)S(1)}, bf16[80,6]{0,1:T(8,128)(2,1)S(1)}, u32[]{:S(2)}, u32[]{:S(2)}) collective-permute-start(bf16[80,6]{0,1:T(8,128)(2,1)S(1)} %bitcast.154), channel_id=1, source_target_pairs={{0,1},{1,2},{2,3},{4,5},{5,6},{6,7},{8,9},{9,10},{10,11},{12,13},{... | collective-permute-start | bytes 2888 | tf_op jit(solution)/shard_map/ppermute | solution.py:25
  66.2 1.3 %collective-permute-start.6 = (bf16[80,6]{0,1:T(8,128)(2,1)S(1)}, bf16[80,6]{0,1:T(8,128)(2,1)S(1)}, u32[]{:S(2)}, u32[]{:S(2)}) collective-permute-start(bf16[80,6]{0,1:T(8,128)(2,1)S(1)} %bitcast.156), channel_id=1, source_target_pairs={{1,0},{2,1},{3,2},{5,4},{6,5},{7,6},{9,8},{10,9},{11,10},{13,12},{... | collective-permute-start | bytes 2888 | tf_op jit(solution)/shard_map/ppermute | solution.py:26
  67.5 1.1 fusion.133
  69.9 1.4 %collective-permute-done.6 = bf16[80,6]{0,1:T(8,128)(2,1)S(1)} collective-permute-done((bf16[80,6]{0,1:T(8,128)(2,1)S(1)}, bf16[80,6]{0,1:T(8,128)(2,1)S(1)}, u32[]{:S(2)}, u32[]{:S(2)}) %collective-permute-start.6) | collective-permute-done | bytes 992 | tf_op jit(solution)/shard_map/ppermute | solution.py:26
  73.1 1.3 %fusion.146 = (bf16[80,2304]{1,0:T(8,128)(2,1)S(1)}, f32[80,2304]{1,0:T(8,128)S(1)}) fusion(f32[80,80]{1,0:T(8,128)S(1)} %copy-done, f32[80,2304]{1,0:T(8,128)S(1)} %fusion.148, f32[80,2304]{1,0:T(8,128)S(1)} %get-tuple-element.48, f32[80,1920]{1,0:T(8,128)S(1)} %copy-done.12, f32[80,384]{1,0:T(8,128)S(1)} %convert_element_type.84, ...), kind=kOutput, calls=%fused_computation.222 | convolution fusion | flops 180080640 | bytes 7052800 | tf_op jit(solution)/shard_map/dot_general | solution.py:66
  75.2 5.2 %collective-permute-start.9 = (bf16[80,384]{1,0:T(8,128)(2,1)S(1)}, bf16[80,384]{1,0:T(8,128)(2,1)}, u32[]{:S(2)}, u32[]{:S(2)}) collective-permute-start(bf16[80,384]{1,0:T(8,128)(2,1)S(1)} %bitcast.143), channel_id=1, source_target_pairs={{0,4},{4,8},{8,12},{1,5},{5,9},{9,13},{2,6},{6,10},{10,14},{3,7},{... | collective-permute-start | bytes 184328 | tf_op jit(solution)/shard_map/ppermute | solution.py:23
  81.0 1.5 %collective-permute-start.8 = (bf16[80,384]{1,0:T(8,128)(2,1)}, bf16[80,384]{1,0:T(8,128)(2,1)}, u32[]{:S(2)}, u32[]{:S(2)}) collective-permute-start(bf16[80,384]{1,0:T(8,128)(2,1)} %bitcast.105), channel_id=1, source_target_pairs={{4,0},{8,4},{12,8},{5,1},{9,5},{13,9},{6,2},{10,6},{14,10},{7,3},{... | collective-permute-start | bytes 184328 | tf_op jit(solution)/shard_map/ppermute | solution.py:24
  82.6 4.0 %collective-permute-start.11 = (bf16[80,6]{0,1:T(8,128)(2,1)S(1)}, bf16[80,6]{0,1:T(8,128)(2,1)S(1)}, u32[]{:S(2)}, u32[]{:S(2)}) collective-permute-start(bf16[80,6]{0,1:T(8,128)(2,1)S(1)} %bitcast.155), channel_id=1, source_target_pairs={{0,1},{1,2},{2,3},{4,5},{5,6},{6,7},{8,9},{9,10},{10,11},{12,13},{... | collective-permute-start | bytes 2888 | tf_op jit(solution)/shard_map/ppermute | solution.py:25
  87.0 1.3 %collective-permute-start.10 = (bf16[80,6]{0,1:T(8,128)(2,1)S(1)}, bf16[80,6]{0,1:T(8,128)(2,1)S(1)}, u32[]{:S(2)}, u32[]{:S(2)}) collective-permute-start(bf16[80,6]{0,1:T(8,128)(2,1)S(1)} %bitcast.157), channel_id=1, source_target_pairs={{1,0},{2,1},{3,2},{5,4},{6,5},{7,6},{9,8},{10,9},{11,10},{13,12},{... | collective-permute-start | bytes 2888 | tf_op jit(solution)/shard_map/ppermute | solution.py:26
  93.3 1.3 %fusion.147 = (bf16[2304,80]{0,1:T(8,128)(2,1)S(1)}, f32[2304,80]{0,1:T(8,128)S(1)}) fusion(f32[80,80]{1,0:T(8,128)S(1)} %copy-done, f32[80,2304]{1,0:T(8,128)S(1)} %fusion.148, f32[80,2304]{1,0:T(8,128)S(1)} %get-tuple-element.50, f32[80,1920]{1,0:T(8,128)S(1)} %copy-done.10, f32[80,384]{1,0:T(8,128)S(1)} %convert_element_type.89, ...), kind=kOutput, calls=%fused_computation.223 | convolution fusion | flops 180080640 | bytes 7052800 | tf_op jit(solution)/shard_map/dot_general | solution.py:66
  94.6 1.2 %fusion.9 = f32[80,256]{1,0:T(8,128)S(1)} fusion(f32[80,256]{1,0:T(8,128)S(1)} %fusion.101, f32[2304,80]{0,1:T(8,128)S(1)} %get-tuple-element.52, pred[256,2304]{1,0:T(32,128)(4,1)S(1)} %copy-done.5), kind=kOutput, calls=%fused_computation.24 | convolution fusion | flops 566272000 | bytes 1490944 | tf_op jit(solution)/shard_map/dot_general | solution.py:147
  96.6 5.0 %all-to-all-start.2 = ((f32[80,4,256]{2,0,1:T(8,128)}), f32[80,4,256]{2,0,1:T(8,128)S(1)}, u32[]{:S(2)}, u32[]{:S(2)}) async-start(f32[80,4,256]{2,0,1:T(8,128)} %broadcast_select_fusion), calls=%async_computation.2 | async-start | bytes 655360 | tf_op jit(solution)/shard_map/all_to_all | solution.py:157
  102.4 9.1 %all-to-all-done.2 = f32[80,4,256]{2,0,1:T(8,128)S(1)} async-done(((f32[80,4,256]{2,0,1:T(8,128)}), f32[80,4,256]{2,0,1:T(8,128)S(1)}, u32[]{:S(2)}, u32[]{:S(2)}) %all-to-all-start.2) | async-done | bytes 327712 | tf_op jit(solution)/shard_map/all_to_all | solution.py:157
  111.7 6.5 %scatter_custom_fusion = f32[80,2048]{0,1:T(8,128)S(1)} fusion(s32[1024]{0:T(1024)S(1)} %bitcast.147, f32[1024,80]{1,0:T(8,128)S(1)} %copy.109, f32[]{:T(128)} %constant.109.clone.1), kind=kCustom, calls=%fused_computation.92 | custom fusion | flops 81920 | bytes 655364 | tf_op jit(solution)/shard_map/scatter-add | solution.py:158
  (164 shorter events, 30.8 us)
Async XLA Ops:
  0.6 31.0 %copy-start = (f32[80,80]{1,0:T(8,128)S(1)}, f32[80,80]{1,0:T(8,128)}, u32[]{:S(2)}) copy-start(f32[80,80]{1,0:T(8,128)} %param.16) | copy-start | bytes 76804
  0.6 11.2 %copy-start.15 = (bf16[80,6,384]{2,0,1:T(8,128)(2,1)S(1)}, bf16[80,6,384]{2,0,1:T(8,128)(2,1)}, u32[]{:S(2)}) copy-start(bf16[80,6,384]{2,0,1:T(8,128)(2,1)} %param.11) | copy-start | bytes 1105924
  0.7 11.3 %copy-start.14 = (bf16[80,8,256]{2,1,0:T(8,128)(2,1)S(1)}, bf16[80,8,256]{2,1,0:T(8,128)(2,1)}, u32[]{:S(2)}) copy-start(bf16[80,8,256]{2,1,0:T(8,128)(2,1)} %param.10) | copy-start | bytes 983044
  3.5 11.9 %copy-start.20 = (s32[1,1,256,1]{2,3,1,0:T(1,128)S(1)}, s32[1,1,256,1]{2,3,1,0:T(1,128)}, u32[]{:S(2)}) copy-start(s32[1,1,256,1]{2,3,1,0:T(1,128)} %param.17) | copy-start | bytes 3076
  3.5 11.9 %copy-start.21 = (s32[1,1,256]{2,1,0:T(1,128)S(1)}, s32[1,1,256]{2,1,0:T(1,128)}, u32[]{:S(2)}) copy-start(s32[1,1,256]{2,1,0:T(1,128)} %param.18) | copy-start | bytes 3076
  3.5 26.6 %collective-permute-start = (bf16[80,640]{1,0:T(8,128)(2,1)}, bf16[80,640]{1,0:T(8,128)(2,1)}, u32[]{:S(2)}, u32[]{:S(2)}) collective-permute-start(bf16[80,640]{1,0:T(8,128)(2,1)} %pad_maximum_fusion), channel_id=1, source_target_pairs={{4,0},{8,4},{12,8},{5,1},{9,5},{13,9},{6,2},{10,6},{14,10},{7,3},{... | collective-permute-start | bytes 307208 | tf_op jit(solution)/shard_map/ppermute | solution.py:24
  5.6 25.3 %collective-permute-start.1 = (bf16[80,640]{1,0:T(8,128)(2,1)}, bf16[80,640]{1,0:T(8,128)(2,1)}, u32[]{:S(2)}, u32[]{:S(2)}) collective-permute-start(bf16[80,640]{1,0:T(8,128)(2,1)} %pad_maximum_fusion.1), channel_id=1, source_target_pairs={{0,4},{4,8},{8,12},{1,5},{5,9},{9,13},{2,6},{6,10},{10,14},{3,7},{... | collective-permute-start | bytes 307208 | tf_op jit(solution)/shard_map/ppermute | solution.py:23
  12.4 15.1 %collective-permute-start.3 = (bf16[80,14]{0,1:T(8,128)(2,1)S(1)}, bf16[80,14]{0,1:T(8,128)(2,1)S(1)}, u32[]{:S(2)}, u32[]{:S(2)}) collective-permute-start(bf16[80,14]{0,1:T(8,128)(2,1)S(1)} %pad_maximum_fusion.3), channel_id=1, source_target_pairs={{0,1},{1,2},{2,3},{4,5},{5,6},{6,7},{8,9},{9,10},{10,11},{12,13},{... | collective-permute-start | bytes 6728 | tf_op jit(solution)/shard_map/ppermute | solution.py:25
  14.1 13.3 %collective-permute-start.2 = (bf16[80,14]{0,1:T(8,128)(2,1)S(1)}, bf16[80,14]{0,1:T(8,128)(2,1)S(1)}, u32[]{:S(2)}, u32[]{:S(2)}) collective-permute-start(bf16[80,14]{0,1:T(8,128)(2,1)S(1)} %pad_maximum_fusion.2), channel_id=1, source_target_pairs={{1,0},{2,1},{3,2},{5,4},{6,5},{7,6},{9,8},{10,9},{11,10},{13,12},{... | collective-permute-start | bytes 6728 | tf_op jit(solution)/shard_map/ppermute | solution.py:26
  16.0 14.0 %all-to-all-start = ((s32[4,256,1]{1,2,0:T(1,128)}), s32[4,256,1]{1,2,0:T(1,128)S(1)}, u32[]{:S(2)}, u32[]{:S(2)}) async-start(s32[4,256,1]{1,2,0:T(1,128)} %compare_select_fusion.1), calls=%async_computation | async-start | bytes 8192 | tf_op jit(solution)/shard_map/all_to_all | solution.py:115
  22.9 1.4 %copy-start.1 = (s32[24]{0:T(128)S(1)}, s32[24]{0:T(128)}, u32[]{:S(2)}) copy-start(s32[24]{0:T(128)} %param.19) | copy-start | bytes 292
  28.8 2.8 %copy-start.22 = (f32[80]{0:T(128)S(1)}, f32[80]{0:T(128)}, u32[]{:S(2)}) copy-start(f32[80]{0:T(128)} %param.12) | copy-start | bytes 964
  34.5 3.2 %copy-start.2 = (f32[80,2048]{1,0:T(8,128)}, f32[80,2048]{1,0:T(8,128)S(1)}, u32[]{:S(2)}) copy-start(f32[80,2048]{1,0:T(8,128)S(1)} %convolution_bitcast_fusion.2) | copy-start | bytes 1966084
  38.6 14.9 %all-to-all-start.1 = ((f32[80,4,256]{2,0,1:T(8,128)}), f32[80,4,256]{2,0,1:T(8,128)S(1)}, u32[]{:S(2)}, u32[]{:S(2)}) async-start(f32[80,4,256]{2,0,1:T(8,128)} %broadcast_select_fusion.1), calls=%async_computation.1 | async-start | bytes 655360 | tf_op jit(solution)/shard_map/all_to_all | solution.py:116
  45.2 8.4 %copy-start.4 = (pred[256,2304]{1,0:T(32,128)(4,1)S(1)}, pred[256,2304]{1,0:T(32,128)(4,1)}, u32[]{:S(2)}) copy-start(pred[256,2304]{1,0:T(32,128)(4,1)} %fusion.6) | copy-start | bytes 1769476
  47.7 6.7 %copy-start.6 = (f32[80,2303]{1,0:T(8,128)S(1)}, f32[80,2303]{1,0:T(8,128)}, u32[]{:S(2)}) copy-start(f32[80,2303]{1,0:T(8,128)} %get-tuple-element.21) | copy-start | bytes 2210884
  47.7 6.7 %copy-start.18 = (f32[80]{0:T(128)S(1)}, f32[80]{0:T(128)}, u32[]{:S(2)}) copy-start(f32[80]{0:T(128)} %param.14) | copy-start | bytes 964
  47.7 6.7 %copy-start.19 = (f32[80]{0:T(128)S(1)}, f32[80]{0:T(128)}, u32[]{:S(2)}) copy-start(f32[80]{0:T(128)} %param.13) | copy-start | bytes 964
  58.5 13.2 %collective-permute-start.5 = (bf16[80,384]{1,0:T(8,128)(2,1)S(1)}, bf16[80,384]{1,0:T(8,128)(2,1)S(1)}, u32[]{:S(2)}, u32[]{:S(2)}) collective-permute-start(bf16[80,384]{1,0:T(8,128)(2,1)S(1)} %bitcast.142), channel_id=1, source_target_pairs={{0,4},{4,8},{8,12},{1,5},{5,9},{9,13},{2,6},{6,10},{10,14},{3,7},{... | collective-permute-start | bytes 184328 | tf_op jit(solution)/shard_map/ppermute | solution.py:23
  61.0 10.8 %collective-permute-start.4 = (bf16[80,384]{1,0:T(8,128)(2,1)S(1)}, bf16[80,384]{1,0:T(8,128)(2,1)S(1)}, u32[]{:S(2)}, u32[]{:S(2)}) collective-permute-start(bf16[80,384]{1,0:T(8,128)(2,1)S(1)} %bitcast.144), channel_id=1, source_target_pairs={{4,0},{8,4},{12,8},{5,1},{9,5},{13,9},{6,2},{10,6},{14,10},{7,3},{... | collective-permute-start | bytes 184328 | tf_op jit(solution)/shard_map/ppermute | solution.py:24
  62.4 6.2 %collective-permute-start.7 = (bf16[80,6]{0,1:T(8,128)(2,1)S(1)}, bf16[80,6]{0,1:T(8,128)(2,1)S(1)}, u32[]{:S(2)}, u32[]{:S(2)}) collective-permute-start(bf16[80,6]{0,1:T(8,128)(2,1)S(1)} %bitcast.154), channel_id=1, source_target_pairs={{0,1},{1,2},{2,3},{4,5},{5,6},{6,7},{8,9},{9,10},{10,11},{12,13},{... | collective-permute-start | bytes 2888 | tf_op jit(solution)/shard_map/ppermute | solution.py:25
  66.2 5.0 %collective-permute-start.6 = (bf16[80,6]{0,1:T(8,128)(2,1)S(1)}, bf16[80,6]{0,1:T(8,128)(2,1)S(1)}, u32[]{:S(2)}, u32[]{:S(2)}) collective-permute-start(bf16[80,6]{0,1:T(8,128)(2,1)S(1)} %bitcast.156), channel_id=1, source_target_pairs={{1,0},{2,1},{3,2},{5,4},{6,5},{7,6},{9,8},{10,9},{11,10},{13,12},{... | collective-permute-start | bytes 2888 | tf_op jit(solution)/shard_map/ppermute | solution.py:26
  71.5 1.4 %copy-start.9 = (f32[10,8,6,384]{3,1,2,0:T(8,128)S(1)}, f32[10,8,6,384]{3,1,2,0:T(8,128)}, u32[]{:S(2)}) copy-start(f32[10,8,6,384]{3,1,2,0:T(8,128)} %copy.134) | copy-start | bytes 2211844
  71.5 1.6 %copy-start.12 = (f32[80,1920]{1,0:T(8,128)S(1)}, f32[80,1920]{1,0:T(8,128)}, u32[]{:S(2)}) copy-start(f32[80,1920]{1,0:T(8,128)} %get-tuple-element.19) | copy-start | bytes 1843204
  75.2 16.3 %collective-permute-start.9 = (bf16[80,384]{1,0:T(8,128)(2,1)S(1)}, bf16[80,384]{1,0:T(8,128)(2,1)}, u32[]{:S(2)}, u32[]{:S(2)}) collective-permute-start(bf16[80,384]{1,0:T(8,128)(2,1)S(1)} %bitcast.143), channel_id=1, source_target_pairs={{0,4},{4,8},{8,12},{1,5},{5,9},{9,13},{2,6},{6,10},{10,14},{3,7},{... | collective-permute-start | bytes 184328 | tf_op jit(solution)/shard_map/ppermute | solution.py:23
  81.0 11.4 %collective-permute-start.8 = (bf16[80,384]{1,0:T(8,128)(2,1)}, bf16[80,384]{1,0:T(8,128)(2,1)}, u32[]{:S(2)}, u32[]{:S(2)}) collective-permute-start(bf16[80,384]{1,0:T(8,128)(2,1)} %bitcast.105), channel_id=1, source_target_pairs={{4,0},{8,4},{12,8},{5,1},{9,5},{13,9},{6,2},{10,6},{14,10},{7,3},{... | collective-permute-start | bytes 184328 | tf_op jit(solution)/shard_map/ppermute | solution.py:24
  82.6 6.8 %collective-permute-start.11 = (bf16[80,6]{0,1:T(8,128)(2,1)S(1)}, bf16[80,6]{0,1:T(8,128)(2,1)S(1)}, u32[]{:S(2)}, u32[]{:S(2)}) collective-permute-start(bf16[80,6]{0,1:T(8,128)(2,1)S(1)} %bitcast.155), channel_id=1, source_target_pairs={{0,1},{1,2},{2,3},{4,5},{5,6},{6,7},{8,9},{9,10},{10,11},{12,13},{... | collective-permute-start | bytes 2888 | tf_op jit(solution)/shard_map/ppermute | solution.py:25
  87.0 4.0 %collective-permute-start.10 = (bf16[80,6]{0,1:T(8,128)(2,1)S(1)}, bf16[80,6]{0,1:T(8,128)(2,1)S(1)}, u32[]{:S(2)}, u32[]{:S(2)}) collective-permute-start(bf16[80,6]{0,1:T(8,128)(2,1)S(1)} %bitcast.157), channel_id=1, source_target_pairs={{1,0},{2,1},{3,2},{5,4},{6,5},{7,6},{9,8},{10,9},{11,10},{13,12},{... | collective-permute-start | bytes 2888 | tf_op jit(solution)/shard_map/ppermute | solution.py:26
  91.2 2.0 %copy-start.8 = (f32[10,8,6,384]{3,1,2,0:T(8,128)S(1)}, f32[10,8,6,384]{3,1,2,0:T(8,128)}, u32[]{:S(2)}) copy-start(f32[10,8,6,384]{3,1,2,0:T(8,128)} %copy.136) | copy-start | bytes 2211844
  91.2 2.0 %copy-start.10 = (f32[80,1920]{1,0:T(8,128)S(1)}, f32[80,1920]{1,0:T(8,128)}, u32[]{:S(2)}) copy-start(f32[80,1920]{1,0:T(8,128)} %get-tuple-element.15) | copy-start | bytes 1843204
  91.3 2.0 %copy-start.11 = (f32[80,1920]{1,0:T(8,128)S(1)}, f32[80,1920]{1,0:T(8,128)}, u32[]{:S(2)}) copy-start(f32[80,1920]{1,0:T(8,128)} %get-tuple-element.16) | copy-start | bytes 1843204
  96.6 14.8 %all-to-all-start.2 = ((f32[80,4,256]{2,0,1:T(8,128)}), f32[80,4,256]{2,0,1:T(8,128)S(1)}, u32[]{:S(2)}, u32[]{:S(2)}) async-start(f32[80,4,256]{2,0,1:T(8,128)} %broadcast_select_fusion), calls=%async_computation.2 | async-start | bytes 655360 | tf_op jit(solution)/shard_map/all_to_all | solution.py:157
  (7 other events, 7.7 us)

commit v3 on v2

--- a/solution.py
+++ b/solution.py
@@ -13,13 +13,21 @@
     return forward, backward
 
 
-def exchange(blocks):
+def edges_3d(block):
+    return (block[:, -1, :], block[:, 0, :], block[:, :, -1], block[:, :, 0])
+
+
+def edges_flat(flat, rows, cols):
+    return (flat[:, (rows - 1) * cols :], flat[:, :cols], flat[:, cols - 1 :: cols], flat[:, ::cols])
+
+
+def exchange(edge_sets):
     fwd_x, bwd_x = shift_pairs(lax.axis_size("gx"))
     fwd_y, bwd_y = shift_pairs(lax.axis_size(Y_AXES))
-    last_rows = jnp.concatenate([b[:, -1, :] for b in blocks], axis=1)
-    first_rows = jnp.concatenate([b[:, 0, :] for b in blocks], axis=1)
-    last_cols = jnp.concatenate([b[:, :, -1] for b in blocks], axis=1)
-    first_cols = jnp.concatenate([b[:, :, 0] for b in blocks], axis=1)
+    last_rows = jnp.concatenate([e[0] for e in edge_sets], axis=1)
+    first_rows = jnp.concatenate([e[1] for e in edge_sets], axis=1)
+    last_cols = jnp.concatenate([e[2] for e in edge_sets], axis=1)
+    first_cols = jnp.concatenate([e[3] for e in edge_sets], axis=1)
     above = lax.ppermute(last_rows, "gx", fwd_x)
     below = lax.ppermute(first_rows, "gx", bwd_x)
     left = lax.ppermute(last_cols, Y_AXES, fwd_y)
@@ -27,8 +35,8 @@
     out = []
     xo = 0
     yo = 0
-    for b in blocks:
-        w, h = b.shape[2], b.shape[1]
+    for e in edge_sets:
+        w, h = e[0].shape[1], e[2].shape[1]
         out.append(
             (above[:, xo : xo + w], below[:, xo : xo + w], left[:, yo : yo + h], right[:, yo : yo + h])
         )
@@ -63,7 +71,7 @@
 
 
 def mix_levels(matrix, flat):
-    return jnp.dot(matrix, flat, precision=HI, preferred_element_type=jnp.float32)
+    return jnp.dot(matrix, flat, precision=lax.Precision.HIGH, preferred_element_type=jnp.float32)
 
 
 def nest_segments(nest_of, first, count):
@@ -78,11 +86,39 @@
     return (left_w, right_w)
 
 
-def block_expansion(block_rows, block_cols, rows, cols, zero):
-    r = lax.broadcasted_iota(jnp.int32, (block_rows * block_cols, rows * cols), 0) + zero
-    p = lax.broadcasted_iota(jnp.int32, (block_rows * block_cols, rows * cols), 1)
-    hit = ((p // cols) // 3 == r // block_cols) & ((p % cols) // 3 == r % block_cols)
-    return hit.astype(jnp.float32)
+def column_expansion(block_cols, cols, zero):
+    b = lax.broadcasted_iota(jnp.int32, (block_cols, cols), 0) + zero
+    c = lax.broadcasted_iota(jnp.int32, (block_cols, cols), 1)
+    return (c // 3 == b).astype(jnp.float32)
+
+
+def expand_blocks(block_flat, block_rows, block_cols, cols, expand):
+    pieces = []
+    for a in range(block_rows):
+        wide = jnp.dot(
+            block_flat[:, a * block_cols : (a + 1) * block_cols],
+            expand,
+            precision=HI,
+            preferred_element_type=jnp.float32,
+        )
+        pieces += [wide, wide, wide]
+    return jnp.concatenate(pieces, axis=1)
+
+
+def block_sums(flat, block_rows, cols, expand):
+    pieces = []
+    for a in range(block_rows):
+        rows3 = (
+            flat[:, (3 * a) * cols : (3 * a + 1) * cols]
+            + flat[:, (3 * a + 1) * cols : (3 * a + 2) * cols]
+        ) + flat[:, (3 * a + 2) * cols : (3 * a + 3) * cols]
+        pieces.append(
+            lax.dot_general(
+                rows3, expand, (((1,), (1,)), ((), ())), precision=HI,
+                preferred_element_type=jnp.float32,
+            )
+        )
+    return jnp.concatenate(pieces, axis=1)
 
 
 def body(parent, nest, nu_parent, nu_nest, relax, feedback, vert_mix, fp_owner, fp_cell, nest_of):
@@ -92,7 +128,7 @@
     here_x = lax.axis_index("gx")
     zero = jnp.minimum(here_x, 0)
 
-    parent_halo, nest_halo = exchange([parent, nest])
+    parent_halo, nest_halo = exchange([edges_3d(parent), edges_3d(nest)])
     centre = parent.astype(jnp.float32).reshape(levels, p_rows * p_cols)
     stencil = flat_stencil(centre, p_rows, p_cols, parent_halo)
     flat_parent = mix_levels(vert_mix, centre + nu_parent[:, None] * stencil)
@@ -126,8 +162,8 @@
 
     block_rows = n_rows // 3
     block_cols = n_cols // 3
-    expand = block_expansion(block_rows, block_cols, n_rows, n_cols, zero)
-    forcing_full = jnp.dot(forcing_flat, expand, precision=HI, preferred_element_type=jnp.float32)
+    expand = column_expansion(block_cols, n_cols, zero)
+    forcing_full = expand_blocks(forcing_flat, block_rows, block_cols, n_cols, expand)
     row_start = here_x * n_rows
     left_w, right_w = row_weights(nest_segments(nest_of, row_start - 1, n_rows + 2))
     up_w = per_row(left_w, n_rows, n_cols)
@@ -137,16 +173,13 @@
     halo = nest_halo
     for turn_no in range(3):
         if turn_no > 0:
-            shaped = nest_state.astype(jnp.bfloat16).reshape(levels, n_rows, n_cols)
-            (halo,) = exchange([shaped])
+            (halo,) = exchange([edges_flat(nest_state.astype(jnp.bfloat16), n_rows, n_cols)])
         stencil_sum = flat_stencil(nest_state, n_rows, n_cols, halo, up_w, down_w)
         moved = nest_state + nu_nest[:, None] * stencil_sum
         moved = moved + relax[:, None] * (forcing_full - moved)
         nest_state = mix_levels(vert_mix, moved)
 
-    block_sum = lax.dot_general(
-        nest_state, expand, (((1,), (1,)), ((), ())), precision=HI, preferred_element_type=jnp.float32
-    )
+    block_sum = block_sums(nest_state, block_rows, n_cols, expand)
     nudge_gap = block_sum / 9.0 - forcing_flat
     if slots >= requests:
         outgoing = jnp.where(chosen[None, :, :], nudge_gap[:, None, :], 0.0)

time: 122 us -> 128 us (1.049)
  other arithmetic: 18.9 us -> 12.5 us
  local copies, waits for them, and re-layouts: 30.1 us -> 36.1 us
  waiting for transfers between devices: 15.1 us -> 19.2 us
  starting transfers between devices: 43.9 us -> 47.5 us
    convert_element_type x12, other arithmetic: 6.43 us -> 0.74 us  [flat_stencil(): above, below, left, right = (h.astype(flat.dtype) for h in halo)]
    slice x11 -> x9, local copies, waits for them, and re-layouts: 2.69 us -> 7.49 us  [the longest x2 2.19 us: edges_flat(): flat[:, ::cols]]
    unnamed x68 -> x109, local copies, waits for them, and re-layouts: 10.8 us -> 15.5 us
    all_to_all x1, waiting for transfers between devices: 4.26 us -> 8.68 us  [body(): lax.all_to_all(jnp.take(flat_parent, served_ids, axis=1), 'gx', split_axi...]
    ppermute x3, waiting for transfers between devices: 0.01 us -> 2.23 us  [exchange(): above = lax.ppermute(last_rows, 'gx', fwd_x)]
    slice x4, local copies, waits for them, and re-layouts: 4.41 us -> 2.42 us  [flat_stencil(): up = jnp.concatenate([above, flat[:, :-cols]], axis=1)]
    all_to_all x1, starting transfers between devices: 4.13 us -> 5.94 us  [body(): lax.all_to_all(wanted, 'gx', split_axis=0, concat_axis=0, tiled=True)]
    ppermute x3, waiting for transfers between devices: 1.7 us -> 0.01 us  [exchange(): right = lax.ppermute(first_cols, Y_AXES, bwd_y)]
  transfers between devices with their start and end apart: 15 -> 15, of which waited for: 4 -> 4; matrix products, arithmetic and copies ran while one was open for 23% -> 14% of each run, Pallas kernels for 0% -> 0%
where the time goes in v3:
time: 128 us; the launch traced here: 127 us
  starting transfers between devices  47.5 us (37%)
  local copies, waits for them, and re-layouts  36.1 us (28%)
  waiting for transfers between devices  19.2 us (15%)
  other arithmetic  12.5 us (10%)
  matrix products  10 us (8%)
  between operations  1.55 us (1%)
    unnamed x109, local copies, waits for them, and re-layouts  15.5 us
    ppermute x3, starting transfers between devices, exchange(): above = lax.ppermute(last_rows, 'gx', fwd_x)  14.4 us
    ppermute x3, starting transfers between devices, exchange(): left = lax.ppermute(last_cols, Y_AXES, fwd_y)  9.09 us
    dot_general x4, matrix products, mix_levels(): jnp.dot(matrix, flat, precision=lax.Precision.HIGH, preferred_element_typ...  8.81 us
    all_to_all x1, waiting for transfers between devices, body(): lax.all_to_all(jnp.take(flat_parent, served_ids, axis=1), 'gx', split_axi...  8.68 us
    all_to_all x1, waiting for transfers between devices, body(): lax.all_to_all(outgoing, 'gx', split_axis=1, concat_axis=1, tiled=True)  8.27 us
    scatter-add x1, other arithmetic, body(): summed = jnp.zeros_like(flat_parent).at[:, served_ids].add(incoming)  6.4 us
    all_to_all x1, starting transfers between devices, body(): lax.all_to_all(wanted, 'gx', split_axis=0, concat_axis=0, tiled=True)  5.94 us
  transfers between devices with their start and end apart: 15, of which 4 were waited for; matrix products, arithmetic and copies ran while one was open for 14% of the time, Pallas kernels for 0%

profile of v3, /device:TPU:0, one launch (start us, length us, event | category | flops | bytes accessed | tf_op | source)
XLA Modules:
  0.0 126.8 jit_solution(422907337478921744)
XLA Ops:
  0.7 1.2 fusion.151
  2.3 1.3 %collective-permute-start.2 = (bf16[80,14]{0,1:T(8,128)(2,1)S(1)}, bf16[80,14]{0,1:T(8,128)(2,1)S(1)}, u32[]{:S(2)}, u32[]{:S(2)}) collective-permute-start(bf16[80,14]{0,1:T(8,128)(2,1)S(1)} %pad_maximum_fusion.2), channel_id=1, source_target_pairs={{1,0},{2,1},{3,2},{5,4},{6,5},{7,6},{9,8},{10,9},{11,10},{13,12},{... | collective-permute-start | bytes 6728 | tf_op jit(solution)/shard_map/ppermute | solution.py:34
  3.9 3.0 %collective-permute-start.3 = (bf16[80,14]{0,1:T(8,128)(2,1)S(1)}, bf16[80,14]{0,1:T(8,128)(2,1)S(1)}, u32[]{:S(2)}, u32[]{:S(2)}) collective-permute-start(bf16[80,14]{0,1:T(8,128)(2,1)S(1)} %pad_maximum_fusion.3), channel_id=1, source_target_pairs={{0,1},{1,2},{2,3},{4,5},{5,6},{6,7},{8,9},{9,10},{10,11},{12,13},{... | collective-permute-start | bytes 6728 | tf_op jit(solution)/shard_map/ppermute | solution.py:33
  7.1 5.0 %collective-permute-start.1 = (bf16[80,640]{1,0:T(8,128)(2,1)S(1)}, bf16[80,640]{1,0:T(8,128)(2,1)S(1)}, u32[]{:S(2)}, u32[]{:S(2)}) collective-permute-start(bf16[80,640]{1,0:T(8,128)(2,1)S(1)} %pad_maximum_fusion.1), channel_id=1, source_target_pairs={{0,4},{4,8},{8,12},{1,5},{5,9},{9,13},{2,6},{6,10},{10,14},{3,7},{... | collective-permute-start | bytes 307208 | tf_op jit(solution)/shard_map/ppermute | solution.py:31
  12.1 1.3 %collective-permute-start = (bf16[80,640]{1,0:T(8,128)(2,1)S(1)}, bf16[80,640]{1,0:T(8,128)(2,1)S(1)}, u32[]{:S(2)}, u32[]{:S(2)}) collective-permute-start(bf16[80,640]{1,0:T(8,128)(2,1)S(1)} %pad_maximum_fusion), channel_id=1, source_target_pairs={{4,0},{8,4},{12,8},{5,1},{9,5},{13,9},{6,2},{10,6},{14,10},{7,3},{... | collective-permute-start | bytes 307208 | tf_op jit(solution)/shard_map/ppermute | solution.py:32
  14.7 5.9 %all-to-all-start = ((s32[4,256,1]{1,2,0:T(1,128)}), s32[4,256,1]{1,2,0:T(1,128)S(1)}, u32[]{:S(2)}, u32[]{:S(2)}) async-start(s32[4,256,1]{1,2,0:T(1,128)} %compare_select_fusion.1), calls=%async_computation | async-start | bytes 8192 | tf_op jit(solution)/shard_map/all_to_all | solution.py:151
  20.7 1.3 fusion.146
  22.0 1.1 fusion.147
  24.9 1.3 %fusion.144 = (f32[80,2303]{1,0:T(8,128)}, f32[80,2303]{1,0:T(8,128)}) fusion(f32[80,2304]{1,0:T(8,128)S(1)} %bitcast.89), kind=kLoop, calls=%fused_computation.213 | loop fusion | bytes 2947840 | tf_op jit(solution)/shard_map/slice | solution.py:65
  26.2 1.2 fusion.145
  36.7 2.8 %convolution_bitcast_fusion.3 = f32[80,2048]{1,0:T(8,128)S(1)} fusion(f32[80,80]{1,0:T(8,128)S(1)} %copy-done, f32[80,2048]{1,0:T(8,128)S(1)} %bitcast.94, f32[80,256]{1,0:T(8,128)S(1)} %slice_convert_fusion.3, f32[80,1792]{1,0:T(8,128)} %get-tuple-element.28, f32[80,1792]{1,0:T(8,128)} %get-tuple-element.27, f32[80,256]{1,0:T(8,128)S(1)} %slice_convert_fusion.2, ...), kind=kOutput, calls=%fused_computation.6 | convolution fusion | flops 80445440 | bytes 5272256 | tf_op jit(solution)/shard_map/dot_general | solution.py:74
  40.3 2.8 %gather_fusion.1 = f32[1024,80]{1,0:T(8,128)S(1)} fusion(f32[80,2048]{0,1:T(8,128)S(1)} %copy.65, s32[1024]{0:T(1024)S(1)} %get-tuple-element.56), kind=kCustom, calls=%fused_computation.1 | custom fusion | bytes 659456 | tf_op jit(solution)/shard_map/jit(_take)/gather | solution.py:153
  44.1 5.2 %all-to-all-start.1 = ((f32[80,4,256]{2,0,1:T(8,128)}), f32[80,4,256]{2,0,1:T(8,128)S(1)}, u32[]{:S(2)}, u32[]{:S(2)}) async-start(f32[80,4,256]{2,0,1:T(8,128)} %broadcast_select_fusion.1), calls=%async_computation.1 | async-start | bytes 655360 | tf_op jit(solution)/shard_map/all_to_all | solution.py:152
  51.1 8.7 %all-to-all-done.1 = f32[80,4,256]{2,0,1:T(8,128)S(1)} async-done(((f32[80,4,256]{2,0,1:T(8,128)}), f32[80,4,256]{2,0,1:T(8,128)S(1)}, u32[]{:S(2)}, u32[]{:S(2)}) %all-to-all-start.1) | async-done | bytes 327712 | tf_op jit(solution)/shard_map/all_to_all | solution.py:152
  62.5 3.2 %fusion.153 = (bf16[80,2304]{1,0:T(8,128)(2,1)}, f32[80,2304]{1,0:T(8,128)S(1)}) fusion(f32[80,80]{1,0:T(8,128)S(1)} %copy-done, f32[80,2304]{1,0:T(8,128)S(1)} %constant_dynamic-update-slice_fusion, f32[80,2304]{1,0:T(8,128)S(1)} %bitcast.91, f32[80,1920]{1,0:T(8,128)} %get-tuple-element.23, f32[80,384]{1,0:T(8,128)S(1)} %slice_convert_fusion, ...), kind=kOutput, calls=%fused_computation.222 | convolution fusion | flops 91607040 | bytes 7052800 | tf_op jit(solution)/shard_map/dot_general | solution.py:74
  65.8 1.1 slice.215
  66.9 1.1 slice.217
  68.9 1.3 %collective-permute-start.6 = (bf16[80,6]{1,0:T(8,128)(2,1)S(1)}, bf16[80,6]{1,0:T(8,128)(2,1)S(1)}, u32[]{:S(2)}, u32[]{:S(2)}) collective-permute-start(bf16[80,6]{1,0:T(8,128)(2,1)S(1)} %slice.215), channel_id=1, source_target_pairs={{1,0},{2,1},{3,2},{5,4},{6,5},{7,6},{9,8},{10,9},{11,10},{13,12},{... | collective-permute-start | bytes 2888 | tf_op jit(solution)/shard_map/ppermute | solution.py:34
  70.2 3.0 %collective-permute-start.7 = (bf16[80,6]{1,0:T(8,128)(2,1)S(1)}, bf16[80,6]{1,0:T(8,128)(2,1)S(1)}, u32[]{:S(2)}, u32[]{:S(2)}) collective-permute-start(bf16[80,6]{1,0:T(8,128)(2,1)S(1)} %slice.217), channel_id=1, source_target_pairs={{0,1},{1,2},{2,3},{4,5},{5,6},{6,7},{8,9},{9,10},{10,11},{12,13},{... | collective-permute-start | bytes 2888 | tf_op jit(solution)/shard_map/ppermute | solution.py:33
  73.5 1.3 %collective-permute-start.4 = (bf16[80,384]{1,0:T(8,128)(2,1)S(1)}, bf16[80,384]{1,0:T(8,128)(2,1)S(1)}, u32[]{:S(2)}, u32[]{:S(2)}) collective-permute-start(bf16[80,384]{1,0:T(8,128)(2,1)S(1)} %get-tuple-element.32), channel_id=1, source_target_pairs={{4,0},{8,4},{12,8},{5,1},{9,5},{13,9},{6,2},{10,6},{14,10},{7,3},{... | collective-permute-start | bytes 184328 | tf_op jit(solution)/shard_map/ppermute | solution.py:32
  74.8 4.5 %collective-permute-start.5 = (bf16[80,384]{1,0:T(8,128)(2,1)S(1)}, bf16[80,384]{1,0:T(8,128)(2,1)S(1)}, u32[]{:S(2)}, u32[]{:S(2)}) collective-permute-start(bf16[80,384]{1,0:T(8,128)(2,1)S(1)} %get-tuple-element.31), channel_id=1, source_target_pairs={{0,4},{4,8},{8,12},{1,5},{5,9},{9,13},{2,6},{6,10},{10,14},{3,7},{... | collective-permute-start | bytes 184328 | tf_op jit(solution)/shard_map/ppermute | solution.py:31
  80.0 1.1 collective-permute-done.5
  81.9 1.8 %fusion.154 = (bf16[80,2304]{1,0:T(8,128)(2,1)}, f32[80,2304]{1,0:T(8,128)S(1)}) fusion(f32[80,80]{1,0:T(8,128)S(1)} %copy-done, f32[80,2304]{1,0:T(8,128)S(1)} %constant_dynamic-update-slice_fusion, f32[80,2304]{1,0:T(8,128)S(1)} %get-tuple-element.48, f32[80,1920]{1,0:T(8,128)S(1)} %get-tuple-element.19, f32[80,384]{1,0:T(8,128)S(1)} %convert_element_type.81, ...), kind=kOutput, calls=%fused_computation.223 | convolution fusion | flops 91607040 | bytes 7052800 | tf_op jit(solution)/shard_map/dot_general | solution.py:74
  83.6 1.1 slice.223
  86.7 1.3 %collective-permute-start.10 = (bf16[80,6]{1,0:T(8,128)(2,1)S(1)}, bf16[80,6]{1,0:T(8,128)(2,1)S(1)}, u32[]{:S(2)}, u32[]{:S(2)}) collective-permute-start(bf16[80,6]{1,0:T(8,128)(2,1)S(1)} %slice.223), channel_id=1, source_target_pairs={{1,0},{2,1},{3,2},{5,4},{6,5},{7,6},{9,8},{10,9},{11,10},{13,12},{... | collective-permute-start | bytes 2888 | tf_op jit(solution)/shard_map/ppermute | solution.py:34
  88.0 3.0 %collective-permute-start.11 = (bf16[80,6]{1,0:T(8,128)(2,1)S(1)}, bf16[80,6]{1,0:T(8,128)(2,1)S(1)}, u32[]{:S(2)}, u32[]{:S(2)}) collective-permute-start(bf16[80,6]{1,0:T(8,128)(2,1)S(1)} %slice.225), channel_id=1, source_target_pairs={{0,1},{1,2},{2,3},{4,5},{5,6},{6,7},{8,9},{9,10},{10,11},{12,13},{... | collective-permute-start | bytes 2888 | tf_op jit(solution)/shard_map/ppermute | solution.py:33
  91.3 1.3 %collective-permute-start.8 = (bf16[80,384]{1,0:T(8,128)(2,1)S(1)}, bf16[80,384]{1,0:T(8,128)(2,1)S(1)}, u32[]{:S(2)}, u32[]{:S(2)}) collective-permute-start(bf16[80,384]{1,0:T(8,128)(2,1)S(1)} %get-tuple-element.30), channel_id=1, source_target_pairs={{4,0},{8,4},{12,8},{5,1},{9,5},{13,9},{6,2},{10,6},{14,10},{7,3},{... | collective-permute-start | bytes 184328 | tf_op jit(solution)/shard_map/ppermute | solution.py:32
  92.6 4.9 %collective-permute-start.9 = (bf16[80,384]{1,0:T(8,128)(2,1)S(1)}, bf16[80,384]{1,0:T(8,128)(2,1)S(1)}, u32[]{:S(2)}, u32[]{:S(2)}) collective-permute-start(bf16[80,384]{1,0:T(8,128)(2,1)S(1)} %get-tuple-element.29), channel_id=1, source_target_pairs={{0,4},{4,8},{8,12},{1,5},{5,9},{9,13},{2,6},{6,10},{10,14},{3,7},{... | collective-permute-start | bytes 184328 | tf_op jit(solution)/shard_map/ppermute | solution.py:31
  98.2 1.1 collective-permute-done.9
  104.1 5.1 %all-to-all-start.2 = ((f32[80,4,256]{2,0,1:T(8,128)}), f32[80,4,256]{2,0,1:T(8,128)S(1)}, u32[]{:S(2)}, u32[]{:S(2)}) async-start(f32[80,4,256]{2,0,1:T(8,128)} %broadcast_select_fusion), calls=%async_computation.2 | async-start | bytes 655360 | tf_op jit(solution)/shard_map/all_to_all | solution.py:190
  109.9 8.3 %all-to-all-done.2 = f32[80,4,256]{2,0,1:T(8,128)S(1)} async-done(((f32[80,4,256]{2,0,1:T(8,128)}), f32[80,4,256]{2,0,1:T(8,128)S(1)}, u32[]{:S(2)}, u32[]{:S(2)}) %all-to-all-start.2) | async-done | bytes 327712 | tf_op jit(solution)/shard_map/all_to_all | solution.py:190
  118.4 6.4 %scatter_custom_fusion = f32[80,2048]{0,1:T(8,128)S(1)} fusion(s32[1024]{0:T(1024)} %bitcast.123, f32[1024,80]{1,0:T(8,128)S(1)} %copy.69, f32[]{:T(128)} %constant.75.clone.1), kind=kCustom, calls=%fused_computation.75 | custom fusion | flops 81920 | bytes 655872 | tf_op jit(solution)/shard_map/scatter-add | solution.py:191
  (197 shorter events, 32.3 us)
Async XLA Ops:
  0.6 35.4 %copy-start = (f32[80,80]{1,0:T(8,128)S(1)}, f32[80,80]{1,0:T(8,128)}, u32[]{:S(2)}) copy-start(f32[80,80]{1,0:T(8,128)} %param.16) | copy-start | bytes 76804
  0.6 1.3 %copy-start.7 = (bf16[80,6,384]{2,0,1:T(8,128)(2,1)S(1)}, bf16[80,6,384]{2,0,1:T(8,128)(2,1)}, u32[]{:S(2)}) copy-start(bf16[80,6,384]{2,0,1:T(8,128)(2,1)} %param.11) | copy-start | bytes 1105924
  2.1 4.8 %copy-start.6 = (bf16[80,8,256]{2,1,0:T(8,128)(2,1)S(1)}, bf16[80,8,256]{2,1,0:T(8,128)(2,1)}, u32[]{:S(2)}) copy-start(bf16[80,8,256]{2,1,0:T(8,128)(2,1)} %param.10) | copy-start | bytes 983044
  2.3 26.3 %collective-permute-start.2 = (bf16[80,14]{0,1:T(8,128)(2,1)S(1)}, bf16[80,14]{0,1:T(8,128)(2,1)S(1)}, u32[]{:S(2)}, u32[]{:S(2)}) collective-permute-start(bf16[80,14]{0,1:T(8,128)(2,1)S(1)} %pad_maximum_fusion.2), channel_id=1, source_target_pairs={{1,0},{2,1},{3,2},{5,4},{6,5},{7,6},{9,8},{10,9},{11,10},{13,12},{... | collective-permute-start | bytes 6728 | tf_op jit(solution)/shard_map/ppermute | solution.py:34
  3.9 24.7 %collective-permute-start.3 = (bf16[80,14]{0,1:T(8,128)(2,1)S(1)}, bf16[80,14]{0,1:T(8,128)(2,1)S(1)}, u32[]{:S(2)}, u32[]{:S(2)}) collective-permute-start(bf16[80,14]{0,1:T(8,128)(2,1)S(1)} %pad_maximum_fusion.3), channel_id=1, source_target_pairs={{0,1},{1,2},{2,3},{4,5},{5,6},{6,7},{8,9},{9,10},{10,11},{12,13},{... | collective-permute-start | bytes 6728 | tf_op jit(solution)/shard_map/ppermute | solution.py:33
  7.1 28.2 %collective-permute-start.1 = (bf16[80,640]{1,0:T(8,128)(2,1)S(1)}, bf16[80,640]{1,0:T(8,128)(2,1)S(1)}, u32[]{:S(2)}, u32[]{:S(2)}) collective-permute-start(bf16[80,640]{1,0:T(8,128)(2,1)S(1)} %pad_maximum_fusion.1), channel_id=1, source_target_pairs={{0,4},{4,8},{8,12},{1,5},{5,9},{9,13},{2,6},{6,10},{10,14},{3,7},{... | collective-permute-start | bytes 307208 | tf_op jit(solution)/shard_map/ppermute | solution.py:31
  12.1 1.3 %copy-start.42 = (s32[1,1,256]{2,1,0:T(1,128)S(1)}, s32[1,1,256]{2,1,0:T(1,128)}, u32[]{:S(2)}) copy-start(s32[1,1,256]{2,1,0:T(1,128)} %param.18) | copy-start | bytes 3076
  12.1 23.2 %collective-permute-start = (bf16[80,640]{1,0:T(8,128)(2,1)S(1)}, bf16[80,640]{1,0:T(8,128)(2,1)S(1)}, u32[]{:S(2)}, u32[]{:S(2)}) collective-permute-start(bf16[80,640]{1,0:T(8,128)(2,1)S(1)} %pad_maximum_fusion), channel_id=1, source_target_pairs={{4,0},{8,4},{12,8},{5,1},{9,5},{13,9},{6,2},{10,6},{14,10},{7,3},{... | collective-permute-start | bytes 307208 | tf_op jit(solution)/shard_map/ppermute | solution.py:32
  14.7 18.1 %all-to-all-start = ((s32[4,256,1]{1,2,0:T(1,128)}), s32[4,256,1]{1,2,0:T(1,128)S(1)}, u32[]{:S(2)}, u32[]{:S(2)}) async-start(s32[4,256,1]{1,2,0:T(1,128)} %compare_select_fusion.1), calls=%async_computation | async-start | bytes 8192 | tf_op jit(solution)/shard_map/all_to_all | solution.py:151
  23.1 4.4 %copy-start.17 = (pred[4,256]{1,0:T(4,128)(4,1)}, pred[4,256]{1,0:T(4,128)(4,1)S(1)}, u32[]{:S(2)}) copy-start(pred[4,256]{1,0:T(4,128)(4,1)S(1)} %iota_compare_fusion) | copy-start | bytes 3076
  44.1 5.2 %copy-start.36 = (s32[8]{0:T(128)S(1)}, s32[8]{0:T(128)}, u32[]{:S(2)}) copy-start(s32[8]{0:T(128)} %and_select_fusion) | copy-start | bytes 100
  44.1 5.5 %copy-start.14 = (bf16[80,640]{1,0:T(8,128)(2,1)S(1)}, bf16[80,640]{1,0:T(8,128)(2,1)}, u32[]{:S(2)}) copy-start(bf16[80,640]{1,0:T(8,128)(2,1)} %copy-done.13) | copy-start | bytes 307204
  44.1 15.7 %all-to-all-start.1 = ((f32[80,4,256]{2,0,1:T(8,128)}), f32[80,4,256]{2,0,1:T(8,128)S(1)}, u32[]{:S(2)}, u32[]{:S(2)}) async-start(f32[80,4,256]{2,0,1:T(8,128)} %broadcast_select_fusion.1), calls=%async_computation.1 | async-start | bytes 655360 | tf_op jit(solution)/shard_map/all_to_all | solution.py:152
  49.5 12.3 %copy-start.9 = (f32[2304]{0:T(1024)}, f32[2304]{0:T(1024)S(1)}, u32[]{:S(2)}) copy-start(f32[2304]{0:T(1024)S(1)} %mul.125) | copy-start | bytes 27652
  49.5 0.9 copy-start.16
  49.6 12.2 %copy-start.11 = (f32[2304]{0:T(1024)}, f32[2304]{0:T(1024)S(1)}, u32[]{:S(2)}) copy-start(f32[2304]{0:T(1024)S(1)} %mul.128) | copy-start | bytes 27652
  60.4 1.4 %copy-start.8 = (f32[80,384]{1,0:T(8,128)S(1)}, f32[80,384]{1,0:T(8,128)}, u32[]{:S(2)}) copy-start(f32[80,384]{1,0:T(8,128)} %slice_convert_fusion.1) | copy-start | bytes 368644
  61.1 1.1 copy-start.4
  61.1 1.3 %copy-start.5 = (f32[80,2303]{1,0:T(8,128)S(1)}, f32[80,2303]{1,0:T(8,128)}, u32[]{:S(2)}) copy-start(f32[80,2303]{1,0:T(8,128)} %get-tuple-element.22) | copy-start | bytes 2210884
  68.9 10.5 %collective-permute-start.6 = (bf16[80,6]{1,0:T(8,128)(2,1)S(1)}, bf16[80,6]{1,0:T(8,128)(2,1)S(1)}, u32[]{:S(2)}, u32[]{:S(2)}) collective-permute-start(bf16[80,6]{1,0:T(8,128)(2,1)S(1)} %slice.215), channel_id=1, source_target_pairs={{1,0},{2,1},{3,2},{5,4},{6,5},{7,6},{9,8},{10,9},{11,10},{13,12},{... | collective-permute-start | bytes 2888 | tf_op jit(solution)/shard_map/ppermute | solution.py:34
  70.2 9.6 %collective-permute-start.7 = (bf16[80,6]{1,0:T(8,128)(2,1)S(1)}, bf16[80,6]{1,0:T(8,128)(2,1)S(1)}, u32[]{:S(2)}, u32[]{:S(2)}) collective-permute-start(bf16[80,6]{1,0:T(8,128)(2,1)S(1)} %slice.217), channel_id=1, source_target_pairs={{0,1},{1,2},{2,3},{4,5},{5,6},{6,7},{8,9},{9,10},{10,11},{12,13},{... | collective-permute-start | bytes 2888 | tf_op jit(solution)/shard_map/ppermute | solution.py:33
  73.5 6.6 %collective-permute-start.4 = (bf16[80,384]{1,0:T(8,128)(2,1)S(1)}, bf16[80,384]{1,0:T(8,128)(2,1)S(1)}, u32[]{:S(2)}, u32[]{:S(2)}) collective-permute-start(bf16[80,384]{1,0:T(8,128)(2,1)S(1)} %get-tuple-element.32), channel_id=1, source_target_pairs={{4,0},{8,4},{12,8},{5,1},{9,5},{13,9},{6,2},{10,6},{14,10},{7,3},{... | collective-permute-start | bytes 184328 | tf_op jit(solution)/shard_map/ppermute | solution.py:32
  74.8 6.4 %collective-permute-start.5 = (bf16[80,384]{1,0:T(8,128)(2,1)S(1)}, bf16[80,384]{1,0:T(8,128)(2,1)S(1)}, u32[]{:S(2)}, u32[]{:S(2)}) collective-permute-start(bf16[80,384]{1,0:T(8,128)(2,1)S(1)} %get-tuple-element.31), channel_id=1, source_target_pairs={{0,4},{4,8},{8,12},{1,5},{5,9},{9,13},{2,6},{6,10},{10,14},{3,7},{... | collective-permute-start | bytes 184328 | tf_op jit(solution)/shard_map/ppermute | solution.py:31
  86.7 10.9 %collective-permute-start.10 = (bf16[80,6]{1,0:T(8,128)(2,1)S(1)}, bf16[80,6]{1,0:T(8,128)(2,1)S(1)}, u32[]{:S(2)}, u32[]{:S(2)}) collective-permute-start(bf16[80,6]{1,0:T(8,128)(2,1)S(1)} %slice.223), channel_id=1, source_target_pairs={{1,0},{2,1},{3,2},{5,4},{6,5},{7,6},{9,8},{10,9},{11,10},{13,12},{... | collective-permute-start | bytes 2888 | tf_op jit(solution)/shard_map/ppermute | solution.py:34
  88.0 9.9 %collective-permute-start.11 = (bf16[80,6]{1,0:T(8,128)(2,1)S(1)}, bf16[80,6]{1,0:T(8,128)(2,1)S(1)}, u32[]{:S(2)}, u32[]{:S(2)}) collective-permute-start(bf16[80,6]{1,0:T(8,128)(2,1)S(1)} %slice.225), channel_id=1, source_target_pairs={{0,1},{1,2},{2,3},{4,5},{5,6},{6,7},{8,9},{9,10},{10,11},{12,13},{... | collective-permute-start | bytes 2888 | tf_op jit(solution)/shard_map/ppermute | solution.py:33
  91.3 6.9 %collective-permute-start.8 = (bf16[80,384]{1,0:T(8,128)(2,1)S(1)}, bf16[80,384]{1,0:T(8,128)(2,1)S(1)}, u32[]{:S(2)}, u32[]{:S(2)}) collective-permute-start(bf16[80,384]{1,0:T(8,128)(2,1)S(1)} %get-tuple-element.30), channel_id=1, source_target_pairs={{4,0},{8,4},{12,8},{5,1},{9,5},{13,9},{6,2},{10,6},{14,10},{7,3},{... | collective-permute-start | bytes 184328 | tf_op jit(solution)/shard_map/ppermute | solution.py:32
  92.6 6.7 %collective-permute-start.9 = (bf16[80,384]{1,0:T(8,128)(2,1)S(1)}, bf16[80,384]{1,0:T(8,128)(2,1)S(1)}, u32[]{:S(2)}, u32[]{:S(2)}) collective-permute-start(bf16[80,384]{1,0:T(8,128)(2,1)S(1)} %get-tuple-element.29), channel_id=1, source_target_pairs={{0,4},{4,8},{8,12},{1,5},{5,9},{9,13},{2,6},{6,10},{10,14},{3,7},{... | collective-permute-start | bytes 184328 | tf_op jit(solution)/shard_map/ppermute | solution.py:31
  100.0 1.0 copy-start.20
  100.0 1.0 copy-start.22
  104.1 14.1 %all-to-all-start.2 = ((f32[80,4,256]{2,0,1:T(8,128)}), f32[80,4,256]{2,0,1:T(8,128)S(1)}, u32[]{:S(2)}, u32[]{:S(2)}) async-start(f32[80,4,256]{2,0,1:T(8,128)} %broadcast_select_fusion), calls=%async_computation.2 | async-start | bytes 655360 | tf_op jit(solution)/shard_map/all_to_all | solution.py:190
  124.8 1.1 copy-start.3
  124.8 1.1 copy-start.44
  (28 other events, 18.6 us)

commit v4 on v3

--- a/solution.py
+++ b/solution.py
@@ -71,7 +71,7 @@
 
 
 def mix_levels(matrix, flat):
-    return jnp.dot(matrix, flat, precision=lax.Precision.HIGH, preferred_element_type=jnp.float32)
+    return jnp.dot(matrix, flat, precision=HI, preferred_element_type=jnp.float32)
 
 
 def nest_segments(nest_of, first, count):
@@ -119,6 +119,22 @@
             )
         )
     return jnp.concatenate(pieces, axis=1)
+
+
+def split3(values):
+    hi = values.astype(jnp.bfloat16)
+    rest = values - hi.astype(jnp.float32)
+    mid = rest.astype(jnp.bfloat16)
+    lo = (rest - mid.astype(jnp.float32)).astype(jnp.bfloat16)
+    return hi, mid, lo
+
+
+def scatter_add_columns(values, ids, width):
+    levels = values.shape[0]
+    onehot = (ids[:, None] == lax.broadcasted_iota(jnp.int32, (1, width), 1)).astype(jnp.bfloat16)
+    parts = jnp.concatenate(split3(values), axis=0)
+    total = jnp.dot(parts, onehot, preferred_element_type=jnp.float32)
+    return (total[:levels] + total[levels : 2 * levels]) + total[2 * levels :]
 
 
 def body(parent, nest, nu_parent, nu_nest, relax, feedback, vert_mix, fp_owner, fp_cell, nest_of):
@@ -188,7 +204,7 @@
     else:
         outgoing = jnp.zeros((levels, tiles_x * slots), jnp.float32).at[:, places].set(nudge_gap)
     incoming = lax.all_to_all(outgoing, "gx", split_axis=1, concat_axis=1, tiled=True)
-    summed = jnp.zeros_like(flat_parent).at[:, served_ids].add(incoming)
+    summed = scatter_add_columns(incoming, served_ids, flat_parent.shape[1])
     parent_out = (flat_parent + feedback[:, None] * summed).astype(jnp.bfloat16)
     return (
         parent_out.reshape(levels, p_rows, p_cols),

time: 128 us -> 125 us (0.977)
  local copies, waits for them, and re-layouts: 36.1 us -> 29 us
  matrix products: 10 us -> 14.1 us
    unnamed x109 -> x85, local copies, waits for them, and re-layouts: 15.5 us -> 6.4 us
    scatter-add x1 -> x0, other arithmetic: 6.4 us -> none  [body(): summed = jnp.zeros_like(flat_parent).at[:, served_ids].add(incoming)]
    convert_element_type x12, other arithmetic: 0.74 us -> 5.73 us  [flat_stencil(): above, below, left, right = (h.astype(flat.dtype) for h in halo)]
    dot_general x4 -> x5, matrix products: 8.81 us -> 12.8 us  [the longest x4 10.9 us: mix_levels(): jnp.dot(matrix, flat, precision=HI, preferred_element_type=jnp.float32)]
    slice x3, local copies, waits for them, and re-layouts: 1.37 us -> 3.45 us  [edges_3d(): return (block[:, -1, :], block[:, 0, :], block[:, :, -1], block[:, :, 0])]
    convert_element_type x4, local copies, waits for them, and re-layouts: 0.38 us -> 1.73 us  [flat_stencil(): above, below, left, right = (h.astype(flat.dtype) for h in halo)]
  transfers between devices with their start and end apart: 15 -> 15, of which waited for: 4 -> 4; matrix products, arithmetic and copies ran while one was open for 14% -> 21% of each run, Pallas kernels for 0% -> 0%
where the time goes in v4:
time: 125 us; the launch traced here: 123 us
  starting transfers between devices  48.1 us (38%)
  local copies, waits for them, and re-layouts  29 us (23%)
  waiting for transfers between devices  18.2 us (15%)
  matrix products  14.1 us (11%)
  other arithmetic  12.4 us (10%)
  between operations  1.59 us (1%)
    ppermute x3, starting transfers between devices, exchange(): above = lax.ppermute(last_rows, 'gx', fwd_x)  15.2 us
    dot_general x4, matrix products, mix_levels(): jnp.dot(matrix, flat, precision=HI, preferred_element_type=jnp.float32)  10.9 us
    ppermute x3, starting transfers between devices, exchange(): left = lax.ppermute(last_cols, Y_AXES, fwd_y)  9.09 us
    all_to_all x1, waiting for transfers between devices, body(): lax.all_to_all(outgoing, 'gx', split_axis=1, concat_axis=1, tiled=True)  8.27 us
    all_to_all x1, waiting for transfers between devices, body(): lax.all_to_all(jnp.take(flat_parent, served_ids, axis=1), 'gx', split_axi...  7.91 us
    unnamed x85, local copies, waits for them, and re-layouts  6.4 us
    all_to_all x1, starting transfers between devices, body(): lax.all_to_all(wanted, 'gx', split_axis=0, concat_axis=0, tiled=True)  5.93 us
    convert_element_type x12, other arithmetic, flat_stencil(): above, below, left, right = (h.astype(flat.dtype) for h in halo)  5.73 us
  transfers between devices with their start and end apart: 15, of which 4 were waited for; matrix products, arithmetic and copies ran while one was open for 21% of the time, Pallas kernels for 0%

profile of v4, /device:TPU:0, one launch (start us, length us, event | category | flops | bytes accessed | tf_op | source)
XLA Modules:
  0.0 123.4 jit_solution(3357395379907205316)
XLA Ops:
  0.7 1.2 fusion.161
  3.2 1.3 %collective-permute-start.2 = (bf16[80,14]{0,1:T(8,128)(2,1)S(1)}, bf16[80,14]{0,1:T(8,128)(2,1)S(1)}, u32[]{:S(2)}, u32[]{:S(2)}) collective-permute-start(bf16[80,14]{0,1:T(8,128)(2,1)S(1)} %pad_maximum_fusion.2), channel_id=1, source_target_pairs={{1,0},{2,1},{3,2},{5,4},{6,5},{7,6},{9,8},{10,9},{11,10},{13,12},{... | collective-permute-start | bytes 6728 | tf_op jit(solution)/shard_map/ppermute | solution.py:34
  4.9 3.0 %collective-permute-start.3 = (bf16[80,14]{0,1:T(8,128)(2,1)S(1)}, bf16[80,14]{0,1:T(8,128)(2,1)S(1)}, u32[]{:S(2)}, u32[]{:S(2)}) collective-permute-start(bf16[80,14]{0,1:T(8,128)(2,1)S(1)} %pad_maximum_fusion.3), channel_id=1, source_target_pairs={{0,1},{1,2},{2,3},{4,5},{5,6},{6,7},{8,9},{9,10},{10,11},{12,13},{... | collective-permute-start | bytes 6728 | tf_op jit(solution)/shard_map/ppermute | solution.py:33
  7.9 1.2 fusion.162
  9.2 5.6 %collective-permute-start.1 = (bf16[80,640]{1,0:T(8,128)(2,1)S(1)}, bf16[80,640]{1,0:T(8,128)(2,1)}, u32[]{:S(2)}, u32[]{:S(2)}) collective-permute-start(bf16[80,640]{1,0:T(8,128)(2,1)S(1)} %pad_maximum_fusion.1), channel_id=1, source_target_pairs={{0,4},{4,8},{8,12},{1,5},{5,9},{9,13},{2,6},{6,10},{10,14},{3,7},{... | collective-permute-start | bytes 307208 | tf_op jit(solution)/shard_map/ppermute | solution.py:31
  15.4 1.3 %collective-permute-start = (bf16[80,640]{1,0:T(8,128)(2,1)}, bf16[80,640]{1,0:T(8,128)(2,1)}, u32[]{:S(2)}, u32[]{:S(2)}) collective-permute-start(bf16[80,640]{1,0:T(8,128)(2,1)} %pad_maximum_fusion), channel_id=1, source_target_pairs={{4,0},{8,4},{12,8},{5,1},{9,5},{13,9},{6,2},{10,6},{14,10},{7,3},{... | collective-permute-start | bytes 307208 | tf_op jit(solution)/shard_map/ppermute | solution.py:32
  17.4 5.9 %all-to-all-start = ((s32[4,256,1]{1,2,0:T(1,128)}), s32[4,256,1]{1,2,0:T(1,128)S(1)}, u32[]{:S(2)}, u32[]{:S(2)}) async-start(s32[4,256,1]{1,2,0:T(1,128)} %compare_select_fusion.1), calls=%async_computation | async-start | bytes 8192 | tf_op jit(solution)/shard_map/all_to_all | solution.py:167
  23.6 1.1 fusion.157
  27.1 1.4 %fusion.154 = (f32[80,2303]{1,0:T(8,128)}, f32[80,2303]{1,0:T(8,128)}) fusion(f32[80,2304]{1,0:T(8,128)S(1)} %bitcast.88), kind=kLoop, calls=%fused_computation.226 | loop fusion | bytes 2947840 | tf_op jit(solution)/shard_map/slice | solution.py:65
  28.5 1.2 fusion.155
  42.0 2.8 %convolution_bitcast_fusion.3 = f32[80,2048]{1,0:T(8,128)S(1)} fusion(f32[80,80]{1,0:T(8,128)S(1)} %copy-done, f32[80,2048]{1,0:T(8,128)S(1)} %bitcast.93, f32[80,256]{1,0:T(8,128)S(1)} %slice_convert_fusion.3, f32[80,1792]{1,0:T(8,128)} %get-tuple-element.28, f32[80,1792]{1,0:T(8,128)} %get-tuple-element.27, f32[80,256]{1,0:T(8,128)S(1)} %slice_convert_fusion.2, ...), kind=kOutput, calls=%fused_computation.8 | convolution fusion | flops 159088640 | bytes 5272256 | tf_op jit(solution)/shard_map/dot_general | solution.py:74
  45.1 2.8 %gather_fusion.1 = f32[1024,80]{1,0:T(8,128)S(1)} fusion(f32[80,2048]{0,1:T(8,128)S(1)} %copy.60, s32[1024]{0:T(1024)S(1)} %get-tuple-element.58), kind=kCustom, calls=%fused_computation.1 | custom fusion | bytes 659456 | tf_op jit(solution)/shard_map/jit(_take)/gather | solution.py:169
  49.0 5.1 %all-to-all-start.1 = ((f32[80,4,256]{2,0,1:T(8,128)}), f32[80,4,256]{2,0,1:T(8,128)S(1)}, u32[]{:S(2)}, u32[]{:S(2)}) async-start(f32[80,4,256]{2,0,1:T(8,128)} %broadcast_select_fusion.1), calls=%async_computation.1 | async-start | bytes 655360 | tf_op jit(solution)/shard_map/all_to_all | solution.py:168
  55.2 1.5 %slice_convert_fusion.1 = f32[80,384]{1,0:T(8,128)} fusion(bf16[80,640]{1,0:T(8,128)(2,1)} %collective-permute-done), kind=kLoop, calls=%fused_computation.151 | loop fusion | flops 30720 | bytes 184320 | tf_op jit(solution)/shard_map/convert_element_type | solution.py:57
  56.7 7.9 %all-to-all-done.1 = f32[80,4,256]{2,0,1:T(8,128)S(1)} async-done(((f32[80,4,256]{2,0,1:T(8,128)}), f32[80,4,256]{2,0,1:T(8,128)S(1)}, u32[]{:S(2)}, u32[]{:S(2)}) %all-to-all-start.1) | async-done | bytes 327712 | tf_op jit(solution)/shard_map/all_to_all | solution.py:168
  65.5 4.0 %fusion.163 = (bf16[80,2304]{1,0:T(8,128)(2,1)}, f32[80,2304]{1,0:T(8,128)S(1)}) fusion(f32[80,80]{1,0:T(8,128)S(1)} %copy-done, f32[80,2304]{1,0:T(8,128)S(1)} %constant_dynamic-update-slice_fusion, f32[80,2304]{1,0:T(8,128)S(1)} %bitcast.90, f32[80,1920]{1,0:T(8,128)} %get-tuple-element.23, f32[80,384]{1,0:T(8,128)S(1)} %slice_convert_fusion, ...), kind=kOutput, calls=%fused_computation.235 | convolution fusion | flops 180080640 | bytes 7052800 | tf_op jit(solution)/shard_map/dot_general | solution.py:74
  69.5 1.1 slice.224
  72.6 1.3 %collective-permute-start.6 = (bf16[80,6]{1,0:T(8,128)(2,1)S(1)}, bf16[80,6]{1,0:T(8,128)(2,1)S(1)}, u32[]{:S(2)}, u32[]{:S(2)}) collective-permute-start(bf16[80,6]{1,0:T(8,128)(2,1)S(1)} %slice.224), channel_id=1, source_target_pairs={{1,0},{2,1},{3,2},{5,4},{6,5},{7,6},{9,8},{10,9},{11,10},{13,12},{... | collective-permute-start | bytes 2888 | tf_op jit(solution)/shard_map/ppermute | solution.py:34
  73.9 3.0 %collective-permute-start.7 = (bf16[80,6]{1,0:T(8,128)(2,1)S(1)}, bf16[80,6]{1,0:T(8,128)(2,1)S(1)}, u32[]{:S(2)}, u32[]{:S(2)}) collective-permute-start(bf16[80,6]{1,0:T(8,128)(2,1)S(1)} %slice.226), channel_id=1, source_target_pairs={{0,1},{1,2},{2,3},{4,5},{5,6},{6,7},{8,9},{9,10},{10,11},{12,13},{... | collective-permute-start | bytes 2888 | tf_op jit(solution)/shard_map/ppermute | solution.py:33
  77.2 1.3 %collective-permute-start.4 = (bf16[80,384]{1,0:T(8,128)(2,1)S(1)}, bf16[80,384]{1,0:T(8,128)(2,1)S(1)}, u32[]{:S(2)}, u32[]{:S(2)}) collective-permute-start(bf16[80,384]{1,0:T(8,128)(2,1)S(1)} %get-tuple-element.32), channel_id=1, source_target_pairs={{4,0},{8,4},{12,8},{5,1},{9,5},{13,9},{6,2},{10,6},{14,10},{7,3},{... | collective-permute-start | bytes 184328 | tf_op jit(solution)/shard_map/ppermute | solution.py:32
  78.5 4.5 %collective-permute-start.5 = (bf16[80,384]{1,0:T(8,128)(2,1)S(1)}, bf16[80,384]{1,0:T(8,128)(2,1)S(1)}, u32[]{:S(2)}, u32[]{:S(2)}) collective-permute-start(bf16[80,384]{1,0:T(8,128)(2,1)S(1)} %get-tuple-element.31), channel_id=1, source_target_pairs={{0,4},{4,8},{8,12},{1,5},{5,9},{9,13},{2,6},{6,10},{10,14},{3,7},{... | collective-permute-start | bytes 184328 | tf_op jit(solution)/shard_map/ppermute | solution.py:31
  83.8 1.1 collective-permute-done.5
  84.9 2.1 %fusion.164 = (bf16[80,2304]{1,0:T(8,128)(2,1)}, f32[80,2304]{1,0:T(8,128)S(1)}) fusion(f32[80,80]{1,0:T(8,128)S(1)} %copy-done, f32[80,2304]{1,0:T(8,128)S(1)} %constant_dynamic-update-slice_fusion, f32[80,2304]{1,0:T(8,128)S(1)} %get-tuple-element.50, f32[80,1920]{1,0:T(8,128)S(1)} %get-tuple-element.19, f32[80,384]{1,0:T(8,128)S(1)} %convert_element_type.97, ...), kind=kOutput, calls=%fused_computation.236 | convolution fusion | flops 180080640 | bytes 7052800 | tf_op jit(solution)/shard_map/dot_general | solution.py:74
  86.9 1.1 slice.232
  90.0 1.3 %collective-permute-start.10 = (bf16[80,6]{1,0:T(8,128)(2,1)S(1)}, bf16[80,6]{1,0:T(8,128)(2,1)S(1)}, u32[]{:S(2)}, u32[]{:S(2)}) collective-permute-start(bf16[80,6]{1,0:T(8,128)(2,1)S(1)} %slice.232), channel_id=1, source_target_pairs={{1,0},{2,1},{3,2},{5,4},{6,5},{7,6},{9,8},{10,9},{11,10},{13,12},{... | collective-permute-start | bytes 2888 | tf_op jit(solution)/shard_map/ppermute | solution.py:34
  91.3 3.0 %collective-permute-start.11 = (bf16[80,6]{1,0:T(8,128)(2,1)S(1)}, bf16[80,6]{1,0:T(8,128)(2,1)S(1)}, u32[]{:S(2)}, u32[]{:S(2)}) collective-permute-start(bf16[80,6]{1,0:T(8,128)(2,1)S(1)} %slice.234), channel_id=1, source_target_pairs={{0,1},{1,2},{2,3},{4,5},{5,6},{6,7},{8,9},{9,10},{10,11},{12,13},{... | collective-permute-start | bytes 2888 | tf_op jit(solution)/shard_map/ppermute | solution.py:33
  94.6 1.3 %collective-permute-start.8 = (bf16[80,384]{1,0:T(8,128)(2,1)S(1)}, bf16[80,384]{1,0:T(8,128)(2,1)S(1)}, u32[]{:S(2)}, u32[]{:S(2)}) collective-permute-start(bf16[80,384]{1,0:T(8,128)(2,1)S(1)} %get-tuple-element.30), channel_id=1, source_target_pairs={{4,0},{8,4},{12,8},{5,1},{9,5},{13,9},{6,2},{10,6},{14,10},{7,3},{... | collective-permute-start | bytes 184328 | tf_op jit(solution)/shard_map/ppermute | solution.py:32
  95.9 5.1 %collective-permute-start.9 = (bf16[80,384]{1,0:T(8,128)(2,1)S(1)}, bf16[80,384]{1,0:T(8,128)(2,1)S(1)}, u32[]{:S(2)}, u32[]{:S(2)}) collective-permute-start(bf16[80,384]{1,0:T(8,128)(2,1)S(1)} %get-tuple-element.29), channel_id=1, source_target_pairs={{0,4},{4,8},{8,12},{1,5},{5,9},{9,13},{2,6},{6,10},{10,14},{3,7},{... | collective-permute-start | bytes 184328 | tf_op jit(solution)/shard_map/ppermute | solution.py:31
  102.7 2.1 %fusion.165 = (bf16[80,2304]{1,0:T(8,128)(2,1)}, f32[80,2304]{1,0:T(8,128)S(1)}) fusion(f32[80,80]{1,0:T(8,128)S(1)} %copy-done, f32[80,2304]{1,0:T(8,128)S(1)} %constant_dynamic-update-slice_fusion, f32[80,2304]{1,0:T(8,128)S(1)} %get-tuple-element.52, f32[80,1920]{1,0:T(8,128)S(1)} %get-tuple-element.15, f32[80,384]{1,0:T(8,128)S(1)} %convert_element_type.102, ...), kind=kOutput, calls=%fused_computation.237 | convolution fusion | flops 180080640 | bytes 7052800 | tf_op jit(solution)/shard_map/dot_general | solution.py:74
  106.3 5.1 %all-to-all-start.2 = ((f32[80,4,256]{2,0,1:T(8,128)}), f32[80,4,256]{2,0,1:T(8,128)S(1)}, u32[]{:S(2)}, u32[]{:S(2)}) async-start(f32[80,4,256]{2,0,1:T(8,128)} %broadcast_select_fusion), calls=%async_computation.2 | async-start | bytes 655360 | tf_op jit(solution)/shard_map/all_to_all | solution.py:206
  112.2 8.3 %all-to-all-done.2 = f32[80,4,256]{2,0,1:T(8,128)S(1)} async-done(((f32[80,4,256]{2,0,1:T(8,128)}), f32[80,4,256]{2,0,1:T(8,128)S(1)}, u32[]{:S(2)}, u32[]{:S(2)}) %all-to-all-start.2) | async-done | bytes 327712 | tf_op jit(solution)/shard_map/all_to_all | solution.py:206
  120.6 1.9 %fusion = f32[240,2048]{1,0:T(8,128)S(1)} fusion(s32[1024]{0:T(1024)S(1)} %bitcast.122, bf16[80,1024]{1,0:T(8,128)(2,1)S(1)} %get-tuple-element.38, bf16[80,1024]{1,0:T(8,128)(2,1)S(1)} %get-tuple-element.37, bf16[80,1024]{1,0:T(8,128)(2,1)S(1)} %convert_element_type.105), kind=kOutput, calls=%fused_computation.3 | convolution fusion | flops 1010204672 | bytes 2461696 | tf_op jit(solution)/shard_map/dot_general | solution.py:136
  (173 shorter events, 31.1 us)
Async XLA Ops:
  0.6 41.3 %copy-start = (f32[80,80]{1,0:T(8,128)S(1)}, f32[80,80]{1,0:T(8,128)}, u32[]{:S(2)}) copy-start(f32[80,80]{1,0:T(8,128)} %param.16) | copy-start | bytes 76804
  0.6 22.6 %copy-start.5 = (bf16[80,8,256]{2,1,0:T(8,128)(2,1)S(1)}, bf16[80,8,256]{2,1,0:T(8,128)(2,1)}, u32[]{:S(2)}) copy-start(bf16[80,8,256]{2,1,0:T(8,128)(2,1)} %param.10) | copy-start | bytes 983044
  0.7 8.5 %copy-start.6 = (bf16[80,6,384]{2,0,1:T(8,128)(2,1)S(1)}, bf16[80,6,384]{2,0,1:T(8,128)(2,1)}, u32[]{:S(2)}) copy-start(bf16[80,6,384]{2,0,1:T(8,128)(2,1)} %param.11) | copy-start | bytes 1105924
  0.7 16.1 %copy-start.24 = (s32[1,1,256,1]{2,3,1,0:T(1,128)S(1)}, s32[1,1,256,1]{2,3,1,0:T(1,128)}, u32[]{:S(2)}) copy-start(s32[1,1,256,1]{2,3,1,0:T(1,128)} %param.17) | copy-start | bytes 3076
  0.7 16.1 %copy-start.29 = (s32[1,1,256]{2,1,0:T(1,128)S(1)}, s32[1,1,256]{2,1,0:T(1,128)}, u32[]{:S(2)}) copy-start(s32[1,1,256]{2,1,0:T(1,128)} %param.18) | copy-start | bytes 3076
  3.2 28.1 %collective-permute-start.2 = (bf16[80,14]{0,1:T(8,128)(2,1)S(1)}, bf16[80,14]{0,1:T(8,128)(2,1)S(1)}, u32[]{:S(2)}, u32[]{:S(2)}) collective-permute-start(bf16[80,14]{0,1:T(8,128)(2,1)S(1)} %pad_maximum_fusion.2), channel_id=1, source_target_pairs={{1,0},{2,1},{3,2},{5,4},{6,5},{7,6},{9,8},{10,9},{11,10},{13,12},{... | collective-permute-start | bytes 6728 | tf_op jit(solution)/shard_map/ppermute | solution.py:34
  4.9 27.1 %collective-permute-start.3 = (bf16[80,14]{0,1:T(8,128)(2,1)S(1)}, bf16[80,14]{0,1:T(8,128)(2,1)S(1)}, u32[]{:S(2)}, u32[]{:S(2)}) collective-permute-start(bf16[80,14]{0,1:T(8,128)(2,1)S(1)} %pad_maximum_fusion.3), channel_id=1, source_target_pairs={{0,1},{1,2},{2,3},{4,5},{5,6},{6,7},{8,9},{9,10},{10,11},{12,13},{... | collective-permute-start | bytes 6728 | tf_op jit(solution)/shard_map/ppermute | solution.py:33
  9.2 31.2 %collective-permute-start.1 = (bf16[80,640]{1,0:T(8,128)(2,1)S(1)}, bf16[80,640]{1,0:T(8,128)(2,1)}, u32[]{:S(2)}, u32[]{:S(2)}) collective-permute-start(bf16[80,640]{1,0:T(8,128)(2,1)S(1)} %pad_maximum_fusion.1), channel_id=1, source_target_pairs={{0,4},{4,8},{8,12},{1,5},{5,9},{9,13},{2,6},{6,10},{10,14},{3,7},{... | collective-permute-start | bytes 307208 | tf_op jit(solution)/shard_map/ppermute | solution.py:31
  15.4 25.7 %collective-permute-start = (bf16[80,640]{1,0:T(8,128)(2,1)}, bf16[80,640]{1,0:T(8,128)(2,1)}, u32[]{:S(2)}, u32[]{:S(2)}) collective-permute-start(bf16[80,640]{1,0:T(8,128)(2,1)} %pad_maximum_fusion), channel_id=1, source_target_pairs={{4,0},{8,4},{12,8},{5,1},{9,5},{13,9},{6,2},{10,6},{14,10},{7,3},{... | collective-permute-start | bytes 307208 | tf_op jit(solution)/shard_map/ppermute | solution.py:32
  17.4 22.3 %all-to-all-start = ((s32[4,256,1]{1,2,0:T(1,128)}), s32[4,256,1]{1,2,0:T(1,128)S(1)}, u32[]{:S(2)}, u32[]{:S(2)}) async-start(s32[4,256,1]{1,2,0:T(1,128)} %compare_select_fusion.1), calls=%async_computation | async-start | bytes 8192 | tf_op jit(solution)/shard_map/all_to_all | solution.py:167
  25.3 4.9 %copy-start.9 = (pred[4,256]{1,0:T(4,128)(4,1)}, pred[4,256]{1,0:T(4,128)(4,1)S(1)}, u32[]{:S(2)}) copy-start(pred[4,256]{1,0:T(4,128)(4,1)S(1)} %iota_compare_fusion.2) | copy-start | bytes 3076
  48.0 16.6 %copy-start.18 = (pred[256]{0:T(512)(128)(4,1)S(1)}, pred[256]{0:T(512)(128)(4,1)}, u32[]{:S(2)}) copy-start(pred[256]{0:T(512)(128)(4,1)} %get-tuple-element.10) | copy-start | bytes 772
  48.0 16.6 %copy-start.20 = (pred[256]{0:T(512)(128)(4,1)S(1)}, pred[256]{0:T(512)(128)(4,1)}, u32[]{:S(2)}) copy-start(pred[256]{0:T(512)(128)(4,1)} %get-tuple-element.11) | copy-start | bytes 772
  48.0 16.6 %copy-start.22 = (pred[256]{0:T(512)(128)(4,1)S(1)}, pred[256]{0:T(512)(128)(4,1)}, u32[]{:S(2)}) copy-start(pred[256]{0:T(512)(128)(4,1)} %get-tuple-element.12) | copy-start | bytes 772
  48.0 16.6 %copy-start.11 = (s32[384]{0:T(512)S(1)}, s32[384]{0:T(512)}, u32[]{:S(2)}) copy-start(s32[384]{0:T(512)} %broadcast_add_fusion) | copy-start | bytes 4612
  48.0 16.6 %copy-start.12 = (s32[384]{0:T(512)S(1)}, s32[384]{0:T(512)}, u32[]{:S(2)}) copy-start(s32[384]{0:T(512)} %iota_divide_fusion) | copy-start | bytes 4612
  48.0 16.6 %copy-start.25 = (pred[384]{0:T(512)(128)(4,1)S(1)}, pred[384]{0:T(512)(128)(4,1)}, u32[]{:S(2)}) copy-start(pred[384]{0:T(512)(128)(4,1)} %fusion.135) | copy-start | bytes 1156
  48.0 16.6 %copy-start.27 = (s32[128]{0:T(128)S(1)}, s32[128]{0:T(128)}, u32[]{:S(2)}) copy-start(s32[128]{0:T(128)} %iota_add_fusion) | copy-start | bytes 1540
  48.2 17.1 %copy-start.4 = (f32[80,2303]{1,0:T(8,128)S(1)}, f32[80,2303]{1,0:T(8,128)}, u32[]{:S(2)}) copy-start(f32[80,2303]{1,0:T(8,128)} %get-tuple-element.21) | copy-start | bytes 2210884
  48.2 17.1 %copy-start.16 = (f32[80]{0:T(128)S(1)}, f32[80]{0:T(128)}, u32[]{:S(2)}) copy-start(f32[80]{0:T(128)} %param.14) | copy-start | bytes 964
  48.2 17.1 %copy-start.17 = (f32[80]{0:T(128)S(1)}, f32[80]{0:T(128)}, u32[]{:S(2)}) copy-start(f32[80]{0:T(128)} %param.13) | copy-start | bytes 964
  49.0 15.6 %all-to-all-start.1 = ((f32[80,4,256]{2,0,1:T(8,128)}), f32[80,4,256]{2,0,1:T(8,128)S(1)}, u32[]{:S(2)}, u32[]{:S(2)}) async-start(f32[80,4,256]{2,0,1:T(8,128)} %broadcast_select_fusion.1), calls=%async_computation.1 | async-start | bytes 655360 | tf_op jit(solution)/shard_map/all_to_all | solution.py:168
  72.6 10.5 %collective-permute-start.6 = (bf16[80,6]{1,0:T(8,128)(2,1)S(1)}, bf16[80,6]{1,0:T(8,128)(2,1)S(1)}, u32[]{:S(2)}, u32[]{:S(2)}) collective-permute-start(bf16[80,6]{1,0:T(8,128)(2,1)S(1)} %slice.224), channel_id=1, source_target_pairs={{1,0},{2,1},{3,2},{5,4},{6,5},{7,6},{9,8},{10,9},{11,10},{13,12},{... | collective-permute-start | bytes 2888 | tf_op jit(solution)/shard_map/ppermute | solution.py:34
  73.9 9.6 %collective-permute-start.7 = (bf16[80,6]{1,0:T(8,128)(2,1)S(1)}, bf16[80,6]{1,0:T(8,128)(2,1)S(1)}, u32[]{:S(2)}, u32[]{:S(2)}) collective-permute-start(bf16[80,6]{1,0:T(8,128)(2,1)S(1)} %slice.226), channel_id=1, source_target_pairs={{0,1},{1,2},{2,3},{4,5},{5,6},{6,7},{8,9},{9,10},{10,11},{12,13},{... | collective-permute-start | bytes 2888 | tf_op jit(solution)/shard_map/ppermute | solution.py:33
  77.2 6.6 %collective-permute-start.4 = (bf16[80,384]{1,0:T(8,128)(2,1)S(1)}, bf16[80,384]{1,0:T(8,128)(2,1)S(1)}, u32[]{:S(2)}, u32[]{:S(2)}) collective-permute-start(bf16[80,384]{1,0:T(8,128)(2,1)S(1)} %get-tuple-element.32), channel_id=1, source_target_pairs={{4,0},{8,4},{12,8},{5,1},{9,5},{13,9},{6,2},{10,6},{14,10},{7,3},{... | collective-permute-start | bytes 184328 | tf_op jit(solution)/shard_map/ppermute | solution.py:32
  78.5 6.4 %collective-permute-start.5 = (bf16[80,384]{1,0:T(8,128)(2,1)S(1)}, bf16[80,384]{1,0:T(8,128)(2,1)S(1)}, u32[]{:S(2)}, u32[]{:S(2)}) collective-permute-start(bf16[80,384]{1,0:T(8,128)(2,1)S(1)} %get-tuple-element.31), channel_id=1, source_target_pairs={{0,4},{4,8},{8,12},{1,5},{5,9},{9,13},{2,6},{6,10},{10,14},{3,7},{... | collective-permute-start | bytes 184328 | tf_op jit(solution)/shard_map/ppermute | solution.py:31
  90.0 11.1 %collective-permute-start.10 = (bf16[80,6]{1,0:T(8,128)(2,1)S(1)}, bf16[80,6]{1,0:T(8,128)(2,1)S(1)}, u32[]{:S(2)}, u32[]{:S(2)}) collective-permute-start(bf16[80,6]{1,0:T(8,128)(2,1)S(1)} %slice.232), channel_id=1, source_target_pairs={{1,0},{2,1},{3,2},{5,4},{6,5},{7,6},{9,8},{10,9},{11,10},{13,12},{... | collective-permute-start | bytes 2888 | tf_op jit(solution)/shard_map/ppermute | solution.py:34
  91.3 10.1 %collective-permute-start.11 = (bf16[80,6]{1,0:T(8,128)(2,1)S(1)}, bf16[80,6]{1,0:T(8,128)(2,1)S(1)}, u32[]{:S(2)}, u32[]{:S(2)}) collective-permute-start(bf16[80,6]{1,0:T(8,128)(2,1)S(1)} %slice.234), channel_id=1, source_target_pairs={{0,1},{1,2},{2,3},{4,5},{5,6},{6,7},{8,9},{9,10},{10,11},{12,13},{... | collective-permute-start | bytes 2888 | tf_op jit(solution)/shard_map/ppermute | solution.py:33
  94.6 7.1 %collective-permute-start.8 = (bf16[80,384]{1,0:T(8,128)(2,1)S(1)}, bf16[80,384]{1,0:T(8,128)(2,1)S(1)}, u32[]{:S(2)}, u32[]{:S(2)}) collective-permute-start(bf16[80,384]{1,0:T(8,128)(2,1)S(1)} %get-tuple-element.30), channel_id=1, source_target_pairs={{4,0},{8,4},{12,8},{5,1},{9,5},{13,9},{6,2},{10,6},{14,10},{7,3},{... | collective-permute-start | bytes 184328 | tf_op jit(solution)/shard_map/ppermute | solution.py:32
  95.9 6.7 %collective-permute-start.9 = (bf16[80,384]{1,0:T(8,128)(2,1)S(1)}, bf16[80,384]{1,0:T(8,128)(2,1)S(1)}, u32[]{:S(2)}, u32[]{:S(2)}) collective-permute-start(bf16[80,384]{1,0:T(8,128)(2,1)S(1)} %get-tuple-element.29), channel_id=1, source_target_pairs={{0,4},{4,8},{8,12},{1,5},{5,9},{9,13},{2,6},{6,10},{10,14},{3,7},{... | collective-permute-start | bytes 184328 | tf_op jit(solution)/shard_map/ppermute | solution.py:31
  104.8 6.6 %copy-start.7 = (bf16[80,2304]{1,0:T(8,128)(2,1)S(1)}, bf16[80,2304]{1,0:T(8,128)(2,1)}, u32[]{:S(2)}) copy-start(bf16[80,2304]{1,0:T(8,128)(2,1)} %get-tuple-element.53) | copy-start | bytes 1105924
  106.3 14.1 %all-to-all-start.2 = ((f32[80,4,256]{2,0,1:T(8,128)}), f32[80,4,256]{2,0,1:T(8,128)S(1)}, u32[]{:S(2)}, u32[]{:S(2)}) async-start(f32[80,4,256]{2,0,1:T(8,128)} %broadcast_select_fusion), calls=%async_computation.2 | async-start | bytes 655360 | tf_op jit(solution)/shard_map/all_to_all | solution.py:206
  (16 other events, 41.7 us)

commit v5 on v4

--- a/solution.py
+++ b/solution.py
@@ -1,6 +1,10 @@
+import functools
+
 import jax
 import jax.numpy as jnp
 from jax import lax
+from jax.experimental import pallas as pl
+from jax.experimental.pallas import tpu as pltpu
 from jax.sharding import PartitionSpec as P
 
 Y_AXES = ("gy", "gz")
@@ -70,6 +74,78 @@
     return down + up + east + west - 4.0 * flat
 
 
+def step_kernel(*refs, rows, cols, nest):
+    if nest:
+        (state_ref, above_ref, below_ref, left_ref, right_ref, forcing_ref, upw_ref, dnw_ref,
+         nu_ref, relax_ref, vm_ref, new_ref, lrow_ref, frow_ref, lcol_ref, fcol_ref, up_sc, dn_sc) = refs
+    else:
+        (state_ref, above_ref, below_ref, left_ref, right_ref, nu_ref, vm_ref,
+         new_ref, lrow_ref, frow_ref, lcol_ref, fcol_ref, up_sc, dn_sc) = refs
+    n = rows * cols
+    state = state_ref[...].astype(jnp.float32)
+    levels = state.shape[0]
+    up_sc[:, 0:cols] = above_ref[...].astype(jnp.float32)
+    up_sc[:, cols:n] = state[:, 0 : n - cols]
+    dn_sc[:, 0 : n - cols] = state[:, cols:n]
+    dn_sc[:, n - cols : n] = below_ref[...].astype(jnp.float32)
+    up = up_sc[...]
+    down = dn_sc[...]
+    lane = lax.broadcasted_iota(jnp.int32, (levels, n), 1)
+    left = left_ref[...].astype(jnp.float32)
+    right = right_ref[...].astype(jnp.float32)
+    west = pltpu.roll(state, 1, 1)
+    east = pltpu.roll(state, n - 1, 1)
+    for r in range(rows):
+        west = jnp.where(lane == r * cols, left[:, r : r + 1], west)
+        east = jnp.where(lane == r * cols + cols - 1, right[:, r : r + 1], east)
+    if nest:
+        down = down * dnw_ref[...]
+        up = up * upw_ref[...]
+    stencil = down + up + east + west - 4.0 * state
+    moved = state + nu_ref[...] * stencil
+    if nest:
+        moved = moved + relax_ref[...] * (forcing_ref[...] - moved)
+    new = jnp.dot(vm_ref[...], moved, precision=HI, preferred_element_type=jnp.float32)
+    new_ref[...] = new
+    lrow_ref[...] = new[:, n - cols : n].astype(jnp.bfloat16)
+    frow_ref[...] = new[:, 0:cols].astype(jnp.bfloat16)
+    narrow = new.astype(jnp.bfloat16)
+    p = lax.broadcasted_iota(jnp.int32, (n, rows), 0)
+    j = lax.broadcasted_iota(jnp.int32, (n, rows), 1)
+    last_sel = (p == j * cols + (cols - 1)).astype(jnp.bfloat16)
+    first_sel = (p == j * cols).astype(jnp.bfloat16)
+    lcol_ref[...] = jnp.dot(narrow, last_sel, preferred_element_type=jnp.float32).astype(jnp.bfloat16)
+    fcol_ref[...] = jnp.dot(narrow, first_sel, preferred_element_type=jnp.float32).astype(jnp.bfloat16)
+
+
+def stencil_step(state, halo, nu, vert_mix, rows, cols, forcing=None, up_w=None, down_w=None, relax=None):
+    levels = state.shape[0]
+    n = rows * cols
+    nest = forcing is not None
+    above, below, left, right = halo
+    if nest:
+        args = (state, above, below, left, right, forcing, up_w[None, :], down_w[None, :],
+                nu[:, None], relax[:, None], vert_mix)
+    else:
+        args = (state, above, below, left, right, nu[:, None], vert_mix)
+    out_shape = (
+        jax.ShapeDtypeStruct((levels, n), jnp.float32),
+        jax.ShapeDtypeStruct((levels, cols), jnp.bfloat16),
+        jax.ShapeDtypeStruct((levels, cols), jnp.bfloat16),
+        jax.ShapeDtypeStruct((levels, rows), jnp.bfloat16),
+        jax.ShapeDtypeStruct((levels, rows), jnp.bfloat16),
+    )
+    flops = 2 * levels * levels * n * 6 + 4 * levels * n * rows + 20 * levels * n
+    moved_bytes = sum(int(a.size) * a.dtype.itemsize for a in args) + levels * n * 4
+    new, lrow, frow, lcol, fcol = pl.pallas_call(
+        functools.partial(step_kernel, rows=rows, cols=cols, nest=nest),
+        out_shape=out_shape,
+        scratch_shapes=[pltpu.VMEM((levels, n), jnp.float32), pltpu.VMEM((levels, n), jnp.float32)],
+        cost_estimate=pl.CostEstimate(flops=flops, bytes_accessed=moved_bytes, transcendentals=0),
+    )(*args)
+    return new, (lrow, frow, lcol, fcol)
+
+
 def mix_levels(matrix, flat):
     return jnp.dot(matrix, flat, precision=HI, preferred_element_type=jnp.float32)
 
@@ -145,9 +221,9 @@
     zero = jnp.minimum(here_x, 0)
 
     parent_halo, nest_halo = exchange([edges_3d(parent), edges_3d(nest)])
-    centre = parent.astype(jnp.float32).reshape(levels, p_rows * p_cols)
-    stencil = flat_stencil(centre, p_rows, p_cols, parent_halo)
-    flat_parent = mix_levels(vert_mix, centre + nu_parent[:, None] * stencil)
+    flat_parent, _ = stencil_step(
+        parent.reshape(levels, p_rows * p_cols), parent_halo, nu_parent, vert_mix, p_rows, p_cols
+    )
 
     owners = fp_owner.reshape(-1)
     cells = fp_cell.reshape(-1)
@@ -185,15 +261,14 @@
     up_w = per_row(left_w, n_rows, n_cols)
     down_w = per_row(right_w, n_rows, n_cols)
 
-    nest_state = nest.astype(jnp.float32).reshape(levels, n_rows * n_cols)
+    nest_state = nest.reshape(levels, n_rows * n_cols)
     halo = nest_halo
     for turn_no in range(3):
         if turn_no > 0:
-            (halo,) = exchange([edges_flat(nest_state.astype(jnp.bfloat16), n_rows, n_cols)])
-        stencil_sum = flat_stencil(nest_state, n_rows, n_cols, halo, up_w, down_w)
-        moved = nest_state + nu_nest[:, None] * stencil_sum
-        moved = moved + relax[:, None] * (forcing_full - moved)
-        nest_state = mix_levels(vert_mix, moved)
+            (halo,) = exchange([edges])
+        nest_state, edges = stencil_step(
+            nest_state, halo, nu_nest, vert_mix, n_rows, n_cols, forcing_full, up_w, down_w, relax
+        )
 
     block_sum = block_sums(nest_state, block_rows, n_cols, expand)
     nudge_gap = block_sum / 9.0 - forcing_flat

time: 125 us -> 113 us (0.904)
  Pallas kernels: 0 us -> 13.1 us
  other arithmetic: 12.4 us -> 3.36 us
  matrix products: 14.1 us -> 5.23 us
  local copies, waits for them, and re-layouts: 29 us -> 21.9 us
  starting transfers between devices: 48.1 us -> 43.7 us
  waiting for transfers between devices: 18.2 us -> 22 us
    pallas_call x0 -> x4, Pallas kernels: none -> 13.1 us  [stencil_step(): pl.pallas_call(functools.partial(step_kernel, rows=rows, cols=cols, nest=...]
    dot_general x4 -> x0, matrix products: 10.9 us -> none  [mix_levels(): jnp.dot(matrix, flat, precision=HI, preferred_element_type=jnp.float32)]
    slice x14 -> x6, local copies, waits for them, and re-layouts: 10.7 us -> 3.85 us  [the longest x2 1.25 us: exchange(): above[:, xo:xo + w]]
    convert_element_type x12 -> x1, other arithmetic: 5.73 us -> 0.04 us  [body(): nest_state.astype(jnp.bfloat16).reshape(levels, n_rows, n_cols)]
    ppermute x3, starting transfers between devices: 15.2 us -> 9.81 us  [exchange(): above = lax.ppermute(last_rows, 'gx', fwd_x)]
    ppermute x3, waiting for transfers between devices: 0.01 us -> 3.95 us  [exchange(): right = lax.ppermute(first_cols, Y_AXES, bwd_y)]
    dot_general x2, matrix products: 0.67 us -> 2.78 us  [block_sums(): lax.dot_general(rows3, expand, (((1,), (1,)), ((), ())), precision=HI, pr...]
    ppermute x3, waiting for transfers between devices: 2.05 us -> 0.01 us  [exchange(): above = lax.ppermute(last_rows, 'gx', fwd_x)]
  transfers between devices with their start and end apart: 15 -> 15, of which waited for: 4 -> 5; matrix products, arithmetic and copies ran while one was open for 21% -> 13% of each run, Pallas kernels for 0% -> 0%
where the time goes in v5:
time: 113 us; the launch traced here: 111 us
  starting transfers between devices  43.7 us (39%)
  waiting for transfers between devices  22 us (19%)
  local copies, waits for them, and re-layouts  21.9 us (19%)
  Pallas kernels  13.1 us (12%)
  matrix products  5.23 us (5%)
  other arithmetic  3.36 us (3%)
  between operations  1.19 us (1%)
    pallas_call x4, Pallas kernels, stencil_step(): pl.pallas_call(functools.partial(step_kernel, rows=rows, cols=cols, nest=...  13.1 us
    ppermute x3, starting transfers between devices, exchange(): above = lax.ppermute(last_rows, 'gx', fwd_x)  9.81 us
    all_to_all x1, waiting for transfers between devices, body(): lax.all_to_all(outgoing, 'gx', split_axis=1, concat_axis=1, tiled=True)  9.03 us
    all_to_all x1, waiting for transfers between devices, body(): lax.all_to_all(jnp.take(flat_parent, served_ids, axis=1), 'gx', split_axi...  8.87 us
    ppermute x3, starting transfers between devices, exchange(): left = lax.ppermute(last_cols, Y_AXES, fwd_y)  8.71 us
    all_to_all x1, starting transfers between devices, body(): lax.all_to_all(wanted, 'gx', split_axis=0, concat_axis=0, tiled=True)  6.35 us
    unnamed x57, local copies, waits for them, and re-layouts  5.77 us
    all_to_all x1, starting transfers between devices, body(): lax.all_to_all(jnp.take(flat_parent, served_ids, axis=1), 'gx', split_axi...  5.71 us
  transfers between devices with their start and end apart: 15, of which 5 were waited for; matrix products, arithmetic and copies ran while one was open for 13% of the time, Pallas kernels for 0%

profile of v5, /device:TPU:0, one launch (start us, length us, event | category | flops | bytes accessed | tf_op | source)
XLA Modules:
  0.0 110.6 jit_solution(15413863745482731841)
XLA Ops:
  0.7 1.3 %compare_select_fusion.1 = s32[4,256,1]{1,2,0:T(1,128)} fusion(s32[256]{0:T(256)} %bitcast.102, s32[256]{0:T(256)} %bitcast.100), kind=kLoop, calls=%fused_computation.67 | loop fusion | flops 2048 | bytes 6144 | tf_op jit(solution)/shard_map/jit(_where)/select_n | solution.py:235
  2.1 6.3 %all-to-all-start = ((s32[4,256,1]{1,2,0:T(1,128)}), s32[4,256,1]{1,2,0:T(1,128)S(1)}, u32[]{:S(2)}, u32[]{:S(2)}) async-start(s32[4,256,1]{1,2,0:T(1,128)} %compare_select_fusion.1), calls=%async_computation | async-start | bytes 8192 | tf_op jit(solution)/shard_map/all_to_all | solution.py:243
  8.4 0.9 slice_bitcast_fusion
  9.3 1.2 %fusion.52 = (bf16[80,1,256]{2,1,0:T(2,128)(2,1)S(1)}, bf16[80,1,256]{2,1,0:T(2,128)(2,1)S(1)}) fusion(bf16[80,8,256]{2,1,0:T(8,128)(2,1)} %param.10), kind=kLoop, calls=%fused_computation.102 | loop fusion | bytes 163840 | tf_op jit(solution)/shard_map/slice | solution.py:21
  10.5 3.9 %collective-permute-start = (bf16[80,640]{1,0:T(8,128)(2,1)S(1)}, bf16[80,640]{1,0:T(8,128)(2,1)S(1)}, u32[]{:S(2)}, u32[]{:S(2)}) collective-permute-start(bf16[80,640]{1,0:T(8,128)(2,1)S(1)} %pad_maximum_fusion), channel_id=1, source_target_pairs={{0,4},{4,8},{8,12},{1,5},{5,9},{9,13},{2,6},{6,10},{10,14},{3,7},{... | collective-permute-start | bytes 307208 | tf_op jit(solution)/shard_map/ppermute | solution.py:35
  14.5 1.3 %collective-permute-start.1 = (bf16[80,640]{1,0:T(8,128)(2,1)S(1)}, bf16[80,640]{1,0:T(8,128)(2,1)S(1)}, u32[]{:S(2)}, u32[]{:S(2)}) collective-permute-start(bf16[80,640]{1,0:T(8,128)(2,1)S(1)} %pad_maximum_fusion.1), channel_id=1, source_target_pairs={{4,0},{8,4},{12,8},{5,1},{9,5},{13,9},{6,2},{10,6},{14,10},{7,3},{... | collective-permute-start | bytes 307208 | tf_op jit(solution)/shard_map/ppermute | solution.py:36
  15.8 1.1 fusion.50
  17.4 1.3 %collective-permute-start.3 = (bf16[80,14]{1,0:T(8,128)(2,1)S(1)}, bf16[80,14]{1,0:T(8,128)(2,1)S(1)}, u32[]{:S(2)}, u32[]{:S(2)}) collective-permute-start(bf16[80,14]{1,0:T(8,128)(2,1)S(1)} %copy.73), channel_id=1, source_target_pairs={{1,0},{2,1},{3,2},{5,4},{6,5},{7,6},{9,8},{10,9},{11,10},{13,12},{... | collective-permute-start | bytes 6728 | tf_op jit(solution)/shard_map/ppermute | solution.py:38
  19.2 3.0 %collective-permute-start.2 = (bf16[80,14]{1,0:T(8,128)(2,1)S(1)}, bf16[80,14]{1,0:T(8,128)(2,1)S(1)}, u32[]{:S(2)}, u32[]{:S(2)}) collective-permute-start(bf16[80,14]{1,0:T(8,128)(2,1)S(1)} %copy.70), channel_id=1, source_target_pairs={{0,1},{1,2},{2,3},{4,5},{5,6},{6,7},{8,9},{9,10},{10,11},{12,13},{... | collective-permute-start | bytes 6728 | tf_op jit(solution)/shard_map/ppermute | solution.py:37
  29.4 2.9 %shard_map.113 = (f32[80,2048]{1,0:T(8,128)}, bf16[80,256]{1,0:T(8,128)(2,1)}, bf16[80,256]{1,0:T(8,128)(2,1)}, bf16[80,8]{1,0:T(8,128)(2,1)}, bf16[80,8]{1,0:T(8,128)(2,1)}) custom-call(bf16[80,2048]{1,0:T(8,128)(2,1)} %bitcast.81, bf16[80,256]{1,0:T(8,128)(2,1)} %slice.153.refs_1_, bf16[80,256]{1,0:T(8,128)(2,1)} %slice.154.refs_2_, ...), custom_call_target="tpu_custom_call" | custom-call | flops 165806080 | bytes 1093440 | tf_op jit(solution)/shard_map/pallas_call | solution.py:140
  32.3 1.4 %copy.76 = f32[80,2048]{0,1:T(8,128)S(1)} copy(f32[80,2048]{1,0:T(8,128)} %get-tuple-element.14) | data formatting | bytes 1310720 | tf_op jit(solution)/shard_map/pallas_call | solution.py:140
  33.8 2.8 %gather_fusion = f32[1024,80]{1,0:T(8,128)S(1)} fusion(f32[80,2048]{0,1:T(8,128)S(1)} %copy.76, s32[1024]{0:T(1024)S(1)} %get-tuple-element.54), kind=kCustom, calls=%fused_computation | custom fusion | bytes 659456 | tf_op jit(solution)/shard_map/jit(_take)/gather | solution.py:245
  37.5 5.7 %all-to-all-start.1 = ((f32[80,4,256]{2,0,1:T(8,128)}), f32[80,4,256]{2,0,1:T(8,128)S(1)}, u32[]{:S(2)}, u32[]{:S(2)}) async-start(f32[80,4,256]{2,0,1:T(8,128)} %broadcast_select_fusion.1), calls=%async_computation.1 | async-start | bytes 655360 | tf_op jit(solution)/shard_map/all_to_all | solution.py:244
  45.9 8.9 %all-to-all-done.1 = f32[80,4,256]{2,0,1:T(8,128)S(1)} async-done(((f32[80,4,256]{2,0,1:T(8,128)}), f32[80,4,256]{2,0,1:T(8,128)S(1)}, u32[]{:S(2)}, u32[]{:S(2)}) %all-to-all-start.1) | async-done | bytes 327712 | tf_op jit(solution)/shard_map/all_to_all | solution.py:244
  56.4 3.4 %shard_map.114 = (f32[80,2304]{1,0:T(8,128)}, bf16[80,384]{1,0:T(8,128)(2,1)}, bf16[80,384]{1,0:T(8,128)(2,1)}, bf16[80,6]{1,0:T(8,128)(2,1)}, bf16[80,6]{1,0:T(8,128)(2,1)}) custom-call(bf16[80,2304]{1,0:T(8,128)(2,1)} %bitcast.75, bf16[80,384]{1,0:T(8,128)(2,1)} %slice.157.refs_1_, bf16[80,384]{1,0:T(8,128)(2,1)} %slice.158.refs_2_, ...), custom_call_target="tpu_custom_call" | custom-call | flops 185057280 | bytes 2012672 | tf_op jit(solution)/shard_map/pallas_call | solution.py:140
  59.7 1.7 %collective-permute-start.4 = (bf16[80,384]{1,0:T(8,128)(2,1)}, bf16[80,384]{1,0:T(8,128)(2,1)S(1)}, u32[]{:S(2)}, u32[]{:S(2)}) collective-permute-start(bf16[80,384]{1,0:T(8,128)(2,1)} %get-tuple-element.16), channel_id=1, source_target_pairs={{0,4},{4,8},{8,12},{1,5},{5,9},{9,13},{2,6},{6,10},{10,14},{3,7},{... | collective-permute-start | bytes 184328 | tf_op jit(solution)/shard_map/ppermute | solution.py:35
  61.5 1.3 %collective-permute-start.5 = (bf16[80,384]{1,0:T(8,128)(2,1)}, bf16[80,384]{1,0:T(8,128)(2,1)S(1)}, u32[]{:S(2)}, u32[]{:S(2)}) collective-permute-start(bf16[80,384]{1,0:T(8,128)(2,1)} %get-tuple-element.17), channel_id=1, source_target_pairs={{4,0},{8,4},{12,8},{5,1},{9,5},{13,9},{6,2},{10,6},{14,10},{7,3},{... | collective-permute-start | bytes 184328 | tf_op jit(solution)/shard_map/ppermute | solution.py:36
  62.8 1.5 %collective-permute-start.6 = (bf16[80,6]{1,0:T(8,128)(2,1)}, bf16[80,6]{1,0:T(8,128)(2,1)S(1)}, u32[]{:S(2)}, u32[]{:S(2)}) collective-permute-start(bf16[80,6]{1,0:T(8,128)(2,1)} %get-tuple-element.18), channel_id=1, source_target_pairs={{0,1},{1,2},{2,3},{4,5},{5,6},{6,7},{8,9},{9,10},{10,11},{12,13},{... | collective-permute-start | bytes 2888 | tf_op jit(solution)/shard_map/ppermute | solution.py:37
  64.3 1.3 %collective-permute-start.7 = (bf16[80,6]{1,0:T(8,128)(2,1)}, bf16[80,6]{1,0:T(8,128)(2,1)S(1)}, u32[]{:S(2)}, u32[]{:S(2)}) collective-permute-start(bf16[80,6]{1,0:T(8,128)(2,1)} %get-tuple-element.19), channel_id=1, source_target_pairs={{1,0},{2,1},{3,2},{5,4},{6,5},{7,6},{9,8},{10,9},{11,10},{13,12},{... | collective-permute-start | bytes 2888 | tf_op jit(solution)/shard_map/ppermute | solution.py:38
  65.7 2.0 %collective-permute-done.7.refs_4_ = bf16[80,6]{1,0:T(8,128)(2,1)S(1)} collective-permute-done((bf16[80,6]{1,0:T(8,128)(2,1)}, bf16[80,6]{1,0:T(8,128)(2,1)S(1)}, u32[]{:S(2)}, u32[]{:S(2)}) %collective-permute-start.7) | collective-permute-done | bytes 992 | tf_op jit(solution)/shard_map/ppermute | solution.py:38
  68.4 3.4 %shard_map.115 = (f32[80,2304]{1,0:T(8,128)}, bf16[80,384]{1,0:T(8,128)(2,1)}, bf16[80,384]{1,0:T(8,128)(2,1)}, bf16[80,6]{1,0:T(8,128)(2,1)}, bf16[80,6]{1,0:T(8,128)(2,1)}) custom-call(f32[80,2304]{1,0:T(8,128)} %get-tuple-element.15.refs_0_, bf16[80,384]{1,0:T(8,128)(2,1)} %copy-done.8, bf16[80,384]{1,0:T(8,128)(2,1)} %copy-done.9, ...), custom_call_target="tpu_custom_call" | custom-call | flops 185057280 | bytes 2381312 | tf_op jit(solution)/shard_map/pallas_call | solution.py:140
  71.8 4.1 %collective-permute-start.8 = (bf16[80,384]{1,0:T(8,128)(2,1)}, bf16[80,384]{1,0:T(8,128)(2,1)S(1)}, u32[]{:S(2)}, u32[]{:S(2)}) collective-permute-start(bf16[80,384]{1,0:T(8,128)(2,1)} %get-tuple-element.21), channel_id=1, source_target_pairs={{0,4},{4,8},{8,12},{1,5},{5,9},{9,13},{2,6},{6,10},{10,14},{3,7},{... | collective-permute-start | bytes 184328 | tf_op jit(solution)/shard_map/ppermute | solution.py:35
  76.0 1.3 %collective-permute-start.9 = (bf16[80,384]{1,0:T(8,128)(2,1)}, bf16[80,384]{1,0:T(8,128)(2,1)S(1)}, u32[]{:S(2)}, u32[]{:S(2)}) collective-permute-start(bf16[80,384]{1,0:T(8,128)(2,1)} %get-tuple-element.22), channel_id=1, source_target_pairs={{4,0},{8,4},{12,8},{5,1},{9,5},{13,9},{6,2},{10,6},{14,10},{7,3},{... | collective-permute-start | bytes 184328 | tf_op jit(solution)/shard_map/ppermute | solution.py:36
  77.3 4.1 %collective-permute-start.10 = (bf16[80,6]{1,0:T(8,128)(2,1)}, bf16[80,6]{1,0:T(8,128)(2,1)S(1)}, u32[]{:S(2)}, u32[]{:S(2)}) collective-permute-start(bf16[80,6]{1,0:T(8,128)(2,1)} %get-tuple-element.23), channel_id=1, source_target_pairs={{0,1},{1,2},{2,3},{4,5},{5,6},{6,7},{8,9},{9,10},{10,11},{12,13},{... | collective-permute-start | bytes 2888 | tf_op jit(solution)/shard_map/ppermute | solution.py:37
  81.4 1.3 %collective-permute-start.11 = (bf16[80,6]{1,0:T(8,128)(2,1)}, bf16[80,6]{1,0:T(8,128)(2,1)S(1)}, u32[]{:S(2)}, u32[]{:S(2)}) collective-permute-start(bf16[80,6]{1,0:T(8,128)(2,1)} %get-tuple-element.24), channel_id=1, source_target_pairs={{1,0},{2,1},{3,2},{5,4},{6,5},{7,6},{9,8},{10,9},{11,10},{13,12},{... | collective-permute-start | bytes 2888 | tf_op jit(solution)/shard_map/ppermute | solution.py:38
  82.7 2.0 %collective-permute-done.11.refs_4_ = bf16[80,6]{1,0:T(8,128)(2,1)S(1)} collective-permute-done((bf16[80,6]{1,0:T(8,128)(2,1)}, bf16[80,6]{1,0:T(8,128)(2,1)S(1)}, u32[]{:S(2)}, u32[]{:S(2)}) %collective-permute-start.11) | collective-permute-done | bytes 992 | tf_op jit(solution)/shard_map/ppermute | solution.py:38
  85.4 3.4 %shard_map.116 = (f32[80,2304]{1,0:T(8,128)}, bf16[80,384]{1,0:T(8,128)(2,1)}, bf16[80,384]{1,0:T(8,128)(2,1)}, bf16[80,6]{1,0:T(8,128)(2,1)}, bf16[80,6]{1,0:T(8,128)(2,1)}) custom-call(f32[80,2304]{1,0:T(8,128)} %get-tuple-element.20.refs_0_, bf16[80,384]{1,0:T(8,128)(2,1)} %copy-done.6, bf16[80,384]{1,0:T(8,128)(2,1)} %copy-done.7, ...), custom_call_target="tpu_custom_call" | custom-call | flops 185057280 | bytes 2381312 | tf_op jit(solution)/shard_map/pallas_call | solution.py:140
  88.8 1.4 %convolution_bitcast_fusion.1 = f32[80,1,128]{2,0,1:T(8,128)S(1)} fusion(f32[80,2304]{1,0:T(8,128)} %get-tuple-element.25, s32[128]{0:T(128)S(1)} %iota_add_fusion, s32[384]{0:T(512)S(1)} %iota_divide_fusion, s32[384]{0:T(512)S(1)} %broadcast_add_fusion, pred[384]{0:T(512)(128)(4,1)S(1)} %fusion.47), kind=kOutput, calls=%fused_computation.6 | convolution fusion | flops 47345664 | bytes 413568 | tf_op jit(solution)/shard_map/dot_general | solution.py:192
  90.2 1.4 %convolution_bitcast_fusion = f32[80,1,128]{2,0,1:T(8,128)S(1)} fusion(f32[80,2304]{1,0:T(8,128)} %get-tuple-element.25, s32[128]{0:T(128)S(1)} %iota_add_fusion, s32[384]{0:T(512)S(1)} %iota_divide_fusion, s32[384]{0:T(512)S(1)} %broadcast_add_fusion, pred[384]{0:T(512)(128)(4,1)S(1)} %fusion.47), kind=kOutput, calls=%fused_computation.5 | convolution fusion | flops 47345664 | bytes 413568 | tf_op jit(solution)/shard_map/dot_general | solution.py:192
  92.4 5.3 %all-to-all-start.2 = ((f32[80,4,256]{2,0,1:T(8,128)}), f32[80,4,256]{2,0,1:T(8,128)S(1)}, u32[]{:S(2)}, u32[]{:S(2)}) async-start(f32[80,4,256]{2,0,1:T(8,128)} %broadcast_select_fusion), calls=%async_computation.2 | async-start | bytes 655360 | tf_op jit(solution)/shard_map/all_to_all | solution.py:281
  98.5 9.0 %all-to-all-done.2 = f32[80,4,256]{2,0,1:T(8,128)S(1)} async-done(((f32[80,4,256]{2,0,1:T(8,128)}), f32[80,4,256]{2,0,1:T(8,128)S(1)}, u32[]{:S(2)}, u32[]{:S(2)}) %all-to-all-start.2) | async-done | bytes 327712 | tf_op jit(solution)/shard_map/all_to_all | solution.py:281
  107.7 1.9 %fusion = f32[240,2048]{1,0:T(8,128)S(1)} fusion(s32[1024]{0:T(1024)S(1)} %bitcast.92, bf16[80,1024]{1,0:T(8,128)(2,1)S(1)} %get-tuple-element.42, bf16[80,1024]{1,0:T(8,128)(2,1)S(1)} %get-tuple-element.41, bf16[80,1024]{1,0:T(8,128)(2,1)S(1)} %convert_element_type.31), kind=kOutput, calls=%fused_computation.3 | convolution fusion | flops 1010204672 | bytes 2461696 | tf_op jit(solution)/shard_map/dot_general | solution.py:212
  (112 shorter events, 17.3 us)
Async XLA Ops:
  0.6 26.8 %copy-start = (s32[24]{0:T(128)S(1)}, s32[24]{0:T(128)}, u32[]{:S(2)}) copy-start(s32[24]{0:T(128)} %param.19) | copy-start | bytes 292
  0.6 21.6 %copy-start.16 = (s32[1,1,256,1]{2,3,1,0:T(1,128)S(1)}, s32[1,1,256,1]{2,3,1,0:T(1,128)}, u32[]{:S(2)}) copy-start(s32[1,1,256,1]{2,3,1,0:T(1,128)} %param.17) | copy-start | bytes 3076
  0.7 24.6 %copy-start.4 = (bf16[80,6,384]{2,0,1:T(8,128)(2,1)S(1)}, bf16[80,6,384]{2,0,1:T(8,128)(2,1)}, u32[]{:S(2)}) copy-start(bf16[80,6,384]{2,0,1:T(8,128)(2,1)} %param.11) | copy-start | bytes 1105924
  0.7 16.2 %copy-start.3 = (bf16[80,8,256]{2,1,0:T(8,128)(2,1)S(1)}, bf16[80,8,256]{2,1,0:T(8,128)(2,1)}, u32[]{:S(2)}) copy-start(bf16[80,8,256]{2,1,0:T(8,128)(2,1)} %param.10) | copy-start | bytes 983044
  0.7 21.7 %copy-start.18 = (f32[80]{0:T(128)S(1)}, f32[80]{0:T(128)}, u32[]{:S(2)}) copy-start(f32[80]{0:T(128)} %param.13) | copy-start | bytes 964
  0.7 22.4 %copy-start.19 = (f32[80]{0:T(128)S(1)}, f32[80]{0:T(128)}, u32[]{:S(2)}) copy-start(f32[80]{0:T(128)} %param.14) | copy-start | bytes 964
  0.7 23.1 %copy-start.20 = (f32[80]{0:T(128)S(1)}, f32[80]{0:T(128)}, u32[]{:S(2)}) copy-start(f32[80]{0:T(128)} %param.12) | copy-start | bytes 964
  2.1 25.4 %all-to-all-start = ((s32[4,256,1]{1,2,0:T(1,128)}), s32[4,256,1]{1,2,0:T(1,128)S(1)}, u32[]{:S(2)}, u32[]{:S(2)}) async-start(s32[4,256,1]{1,2,0:T(1,128)} %compare_select_fusion.1), calls=%async_computation | async-start | bytes 8192 | tf_op jit(solution)/shard_map/all_to_all | solution.py:243
  10.5 17.6 %collective-permute-start = (bf16[80,640]{1,0:T(8,128)(2,1)S(1)}, bf16[80,640]{1,0:T(8,128)(2,1)S(1)}, u32[]{:S(2)}, u32[]{:S(2)}) collective-permute-start(bf16[80,640]{1,0:T(8,128)(2,1)S(1)} %pad_maximum_fusion), channel_id=1, source_target_pairs={{0,4},{4,8},{8,12},{1,5},{5,9},{9,13},{2,6},{6,10},{10,14},{3,7},{... | collective-permute-start | bytes 307208 | tf_op jit(solution)/shard_map/ppermute | solution.py:35
  14.5 14.3 %collective-permute-start.1 = (bf16[80,640]{1,0:T(8,128)(2,1)S(1)}, bf16[80,640]{1,0:T(8,128)(2,1)S(1)}, u32[]{:S(2)}, u32[]{:S(2)}) collective-permute-start(bf16[80,640]{1,0:T(8,128)(2,1)S(1)} %pad_maximum_fusion.1), channel_id=1, source_target_pairs={{4,0},{8,4},{12,8},{5,1},{9,5},{13,9},{6,2},{10,6},{14,10},{7,3},{... | collective-permute-start | bytes 307208 | tf_op jit(solution)/shard_map/ppermute | solution.py:36
  17.4 8.6 %collective-permute-start.3 = (bf16[80,14]{1,0:T(8,128)(2,1)S(1)}, bf16[80,14]{1,0:T(8,128)(2,1)S(1)}, u32[]{:S(2)}, u32[]{:S(2)}) collective-permute-start(bf16[80,14]{1,0:T(8,128)(2,1)S(1)} %copy.73), channel_id=1, source_target_pairs={{1,0},{2,1},{3,2},{5,4},{6,5},{7,6},{9,8},{10,9},{11,10},{13,12},{... | collective-permute-start | bytes 6728 | tf_op jit(solution)/shard_map/ppermute | solution.py:38
  19.2 7.6 %collective-permute-start.2 = (bf16[80,14]{1,0:T(8,128)(2,1)S(1)}, bf16[80,14]{1,0:T(8,128)(2,1)S(1)}, u32[]{:S(2)}, u32[]{:S(2)}) collective-permute-start(bf16[80,14]{1,0:T(8,128)(2,1)S(1)} %copy.70), channel_id=1, source_target_pairs={{0,1},{1,2},{2,3},{4,5},{5,6},{6,7},{8,9},{9,10},{10,11},{12,13},{... | collective-permute-start | bytes 6728 | tf_op jit(solution)/shard_map/ppermute | solution.py:37
  26.1 3.3 %copy-start.14 = (bf16[80,14]{1,0:T(8,128)(2,1)}, bf16[80,14]{1,0:T(8,128)(2,1)S(1)}, u32[]{:S(2)}) copy-start(bf16[80,14]{1,0:T(8,128)(2,1)S(1)} %collective-permute-done.3) | copy-start | bytes 6724
  26.8 2.6 %copy-start.15 = (bf16[80,14]{1,0:T(8,128)(2,1)}, bf16[80,14]{1,0:T(8,128)(2,1)S(1)}, u32[]{:S(2)}) copy-start(bf16[80,14]{1,0:T(8,128)(2,1)S(1)} %collective-permute-done.2) | copy-start | bytes 6724
  37.5 17.3 %all-to-all-start.1 = ((f32[80,4,256]{2,0,1:T(8,128)}), f32[80,4,256]{2,0,1:T(8,128)S(1)}, u32[]{:S(2)}, u32[]{:S(2)}) async-start(f32[80,4,256]{2,0,1:T(8,128)} %broadcast_select_fusion.1), calls=%async_computation.1 | async-start | bytes 655360 | tf_op jit(solution)/shard_map/all_to_all | solution.py:244
  55.5 0.9 copy-start.1
  59.7 7.9 %collective-permute-start.4 = (bf16[80,384]{1,0:T(8,128)(2,1)}, bf16[80,384]{1,0:T(8,128)(2,1)S(1)}, u32[]{:S(2)}, u32[]{:S(2)}) collective-permute-start(bf16[80,384]{1,0:T(8,128)(2,1)} %get-tuple-element.16), channel_id=1, source_target_pairs={{0,4},{4,8},{8,12},{1,5},{5,9},{9,13},{2,6},{6,10},{10,14},{3,7},{... | collective-permute-start | bytes 184328 | tf_op jit(solution)/shard_map/ppermute | solution.py:35
  61.5 6.3 %collective-permute-start.5 = (bf16[80,384]{1,0:T(8,128)(2,1)}, bf16[80,384]{1,0:T(8,128)(2,1)S(1)}, u32[]{:S(2)}, u32[]{:S(2)}) collective-permute-start(bf16[80,384]{1,0:T(8,128)(2,1)} %get-tuple-element.17), channel_id=1, source_target_pairs={{4,0},{8,4},{12,8},{5,1},{9,5},{13,9},{6,2},{10,6},{14,10},{7,3},{... | collective-permute-start | bytes 184328 | tf_op jit(solution)/shard_map/ppermute | solution.py:36
  62.8 2.9 %collective-permute-start.6 = (bf16[80,6]{1,0:T(8,128)(2,1)}, bf16[80,6]{1,0:T(8,128)(2,1)S(1)}, u32[]{:S(2)}, u32[]{:S(2)}) collective-permute-start(bf16[80,6]{1,0:T(8,128)(2,1)} %get-tuple-element.18), channel_id=1, source_target_pairs={{0,1},{1,2},{2,3},{4,5},{5,6},{6,7},{8,9},{9,10},{10,11},{12,13},{... | collective-permute-start | bytes 2888 | tf_op jit(solution)/shard_map/ppermute | solution.py:37
  64.3 3.3 %collective-permute-start.7 = (bf16[80,6]{1,0:T(8,128)(2,1)}, bf16[80,6]{1,0:T(8,128)(2,1)S(1)}, u32[]{:S(2)}, u32[]{:S(2)}) collective-permute-start(bf16[80,6]{1,0:T(8,128)(2,1)} %get-tuple-element.19), channel_id=1, source_target_pairs={{1,0},{2,1},{3,2},{5,4},{6,5},{7,6},{9,8},{10,9},{11,10},{13,12},{... | collective-permute-start | bytes 2888 | tf_op jit(solution)/shard_map/ppermute | solution.py:38
  65.6 2.2 %copy-start.12 = (bf16[80,6]{1,0:T(8,128)(2,1)}, bf16[80,6]{1,0:T(8,128)(2,1)S(1)}, u32[]{:S(2)}) copy-start(bf16[80,6]{1,0:T(8,128)(2,1)S(1)} %collective-permute-done.6.refs_3_) | copy-start | bytes 2884
  67.6 0.6 copy-start.8
  71.8 12.9 %collective-permute-start.8 = (bf16[80,384]{1,0:T(8,128)(2,1)}, bf16[80,384]{1,0:T(8,128)(2,1)S(1)}, u32[]{:S(2)}, u32[]{:S(2)}) collective-permute-start(bf16[80,384]{1,0:T(8,128)(2,1)} %get-tuple-element.21), channel_id=1, source_target_pairs={{0,4},{4,8},{8,12},{1,5},{5,9},{9,13},{2,6},{6,10},{10,14},{3,7},{... | collective-permute-start | bytes 184328 | tf_op jit(solution)/shard_map/ppermute | solution.py:35
  76.0 8.8 %collective-permute-start.9 = (bf16[80,384]{1,0:T(8,128)(2,1)}, bf16[80,384]{1,0:T(8,128)(2,1)S(1)}, u32[]{:S(2)}, u32[]{:S(2)}) collective-permute-start(bf16[80,384]{1,0:T(8,128)(2,1)} %get-tuple-element.22), channel_id=1, source_target_pairs={{4,0},{8,4},{12,8},{5,1},{9,5},{13,9},{6,2},{10,6},{14,10},{7,3},{... | collective-permute-start | bytes 184328 | tf_op jit(solution)/shard_map/ppermute | solution.py:36
  77.3 5.5 %collective-permute-start.10 = (bf16[80,6]{1,0:T(8,128)(2,1)}, bf16[80,6]{1,0:T(8,128)(2,1)S(1)}, u32[]{:S(2)}, u32[]{:S(2)}) collective-permute-start(bf16[80,6]{1,0:T(8,128)(2,1)} %get-tuple-element.23), channel_id=1, source_target_pairs={{0,1},{1,2},{2,3},{4,5},{5,6},{6,7},{8,9},{9,10},{10,11},{12,13},{... | collective-permute-start | bytes 2888 | tf_op jit(solution)/shard_map/ppermute | solution.py:37
  81.4 3.3 %collective-permute-start.11 = (bf16[80,6]{1,0:T(8,128)(2,1)}, bf16[80,6]{1,0:T(8,128)(2,1)S(1)}, u32[]{:S(2)}, u32[]{:S(2)}) collective-permute-start(bf16[80,6]{1,0:T(8,128)(2,1)} %get-tuple-element.24), channel_id=1, source_target_pairs={{1,0},{2,1},{3,2},{5,4},{6,5},{7,6},{9,8},{10,9},{11,10},{13,12},{... | collective-permute-start | bytes 2888 | tf_op jit(solution)/shard_map/ppermute | solution.py:38
  82.7 2.0 %copy-start.10 = (bf16[80,6]{1,0:T(8,128)(2,1)}, bf16[80,6]{1,0:T(8,128)(2,1)S(1)}, u32[]{:S(2)}) copy-start(bf16[80,6]{1,0:T(8,128)(2,1)S(1)} %collective-permute-done.10.refs_3_) | copy-start | bytes 2884
  84.7 0.6 copy-start.7
  88.8 8.9 %copy-start.5 = (f32[80,2304]{1,0:T(8,128)S(1)}, f32[80,2304]{1,0:T(8,128)}, u32[]{:S(2)}) copy-start(f32[80,2304]{1,0:T(8,128)} %get-tuple-element.25) | copy-start | bytes 2211844
  92.4 15.2 %all-to-all-start.2 = ((f32[80,4,256]{2,0,1:T(8,128)}), f32[80,4,256]{2,0,1:T(8,128)S(1)}, u32[]{:S(2)}, u32[]{:S(2)}) async-start(f32[80,4,256]{2,0,1:T(8,128)} %broadcast_select_fusion), calls=%async_computation.2 | async-start | bytes 655360 | tf_op jit(solution)/shard_map/all_to_all | solution.py:281
  107.7 1.9 %copy-start.2 = (f32[80,2048]{1,0:T(8,128)S(1)}, f32[80,2048]{1,0:T(8,128)}, u32[]{:S(2)}) copy-start(f32[80,2048]{1,0:T(8,128)} %get-tuple-element.14) | copy-start | bytes 1966084
  107.7 1.9 %copy-start.17 = (f32[80]{0:T(128)S(1)}, f32[80]{0:T(128)}, u32[]{:S(2)}) copy-start(f32[80]{0:T(128)} %param.15) | copy-start | bytes 964
  (4 other events, 2.4 us)

commit v6 on v5

--- a/solution.py
+++ b/solution.py
@@ -205,6 +205,18 @@
     return hi, mid, lo
 
 
+def shifted_pairs(count, shift):
+    return [(i, (i + shift) % count) for i in range(count)]
+
+
+def gather_columns(values, ids):
+    levels, width = values.shape
+    onehot = (lax.broadcasted_iota(jnp.int32, (width, 1), 0) == ids[None, :]).astype(jnp.bfloat16)
+    parts = jnp.concatenate(split3(values), axis=0)
+    total = jnp.dot(parts, onehot, preferred_element_type=jnp.float32)
+    return (total[:levels] + total[levels : 2 * levels]) + total[2 * levels :]
+
+
 def scatter_add_columns(values, ids, width):
     levels = values.shape[0]
     onehot = (ids[:, None] == lax.broadcasted_iota(jnp.int32, (1, width), 1)).astype(jnp.bfloat16)
@@ -229,27 +241,34 @@
     cells = fp_cell.reshape(-1)
     requests = owners.shape[0]
     slots = 4 * requests // tiles_x
-    owner_ids = jnp.arange(tiles_x, dtype=jnp.int32)
-    if slots >= requests:
-        chosen = owners[None, :] == owner_ids[:, None]
+    by_shift = slots >= requests
+    if by_shift:
+        rel = (owners - here_x + tiles_x) % tiles_x
+        chosen = rel[None, :] == jnp.arange(tiles_x, dtype=jnp.int32)[:, None]
         wanted = jnp.where(chosen, cells[None, :], 0)
-        wanted = jnp.pad(wanted, ((0, 0), (0, slots - requests))).reshape(-1)
+        served = [wanted[0]] + [
+            lax.ppermute(wanted[s], "gx", shifted_pairs(tiles_x, s)) for s in range(1, tiles_x)
+        ]
+        served_ids = jnp.concatenate(served, axis=0)
+        replies = gather_columns(flat_parent, served_ids)
+        back = [replies[:, 0:requests]] + [
+            lax.ppermute(replies[:, s * requests : (s + 1) * requests], "gx", shifted_pairs(tiles_x, -s))
+            for s in range(1, tiles_x)
+        ]
+        forcing_flat = back[0]
+        for s in range(1, tiles_x):
+            forcing_flat = jnp.where(chosen[s][None, :], back[s], forcing_flat)
     else:
+        owner_ids = jnp.arange(tiles_x, dtype=jnp.int32)
         onehot = (owners[:, None] == owner_ids[None, :]).astype(jnp.int32)
         before = jnp.cumsum(onehot, axis=0) - onehot
         order_in = jnp.sum(before * onehot, axis=1)
         places = owners * slots + order_in
         wanted = jnp.zeros((tiles_x * slots,), jnp.int32).at[places].set(cells)
-    served_ids = lax.all_to_all(wanted, "gx", split_axis=0, concat_axis=0, tiled=True)
-    answers = lax.all_to_all(
-        jnp.take(flat_parent, served_ids, axis=1), "gx", split_axis=1, concat_axis=1, tiled=True
-    )
-    if slots >= requests:
-        answers = answers.reshape(levels, tiles_x, slots)[:, :, :requests]
-        forcing_flat = answers[:, 0, :]
-        for o in range(1, tiles_x):
-            forcing_flat = jnp.where(chosen[o][None, :], answers[:, o, :], forcing_flat)
-    else:
+        served_ids = lax.all_to_all(wanted, "gx", split_axis=0, concat_axis=0, tiled=True)
+        answers = lax.all_to_all(
+            gather_columns(flat_parent, served_ids), "gx", split_axis=1, concat_axis=1, tiled=True
+        )
         forcing_flat = jnp.take(answers, places, axis=1)
 
     block_rows = n_rows // 3
@@ -272,13 +291,16 @@
 
     block_sum = block_sums(nest_state, block_rows, n_cols, expand)
     nudge_gap = block_sum / 9.0 - forcing_flat
-    if slots >= requests:
-        outgoing = jnp.where(chosen[None, :, :], nudge_gap[:, None, :], 0.0)
-        outgoing = jnp.pad(outgoing, ((0, 0), (0, 0), (0, slots - requests)))
-        outgoing = outgoing.reshape(levels, tiles_x * slots)
+    if by_shift:
+        outgoing = jnp.where(chosen[:, None, :], nudge_gap[None, :, :], 0.0)
+        incoming = jnp.concatenate(
+            [outgoing[0]]
+            + [lax.ppermute(outgoing[s], "gx", shifted_pairs(tiles_x, s)) for s in range(1, tiles_x)],
+            axis=1,
+        )
     else:
         outgoing = jnp.zeros((levels, tiles_x * slots), jnp.float32).at[:, places].set(nudge_gap)
-    incoming = lax.all_to_all(outgoing, "gx", split_axis=1, concat_axis=1, tiled=True)
+        incoming = lax.all_to_all(outgoing, "gx", split_axis=1, concat_axis=1, tiled=True)
     summed = scatter_add_columns(incoming, served_ids, flat_parent.shape[1])
     parent_out = (flat_parent + feedback[:, None] * summed).astype(jnp.bfloat16)
     return (

time: 113 us -> 103 us (0.912); the launches traced: 111 us -> 103 us
  waiting for transfers between devices: 22 us -> 16.2 us
  local copies, waits for them, and re-layouts: 21.9 us -> 18.1 us
  matrix products: 5.23 us -> 7.02 us
    all_to_all x3 -> x0, waiting for transfers between devices: 17.9 us -> none  [the longest x1 9.03 us: body(): lax.all_to_all(outgoing, 'gx', split_axis=1, concat_axis=1, tiled=True)]
    all_to_all x3 -> x0, starting transfers between devices: 17.4 us -> none  [the longest x1 6.35 us: body(): lax.all_to_all(wanted, 'gx', split_axis=0, concat_axis=0, tiled=True)]
    ppermute x0 -> x9, starting transfers between devices: none -> 16.3 us  [the longest x3 6.14 us: body(): lax.ppermute(wanted[s], 'gx', shifted_pairs(tiles_x, s))]
    ppermute x0 -> x9, waiting for transfers between devices: none -> 11.9 us  [the longest x3 6.11 us: body(): lax.ppermute(outgoing[s], 'gx', shifted_pairs(tiles_x, s))]
    gather x2 -> x0, local copies, waits for them, and re-layouts: 3 us -> none  [body(): jnp.take(flat_parent, served_ids, axis=1)]
    dot_general x0 -> x1, matrix products: none -> 1.78 us  [gather_columns(): total = jnp.dot(parts, onehot, preferred_element_type=jnp.float32)]
    select_n x4 -> x3, other arithmetic: 1.54 us -> 0.06 us  [the longest x1 0.03 us: body(): outgoing = jnp.where(chosen[:, None, :], nudge_gap[None, :, :], 0.0)]
    convert_element_type x1 -> x2, other arithmetic: 0.02 us -> 1.44 us  [split3(): hi = values.astype(jnp.bfloat16)]
  transfers between devices with their start and end apart: 15 -> 21, of which waited for: 5 -> 5; matrix products, arithmetic and copies ran while one was open for 13% -> 14% of each run, Pallas kernels for 0% -> 0%
where the time goes in v6:
time: 103 us
  starting transfers between devices  43.6 us (42%)
  local copies, waits for them, and re-layouts  18.1 us (18%)
  waiting for transfers between devices  16.2 us (16%)
  Pallas kernels  13.2 us (13%)
  matrix products  7.02 us (7%)
  other arithmetic  3.4 us (3%)
  between operations  1.22 us (1%)
    pallas_call x4, Pallas kernels, stencil_step(): pl.pallas_call(functools.partial(step_kernel, rows=rows, cols=cols, nest=...  13.2 us
    ppermute x3, starting transfers between devices, exchange(): above = lax.ppermute(last_rows, 'gx', fwd_x)  10.6 us
    ppermute x3, starting transfers between devices, exchange(): left = lax.ppermute(last_cols, Y_AXES, fwd_y)  9.01 us
    unnamed x58, local copies, waits for them, and re-layouts  6.31 us
    ppermute x3, starting transfers between devices, body(): lax.ppermute(wanted[s], 'gx', shifted_pairs(tiles_x, s))  6.14 us
    ppermute x3, waiting for transfers between devices, body(): lax.ppermute(outgoing[s], 'gx', shifted_pairs(tiles_x, s))  6.11 us
    ppermute x3, starting transfers between devices, body(): lax.ppermute(outgoing[s], 'gx', shifted_pairs(tiles_x, s))  5.98 us
    ppermute x3, waiting for transfers between devices, body(): lax.ppermute(replies[:, s * requests:(s + 1) * requests], 'gx', shifted_p...  5.77 us
  transfers between devices with their start and end apart: 21, of which 5 were waited for; matrix products, arithmetic and copies ran while one was open for 14% of the time, Pallas kernels for 0%

profile of v6, /device:TPU:0, one launch (start us, length us, event | category | flops | bytes accessed | tf_op | source)
XLA Modules:
  0.0 102.8 jit_solution(2264603678083835201)
XLA Ops:
  2.1 5.1 %collective-permute-start.6 = (s32[256]{0:T(256)S(1)}, s32[256]{0:T(256)S(1)}, u32[]{:S(2)}, u32[]{:S(2)}) collective-permute-start(s32[256]{0:T(256)S(1)} %bitcast.80), channel_id=1, source_target_pairs={{0,12},{4,0},{8,4},{12,8},{1,13},{5,1},{9,5},{13,9},{2,14},{6,2},{... | collective-permute-start | bytes 3080 | tf_op jit(solution)/shard_map/ppermute | solution.py:250
  9.1 1.2 %fusion.66 = (bf16[80,1,256]{2,1,0:T(2,128)(2,1)S(1)}, bf16[80,1,256]{2,1,0:T(2,128)(2,1)S(1)}) fusion(bf16[80,8,256]{2,1,0:T(8,128)(2,1)} %param.10), kind=kLoop, calls=%fused_computation.123 | loop fusion | bytes 163840 | tf_op jit(solution)/shard_map/slice | solution.py:21
  10.4 4.5 %collective-permute-start = (bf16[80,640]{1,0:T(8,128)(2,1)S(1)}, bf16[80,640]{1,0:T(8,128)(2,1)S(1)}, u32[]{:S(2)}, u32[]{:S(2)}) collective-permute-start(bf16[80,640]{1,0:T(8,128)(2,1)S(1)} %pad_maximum_fusion.1), channel_id=1, source_target_pairs={{0,4},{4,8},{8,12},{1,5},{5,9},{9,13},{2,6},{6,10},{10,14},{3,7},{... | collective-permute-start | bytes 307208 | tf_op jit(solution)/shard_map/ppermute | solution.py:35
  15.0 1.3 %collective-permute-start.1 = (bf16[80,640]{1,0:T(8,128)(2,1)S(1)}, bf16[80,640]{1,0:T(8,128)(2,1)S(1)}, u32[]{:S(2)}, u32[]{:S(2)}) collective-permute-start(bf16[80,640]{1,0:T(8,128)(2,1)S(1)} %pad_maximum_fusion.2), channel_id=1, source_target_pairs={{4,0},{8,4},{12,8},{5,1},{9,5},{13,9},{6,2},{10,6},{14,10},{7,3},{... | collective-permute-start | bytes 307208 | tf_op jit(solution)/shard_map/ppermute | solution.py:36
  16.3 1.1 %fusion.63 = (bf16[80,6,1]{2,0,1:T(8,128)(2,1)S(1)}, bf16[80,6,1]{2,0,1:T(8,128)(2,1)S(1)}) fusion(bf16[80,6,384]{2,0,1:T(8,128)(2,1)} %param.11), kind=kLoop, calls=%fused_computation.120 | loop fusion | bytes 3840 | tf_op jit(solution)/shard_map/slice | solution.py:21
  24.2 1.3 %collective-permute-start.3 = (bf16[80,14]{1,0:T(8,128)(2,1)S(1)}, bf16[80,14]{1,0:T(8,128)(2,1)S(1)}, u32[]{:S(2)}, u32[]{:S(2)}) collective-permute-start(bf16[80,14]{1,0:T(8,128)(2,1)S(1)} %copy.49), channel_id=1, source_target_pairs={{1,0},{2,1},{3,2},{5,4},{6,5},{7,6},{9,8},{10,9},{11,10},{13,12},{... | collective-permute-start | bytes 6728 | tf_op jit(solution)/shard_map/ppermute | solution.py:38
  25.5 3.0 %collective-permute-start.2 = (bf16[80,14]{1,0:T(8,128)(2,1)S(1)}, bf16[80,14]{1,0:T(8,128)(2,1)S(1)}, u32[]{:S(2)}, u32[]{:S(2)}) collective-permute-start(bf16[80,14]{1,0:T(8,128)(2,1)S(1)} %copy.46), channel_id=1, source_target_pairs={{0,1},{1,2},{2,3},{4,5},{5,6},{6,7},{8,9},{9,10},{10,11},{12,13},{... | collective-permute-start | bytes 6728 | tf_op jit(solution)/shard_map/ppermute | solution.py:37
  30.4 2.9 %shard_map.113 = (f32[80,2048]{1,0:T(8,128)}, bf16[80,256]{1,0:T(8,128)(2,1)}, bf16[80,256]{1,0:T(8,128)(2,1)}, bf16[80,8]{1,0:T(8,128)(2,1)}, bf16[80,8]{1,0:T(8,128)(2,1)}) custom-call(bf16[80,2048]{1,0:T(8,128)(2,1)} %bitcast.59, bf16[80,256]{1,0:T(8,128)(2,1)} %slice.195.refs_1_, bf16[80,256]{1,0:T(8,128)(2,1)} %slice.196.refs_2_, ...), custom_call_target="tpu_custom_call" | custom-call | flops 165806080 | bytes 1093440 | tf_op jit(solution)/shard_map/pallas_call | solution.py:140
  33.4 1.4 %fusion.62 = (bf16[80,2048]{1,0:T(8,128)(2,1)S(1)}, bf16[80,2048]{1,0:T(8,128)(2,1)S(1)}, bf16[80,2048]{1,0:T(8,128)(2,1)S(1)}) fusion(f32[80,2048]{1,0:T(8,128)} %get-tuple-element.14), kind=kLoop, calls=%fused_computation.119 | loop fusion | flops 1146880 | bytes 1638400 | tf_op jit(solution)/shard_map/convert_element_type | solution.py:201
  34.8 1.8 %fusion = f32[240,1024]{1,0:T(8,128)S(1)} fusion(s32[1024]{0:T(1024)S(1)} %pad_add_fusion, bf16[80,2048]{1,0:T(8,128)(2,1)S(1)} %get-tuple-element.36, bf16[80,2048]{1,0:T(8,128)(2,1)S(1)} %get-tuple-element.37, bf16[80,2048]{1,0:T(8,128)(2,1)S(1)} %get-tuple-element.35), kind=kOutput, calls=%fused_computation.3 | convolution fusion | flops 1011679232 | bytes 1970176 | tf_op jit(solution)/shard_map/dot_general | solution.py:216
  36.7 3.0 %collective-permute-start.9 = (f32[80,256]{1,0:T(8,128)S(1)}, f32[80,256]{1,0:T(8,128)S(1)}, u32[]{:S(2)}, u32[]{:S(2)}) collective-permute-start(f32[80,256]{1,0:T(8,128)S(1)} %get-tuple-element.48), channel_id=1, source_target_pairs={{0,12},{4,0},{8,4},{12,8},{1,13},{5,1},{9,5},{13,9},{2,14},{6,2},{... | collective-permute-start | bytes 245768 | tf_op jit(solution)/shard_map/ppermute | solution.py:255
  39.7 1.1 %collective-permute-start.8 = (f32[80,256]{1,0:T(8,128)S(1)}, f32[80,256]{1,0:T(8,128)S(1)}, u32[]{:S(2)}, u32[]{:S(2)}) collective-permute-start(f32[80,256]{1,0:T(8,128)S(1)} %get-tuple-element.49), channel_id=1, source_target_pairs={{0,8},{4,12},{8,0},{12,4},{1,9},{5,13},{9,1},{13,5},{2,10},{6,14},... | collective-permute-start | bytes 245768 | tf_op jit(solution)/shard_map/ppermute | solution.py:255
  43.5 5.8 %collective-permute-done.8 = f32[80,256]{1,0:T(8,128)S(1)} collective-permute-done((f32[80,256]{1,0:T(8,128)S(1)}, f32[80,256]{1,0:T(8,128)S(1)}, u32[]{:S(2)}, u32[]{:S(2)}) %collective-permute-start.8) | collective-permute-done | bytes 81952 | tf_op jit(solution)/shard_map/ppermute | solution.py:255
  50.8 3.4 %shard_map.114 = (f32[80,2304]{1,0:T(8,128)}, bf16[80,384]{1,0:T(8,128)(2,1)}, bf16[80,384]{1,0:T(8,128)(2,1)}, bf16[80,6]{1,0:T(8,128)(2,1)}, bf16[80,6]{1,0:T(8,128)(2,1)}) custom-call(bf16[80,2304]{1,0:T(8,128)(2,1)} %bitcast.55, bf16[80,384]{1,0:T(8,128)(2,1)} %slice.199.refs_1_, bf16[80,384]{1,0:T(8,128)(2,1)} %slice.200.refs_2_, ...), custom_call_target="tpu_custom_call" | custom-call | flops 185057280 | bytes 2012672 | tf_op jit(solution)/shard_map/pallas_call | solution.py:140
  54.3 1.5 %collective-permute-start.10 = (bf16[80,384]{1,0:T(8,128)(2,1)}, bf16[80,384]{1,0:T(8,128)(2,1)S(1)}, u32[]{:S(2)}, u32[]{:S(2)}) collective-permute-start(bf16[80,384]{1,0:T(8,128)(2,1)} %get-tuple-element.16), channel_id=1, source_target_pairs={{0,4},{4,8},{8,12},{1,5},{5,9},{9,13},{2,6},{6,10},{10,14},{3,7},{... | collective-permute-start | bytes 184328 | tf_op jit(solution)/shard_map/ppermute | solution.py:35
  55.7 1.3 %collective-permute-start.11 = (bf16[80,384]{1,0:T(8,128)(2,1)}, bf16[80,384]{1,0:T(8,128)(2,1)S(1)}, u32[]{:S(2)}, u32[]{:S(2)}) collective-permute-start(bf16[80,384]{1,0:T(8,128)(2,1)} %get-tuple-element.17), channel_id=1, source_target_pairs={{4,0},{8,4},{12,8},{5,1},{9,5},{13,9},{6,2},{10,6},{14,10},{7,3},{... | collective-permute-start | bytes 184328 | tf_op jit(solution)/shard_map/ppermute | solution.py:36
  57.0 1.8 %collective-permute-start.12 = (bf16[80,6]{1,0:T(8,128)(2,1)}, bf16[80,6]{1,0:T(8,128)(2,1)S(1)}, u32[]{:S(2)}, u32[]{:S(2)}) collective-permute-start(bf16[80,6]{1,0:T(8,128)(2,1)} %get-tuple-element.18), channel_id=1, source_target_pairs={{0,1},{1,2},{2,3},{4,5},{5,6},{6,7},{8,9},{9,10},{10,11},{12,13},{... | collective-permute-start | bytes 2888 | tf_op jit(solution)/shard_map/ppermute | solution.py:37
  58.9 1.3 %collective-permute-start.13 = (bf16[80,6]{1,0:T(8,128)(2,1)}, bf16[80,6]{1,0:T(8,128)(2,1)S(1)}, u32[]{:S(2)}, u32[]{:S(2)}) collective-permute-start(bf16[80,6]{1,0:T(8,128)(2,1)} %get-tuple-element.19), channel_id=1, source_target_pairs={{1,0},{2,1},{3,2},{5,4},{6,5},{7,6},{9,8},{10,9},{11,10},{13,12},{... | collective-permute-start | bytes 2888 | tf_op jit(solution)/shard_map/ppermute | solution.py:38
  60.2 2.2 %collective-permute-done.13.refs_4_ = bf16[80,6]{1,0:T(8,128)(2,1)S(1)} collective-permute-done((bf16[80,6]{1,0:T(8,128)(2,1)}, bf16[80,6]{1,0:T(8,128)(2,1)S(1)}, u32[]{:S(2)}, u32[]{:S(2)}) %collective-permute-start.13) | collective-permute-done | bytes 992 | tf_op jit(solution)/shard_map/ppermute | solution.py:38
  63.1 3.4 %shard_map.115 = (f32[80,2304]{1,0:T(8,128)}, bf16[80,384]{1,0:T(8,128)(2,1)}, bf16[80,384]{1,0:T(8,128)(2,1)}, bf16[80,6]{1,0:T(8,128)(2,1)}, bf16[80,6]{1,0:T(8,128)(2,1)}) custom-call(f32[80,2304]{1,0:T(8,128)} %get-tuple-element.15.refs_0_, bf16[80,384]{1,0:T(8,128)(2,1)} %copy-done.8, bf16[80,384]{1,0:T(8,128)(2,1)} %copy-done.9, ...), custom_call_target="tpu_custom_call" | custom-call | flops 185057280 | bytes 2381312 | tf_op jit(solution)/shard_map/pallas_call | solution.py:140
  66.6 4.6 %collective-permute-start.14 = (bf16[80,384]{1,0:T(8,128)(2,1)}, bf16[80,384]{1,0:T(8,128)(2,1)S(1)}, u32[]{:S(2)}, u32[]{:S(2)}) collective-permute-start(bf16[80,384]{1,0:T(8,128)(2,1)} %get-tuple-element.21), channel_id=1, source_target_pairs={{0,4},{4,8},{8,12},{1,5},{5,9},{9,13},{2,6},{6,10},{10,14},{3,7},{... | collective-permute-start | bytes 184328 | tf_op jit(solution)/shard_map/ppermute | solution.py:35
  71.2 1.3 %collective-permute-start.15 = (bf16[80,384]{1,0:T(8,128)(2,1)}, bf16[80,384]{1,0:T(8,128)(2,1)S(1)}, u32[]{:S(2)}, u32[]{:S(2)}) collective-permute-start(bf16[80,384]{1,0:T(8,128)(2,1)} %get-tuple-element.22), channel_id=1, source_target_pairs={{4,0},{8,4},{12,8},{5,1},{9,5},{13,9},{6,2},{10,6},{14,10},{7,3},{... | collective-permute-start | bytes 184328 | tf_op jit(solution)/shard_map/ppermute | solution.py:36
  72.5 4.1 %collective-permute-start.16 = (bf16[80,6]{1,0:T(8,128)(2,1)}, bf16[80,6]{1,0:T(8,128)(2,1)S(1)}, u32[]{:S(2)}, u32[]{:S(2)}) collective-permute-start(bf16[80,6]{1,0:T(8,128)(2,1)} %get-tuple-element.23), channel_id=1, source_target_pairs={{0,1},{1,2},{2,3},{4,5},{5,6},{6,7},{8,9},{9,10},{10,11},{12,13},{... | collective-permute-start | bytes 2888 | tf_op jit(solution)/shard_map/ppermute | solution.py:37
  76.6 1.3 %collective-permute-start.17 = (bf16[80,6]{1,0:T(8,128)(2,1)}, bf16[80,6]{1,0:T(8,128)(2,1)S(1)}, u32[]{:S(2)}, u32[]{:S(2)}) collective-permute-start(bf16[80,6]{1,0:T(8,128)(2,1)} %get-tuple-element.24), channel_id=1, source_target_pairs={{1,0},{2,1},{3,2},{5,4},{6,5},{7,6},{9,8},{10,9},{11,10},{13,12},{... | collective-permute-start | bytes 2888 | tf_op jit(solution)/shard_map/ppermute | solution.py:38
  78.0 2.0 %collective-permute-done.17.refs_4_ = bf16[80,6]{1,0:T(8,128)(2,1)S(1)} collective-permute-done((bf16[80,6]{1,0:T(8,128)(2,1)}, bf16[80,6]{1,0:T(8,128)(2,1)S(1)}, u32[]{:S(2)}, u32[]{:S(2)}) %collective-permute-start.17) | collective-permute-done | bytes 992 | tf_op jit(solution)/shard_map/ppermute | solution.py:38
  80.6 3.4 %shard_map.116 = (f32[80,2304]{1,0:T(8,128)}, bf16[80,384]{1,0:T(8,128)(2,1)}, bf16[80,384]{1,0:T(8,128)(2,1)}, bf16[80,6]{1,0:T(8,128)(2,1)}, bf16[80,6]{1,0:T(8,128)(2,1)}) custom-call(f32[80,2304]{1,0:T(8,128)} %get-tuple-element.20.refs_0_, bf16[80,384]{1,0:T(8,128)(2,1)} %copy-done.6, bf16[80,384]{1,0:T(8,128)(2,1)} %copy-done.7, ...), custom_call_target="tpu_custom_call" | custom-call | flops 185057280 | bytes 2381312 | tf_op jit(solution)/shard_map/pallas_call | solution.py:140
  84.0 1.4 %fusion.20 = f32[80,128]{1,0:T(8,128)S(1)} fusion(f32[80,2304]{1,0:T(8,128)} %get-tuple-element.25, s32[128]{0:T(128)S(1)} %iota_add_fusion, s32[384]{0:T(512)S(1)} %get-tuple-element.65, s32[384]{0:T(512)S(1)} %get-tuple-element.66, pred[384]{0:T(512)(128)(4,1)S(1)} %fusion.57), kind=kOutput, calls=%fused_computation.34 | convolution fusion | flops 47345664 | bytes 413568 | tf_op jit(solution)/shard_map/dot_general | solution.py:192
  85.5 1.4 %fusion.19 = f32[80,128]{1,0:T(8,128)S(1)} fusion(f32[80,2304]{1,0:T(8,128)} %get-tuple-element.25, s32[128]{0:T(128)S(1)} %iota_add_fusion, s32[384]{0:T(512)S(1)} %get-tuple-element.65, s32[384]{0:T(512)S(1)} %get-tuple-element.66, pred[384]{0:T(512)(128)(4,1)S(1)} %fusion.57), kind=kOutput, calls=%fused_computation.33 | convolution fusion | flops 47345664 | bytes 413568 | tf_op jit(solution)/shard_map/dot_general | solution.py:192
  86.9 4.0 %collective-permute-start.20 = (f32[80,256]{1,0:T(8,128)S(1)}, f32[80,256]{1,0:T(8,128)S(1)}, u32[]{:S(2)}, u32[]{:S(2)}) collective-permute-start(f32[80,256]{1,0:T(8,128)S(1)} %get-tuple-element.45), channel_id=1, source_target_pairs={{0,12},{4,0},{8,4},{12,8},{1,13},{5,1},{9,5},{13,9},{2,14},{6,2},{... | collective-permute-start | bytes 245768 | tf_op jit(solution)/shard_map/ppermute | solution.py:298
  91.1 1.8 %collective-permute-start.18 = (f32[80,256]{1,0:T(8,128)S(1)}, f32[80,256]{1,0:T(8,128)S(1)}, u32[]{:S(2)}, u32[]{:S(2)}) collective-permute-start(f32[80,256]{1,0:T(8,128)S(1)} %get-tuple-element.47), channel_id=1, source_target_pairs={{0,4},{4,8},{8,12},{12,0},{1,5},{5,9},{9,13},{13,1},{2,6},{6,10},{... | collective-permute-start | bytes 245768 | tf_op jit(solution)/shard_map/ppermute | solution.py:298
  93.7 6.1 %collective-permute-done.19 = f32[80,256]{1,0:T(8,128)S(1)} collective-permute-done((f32[80,256]{1,0:T(8,128)S(1)}, f32[80,256]{1,0:T(8,128)S(1)}, u32[]{:S(2)}, u32[]{:S(2)}) %collective-permute-start.19) | collective-permute-done | bytes 81952 | tf_op jit(solution)/shard_map/ppermute | solution.py:298
  99.9 1.9 %fusion.1 = f32[240,2048]{1,0:T(8,128)S(1)} fusion(s32[1024]{0:T(1024)S(1)} %pad_add_fusion, bf16[80,1024]{1,0:T(8,128)(2,1)S(1)} %get-tuple-element.43, bf16[80,1024]{1,0:T(8,128)(2,1)S(1)} %get-tuple-element.42, bf16[80,1024]{1,0:T(8,128)(2,1)S(1)} %fusion.52), kind=kOutput, calls=%fused_computation.4 | convolution fusion | flops 1010204672 | bytes 2461696 | tf_op jit(solution)/shard_map/dot_general | solution.py:224
  (126 shorter events, 19.7 us)
Async XLA Ops:
  0.6 16.9 %copy-start = (s32[24]{0:T(128)S(1)}, s32[24]{0:T(128)}, u32[]{:S(2)}) copy-start(s32[24]{0:T(128)} %param.19) | copy-start | bytes 292
  0.6 16.7 %copy-start.3 = (bf16[80,8,256]{2,1,0:T(8,128)(2,1)S(1)}, bf16[80,8,256]{2,1,0:T(8,128)(2,1)}, u32[]{:S(2)}) copy-start(bf16[80,8,256]{2,1,0:T(8,128)(2,1)} %param.10) | copy-start | bytes 983044
  0.7 19.6 %copy-start.19 = (f32[80]{0:T(128)S(1)}, f32[80]{0:T(128)}, u32[]{:S(2)}) copy-start(f32[80]{0:T(128)} %param.13) | copy-start | bytes 964
  0.7 20.3 %copy-start.20 = (f32[80]{0:T(128)S(1)}, f32[80]{0:T(128)}, u32[]{:S(2)}) copy-start(f32[80]{0:T(128)} %param.14) | copy-start | bytes 964
  0.7 21.0 %copy-start.21 = (f32[80]{0:T(128)S(1)}, f32[80]{0:T(128)}, u32[]{:S(2)}) copy-start(f32[80]{0:T(128)} %param.12) | copy-start | bytes 964
  2.1 22.1 %collective-permute-start.6 = (s32[256]{0:T(256)S(1)}, s32[256]{0:T(256)S(1)}, u32[]{:S(2)}, u32[]{:S(2)}) collective-permute-start(s32[256]{0:T(256)S(1)} %bitcast.80), channel_id=1, source_target_pairs={{0,12},{4,0},{8,4},{12,8},{1,13},{5,1},{9,5},{13,9},{2,14},{6,2},{... | collective-permute-start | bytes 3080 | tf_op jit(solution)/shard_map/ppermute | solution.py:250
  7.2 18.2 %collective-permute-start.5 = (s32[256]{0:T(256)S(1)}, s32[256]{0:T(256)S(1)}, u32[]{:S(2)}, u32[]{:S(2)}) collective-permute-start(s32[256]{0:T(256)S(1)} %bitcast.79), channel_id=1, source_target_pairs={{0,8},{4,12},{8,0},{12,4},{1,9},{5,13},{9,1},{13,5},{2,10},{6,14},... | collective-permute-start | bytes 3080 | tf_op jit(solution)/shard_map/ppermute | solution.py:250
  7.2 21.3 %collective-permute-start.4 = (s32[256]{0:T(256)S(1)}, s32[256]{0:T(256)S(1)}, u32[]{:S(2)}, u32[]{:S(2)}) collective-permute-start(s32[256]{0:T(256)S(1)} %bitcast.78), channel_id=1, source_target_pairs={{0,4},{4,8},{8,12},{12,0},{1,5},{5,9},{9,13},{13,1},{2,6},{6,10},{... | collective-permute-start | bytes 3080 | tf_op jit(solution)/shard_map/ppermute | solution.py:250
  10.3 13.0 %copy-start.4 = (bf16[80,6,384]{2,0,1:T(8,128)(2,1)S(1)}, bf16[80,6,384]{2,0,1:T(8,128)(2,1)}, u32[]{:S(2)}) copy-start(bf16[80,6,384]{2,0,1:T(8,128)(2,1)} %param.11) | copy-start | bytes 1105924
  10.4 18.1 %collective-permute-start = (bf16[80,640]{1,0:T(8,128)(2,1)S(1)}, bf16[80,640]{1,0:T(8,128)(2,1)S(1)}, u32[]{:S(2)}, u32[]{:S(2)}) collective-permute-start(bf16[80,640]{1,0:T(8,128)(2,1)S(1)} %pad_maximum_fusion.1), channel_id=1, source_target_pairs={{0,4},{4,8},{8,12},{1,5},{5,9},{9,13},{2,6},{6,10},{10,14},{3,7},{... | collective-permute-start | bytes 307208 | tf_op jit(solution)/shard_map/ppermute | solution.py:35
  15.0 14.2 %collective-permute-start.1 = (bf16[80,640]{1,0:T(8,128)(2,1)S(1)}, bf16[80,640]{1,0:T(8,128)(2,1)S(1)}, u32[]{:S(2)}, u32[]{:S(2)}) collective-permute-start(bf16[80,640]{1,0:T(8,128)(2,1)S(1)} %pad_maximum_fusion.2), channel_id=1, source_target_pairs={{4,0},{8,4},{12,8},{5,1},{9,5},{13,9},{6,2},{10,6},{14,10},{7,3},{... | collective-permute-start | bytes 307208 | tf_op jit(solution)/shard_map/ppermute | solution.py:36
  24.2 5.6 %collective-permute-start.3 = (bf16[80,14]{1,0:T(8,128)(2,1)S(1)}, bf16[80,14]{1,0:T(8,128)(2,1)S(1)}, u32[]{:S(2)}, u32[]{:S(2)}) collective-permute-start(bf16[80,14]{1,0:T(8,128)(2,1)S(1)} %copy.49), channel_id=1, source_target_pairs={{1,0},{2,1},{3,2},{5,4},{6,5},{7,6},{9,8},{10,9},{11,10},{13,12},{... | collective-permute-start | bytes 6728 | tf_op jit(solution)/shard_map/ppermute | solution.py:38
  25.5 4.3 %collective-permute-start.2 = (bf16[80,14]{1,0:T(8,128)(2,1)S(1)}, bf16[80,14]{1,0:T(8,128)(2,1)S(1)}, u32[]{:S(2)}, u32[]{:S(2)}) collective-permute-start(bf16[80,14]{1,0:T(8,128)(2,1)S(1)} %copy.46), channel_id=1, source_target_pairs={{0,1},{1,2},{2,3},{4,5},{5,6},{6,7},{8,9},{9,10},{10,11},{12,13},{... | collective-permute-start | bytes 6728 | tf_op jit(solution)/shard_map/ppermute | solution.py:37
  34.8 6.1 %copy-start.15 = (bf16[80,14]{1,0:T(8,128)(2,1)S(1)}, bf16[80,14]{1,0:T(8,128)(2,1)}, u32[]{:S(2)}) copy-start(bf16[80,14]{1,0:T(8,128)(2,1)} %copy-done.14) | copy-start | bytes 6724
  34.8 6.7 %copy-start.17 = (bf16[80,14]{1,0:T(8,128)(2,1)S(1)}, bf16[80,14]{1,0:T(8,128)(2,1)}, u32[]{:S(2)}) copy-start(bf16[80,14]{1,0:T(8,128)(2,1)} %copy-done.16) | copy-start | bytes 6724
  36.7 6.8 %collective-permute-start.9 = (f32[80,256]{1,0:T(8,128)S(1)}, f32[80,256]{1,0:T(8,128)S(1)}, u32[]{:S(2)}, u32[]{:S(2)}) collective-permute-start(f32[80,256]{1,0:T(8,128)S(1)} %get-tuple-element.48), channel_id=1, source_target_pairs={{0,12},{4,0},{8,4},{12,8},{1,13},{5,1},{9,5},{13,9},{2,14},{6,2},{... | collective-permute-start | bytes 245768 | tf_op jit(solution)/shard_map/ppermute | solution.py:255
  39.7 9.5 %collective-permute-start.8 = (f32[80,256]{1,0:T(8,128)S(1)}, f32[80,256]{1,0:T(8,128)S(1)}, u32[]{:S(2)}, u32[]{:S(2)}) collective-permute-start(f32[80,256]{1,0:T(8,128)S(1)} %get-tuple-element.49), channel_id=1, source_target_pairs={{0,8},{4,12},{8,0},{12,4},{1,9},{5,13},{9,1},{13,5},{2,10},{6,14},... | collective-permute-start | bytes 245768 | tf_op jit(solution)/shard_map/ppermute | solution.py:255
  40.8 8.4 %collective-permute-start.7 = (f32[80,256]{1,0:T(8,128)S(1)}, f32[80,256]{1,0:T(8,128)S(1)}, u32[]{:S(2)}, u32[]{:S(2)}) collective-permute-start(f32[80,256]{1,0:T(8,128)S(1)} %get-tuple-element.50), channel_id=1, source_target_pairs={{0,4},{4,8},{8,12},{12,0},{1,5},{5,9},{9,13},{13,1},{2,6},{6,10},{... | collective-permute-start | bytes 245768 | tf_op jit(solution)/shard_map/ppermute | solution.py:255
  54.3 8.1 %collective-permute-start.10 = (bf16[80,384]{1,0:T(8,128)(2,1)}, bf16[80,384]{1,0:T(8,128)(2,1)S(1)}, u32[]{:S(2)}, u32[]{:S(2)}) collective-permute-start(bf16[80,384]{1,0:T(8,128)(2,1)} %get-tuple-element.16), channel_id=1, source_target_pairs={{0,4},{4,8},{8,12},{1,5},{5,9},{9,13},{2,6},{6,10},{10,14},{3,7},{... | collective-permute-start | bytes 184328 | tf_op jit(solution)/shard_map/ppermute | solution.py:35
  55.7 6.8 %collective-permute-start.11 = (bf16[80,384]{1,0:T(8,128)(2,1)}, bf16[80,384]{1,0:T(8,128)(2,1)S(1)}, u32[]{:S(2)}, u32[]{:S(2)}) collective-permute-start(bf16[80,384]{1,0:T(8,128)(2,1)} %get-tuple-element.17), channel_id=1, source_target_pairs={{4,0},{8,4},{12,8},{5,1},{9,5},{13,9},{6,2},{10,6},{14,10},{7,3},{... | collective-permute-start | bytes 184328 | tf_op jit(solution)/shard_map/ppermute | solution.py:36
  57.0 3.2 %collective-permute-start.12 = (bf16[80,6]{1,0:T(8,128)(2,1)}, bf16[80,6]{1,0:T(8,128)(2,1)S(1)}, u32[]{:S(2)}, u32[]{:S(2)}) collective-permute-start(bf16[80,6]{1,0:T(8,128)(2,1)} %get-tuple-element.18), channel_id=1, source_target_pairs={{0,1},{1,2},{2,3},{4,5},{5,6},{6,7},{8,9},{9,10},{10,11},{12,13},{... | collective-permute-start | bytes 2888 | tf_op jit(solution)/shard_map/ppermute | solution.py:37
  58.9 3.5 %collective-permute-start.13 = (bf16[80,6]{1,0:T(8,128)(2,1)}, bf16[80,6]{1,0:T(8,128)(2,1)S(1)}, u32[]{:S(2)}, u32[]{:S(2)}) collective-permute-start(bf16[80,6]{1,0:T(8,128)(2,1)} %get-tuple-element.19), channel_id=1, source_target_pairs={{1,0},{2,1},{3,2},{5,4},{6,5},{7,6},{9,8},{10,9},{11,10},{13,12},{... | collective-permute-start | bytes 2888 | tf_op jit(solution)/shard_map/ppermute | solution.py:38
  60.2 2.3 %copy-start.12 = (bf16[80,6]{1,0:T(8,128)(2,1)}, bf16[80,6]{1,0:T(8,128)(2,1)S(1)}, u32[]{:S(2)}) copy-start(bf16[80,6]{1,0:T(8,128)(2,1)S(1)} %collective-permute-done.12.refs_3_) | copy-start | bytes 2884
  66.6 13.4 %collective-permute-start.14 = (bf16[80,384]{1,0:T(8,128)(2,1)}, bf16[80,384]{1,0:T(8,128)(2,1)S(1)}, u32[]{:S(2)}, u32[]{:S(2)}) collective-permute-start(bf16[80,384]{1,0:T(8,128)(2,1)} %get-tuple-element.21), channel_id=1, source_target_pairs={{0,4},{4,8},{8,12},{1,5},{5,9},{9,13},{2,6},{6,10},{10,14},{3,7},{... | collective-permute-start | bytes 184328 | tf_op jit(solution)/shard_map/ppermute | solution.py:35
  71.2 8.8 %collective-permute-start.15 = (bf16[80,384]{1,0:T(8,128)(2,1)}, bf16[80,384]{1,0:T(8,128)(2,1)S(1)}, u32[]{:S(2)}, u32[]{:S(2)}) collective-permute-start(bf16[80,384]{1,0:T(8,128)(2,1)} %get-tuple-element.22), channel_id=1, source_target_pairs={{4,0},{8,4},{12,8},{5,1},{9,5},{13,9},{6,2},{10,6},{14,10},{7,3},{... | collective-permute-start | bytes 184328 | tf_op jit(solution)/shard_map/ppermute | solution.py:36
  72.5 5.5 %collective-permute-start.16 = (bf16[80,6]{1,0:T(8,128)(2,1)}, bf16[80,6]{1,0:T(8,128)(2,1)S(1)}, u32[]{:S(2)}, u32[]{:S(2)}) collective-permute-start(bf16[80,6]{1,0:T(8,128)(2,1)} %get-tuple-element.23), channel_id=1, source_target_pairs={{0,1},{1,2},{2,3},{4,5},{5,6},{6,7},{8,9},{9,10},{10,11},{12,13},{... | collective-permute-start | bytes 2888 | tf_op jit(solution)/shard_map/ppermute | solution.py:37
  76.6 3.3 %collective-permute-start.17 = (bf16[80,6]{1,0:T(8,128)(2,1)}, bf16[80,6]{1,0:T(8,128)(2,1)S(1)}, u32[]{:S(2)}, u32[]{:S(2)}) collective-permute-start(bf16[80,6]{1,0:T(8,128)(2,1)} %get-tuple-element.24), channel_id=1, source_target_pairs={{1,0},{2,1},{3,2},{5,4},{6,5},{7,6},{9,8},{10,9},{11,10},{13,12},{... | collective-permute-start | bytes 2888 | tf_op jit(solution)/shard_map/ppermute | solution.py:38
  78.0 2.0 %copy-start.10 = (bf16[80,6]{1,0:T(8,128)(2,1)}, bf16[80,6]{1,0:T(8,128)(2,1)S(1)}, u32[]{:S(2)}) copy-start(bf16[80,6]{1,0:T(8,128)(2,1)S(1)} %collective-permute-done.16.refs_3_) | copy-start | bytes 2884
  84.0 8.9 %copy-start.5 = (f32[80,2304]{1,0:T(8,128)S(1)}, f32[80,2304]{1,0:T(8,128)}, u32[]{:S(2)}) copy-start(f32[80,2304]{1,0:T(8,128)} %get-tuple-element.25) | copy-start | bytes 2211844
  86.9 6.8 %collective-permute-start.20 = (f32[80,256]{1,0:T(8,128)S(1)}, f32[80,256]{1,0:T(8,128)S(1)}, u32[]{:S(2)}, u32[]{:S(2)}) collective-permute-start(f32[80,256]{1,0:T(8,128)S(1)} %get-tuple-element.45), channel_id=1, source_target_pairs={{0,12},{4,0},{8,4},{12,8},{1,13},{5,1},{9,5},{13,9},{2,14},{6,2},{... | collective-permute-start | bytes 245768 | tf_op jit(solution)/shard_map/ppermute | solution.py:298
  90.9 8.9 %collective-permute-start.19 = (f32[80,256]{1,0:T(8,128)S(1)}, f32[80,256]{1,0:T(8,128)S(1)}, u32[]{:S(2)}, u32[]{:S(2)}) collective-permute-start(f32[80,256]{1,0:T(8,128)S(1)} %get-tuple-element.46), channel_id=1, source_target_pairs={{0,8},{4,12},{8,0},{12,4},{1,9},{5,13},{9,1},{13,5},{2,10},{6,14},... | collective-permute-start | bytes 245768 | tf_op jit(solution)/shard_map/ppermute | solution.py:298
  91.1 8.7 %collective-permute-start.18 = (f32[80,256]{1,0:T(8,128)S(1)}, f32[80,256]{1,0:T(8,128)S(1)}, u32[]{:S(2)}, u32[]{:S(2)}) collective-permute-start(f32[80,256]{1,0:T(8,128)S(1)} %get-tuple-element.47), channel_id=1, source_target_pairs={{0,4},{4,8},{8,12},{12,0},{1,5},{5,9},{9,13},{13,1},{2,6},{6,10},{... | collective-permute-start | bytes 245768 | tf_op jit(solution)/shard_map/ppermute | solution.py:298
  (11 other events, 9.6 us)

commit v7 on v6

--- a/solution.py
+++ b/solution.py
@@ -198,11 +198,11 @@
 
 
 def split3(values):
-    hi = values.astype(jnp.bfloat16)
-    rest = values - hi.astype(jnp.float32)
-    mid = rest.astype(jnp.bfloat16)
-    lo = (rest - mid.astype(jnp.float32)).astype(jnp.bfloat16)
-    return hi, mid, lo
+    hi = lax.reduce_precision(values, exponent_bits=8, mantissa_bits=7)
+    rest = values - hi
+    mid = lax.reduce_precision(rest, exponent_bits=8, mantissa_bits=7)
+    lo = rest - mid
+    return hi.astype(jnp.bfloat16), mid.astype(jnp.bfloat16), lo.astype(jnp.bfloat16)
 
 
 def shifted_pairs(count, shift):

time: 103 us -> 103 us (level)
  no operation moved by 1% of the time
where the time goes in v7:
time: 103 us
  starting transfers between devices  43.6 us (42%)
  local copies, waits for them, and re-layouts  18.1 us (18%)
  waiting for transfers between devices  16.2 us (16%)
  Pallas kernels  13.2 us (13%)
  matrix products  7.02 us (7%)
  other arithmetic  3.25 us (3%)
  between operations  1.21 us (1%)
    pallas_call x4, Pallas kernels, stencil_step(): pl.pallas_call(functools.partial(step_kernel, rows=rows, cols=cols, nest=...  13.2 us
    ppermute x3, starting transfers between devices, exchange(): above = lax.ppermute(last_rows, 'gx', fwd_x)  10.6 us
    ppermute x3, starting transfers between devices, exchange(): left = lax.ppermute(last_cols, Y_AXES, fwd_y)  9.01 us
    unnamed x58, local copies, waits for them, and re-layouts  6.31 us
    ppermute x3, starting transfers between devices, body(): lax.ppermute(wanted[s], 'gx', shifted_pairs(tiles_x, s))  6.14 us
    ppermute x3, waiting for transfers between devices, body(): lax.ppermute(outgoing[s], 'gx', shifted_pairs(tiles_x, s))  6.11 us
    ppermute x3, starting transfers between devices, body(): lax.ppermute(outgoing[s], 'gx', shifted_pairs(tiles_x, s))  5.98 us
    ppermute x3, waiting for transfers between devices, body(): lax.ppermute(replies[:, s * requests:(s + 1) * requests], 'gx', shifted_p...  5.77 us
  transfers between devices with their start and end apart: 21, of which 5 were waited for; matrix products, arithmetic and copies ran while one was open for 14% of the time, Pallas kernels for 0%

profile of v7, /device:TPU:0, one launch (start us, length us, event | category | flops | bytes accessed | tf_op | source)
XLA Modules:
  0.0 102.6 jit_solution(15976065488554313278)
XLA Ops:
  2.1 5.1 %collective-permute-start.6 = (s32[256]{0:T(256)S(1)}, s32[256]{0:T(256)S(1)}, u32[]{:S(2)}, u32[]{:S(2)}) collective-permute-start(s32[256]{0:T(256)S(1)} %bitcast.80), channel_id=1, source_target_pairs={{0,12},{4,0},{8,4},{12,8},{1,13},{5,1},{9,5},{13,9},{2,14},{6,2},{... | collective-permute-start | bytes 3080 | tf_op jit(solution)/shard_map/ppermute | solution.py:250
  9.1 1.2 %fusion.64 = (bf16[80,1,256]{2,1,0:T(2,128)(2,1)S(1)}, bf16[80,1,256]{2,1,0:T(2,128)(2,1)S(1)}) fusion(bf16[80,8,256]{2,1,0:T(8,128)(2,1)} %param.10), kind=kLoop, calls=%fused_computation.125 | loop fusion | bytes 163840 | tf_op jit(solution)/shard_map/slice | solution.py:21
  10.4 4.5 %collective-permute-start = (bf16[80,640]{1,0:T(8,128)(2,1)S(1)}, bf16[80,640]{1,0:T(8,128)(2,1)S(1)}, u32[]{:S(2)}, u32[]{:S(2)}) collective-permute-start(bf16[80,640]{1,0:T(8,128)(2,1)S(1)} %pad_maximum_fusion.1), channel_id=1, source_target_pairs={{0,4},{4,8},{8,12},{1,5},{5,9},{9,13},{2,6},{6,10},{10,14},{3,7},{... | collective-permute-start | bytes 307208 | tf_op jit(solution)/shard_map/ppermute | solution.py:35
  15.0 1.3 %collective-permute-start.1 = (bf16[80,640]{1,0:T(8,128)(2,1)S(1)}, bf16[80,640]{1,0:T(8,128)(2,1)S(1)}, u32[]{:S(2)}, u32[]{:S(2)}) collective-permute-start(bf16[80,640]{1,0:T(8,128)(2,1)S(1)} %pad_maximum_fusion.2), channel_id=1, source_target_pairs={{4,0},{8,4},{12,8},{5,1},{9,5},{13,9},{6,2},{10,6},{14,10},{7,3},{... | collective-permute-start | bytes 307208 | tf_op jit(solution)/shard_map/ppermute | solution.py:36
  16.3 1.1 %fusion.61 = (bf16[80,6,1]{2,0,1:T(8,128)(2,1)S(1)}, bf16[80,6,1]{2,0,1:T(8,128)(2,1)S(1)}) fusion(bf16[80,6,384]{2,0,1:T(8,128)(2,1)} %param.11), kind=kLoop, calls=%fused_computation.122 | loop fusion | bytes 3840 | tf_op jit(solution)/shard_map/slice | solution.py:21
  24.2 1.3 %collective-permute-start.3 = (bf16[80,14]{1,0:T(8,128)(2,1)S(1)}, bf16[80,14]{1,0:T(8,128)(2,1)S(1)}, u32[]{:S(2)}, u32[]{:S(2)}) collective-permute-start(bf16[80,14]{1,0:T(8,128)(2,1)S(1)} %copy.49), channel_id=1, source_target_pairs={{1,0},{2,1},{3,2},{5,4},{6,5},{7,6},{9,8},{10,9},{11,10},{13,12},{... | collective-permute-start | bytes 6728 | tf_op jit(solution)/shard_map/ppermute | solution.py:38
  25.5 3.0 %collective-permute-start.2 = (bf16[80,14]{1,0:T(8,128)(2,1)S(1)}, bf16[80,14]{1,0:T(8,128)(2,1)S(1)}, u32[]{:S(2)}, u32[]{:S(2)}) collective-permute-start(bf16[80,14]{1,0:T(8,128)(2,1)S(1)} %copy.46), channel_id=1, source_target_pairs={{0,1},{1,2},{2,3},{4,5},{5,6},{6,7},{8,9},{9,10},{10,11},{12,13},{... | collective-permute-start | bytes 6728 | tf_op jit(solution)/shard_map/ppermute | solution.py:37
  30.4 2.9 %shard_map.113 = (f32[80,2048]{1,0:T(8,128)}, bf16[80,256]{1,0:T(8,128)(2,1)}, bf16[80,256]{1,0:T(8,128)(2,1)}, bf16[80,8]{1,0:T(8,128)(2,1)}, bf16[80,8]{1,0:T(8,128)(2,1)}) custom-call(bf16[80,2048]{1,0:T(8,128)(2,1)} %bitcast.59, bf16[80,256]{1,0:T(8,128)(2,1)} %slice.195.refs_1_, bf16[80,256]{1,0:T(8,128)(2,1)} %slice.196.refs_2_, ...), custom_call_target="tpu_custom_call" | custom-call | flops 165806080 | bytes 1093440 | tf_op jit(solution)/shard_map/pallas_call | solution.py:140
  33.4 1.2 %reduce-precision_convert_fusion.1 = (bf16[80,2048]{1,0:T(8,128)(2,1)S(1)}, bf16[80,2048]{1,0:T(8,128)(2,1)S(1)}, bf16[80,2048]{1,0:T(8,128)(2,1)S(1)}) fusion(f32[80,2048]{1,0:T(8,128)} %get-tuple-element.14), kind=kLoop, calls=%fused_computation.15 | loop fusion | flops 1146880 | bytes 1638400 | tf_op jit(solution)/shard_map/convert_element_type | solution.py:205
  34.6 1.8 %fusion = f32[240,1024]{1,0:T(8,128)S(1)} fusion(s32[1024]{0:T(1024)S(1)} %pad_add_fusion, bf16[80,2048]{1,0:T(8,128)(2,1)S(1)} %get-tuple-element.36, bf16[80,2048]{1,0:T(8,128)(2,1)S(1)} %get-tuple-element.37, bf16[80,2048]{1,0:T(8,128)(2,1)S(1)} %get-tuple-element.35), kind=kOutput, calls=%fused_computation.3 | convolution fusion | flops 1011679232 | bytes 1970176 | tf_op jit(solution)/shard_map/dot_general | solution.py:216
  36.5 3.0 %collective-permute-start.9 = (f32[80,256]{1,0:T(8,128)S(1)}, f32[80,256]{1,0:T(8,128)S(1)}, u32[]{:S(2)}, u32[]{:S(2)}) collective-permute-start(f32[80,256]{1,0:T(8,128)S(1)} %get-tuple-element.49), channel_id=1, source_target_pairs={{0,12},{4,0},{8,4},{12,8},{1,13},{5,1},{9,5},{13,9},{2,14},{6,2},{... | collective-permute-start | bytes 245768 | tf_op jit(solution)/shard_map/ppermute | solution.py:255
  39.5 1.1 %collective-permute-start.8 = (f32[80,256]{1,0:T(8,128)S(1)}, f32[80,256]{1,0:T(8,128)S(1)}, u32[]{:S(2)}, u32[]{:S(2)}) collective-permute-start(f32[80,256]{1,0:T(8,128)S(1)} %get-tuple-element.50), channel_id=1, source_target_pairs={{0,8},{4,12},{8,0},{12,4},{1,9},{5,13},{9,1},{13,5},{2,10},{6,14},... | collective-permute-start | bytes 245768 | tf_op jit(solution)/shard_map/ppermute | solution.py:255
  43.3 5.8 %collective-permute-done.8 = f32[80,256]{1,0:T(8,128)S(1)} collective-permute-done((f32[80,256]{1,0:T(8,128)S(1)}, f32[80,256]{1,0:T(8,128)S(1)}, u32[]{:S(2)}, u32[]{:S(2)}) %collective-permute-start.8) | collective-permute-done | bytes 81952 | tf_op jit(solution)/shard_map/ppermute | solution.py:255
  50.6 3.4 %shard_map.114 = (f32[80,2304]{1,0:T(8,128)}, bf16[80,384]{1,0:T(8,128)(2,1)}, bf16[80,384]{1,0:T(8,128)(2,1)}, bf16[80,6]{1,0:T(8,128)(2,1)}, bf16[80,6]{1,0:T(8,128)(2,1)}) custom-call(bf16[80,2304]{1,0:T(8,128)(2,1)} %bitcast.55, bf16[80,384]{1,0:T(8,128)(2,1)} %slice.199.refs_1_, bf16[80,384]{1,0:T(8,128)(2,1)} %slice.200.refs_2_, ...), custom_call_target="tpu_custom_call" | custom-call | flops 185057280 | bytes 2012672 | tf_op jit(solution)/shard_map/pallas_call | solution.py:140
  54.1 1.5 %collective-permute-start.10 = (bf16[80,384]{1,0:T(8,128)(2,1)}, bf16[80,384]{1,0:T(8,128)(2,1)S(1)}, u32[]{:S(2)}, u32[]{:S(2)}) collective-permute-start(bf16[80,384]{1,0:T(8,128)(2,1)} %get-tuple-element.16), channel_id=1, source_target_pairs={{0,4},{4,8},{8,12},{1,5},{5,9},{9,13},{2,6},{6,10},{10,14},{3,7},{... | collective-permute-start | bytes 184328 | tf_op jit(solution)/shard_map/ppermute | solution.py:35
  55.6 1.3 %collective-permute-start.11 = (bf16[80,384]{1,0:T(8,128)(2,1)}, bf16[80,384]{1,0:T(8,128)(2,1)S(1)}, u32[]{:S(2)}, u32[]{:S(2)}) collective-permute-start(bf16[80,384]{1,0:T(8,128)(2,1)} %get-tuple-element.17), channel_id=1, source_target_pairs={{4,0},{8,4},{12,8},{5,1},{9,5},{13,9},{6,2},{10,6},{14,10},{7,3},{... | collective-permute-start | bytes 184328 | tf_op jit(solution)/shard_map/ppermute | solution.py:36
  56.9 1.8 %collective-permute-start.12 = (bf16[80,6]{1,0:T(8,128)(2,1)}, bf16[80,6]{1,0:T(8,128)(2,1)S(1)}, u32[]{:S(2)}, u32[]{:S(2)}) collective-permute-start(bf16[80,6]{1,0:T(8,128)(2,1)} %get-tuple-element.18), channel_id=1, source_target_pairs={{0,1},{1,2},{2,3},{4,5},{5,6},{6,7},{8,9},{9,10},{10,11},{12,13},{... | collective-permute-start | bytes 2888 | tf_op jit(solution)/shard_map/ppermute | solution.py:37
  58.7 1.3 %collective-permute-start.13 = (bf16[80,6]{1,0:T(8,128)(2,1)}, bf16[80,6]{1,0:T(8,128)(2,1)S(1)}, u32[]{:S(2)}, u32[]{:S(2)}) collective-permute-start(bf16[80,6]{1,0:T(8,128)(2,1)} %get-tuple-element.19), channel_id=1, source_target_pairs={{1,0},{2,1},{3,2},{5,4},{6,5},{7,6},{9,8},{10,9},{11,10},{13,12},{... | collective-permute-start | bytes 2888 | tf_op jit(solution)/shard_map/ppermute | solution.py:38
  60.0 2.2 %collective-permute-done.13.refs_4_ = bf16[80,6]{1,0:T(8,128)(2,1)S(1)} collective-permute-done((bf16[80,6]{1,0:T(8,128)(2,1)}, bf16[80,6]{1,0:T(8,128)(2,1)S(1)}, u32[]{:S(2)}, u32[]{:S(2)}) %collective-permute-start.13) | collective-permute-done | bytes 992 | tf_op jit(solution)/shard_map/ppermute | solution.py:38
  63.0 3.4 %shard_map.115 = (f32[80,2304]{1,0:T(8,128)}, bf16[80,384]{1,0:T(8,128)(2,1)}, bf16[80,384]{1,0:T(8,128)(2,1)}, bf16[80,6]{1,0:T(8,128)(2,1)}, bf16[80,6]{1,0:T(8,128)(2,1)}) custom-call(f32[80,2304]{1,0:T(8,128)} %get-tuple-element.15.refs_0_, bf16[80,384]{1,0:T(8,128)(2,1)} %copy-done.8, bf16[80,384]{1,0:T(8,128)(2,1)} %copy-done.9, ...), custom_call_target="tpu_custom_call" | custom-call | flops 185057280 | bytes 2381312 | tf_op jit(solution)/shard_map/pallas_call | solution.py:140
  66.4 4.6 %collective-permute-start.14 = (bf16[80,384]{1,0:T(8,128)(2,1)}, bf16[80,384]{1,0:T(8,128)(2,1)S(1)}, u32[]{:S(2)}, u32[]{:S(2)}) collective-permute-start(bf16[80,384]{1,0:T(8,128)(2,1)} %get-tuple-element.21), channel_id=1, source_target_pairs={{0,4},{4,8},{8,12},{1,5},{5,9},{9,13},{2,6},{6,10},{10,14},{3,7},{... | collective-permute-start | bytes 184328 | tf_op jit(solution)/shard_map/ppermute | solution.py:35
  71.0 1.3 %collective-permute-start.15 = (bf16[80,384]{1,0:T(8,128)(2,1)}, bf16[80,384]{1,0:T(8,128)(2,1)S(1)}, u32[]{:S(2)}, u32[]{:S(2)}) collective-permute-start(bf16[80,384]{1,0:T(8,128)(2,1)} %get-tuple-element.22), channel_id=1, source_target_pairs={{4,0},{8,4},{12,8},{5,1},{9,5},{13,9},{6,2},{10,6},{14,10},{7,3},{... | collective-permute-start | bytes 184328 | tf_op jit(solution)/shard_map/ppermute | solution.py:36
  72.3 4.1 %collective-permute-start.16 = (bf16[80,6]{1,0:T(8,128)(2,1)}, bf16[80,6]{1,0:T(8,128)(2,1)S(1)}, u32[]{:S(2)}, u32[]{:S(2)}) collective-permute-start(bf16[80,6]{1,0:T(8,128)(2,1)} %get-tuple-element.23), channel_id=1, source_target_pairs={{0,1},{1,2},{2,3},{4,5},{5,6},{6,7},{8,9},{9,10},{10,11},{12,13},{... | collective-permute-start | bytes 2888 | tf_op jit(solution)/shard_map/ppermute | solution.py:37
  76.5 1.3 %collective-permute-start.17 = (bf16[80,6]{1,0:T(8,128)(2,1)}, bf16[80,6]{1,0:T(8,128)(2,1)S(1)}, u32[]{:S(2)}, u32[]{:S(2)}) collective-permute-start(bf16[80,6]{1,0:T(8,128)(2,1)} %get-tuple-element.24), channel_id=1, source_target_pairs={{1,0},{2,1},{3,2},{5,4},{6,5},{7,6},{9,8},{10,9},{11,10},{13,12},{... | collective-permute-start | bytes 2888 | tf_op jit(solution)/shard_map/ppermute | solution.py:38
  77.8 2.0 %collective-permute-done.17.refs_4_ = bf16[80,6]{1,0:T(8,128)(2,1)S(1)} collective-permute-done((bf16[80,6]{1,0:T(8,128)(2,1)}, bf16[80,6]{1,0:T(8,128)(2,1)S(1)}, u32[]{:S(2)}, u32[]{:S(2)}) %collective-permute-start.17) | collective-permute-done | bytes 992 | tf_op jit(solution)/shard_map/ppermute | solution.py:38
  80.4 3.4 %shard_map.116 = (f32[80,2304]{1,0:T(8,128)}, bf16[80,384]{1,0:T(8,128)(2,1)}, bf16[80,384]{1,0:T(8,128)(2,1)}, bf16[80,6]{1,0:T(8,128)(2,1)}, bf16[80,6]{1,0:T(8,128)(2,1)}) custom-call(f32[80,2304]{1,0:T(8,128)} %get-tuple-element.20.refs_0_, bf16[80,384]{1,0:T(8,128)(2,1)} %copy-done.6, bf16[80,384]{1,0:T(8,128)(2,1)} %copy-done.7, ...), custom_call_target="tpu_custom_call" | custom-call | flops 185057280 | bytes 2381312 | tf_op jit(solution)/shard_map/pallas_call | solution.py:140
  83.9 1.4 %fusion.20 = f32[80,128]{1,0:T(8,128)S(1)} fusion(f32[80,2304]{1,0:T(8,128)} %get-tuple-element.25, s32[128]{0:T(128)S(1)} %iota_add_fusion, s32[384]{0:T(512)S(1)} %get-tuple-element.66, s32[384]{0:T(512)S(1)} %get-tuple-element.67, pred[384]{0:T(512)(128)(4,1)S(1)} %fusion.56), kind=kOutput, calls=%fused_computation.38 | convolution fusion | flops 47345664 | bytes 413568 | tf_op jit(solution)/shard_map/dot_general | solution.py:192
  85.3 1.4 %fusion.19 = f32[80,128]{1,0:T(8,128)S(1)} fusion(f32[80,2304]{1,0:T(8,128)} %get-tuple-element.25, s32[128]{0:T(128)S(1)} %iota_add_fusion, s32[384]{0:T(512)S(1)} %get-tuple-element.66, s32[384]{0:T(512)S(1)} %get-tuple-element.67, pred[384]{0:T(512)(128)(4,1)S(1)} %fusion.56), kind=kOutput, calls=%fused_computation.37 | convolution fusion | flops 47345664 | bytes 413568 | tf_op jit(solution)/shard_map/dot_general | solution.py:192
  86.7 4.0 %collective-permute-start.20 = (f32[80,256]{1,0:T(8,128)S(1)}, f32[80,256]{1,0:T(8,128)S(1)}, u32[]{:S(2)}, u32[]{:S(2)}) collective-permute-start(f32[80,256]{1,0:T(8,128)S(1)} %get-tuple-element.46), channel_id=1, source_target_pairs={{0,12},{4,0},{8,4},{12,8},{1,13},{5,1},{9,5},{13,9},{2,14},{6,2},{... | collective-permute-start | bytes 245768 | tf_op jit(solution)/shard_map/ppermute | solution.py:298
  90.9 1.8 %collective-permute-start.18 = (f32[80,256]{1,0:T(8,128)S(1)}, f32[80,256]{1,0:T(8,128)S(1)}, u32[]{:S(2)}, u32[]{:S(2)}) collective-permute-start(f32[80,256]{1,0:T(8,128)S(1)} %get-tuple-element.48), channel_id=1, source_target_pairs={{0,4},{4,8},{8,12},{12,0},{1,5},{5,9},{9,13},{13,1},{2,6},{6,10},{... | collective-permute-start | bytes 245768 | tf_op jit(solution)/shard_map/ppermute | solution.py:298
  93.5 6.1 %collective-permute-done.19 = f32[80,256]{1,0:T(8,128)S(1)} collective-permute-done((f32[80,256]{1,0:T(8,128)S(1)}, f32[80,256]{1,0:T(8,128)S(1)}, u32[]{:S(2)}, u32[]{:S(2)}) %collective-permute-start.19) | collective-permute-done | bytes 81952 | tf_op jit(solution)/shard_map/ppermute | solution.py:298
  99.7 1.9 %fusion.1 = f32[240,2048]{1,0:T(8,128)S(1)} fusion(s32[1024]{0:T(1024)S(1)} %pad_add_fusion, bf16[80,1024]{1,0:T(8,128)(2,1)S(1)} %get-tuple-element.44, bf16[80,1024]{1,0:T(8,128)(2,1)S(1)} %get-tuple-element.43, bf16[80,1024]{1,0:T(8,128)(2,1)S(1)} %get-tuple-element.42), kind=kOutput, calls=%fused_computation.4 | convolution fusion | flops 1010204672 | bytes 2461696 | tf_op jit(solution)/shard_map/dot_general | solution.py:224
  (125 shorter events, 19.8 us)
Async XLA Ops:
  0.6 16.9 %copy-start = (s32[24]{0:T(128)S(1)}, s32[24]{0:T(128)}, u32[]{:S(2)}) copy-start(s32[24]{0:T(128)} %param.19) | copy-start | bytes 292
  0.6 16.7 %copy-start.3 = (bf16[80,8,256]{2,1,0:T(8,128)(2,1)S(1)}, bf16[80,8,256]{2,1,0:T(8,128)(2,1)}, u32[]{:S(2)}) copy-start(bf16[80,8,256]{2,1,0:T(8,128)(2,1)} %param.10) | copy-start | bytes 983044
  0.7 19.6 %copy-start.19 = (f32[80]{0:T(128)S(1)}, f32[80]{0:T(128)}, u32[]{:S(2)}) copy-start(f32[80]{0:T(128)} %param.13) | copy-start | bytes 964
  0.7 20.3 %copy-start.20 = (f32[80]{0:T(128)S(1)}, f32[80]{0:T(128)}, u32[]{:S(2)}) copy-start(f32[80]{0:T(128)} %param.14) | copy-start | bytes 964
  0.7 21.0 %copy-start.21 = (f32[80]{0:T(128)S(1)}, f32[80]{0:T(128)}, u32[]{:S(2)}) copy-start(f32[80]{0:T(128)} %param.12) | copy-start | bytes 964
  2.1 22.1 %collective-permute-start.6 = (s32[256]{0:T(256)S(1)}, s32[256]{0:T(256)S(1)}, u32[]{:S(2)}, u32[]{:S(2)}) collective-permute-start(s32[256]{0:T(256)S(1)} %bitcast.80), channel_id=1, source_target_pairs={{0,12},{4,0},{8,4},{12,8},{1,13},{5,1},{9,5},{13,9},{2,14},{6,2},{... | collective-permute-start | bytes 3080 | tf_op jit(solution)/shard_map/ppermute | solution.py:250
  7.2 18.2 %collective-permute-start.5 = (s32[256]{0:T(256)S(1)}, s32[256]{0:T(256)S(1)}, u32[]{:S(2)}, u32[]{:S(2)}) collective-permute-start(s32[256]{0:T(256)S(1)} %bitcast.79), channel_id=1, source_target_pairs={{0,8},{4,12},{8,0},{12,4},{1,9},{5,13},{9,1},{13,5},{2,10},{6,14},... | collective-permute-start | bytes 3080 | tf_op jit(solution)/shard_map/ppermute | solution.py:250
  7.2 21.3 %collective-permute-start.4 = (s32[256]{0:T(256)S(1)}, s32[256]{0:T(256)S(1)}, u32[]{:S(2)}, u32[]{:S(2)}) collective-permute-start(s32[256]{0:T(256)S(1)} %bitcast.78), channel_id=1, source_target_pairs={{0,4},{4,8},{8,12},{12,0},{1,5},{5,9},{9,13},{13,1},{2,6},{6,10},{... | collective-permute-start | bytes 3080 | tf_op jit(solution)/shard_map/ppermute | solution.py:250
  10.3 13.0 %copy-start.4 = (bf16[80,6,384]{2,0,1:T(8,128)(2,1)S(1)}, bf16[80,6,384]{2,0,1:T(8,128)(2,1)}, u32[]{:S(2)}) copy-start(bf16[80,6,384]{2,0,1:T(8,128)(2,1)} %param.11) | copy-start | bytes 1105924
  10.4 18.1 %collective-permute-start = (bf16[80,640]{1,0:T(8,128)(2,1)S(1)}, bf16[80,640]{1,0:T(8,128)(2,1)S(1)}, u32[]{:S(2)}, u32[]{:S(2)}) collective-permute-start(bf16[80,640]{1,0:T(8,128)(2,1)S(1)} %pad_maximum_fusion.1), channel_id=1, source_target_pairs={{0,4},{4,8},{8,12},{1,5},{5,9},{9,13},{2,6},{6,10},{10,14},{3,7},{... | collective-permute-start | bytes 307208 | tf_op jit(solution)/shard_map/ppermute | solution.py:35
  15.0 14.2 %collective-permute-start.1 = (bf16[80,640]{1,0:T(8,128)(2,1)S(1)}, bf16[80,640]{1,0:T(8,128)(2,1)S(1)}, u32[]{:S(2)}, u32[]{:S(2)}) collective-permute-start(bf16[80,640]{1,0:T(8,128)(2,1)S(1)} %pad_maximum_fusion.2), channel_id=1, source_target_pairs={{4,0},{8,4},{12,8},{5,1},{9,5},{13,9},{6,2},{10,6},{14,10},{7,3},{... | collective-permute-start | bytes 307208 | tf_op jit(solution)/shard_map/ppermute | solution.py:36
  24.2 5.6 %collective-permute-start.3 = (bf16[80,14]{1,0:T(8,128)(2,1)S(1)}, bf16[80,14]{1,0:T(8,128)(2,1)S(1)}, u32[]{:S(2)}, u32[]{:S(2)}) collective-permute-start(bf16[80,14]{1,0:T(8,128)(2,1)S(1)} %copy.49), channel_id=1, source_target_pairs={{1,0},{2,1},{3,2},{5,4},{6,5},{7,6},{9,8},{10,9},{11,10},{13,12},{... | collective-permute-start | bytes 6728 | tf_op jit(solution)/shard_map/ppermute | solution.py:38
  25.5 4.3 %collective-permute-start.2 = (bf16[80,14]{1,0:T(8,128)(2,1)S(1)}, bf16[80,14]{1,0:T(8,128)(2,1)S(1)}, u32[]{:S(2)}, u32[]{:S(2)}) collective-permute-start(bf16[80,14]{1,0:T(8,128)(2,1)S(1)} %copy.46), channel_id=1, source_target_pairs={{0,1},{1,2},{2,3},{4,5},{5,6},{6,7},{8,9},{9,10},{10,11},{12,13},{... | collective-permute-start | bytes 6728 | tf_op jit(solution)/shard_map/ppermute | solution.py:37
  34.6 6.1 %copy-start.15 = (bf16[80,14]{1,0:T(8,128)(2,1)S(1)}, bf16[80,14]{1,0:T(8,128)(2,1)}, u32[]{:S(2)}) copy-start(bf16[80,14]{1,0:T(8,128)(2,1)} %copy-done.14) | copy-start | bytes 6724
  34.6 6.7 %copy-start.17 = (bf16[80,14]{1,0:T(8,128)(2,1)S(1)}, bf16[80,14]{1,0:T(8,128)(2,1)}, u32[]{:S(2)}) copy-start(bf16[80,14]{1,0:T(8,128)(2,1)} %copy-done.16) | copy-start | bytes 6724
  36.5 6.8 %collective-permute-start.9 = (f32[80,256]{1,0:T(8,128)S(1)}, f32[80,256]{1,0:T(8,128)S(1)}, u32[]{:S(2)}, u32[]{:S(2)}) collective-permute-start(f32[80,256]{1,0:T(8,128)S(1)} %get-tuple-element.49), channel_id=1, source_target_pairs={{0,12},{4,0},{8,4},{12,8},{1,13},{5,1},{9,5},{13,9},{2,14},{6,2},{... | collective-permute-start | bytes 245768 | tf_op jit(solution)/shard_map/ppermute | solution.py:255
  39.5 9.5 %collective-permute-start.8 = (f32[80,256]{1,0:T(8,128)S(1)}, f32[80,256]{1,0:T(8,128)S(1)}, u32[]{:S(2)}, u32[]{:S(2)}) collective-permute-start(f32[80,256]{1,0:T(8,128)S(1)} %get-tuple-element.50), channel_id=1, source_target_pairs={{0,8},{4,12},{8,0},{12,4},{1,9},{5,13},{9,1},{13,5},{2,10},{6,14},... | collective-permute-start | bytes 245768 | tf_op jit(solution)/shard_map/ppermute | solution.py:255
  40.7 8.4 %collective-permute-start.7 = (f32[80,256]{1,0:T(8,128)S(1)}, f32[80,256]{1,0:T(8,128)S(1)}, u32[]{:S(2)}, u32[]{:S(2)}) collective-permute-start(f32[80,256]{1,0:T(8,128)S(1)} %get-tuple-element.51), channel_id=1, source_target_pairs={{0,4},{4,8},{8,12},{12,0},{1,5},{5,9},{9,13},{13,1},{2,6},{6,10},{... | collective-permute-start | bytes 245768 | tf_op jit(solution)/shard_map/ppermute | solution.py:255
  54.1 8.1 %collective-permute-start.10 = (bf16[80,384]{1,0:T(8,128)(2,1)}, bf16[80,384]{1,0:T(8,128)(2,1)S(1)}, u32[]{:S(2)}, u32[]{:S(2)}) collective-permute-start(bf16[80,384]{1,0:T(8,128)(2,1)} %get-tuple-element.16), channel_id=1, source_target_pairs={{0,4},{4,8},{8,12},{1,5},{5,9},{9,13},{2,6},{6,10},{10,14},{3,7},{... | collective-permute-start | bytes 184328 | tf_op jit(solution)/shard_map/ppermute | solution.py:35
  55.6 6.8 %collective-permute-start.11 = (bf16[80,384]{1,0:T(8,128)(2,1)}, bf16[80,384]{1,0:T(8,128)(2,1)S(1)}, u32[]{:S(2)}, u32[]{:S(2)}) collective-permute-start(bf16[80,384]{1,0:T(8,128)(2,1)} %get-tuple-element.17), channel_id=1, source_target_pairs={{4,0},{8,4},{12,8},{5,1},{9,5},{13,9},{6,2},{10,6},{14,10},{7,3},{... | collective-permute-start | bytes 184328 | tf_op jit(solution)/shard_map/ppermute | solution.py:36
  56.9 3.2 %collective-permute-start.12 = (bf16[80,6]{1,0:T(8,128)(2,1)}, bf16[80,6]{1,0:T(8,128)(2,1)S(1)}, u32[]{:S(2)}, u32[]{:S(2)}) collective-permute-start(bf16[80,6]{1,0:T(8,128)(2,1)} %get-tuple-element.18), channel_id=1, source_target_pairs={{0,1},{1,2},{2,3},{4,5},{5,6},{6,7},{8,9},{9,10},{10,11},{12,13},{... | collective-permute-start | bytes 2888 | tf_op jit(solution)/shard_map/ppermute | solution.py:37
  58.7 3.5 %collective-permute-start.13 = (bf16[80,6]{1,0:T(8,128)(2,1)}, bf16[80,6]{1,0:T(8,128)(2,1)S(1)}, u32[]{:S(2)}, u32[]{:S(2)}) collective-permute-start(bf16[80,6]{1,0:T(8,128)(2,1)} %get-tuple-element.19), channel_id=1, source_target_pairs={{1,0},{2,1},{3,2},{5,4},{6,5},{7,6},{9,8},{10,9},{11,10},{13,12},{... | collective-permute-start | bytes 2888 | tf_op jit(solution)/shard_map/ppermute | solution.py:38
  60.0 2.3 %copy-start.12 = (bf16[80,6]{1,0:T(8,128)(2,1)}, bf16[80,6]{1,0:T(8,128)(2,1)S(1)}, u32[]{:S(2)}) copy-start(bf16[80,6]{1,0:T(8,128)(2,1)S(1)} %collective-permute-done.12.refs_3_) | copy-start | bytes 2884
  66.4 13.4 %collective-permute-start.14 = (bf16[80,384]{1,0:T(8,128)(2,1)}, bf16[80,384]{1,0:T(8,128)(2,1)S(1)}, u32[]{:S(2)}, u32[]{:S(2)}) collective-permute-start(bf16[80,384]{1,0:T(8,128)(2,1)} %get-tuple-element.21), channel_id=1, source_target_pairs={{0,4},{4,8},{8,12},{1,5},{5,9},{9,13},{2,6},{6,10},{10,14},{3,7},{... | collective-permute-start | bytes 184328 | tf_op jit(solution)/shard_map/ppermute | solution.py:35
  71.0 8.8 %collective-permute-start.15 = (bf16[80,384]{1,0:T(8,128)(2,1)}, bf16[80,384]{1,0:T(8,128)(2,1)S(1)}, u32[]{:S(2)}, u32[]{:S(2)}) collective-permute-start(bf16[80,384]{1,0:T(8,128)(2,1)} %get-tuple-element.22), channel_id=1, source_target_pairs={{4,0},{8,4},{12,8},{5,1},{9,5},{13,9},{6,2},{10,6},{14,10},{7,3},{... | collective-permute-start | bytes 184328 | tf_op jit(solution)/shard_map/ppermute | solution.py:36
  72.3 5.5 %collective-permute-start.16 = (bf16[80,6]{1,0:T(8,128)(2,1)}, bf16[80,6]{1,0:T(8,128)(2,1)S(1)}, u32[]{:S(2)}, u32[]{:S(2)}) collective-permute-start(bf16[80,6]{1,0:T(8,128)(2,1)} %get-tuple-element.23), channel_id=1, source_target_pairs={{0,1},{1,2},{2,3},{4,5},{5,6},{6,7},{8,9},{9,10},{10,11},{12,13},{... | collective-permute-start | bytes 2888 | tf_op jit(solution)/shard_map/ppermute | solution.py:37
  76.5 3.3 %collective-permute-start.17 = (bf16[80,6]{1,0:T(8,128)(2,1)}, bf16[80,6]{1,0:T(8,128)(2,1)S(1)}, u32[]{:S(2)}, u32[]{:S(2)}) collective-permute-start(bf16[80,6]{1,0:T(8,128)(2,1)} %get-tuple-element.24), channel_id=1, source_target_pairs={{1,0},{2,1},{3,2},{5,4},{6,5},{7,6},{9,8},{10,9},{11,10},{13,12},{... | collective-permute-start | bytes 2888 | tf_op jit(solution)/shard_map/ppermute | solution.py:38
  77.8 2.0 %copy-start.10 = (bf16[80,6]{1,0:T(8,128)(2,1)}, bf16[80,6]{1,0:T(8,128)(2,1)S(1)}, u32[]{:S(2)}) copy-start(bf16[80,6]{1,0:T(8,128)(2,1)S(1)} %collective-permute-done.16.refs_3_) | copy-start | bytes 2884
  83.9 8.9 %copy-start.5 = (f32[80,2304]{1,0:T(8,128)S(1)}, f32[80,2304]{1,0:T(8,128)}, u32[]{:S(2)}) copy-start(f32[80,2304]{1,0:T(8,128)} %get-tuple-element.25) | copy-start | bytes 2211844
  86.7 6.8 %collective-permute-start.20 = (f32[80,256]{1,0:T(8,128)S(1)}, f32[80,256]{1,0:T(8,128)S(1)}, u32[]{:S(2)}, u32[]{:S(2)}) collective-permute-start(f32[80,256]{1,0:T(8,128)S(1)} %get-tuple-element.46), channel_id=1, source_target_pairs={{0,12},{4,0},{8,4},{12,8},{1,13},{5,1},{9,5},{13,9},{2,14},{6,2},{... | collective-permute-start | bytes 245768 | tf_op jit(solution)/shard_map/ppermute | solution.py:298
  90.7 8.9 %collective-permute-start.19 = (f32[80,256]{1,0:T(8,128)S(1)}, f32[80,256]{1,0:T(8,128)S(1)}, u32[]{:S(2)}, u32[]{:S(2)}) collective-permute-start(f32[80,256]{1,0:T(8,128)S(1)} %get-tuple-element.47), channel_id=1, source_target_pairs={{0,8},{4,12},{8,0},{12,4},{1,9},{5,13},{9,1},{13,5},{2,10},{6,14},... | collective-permute-start | bytes 245768 | tf_op jit(solution)/shard_map/ppermute | solution.py:298
  90.9 8.7 %collective-permute-start.18 = (f32[80,256]{1,0:T(8,128)S(1)}, f32[80,256]{1,0:T(8,128)S(1)}, u32[]{:S(2)}, u32[]{:S(2)}) collective-permute-start(f32[80,256]{1,0:T(8,128)S(1)} %get-tuple-element.48), channel_id=1, source_target_pairs={{0,4},{4,8},{8,12},{12,0},{1,5},{5,9},{9,13},{13,1},{2,6},{6,10},{... | collective-permute-start | bytes 245768 | tf_op jit(solution)/shard_map/ppermute | solution.py:298
  (11 other events, 9.6 us)

commit v8 on v7

--- a/solution.py
+++ b/solution.py
@@ -40,12 +40,9 @@
     xo = 0
     yo = 0
     for e in edge_sets:
-        w, h = e[0].shape[1], e[2].shape[1]
-        out.append(
-            (above[:, xo : xo + w], below[:, xo : xo + w], left[:, yo : yo + h], right[:, yo : yo + h])
-        )
-        xo += w
-        yo += h
+        out.append(((above, below, left, right), xo, yo))
+        xo += e[0].shape[1]
+        yo += e[2].shape[1]
     return out
 
 
@@ -74,60 +71,76 @@
     return down + up + east + west - 4.0 * flat
 
 
-def step_kernel(*refs, rows, cols, nest):
+def step_kernel(*refs, rows, cols, xo, nu_k, relax_k, nest):
     if nest:
-        (state_ref, above_ref, below_ref, left_ref, right_ref, forcing_ref, upw_ref, dnw_ref,
-         nu_ref, relax_ref, vm_ref, new_ref, lrow_ref, frow_ref, lcol_ref, fcol_ref, up_sc, dn_sc) = refs
+        (state_ref, above_ref, below_ref, left_ref, right_ref, inj_first_ref, inj_last_ref,
+         sel_first_ref, sel_last_ref, coef_ref, vm_ref, forcing_ref, upw_ref, dnw_ref,
+         new_ref, lrow_ref, frow_ref, lcol_ref, fcol_ref, up_sc, dn_sc) = refs
     else:
-        (state_ref, above_ref, below_ref, left_ref, right_ref, nu_ref, vm_ref,
+        (state_ref, above_ref, below_ref, left_ref, right_ref, inj_first_ref, inj_last_ref,
+         sel_first_ref, sel_last_ref, coef_ref, vm_ref,
          new_ref, lrow_ref, frow_ref, lcol_ref, fcol_ref, up_sc, dn_sc) = refs
     n = rows * cols
     state = state_ref[...].astype(jnp.float32)
-    levels = state.shape[0]
-    up_sc[:, 0:cols] = above_ref[...].astype(jnp.float32)
+    up_sc[:, 0:cols] = above_ref[:, xo : xo + cols].astype(jnp.float32)
     up_sc[:, cols:n] = state[:, 0 : n - cols]
     dn_sc[:, 0 : n - cols] = state[:, cols:n]
-    dn_sc[:, n - cols : n] = below_ref[...].astype(jnp.float32)
+    dn_sc[:, n - cols : n] = below_ref[:, xo : xo + cols].astype(jnp.float32)
     up = up_sc[...]
     down = dn_sc[...]
-    lane = lax.broadcasted_iota(jnp.int32, (levels, n), 1)
-    left = left_ref[...].astype(jnp.float32)
-    right = right_ref[...].astype(jnp.float32)
-    west = pltpu.roll(state, 1, 1)
-    east = pltpu.roll(state, n - 1, 1)
-    for r in range(rows):
-        west = jnp.where(lane == r * cols, left[:, r : r + 1], west)
-        east = jnp.where(lane == r * cols + cols - 1, right[:, r : r + 1], east)
+    sel_first = sel_first_ref[...]
+    sel_last = sel_last_ref[...]
+    at_first = jnp.sum(sel_first.astype(jnp.float32), axis=0, keepdims=True) > 0.5
+    at_last = jnp.sum(sel_last.astype(jnp.float32), axis=0, keepdims=True) > 0.5
+    left_full = jnp.dot(
+        left_ref[...].astype(jnp.bfloat16), inj_first_ref[...], preferred_element_type=jnp.float32
+    )
+    right_full = jnp.dot(
+        right_ref[...].astype(jnp.bfloat16), inj_last_ref[...], preferred_element_type=jnp.float32
+    )
+    west = jnp.where(at_first, left_full, pltpu.roll(state, 1, 1))
+    east = jnp.where(at_last, right_full, pltpu.roll(state, n - 1, 1))
     if nest:
         down = down * dnw_ref[...]
         up = up * upw_ref[...]
     stencil = down + up + east + west - 4.0 * state
-    moved = state + nu_ref[...] * stencil
+    moved = state + coef_ref[:, nu_k : nu_k + 1] * stencil
     if nest:
-        moved = moved + relax_ref[...] * (forcing_ref[...] - moved)
+        moved = moved + coef_ref[:, relax_k : relax_k + 1] * (forcing_ref[...] - moved)
     new = jnp.dot(vm_ref[...], moved, precision=HI, preferred_element_type=jnp.float32)
     new_ref[...] = new
     lrow_ref[...] = new[:, n - cols : n].astype(jnp.bfloat16)
     frow_ref[...] = new[:, 0:cols].astype(jnp.bfloat16)
     narrow = new.astype(jnp.bfloat16)
-    p = lax.broadcasted_iota(jnp.int32, (n, rows), 0)
-    j = lax.broadcasted_iota(jnp.int32, (n, rows), 1)
-    last_sel = (p == j * cols + (cols - 1)).astype(jnp.bfloat16)
-    first_sel = (p == j * cols).astype(jnp.bfloat16)
-    lcol_ref[...] = jnp.dot(narrow, last_sel, preferred_element_type=jnp.float32).astype(jnp.bfloat16)
-    fcol_ref[...] = jnp.dot(narrow, first_sel, preferred_element_type=jnp.float32).astype(jnp.bfloat16)
-
-
-def stencil_step(state, halo, nu, vert_mix, rows, cols, forcing=None, up_w=None, down_w=None, relax=None):
+    pick = (((1,), (1,)), ((), ()))
+    lcol_ref[...] = lax.dot_general(
+        narrow, sel_last, pick, preferred_element_type=jnp.float32
+    ).astype(jnp.bfloat16)
+    fcol_ref[...] = lax.dot_general(
+        narrow, sel_first, pick, preferred_element_type=jnp.float32
+    ).astype(jnp.bfloat16)
+
+
+def row_onehots(width, offset, rows, cols, zero):
+    j = lax.broadcasted_iota(jnp.int32, (width, rows * cols), 0) + zero
+    p = lax.broadcasted_iota(jnp.int32, (width, rows * cols), 1)
+    inside = (j >= offset) & (j < offset + rows)
+    first = inside & (p == (j - offset) * cols)
+    last = inside & (p == (j - offset) * cols + (cols - 1))
+    return first.astype(jnp.bfloat16), last.astype(jnp.bfloat16)
+
+
+def stencil_step(state, halo, xo, yo, coefs, nu_k, vert_mix, rows, cols, zero,
+                 forcing=None, up_w=None, down_w=None, relax_k=0):
     levels = state.shape[0]
     n = rows * cols
     nest = forcing is not None
     above, below, left, right = halo
+    inj_first, inj_last = row_onehots(left.shape[1], yo, rows, cols, zero)
+    sel_first, sel_last = row_onehots(rows, 0, rows, cols, zero)
+    args = (state, above, below, left, right, inj_first, inj_last, sel_first, sel_last, coefs, vert_mix)
     if nest:
-        args = (state, above, below, left, right, forcing, up_w[None, :], down_w[None, :],
-                nu[:, None], relax[:, None], vert_mix)
-    else:
-        args = (state, above, below, left, right, nu[:, None], vert_mix)
+        args = args + (forcing, up_w[None, :], down_w[None, :])
     out_shape = (
         jax.ShapeDtypeStruct((levels, n), jnp.float32),
         jax.ShapeDtypeStruct((levels, cols), jnp.bfloat16),
@@ -135,10 +148,12 @@
         jax.ShapeDtypeStruct((levels, rows), jnp.bfloat16),
         jax.ShapeDtypeStruct((levels, rows), jnp.bfloat16),
     )
-    flops = 2 * levels * levels * n * 6 + 4 * levels * n * rows + 20 * levels * n
+    flops = 2 * levels * levels * n * 6 + 4 * levels * n * 16 + 20 * levels * n
     moved_bytes = sum(int(a.size) * a.dtype.itemsize for a in args) + levels * n * 4
     new, lrow, frow, lcol, fcol = pl.pallas_call(
-        functools.partial(step_kernel, rows=rows, cols=cols, nest=nest),
+        functools.partial(
+            step_kernel, rows=rows, cols=cols, xo=xo, nu_k=nu_k, relax_k=relax_k, nest=nest
+        ),
         out_shape=out_shape,
         scratch_shapes=[pltpu.VMEM((levels, n), jnp.float32), pltpu.VMEM((levels, n), jnp.float32)],
         cost_estimate=pl.CostEstimate(flops=flops, bytes_accessed=moved_bytes, transcendentals=0),
@@ -233,8 +248,10 @@
     zero = jnp.minimum(here_x, 0)
 
     parent_halo, nest_halo = exchange([edges_3d(parent), edges_3d(nest)])
+    coefs = jnp.stack([nu_parent, nu_nest, relax], axis=1)
     flat_parent, _ = stencil_step(
-        parent.reshape(levels, p_rows * p_cols), parent_halo, nu_parent, vert_mix, p_rows, p_cols
+        parent.reshape(levels, p_rows * p_cols), parent_halo[0], parent_halo[1], parent_halo[2],
+        coefs, 0, vert_mix, p_rows, p_cols, zero,
     )
 
     owners = fp_owner.reshape(-1)
@@ -286,7 +303,8 @@
         if turn_no > 0:
             (halo,) = exchange([edges])
         nest_state, edges = stencil_step(
-            nest_state, halo, nu_nest, vert_mix, n_rows, n_cols, forcing_full, up_w, down_w, relax
+            nest_state, halo[0], halo[1], halo[2], coefs, 1, vert_mix, n_rows, n_cols, zero,
+            forcing_full, up_w, down_w, 2,
         )
 
     block_sum = block_sums(nest_state, block_rows, n_cols, expand)

time: 103 us -> 106 us (1.029)
  local copies, waits for them, and re-layouts: 18.1 us -> 12.9 us
  waiting for transfers between devices: 16.2 us -> 19.9 us
  other arithmetic: 3.25 us -> 6.25 us
  Pallas kernels: 13.2 us -> 14.4 us
    slice x6 -> x0, local copies, waits for them, and re-layouts: 3.86 us -> none  [the longest x2 1.25 us: exchange(): below[:, xo:xo + w]]
    convert_element_type x0 -> x4, other arithmetic: none -> 2.94 us  [row_onehots(): return (first.astype(jnp.bfloat16), last.astype(jnp.bfloat16))]
    ppermute x3, waiting for transfers between devices: 5.77 us -> 8.33 us  [body(): lax.ppermute(replies[:, s * requests:(s + 1) * requests], 'gx', shifted_p...]
    broadcast_in_dim x3 -> x0, local copies, waits for them, and re-layouts: 2.13 us -> none  [the longest x1 0.71 us: stencil_step(): args = (state, above, below, left, right, nu[:, None], vert_mix)]
    pallas_call x4, Pallas kernels: 13.2 us -> 14.4 us  [stencil_step(): pl.pallas_call(functools.partial(step_kernel, rows=rows, cols=cols, xo=xo...]
  transfers between devices with their start and end apart: 21 -> 21, of which waited for: 5 -> 6; matrix products, arithmetic and copies ran while one was open for 14% -> 12% of each run, Pallas kernels for 0% -> 0%
where the time goes in v8:
time: 106 us
  starting transfers between devices  43.7 us (41%)
  waiting for transfers between devices  19.9 us (19%)
  Pallas kernels  14.4 us (14%)
  local copies, waits for them, and re-layouts  12.9 us (12%)
  matrix products  7.02 us (7%)
  other arithmetic  6.25 us (6%)
  between operations  1.3 us (1%)
    pallas_call x4, Pallas kernels, stencil_step(): pl.pallas_call(functools.partial(step_kernel, rows=rows, cols=cols, xo=xo...  14.4 us
    ppermute x3, starting transfers between devices, exchange(): above = lax.ppermute(last_rows, 'gx', fwd_x)  10.7 us
    ppermute x3, starting transfers between devices, exchange(): left = lax.ppermute(last_cols, Y_AXES, fwd_y)  8.9 us
    ppermute x3, waiting for transfers between devices, body(): lax.ppermute(replies[:, s * requests:(s + 1) * requests], 'gx', shifted_p...  8.33 us
    unnamed x58, local copies, waits for them, and re-layouts  6.37 us
    ppermute x3, starting transfers between devices, body(): lax.ppermute(wanted[s], 'gx', shifted_pairs(tiles_x, s))  6.14 us
    ppermute x3, waiting for transfers between devices, body(): lax.ppermute(outgoing[s], 'gx', shifted_pairs(tiles_x, s))  6.11 us
    ppermute x3, starting transfers between devices, body(): lax.ppermute(outgoing[s], 'gx', shifted_pairs(tiles_x, s))  5.98 us
  transfers between devices with their start and end apart: 21, of which 6 were waited for; matrix products, arithmetic and copies ran while one was open for 12% of the time, Pallas kernels for 0%

profile of v8, /device:TPU:0, one launch (start us, length us, event | category | flops | bytes accessed | tf_op | source)
XLA Modules:
  0.0 105.5 jit_solution(17386866278735980949)
XLA Ops:
  2.1 5.1 %collective-permute-start.6 = (s32[256]{0:T(256)S(1)}, s32[256]{0:T(256)S(1)}, u32[]{:S(2)}, u32[]{:S(2)}) collective-permute-start(s32[256]{0:T(256)S(1)} %bitcast.76), channel_id=1, source_target_pairs={{0,12},{4,0},{8,4},{12,8},{1,13},{5,1},{9,5},{13,9},{2,14},{6,2},{... | collective-permute-start | bytes 3080 | tf_op jit(solution)/shard_map/ppermute | solution.py:267
  9.1 1.2 %fusion.83 = (bf16[80,1,256]{2,1,0:T(2,128)(2,1)S(1)}, bf16[80,1,256]{2,1,0:T(2,128)(2,1)S(1)}) fusion(bf16[80,8,256]{2,1,0:T(8,128)(2,1)} %param.10), kind=kLoop, calls=%fused_computation.165 | loop fusion | bytes 163840 | tf_op jit(solution)/shard_map/slice | solution.py:21
  10.4 4.4 %collective-permute-start = (bf16[80,640]{1,0:T(8,128)(2,1)S(1)}, bf16[80,640]{1,0:T(8,128)(2,1)S(1)}, u32[]{:S(2)}, u32[]{:S(2)}) collective-permute-start(bf16[80,640]{1,0:T(8,128)(2,1)S(1)} %pad_maximum_fusion.1), channel_id=1, source_target_pairs={{0,4},{4,8},{8,12},{1,5},{5,9},{9,13},{2,6},{6,10},{10,14},{3,7},{... | collective-permute-start | bytes 307208 | tf_op jit(solution)/shard_map/ppermute | solution.py:35
  14.8 1.4 %collective-permute-start.1 = (bf16[80,640]{1,0:T(8,128)(2,1)S(1)}, bf16[80,640]{1,0:T(8,128)(2,1)S(1)}, u32[]{:S(2)}, u32[]{:S(2)}) collective-permute-start(bf16[80,640]{1,0:T(8,128)(2,1)S(1)} %pad_maximum_fusion.2), channel_id=1, source_target_pairs={{4,0},{8,4},{12,8},{5,1},{9,5},{13,9},{6,2},{10,6},{14,10},{7,3},{... | collective-permute-start | bytes 307208 | tf_op jit(solution)/shard_map/ppermute | solution.py:36
  25.8 1.3 %collective-permute-start.3 = (bf16[80,14]{1,0:T(8,128)(2,1)S(1)}, bf16[80,14]{1,0:T(8,128)(2,1)S(1)}, u32[]{:S(2)}, u32[]{:S(2)}) collective-permute-start(bf16[80,14]{1,0:T(8,128)(2,1)S(1)} %copy.41), channel_id=1, source_target_pairs={{1,0},{2,1},{3,2},{5,4},{6,5},{7,6},{9,8},{10,9},{11,10},{13,12},{... | collective-permute-start | bytes 6728 | tf_op jit(solution)/shard_map/ppermute | solution.py:38
  27.1 3.0 %collective-permute-start.2 = (bf16[80,14]{1,0:T(8,128)(2,1)S(1)}, bf16[80,14]{1,0:T(8,128)(2,1)S(1)}, u32[]{:S(2)}, u32[]{:S(2)}) collective-permute-start(bf16[80,14]{1,0:T(8,128)(2,1)S(1)} %copy.38), channel_id=1, source_target_pairs={{0,1},{1,2},{2,3},{4,5},{5,6},{6,7},{8,9},{9,10},{10,11},{12,13},{... | collective-permute-start | bytes 6728 | tf_op jit(solution)/shard_map/ppermute | solution.py:37
  31.7 3.2 %shard_map.113 = (f32[80,2048]{1,0:T(8,128)}, bf16[80,256]{1,0:T(8,128)(2,1)}, bf16[80,256]{1,0:T(8,128)(2,1)}, bf16[80,8]{1,0:T(8,128)(2,1)}, bf16[80,8]{1,0:T(8,128)(2,1)}) custom-call(bf16[80,2048]{1,0:T(8,128)(2,1)} %bitcast.56, bf16[80,640]{1,0:T(8,128)(2,1)} %copy-done.6, bf16[80,640]{1,0:T(8,128)(2,1)} %copy-done.7, bf16[80,14]{1,0:T(8,128)(2,1)} %copy-done.9, ...), custom_call_target="tpu_custom_call" | custom-call | flops 171048960 | bytes 1399104 | tf_op jit(solution)/shard_map/pallas_call | solution.py:153
  34.9 1.2 %reduce-precision_convert_fusion.1 = (bf16[80,2048]{1,0:T(8,128)(2,1)S(1)}, bf16[80,2048]{1,0:T(8,128)(2,1)S(1)}, bf16[80,2048]{1,0:T(8,128)(2,1)S(1)}) fusion(f32[80,2048]{1,0:T(8,128)} %get-tuple-element.14), kind=kLoop, calls=%fused_computation.15 | loop fusion | flops 1146880 | bytes 1638400 | tf_op jit(solution)/shard_map/convert_element_type | solution.py:220
  36.2 1.8 %fusion = f32[240,1024]{1,0:T(8,128)S(1)} fusion(s32[1024]{0:T(1024)S(1)} %pad_add_fusion, bf16[80,2048]{1,0:T(8,128)(2,1)S(1)} %get-tuple-element.36, bf16[80,2048]{1,0:T(8,128)(2,1)S(1)} %get-tuple-element.37, bf16[80,2048]{1,0:T(8,128)(2,1)S(1)} %get-tuple-element.35), kind=kOutput, calls=%fused_computation.3 | convolution fusion | flops 1011679232 | bytes 1970176 | tf_op jit(solution)/shard_map/dot_general | solution.py:231
  38.1 3.0 %collective-permute-start.9 = (f32[80,256]{1,0:T(8,128)S(1)}, f32[80,256]{1,0:T(8,128)S(1)}, u32[]{:S(2)}, u32[]{:S(2)}) collective-permute-start(f32[80,256]{1,0:T(8,128)S(1)} %get-tuple-element.49), channel_id=1, source_target_pairs={{0,12},{4,0},{8,4},{12,8},{1,13},{5,1},{9,5},{13,9},{2,14},{6,2},{... | collective-permute-start | bytes 245768 | tf_op jit(solution)/shard_map/ppermute | solution.py:272
  41.1 1.1 %collective-permute-start.8 = (f32[80,256]{1,0:T(8,128)S(1)}, f32[80,256]{1,0:T(8,128)S(1)}, u32[]{:S(2)}, u32[]{:S(2)}) collective-permute-start(f32[80,256]{1,0:T(8,128)S(1)} %get-tuple-element.50), channel_id=1, source_target_pairs={{0,8},{4,12},{8,0},{12,4},{1,9},{5,13},{9,1},{13,5},{2,10},{6,14},... | collective-permute-start | bytes 245768 | tf_op jit(solution)/shard_map/ppermute | solution.py:272
  42.2 1.5 %collective-permute-done.9 = f32[80,256]{1,0:T(8,128)S(1)} collective-permute-done((f32[80,256]{1,0:T(8,128)S(1)}, f32[80,256]{1,0:T(8,128)S(1)}, u32[]{:S(2)}, u32[]{:S(2)}) %collective-permute-start.9) | collective-permute-done | bytes 81952 | tf_op jit(solution)/shard_map/ppermute | solution.py:272
  43.8 6.8 %collective-permute-done.8 = f32[80,256]{1,0:T(8,128)S(1)} collective-permute-done((f32[80,256]{1,0:T(8,128)S(1)}, f32[80,256]{1,0:T(8,128)S(1)}, u32[]{:S(2)}, u32[]{:S(2)}) %collective-permute-start.8) | collective-permute-done | bytes 81952 | tf_op jit(solution)/shard_map/ppermute | solution.py:272
  52.1 3.7 %shard_map.114 = (f32[80,2304]{1,0:T(8,128)}, bf16[80,384]{1,0:T(8,128)(2,1)}, bf16[80,384]{1,0:T(8,128)(2,1)}, bf16[80,6]{1,0:T(8,128)(2,1)}, bf16[80,6]{1,0:T(8,128)(2,1)}) custom-call(bf16[80,2304]{1,0:T(8,128)(2,1)} %bitcast.53, bf16[80,640]{1,0:T(8,128)(2,1)} %copy-done.6, bf16[80,640]{1,0:T(8,128)(2,1)} %copy-done.7, bf16[80,14]{1,0:T(8,128)(2,1)} %copy-done.9, ...), custom_call_target="tpu_custom_call" | custom-call | flops 192430080 | bytes 2281792 | tf_op jit(solution)/shard_map/pallas_call | solution.py:153
  55.8 1.6 %collective-permute-start.10 = (bf16[80,384]{1,0:T(8,128)(2,1)}, bf16[80,384]{1,0:T(8,128)(2,1)S(1)}, u32[]{:S(2)}, u32[]{:S(2)}) collective-permute-start(bf16[80,384]{1,0:T(8,128)(2,1)} %get-tuple-element.16), channel_id=1, source_target_pairs={{0,4},{4,8},{8,12},{1,5},{5,9},{9,13},{2,6},{6,10},{10,14},{3,7},{... | collective-permute-start | bytes 184328 | tf_op jit(solution)/shard_map/ppermute | solution.py:35
  57.4 1.3 %collective-permute-start.11 = (bf16[80,384]{1,0:T(8,128)(2,1)}, bf16[80,384]{1,0:T(8,128)(2,1)S(1)}, u32[]{:S(2)}, u32[]{:S(2)}) collective-permute-start(bf16[80,384]{1,0:T(8,128)(2,1)} %get-tuple-element.17), channel_id=1, source_target_pairs={{4,0},{8,4},{12,8},{5,1},{9,5},{13,9},{6,2},{10,6},{14,10},{7,3},{... | collective-permute-start | bytes 184328 | tf_op jit(solution)/shard_map/ppermute | solution.py:36
  58.7 1.7 %collective-permute-start.12 = (bf16[80,6]{1,0:T(8,128)(2,1)}, bf16[80,6]{1,0:T(8,128)(2,1)S(1)}, u32[]{:S(2)}, u32[]{:S(2)}) collective-permute-start(bf16[80,6]{1,0:T(8,128)(2,1)} %get-tuple-element.18), channel_id=1, source_target_pairs={{0,1},{1,2},{2,3},{4,5},{5,6},{6,7},{8,9},{9,10},{10,11},{12,13},{... | collective-permute-start | bytes 2888 | tf_op jit(solution)/shard_map/ppermute | solution.py:37
  60.4 1.3 %collective-permute-start.13 = (bf16[80,6]{1,0:T(8,128)(2,1)}, bf16[80,6]{1,0:T(8,128)(2,1)S(1)}, u32[]{:S(2)}, u32[]{:S(2)}) collective-permute-start(bf16[80,6]{1,0:T(8,128)(2,1)} %get-tuple-element.19), channel_id=1, source_target_pairs={{1,0},{2,1},{3,2},{5,4},{6,5},{7,6},{9,8},{10,9},{11,10},{13,12},{... | collective-permute-start | bytes 2888 | tf_op jit(solution)/shard_map/ppermute | solution.py:38
  61.8 2.7 %collective-permute-done.13.refs_4_ = bf16[80,6]{1,0:T(8,128)(2,1)S(1)} collective-permute-done((bf16[80,6]{1,0:T(8,128)(2,1)}, bf16[80,6]{1,0:T(8,128)(2,1)S(1)}, u32[]{:S(2)}, u32[]{:S(2)}) %collective-permute-start.13) | collective-permute-done | bytes 992 | tf_op jit(solution)/shard_map/ppermute | solution.py:38
  65.1 3.7 %shard_map.115 = (f32[80,2304]{1,0:T(8,128)}, bf16[80,384]{1,0:T(8,128)(2,1)}, bf16[80,384]{1,0:T(8,128)(2,1)}, bf16[80,6]{1,0:T(8,128)(2,1)}, bf16[80,6]{1,0:T(8,128)(2,1)}) custom-call(f32[80,2304]{1,0:T(8,128)} %get-tuple-element.15.refs_0_, bf16[80,384]{1,0:T(8,128)(2,1)} %copy-done.12, bf16[80,384]{1,0:T(8,128)(2,1)} %copy-done.13, ...), custom_call_target="tpu_custom_call" | custom-call | flops 192430080 | bytes 2492224 | tf_op jit(solution)/shard_map/pallas_call | solution.py:153
  68.9 4.7 %collective-permute-start.14 = (bf16[80,384]{1,0:T(8,128)(2,1)}, bf16[80,384]{1,0:T(8,128)(2,1)S(1)}, u32[]{:S(2)}, u32[]{:S(2)}) collective-permute-start(bf16[80,384]{1,0:T(8,128)(2,1)} %get-tuple-element.21), channel_id=1, source_target_pairs={{0,4},{4,8},{8,12},{1,5},{5,9},{9,13},{2,6},{6,10},{10,14},{3,7},{... | collective-permute-start | bytes 184328 | tf_op jit(solution)/shard_map/ppermute | solution.py:35
  73.6 1.3 %collective-permute-start.15 = (bf16[80,384]{1,0:T(8,128)(2,1)}, bf16[80,384]{1,0:T(8,128)(2,1)S(1)}, u32[]{:S(2)}, u32[]{:S(2)}) collective-permute-start(bf16[80,384]{1,0:T(8,128)(2,1)} %get-tuple-element.22), channel_id=1, source_target_pairs={{4,0},{8,4},{12,8},{5,1},{9,5},{13,9},{6,2},{10,6},{14,10},{7,3},{... | collective-permute-start | bytes 184328 | tf_op jit(solution)/shard_map/ppermute | solution.py:36
  74.9 4.1 %collective-permute-start.16 = (bf16[80,6]{1,0:T(8,128)(2,1)}, bf16[80,6]{1,0:T(8,128)(2,1)S(1)}, u32[]{:S(2)}, u32[]{:S(2)}) collective-permute-start(bf16[80,6]{1,0:T(8,128)(2,1)} %get-tuple-element.23), channel_id=1, source_target_pairs={{0,1},{1,2},{2,3},{4,5},{5,6},{6,7},{8,9},{9,10},{10,11},{12,13},{... | collective-permute-start | bytes 2888 | tf_op jit(solution)/shard_map/ppermute | solution.py:37
  79.0 1.3 %collective-permute-start.17 = (bf16[80,6]{1,0:T(8,128)(2,1)}, bf16[80,6]{1,0:T(8,128)(2,1)S(1)}, u32[]{:S(2)}, u32[]{:S(2)}) collective-permute-start(bf16[80,6]{1,0:T(8,128)(2,1)} %get-tuple-element.24), channel_id=1, source_target_pairs={{1,0},{2,1},{3,2},{5,4},{6,5},{7,6},{9,8},{10,9},{11,10},{13,12},{... | collective-permute-start | bytes 2888 | tf_op jit(solution)/shard_map/ppermute | solution.py:38
  80.4 2.0 %collective-permute-done.17.refs_4_ = bf16[80,6]{1,0:T(8,128)(2,1)S(1)} collective-permute-done((bf16[80,6]{1,0:T(8,128)(2,1)}, bf16[80,6]{1,0:T(8,128)(2,1)S(1)}, u32[]{:S(2)}, u32[]{:S(2)}) %collective-permute-start.17) | collective-permute-done | bytes 992 | tf_op jit(solution)/shard_map/ppermute | solution.py:38
  83.0 3.7 %shard_map.116 = (f32[80,2304]{1,0:T(8,128)}, bf16[80,384]{1,0:T(8,128)(2,1)}, bf16[80,384]{1,0:T(8,128)(2,1)}, bf16[80,6]{1,0:T(8,128)(2,1)}, bf16[80,6]{1,0:T(8,128)(2,1)}) custom-call(f32[80,2304]{1,0:T(8,128)} %get-tuple-element.20.refs_0_, bf16[80,384]{1,0:T(8,128)(2,1)} %copy-done.10, bf16[80,384]{1,0:T(8,128)(2,1)} %copy-done.11, ...), custom_call_target="tpu_custom_call" | custom-call | flops 192430080 | bytes 2492224 | tf_op jit(solution)/shard_map/pallas_call | solution.py:153
  86.7 1.4 %fusion.20 = f32[80,128]{1,0:T(8,128)S(1)} fusion(f32[80,2304]{1,0:T(8,128)} %get-tuple-element.25, s32[128]{0:T(128)S(1)} %iota_add_fusion, s32[384]{0:T(512)S(1)} %get-tuple-element.84, s32[384]{0:T(512)S(1)} %get-tuple-element.85, pred[384]{0:T(512)(128)(4,1)S(1)} %fusion.72), kind=kOutput, calls=%fused_computation.38 | convolution fusion | flops 47345664 | bytes 413568 | tf_op jit(solution)/shard_map/dot_general | solution.py:207
  88.2 1.4 %fusion.19 = f32[80,128]{1,0:T(8,128)S(1)} fusion(f32[80,2304]{1,0:T(8,128)} %get-tuple-element.25, s32[128]{0:T(128)S(1)} %iota_add_fusion, s32[384]{0:T(512)S(1)} %get-tuple-element.84, s32[384]{0:T(512)S(1)} %get-tuple-element.85, pred[384]{0:T(512)(128)(4,1)S(1)} %fusion.72), kind=kOutput, calls=%fused_computation.37 | convolution fusion | flops 47345664 | bytes 413568 | tf_op jit(solution)/shard_map/dot_general | solution.py:207
  89.6 4.0 %collective-permute-start.20 = (f32[80,256]{1,0:T(8,128)S(1)}, f32[80,256]{1,0:T(8,128)S(1)}, u32[]{:S(2)}, u32[]{:S(2)}) collective-permute-start(f32[80,256]{1,0:T(8,128)S(1)} %get-tuple-element.46), channel_id=1, source_target_pairs={{0,12},{4,0},{8,4},{12,8},{1,13},{5,1},{9,5},{13,9},{2,14},{6,2},{... | collective-permute-start | bytes 245768 | tf_op jit(solution)/shard_map/ppermute | solution.py:316
  93.8 1.8 %collective-permute-start.18 = (f32[80,256]{1,0:T(8,128)S(1)}, f32[80,256]{1,0:T(8,128)S(1)}, u32[]{:S(2)}, u32[]{:S(2)}) collective-permute-start(f32[80,256]{1,0:T(8,128)S(1)} %get-tuple-element.48), channel_id=1, source_target_pairs={{0,4},{4,8},{8,12},{12,0},{1,5},{5,9},{9,13},{13,1},{2,6},{6,10},{... | collective-permute-start | bytes 245768 | tf_op jit(solution)/shard_map/ppermute | solution.py:316
  96.4 6.1 %collective-permute-done.19 = f32[80,256]{1,0:T(8,128)S(1)} collective-permute-done((f32[80,256]{1,0:T(8,128)S(1)}, f32[80,256]{1,0:T(8,128)S(1)}, u32[]{:S(2)}, u32[]{:S(2)}) %collective-permute-start.19) | collective-permute-done | bytes 81952 | tf_op jit(solution)/shard_map/ppermute | solution.py:316
  102.6 1.9 %fusion.1 = f32[240,2048]{1,0:T(8,128)S(1)} fusion(s32[1024]{0:T(1024)S(1)} %pad_add_fusion, bf16[80,1024]{1,0:T(8,128)(2,1)S(1)} %get-tuple-element.44, bf16[80,1024]{1,0:T(8,128)(2,1)S(1)} %get-tuple-element.43, bf16[80,1024]{1,0:T(8,128)(2,1)S(1)} %get-tuple-element.42), kind=kOutput, calls=%fused_computation.4 | convolution fusion | flops 1010204672 | bytes 2461696 | tf_op jit(solution)/shard_map/dot_general | solution.py:239
  (129 shorter events, 19.3 us)
Async XLA Ops:
  0.6 17.0 %copy-start = (s32[24]{0:T(128)S(1)}, s32[24]{0:T(128)}, u32[]{:S(2)}) copy-start(s32[24]{0:T(128)} %param.19) | copy-start | bytes 292
  0.6 16.8 %copy-start.3 = (bf16[80,8,256]{2,1,0:T(8,128)(2,1)S(1)}, bf16[80,8,256]{2,1,0:T(8,128)(2,1)}, u32[]{:S(2)}) copy-start(bf16[80,8,256]{2,1,0:T(8,128)(2,1)} %param.10) | copy-start | bytes 983044
  0.7 18.4 %copy-start.19 = (f32[80]{0:T(128)S(1)}, f32[80]{0:T(128)}, u32[]{:S(2)}) copy-start(f32[80]{0:T(128)} %param.14) | copy-start | bytes 964
  0.7 18.4 %copy-start.20 = (f32[80]{0:T(128)S(1)}, f32[80]{0:T(128)}, u32[]{:S(2)}) copy-start(f32[80]{0:T(128)} %param.13) | copy-start | bytes 964
  0.7 18.4 %copy-start.21 = (f32[80]{0:T(128)S(1)}, f32[80]{0:T(128)}, u32[]{:S(2)}) copy-start(f32[80]{0:T(128)} %param.12) | copy-start | bytes 964
  2.1 23.7 %collective-permute-start.6 = (s32[256]{0:T(256)S(1)}, s32[256]{0:T(256)S(1)}, u32[]{:S(2)}, u32[]{:S(2)}) collective-permute-start(s32[256]{0:T(256)S(1)} %bitcast.76), channel_id=1, source_target_pairs={{0,12},{4,0},{8,4},{12,8},{1,13},{5,1},{9,5},{13,9},{2,14},{6,2},{... | collective-permute-start | bytes 3080 | tf_op jit(solution)/shard_map/ppermute | solution.py:267
  7.2 19.9 %collective-permute-start.5 = (s32[256]{0:T(256)S(1)}, s32[256]{0:T(256)S(1)}, u32[]{:S(2)}, u32[]{:S(2)}) collective-permute-start(s32[256]{0:T(256)S(1)} %bitcast.75), channel_id=1, source_target_pairs={{0,8},{4,12},{8,0},{12,4},{1,9},{5,13},{9,1},{13,5},{2,10},{6,14},... | collective-permute-start | bytes 3080 | tf_op jit(solution)/shard_map/ppermute | solution.py:267
  7.2 22.9 %collective-permute-start.4 = (s32[256]{0:T(256)S(1)}, s32[256]{0:T(256)S(1)}, u32[]{:S(2)}, u32[]{:S(2)}) collective-permute-start(s32[256]{0:T(256)S(1)} %bitcast.74), channel_id=1, source_target_pairs={{0,4},{4,8},{8,12},{12,0},{1,5},{5,9},{9,13},{13,1},{2,6},{6,10},{... | collective-permute-start | bytes 3080 | tf_op jit(solution)/shard_map/ppermute | solution.py:267
  10.4 20.6 %collective-permute-start = (bf16[80,640]{1,0:T(8,128)(2,1)S(1)}, bf16[80,640]{1,0:T(8,128)(2,1)S(1)}, u32[]{:S(2)}, u32[]{:S(2)}) collective-permute-start(bf16[80,640]{1,0:T(8,128)(2,1)S(1)} %pad_maximum_fusion.1), channel_id=1, source_target_pairs={{0,4},{4,8},{8,12},{1,5},{5,9},{9,13},{2,6},{6,10},{10,14},{3,7},{... | collective-permute-start | bytes 307208 | tf_op jit(solution)/shard_map/ppermute | solution.py:35
  14.8 10.3 %copy-start.4 = (bf16[80,6,384]{2,0,1:T(8,128)(2,1)S(1)}, bf16[80,6,384]{2,0,1:T(8,128)(2,1)}, u32[]{:S(2)}) copy-start(bf16[80,6,384]{2,0,1:T(8,128)(2,1)} %param.11) | copy-start | bytes 1105924
  14.8 16.2 %collective-permute-start.1 = (bf16[80,640]{1,0:T(8,128)(2,1)S(1)}, bf16[80,640]{1,0:T(8,128)(2,1)S(1)}, u32[]{:S(2)}, u32[]{:S(2)}) collective-permute-start(bf16[80,640]{1,0:T(8,128)(2,1)S(1)} %pad_maximum_fusion.2), channel_id=1, source_target_pairs={{4,0},{8,4},{12,8},{5,1},{9,5},{13,9},{6,2},{10,6},{14,10},{7,3},{... | collective-permute-start | bytes 307208 | tf_op jit(solution)/shard_map/ppermute | solution.py:36
  25.8 4.4 %collective-permute-start.3 = (bf16[80,14]{1,0:T(8,128)(2,1)S(1)}, bf16[80,14]{1,0:T(8,128)(2,1)S(1)}, u32[]{:S(2)}, u32[]{:S(2)}) collective-permute-start(bf16[80,14]{1,0:T(8,128)(2,1)S(1)} %copy.41), channel_id=1, source_target_pairs={{1,0},{2,1},{3,2},{5,4},{6,5},{7,6},{9,8},{10,9},{11,10},{13,12},{... | collective-permute-start | bytes 6728 | tf_op jit(solution)/shard_map/ppermute | solution.py:38
  27.1 3.9 %collective-permute-start.2 = (bf16[80,14]{1,0:T(8,128)(2,1)S(1)}, bf16[80,14]{1,0:T(8,128)(2,1)S(1)}, u32[]{:S(2)}, u32[]{:S(2)}) collective-permute-start(bf16[80,14]{1,0:T(8,128)(2,1)S(1)} %copy.38), channel_id=1, source_target_pairs={{0,1},{1,2},{2,3},{4,5},{5,6},{6,7},{8,9},{9,10},{10,11},{12,13},{... | collective-permute-start | bytes 6728 | tf_op jit(solution)/shard_map/ppermute | solution.py:37
  38.1 5.7 %collective-permute-start.9 = (f32[80,256]{1,0:T(8,128)S(1)}, f32[80,256]{1,0:T(8,128)S(1)}, u32[]{:S(2)}, u32[]{:S(2)}) collective-permute-start(f32[80,256]{1,0:T(8,128)S(1)} %get-tuple-element.49), channel_id=1, source_target_pairs={{0,12},{4,0},{8,4},{12,8},{1,13},{5,1},{9,5},{13,9},{2,14},{6,2},{... | collective-permute-start | bytes 245768 | tf_op jit(solution)/shard_map/ppermute | solution.py:272
  41.1 9.5 %collective-permute-start.8 = (f32[80,256]{1,0:T(8,128)S(1)}, f32[80,256]{1,0:T(8,128)S(1)}, u32[]{:S(2)}, u32[]{:S(2)}) collective-permute-start(f32[80,256]{1,0:T(8,128)S(1)} %get-tuple-element.50), channel_id=1, source_target_pairs={{0,8},{4,12},{8,0},{12,4},{1,9},{5,13},{9,1},{13,5},{2,10},{6,14},... | collective-permute-start | bytes 245768 | tf_op jit(solution)/shard_map/ppermute | solution.py:272
  42.2 8.4 %collective-permute-start.7 = (f32[80,256]{1,0:T(8,128)S(1)}, f32[80,256]{1,0:T(8,128)S(1)}, u32[]{:S(2)}, u32[]{:S(2)}) collective-permute-start(f32[80,256]{1,0:T(8,128)S(1)} %get-tuple-element.51), channel_id=1, source_target_pairs={{0,4},{4,8},{8,12},{12,0},{1,5},{5,9},{9,13},{13,1},{2,6},{6,10},{... | collective-permute-start | bytes 245768 | tf_op jit(solution)/shard_map/ppermute | solution.py:272
  55.8 8.7 %collective-permute-start.10 = (bf16[80,384]{1,0:T(8,128)(2,1)}, bf16[80,384]{1,0:T(8,128)(2,1)S(1)}, u32[]{:S(2)}, u32[]{:S(2)}) collective-permute-start(bf16[80,384]{1,0:T(8,128)(2,1)} %get-tuple-element.16), channel_id=1, source_target_pairs={{0,4},{4,8},{8,12},{1,5},{5,9},{9,13},{2,6},{6,10},{10,14},{3,7},{... | collective-permute-start | bytes 184328 | tf_op jit(solution)/shard_map/ppermute | solution.py:35
  57.4 7.1 %collective-permute-start.11 = (bf16[80,384]{1,0:T(8,128)(2,1)}, bf16[80,384]{1,0:T(8,128)(2,1)S(1)}, u32[]{:S(2)}, u32[]{:S(2)}) collective-permute-start(bf16[80,384]{1,0:T(8,128)(2,1)} %get-tuple-element.17), channel_id=1, source_target_pairs={{4,0},{8,4},{12,8},{5,1},{9,5},{13,9},{6,2},{10,6},{14,10},{7,3},{... | collective-permute-start | bytes 184328 | tf_op jit(solution)/shard_map/ppermute | solution.py:36
  58.7 3.0 %collective-permute-start.12 = (bf16[80,6]{1,0:T(8,128)(2,1)}, bf16[80,6]{1,0:T(8,128)(2,1)S(1)}, u32[]{:S(2)}, u32[]{:S(2)}) collective-permute-start(bf16[80,6]{1,0:T(8,128)(2,1)} %get-tuple-element.18), channel_id=1, source_target_pairs={{0,1},{1,2},{2,3},{4,5},{5,6},{6,7},{8,9},{9,10},{10,11},{12,13},{... | collective-permute-start | bytes 2888 | tf_op jit(solution)/shard_map/ppermute | solution.py:37
  60.4 4.0 %collective-permute-start.13 = (bf16[80,6]{1,0:T(8,128)(2,1)}, bf16[80,6]{1,0:T(8,128)(2,1)S(1)}, u32[]{:S(2)}, u32[]{:S(2)}) collective-permute-start(bf16[80,6]{1,0:T(8,128)(2,1)} %get-tuple-element.19), channel_id=1, source_target_pairs={{1,0},{2,1},{3,2},{5,4},{6,5},{7,6},{9,8},{10,9},{11,10},{13,12},{... | collective-permute-start | bytes 2888 | tf_op jit(solution)/shard_map/ppermute | solution.py:38
  61.8 2.8 %copy-start.16 = (bf16[80,6]{1,0:T(8,128)(2,1)}, bf16[80,6]{1,0:T(8,128)(2,1)S(1)}, u32[]{:S(2)}) copy-start(bf16[80,6]{1,0:T(8,128)(2,1)S(1)} %collective-permute-done.12.refs_3_) | copy-start | bytes 2884
  68.9 13.5 %collective-permute-start.14 = (bf16[80,384]{1,0:T(8,128)(2,1)}, bf16[80,384]{1,0:T(8,128)(2,1)S(1)}, u32[]{:S(2)}, u32[]{:S(2)}) collective-permute-start(bf16[80,384]{1,0:T(8,128)(2,1)} %get-tuple-element.21), channel_id=1, source_target_pairs={{0,4},{4,8},{8,12},{1,5},{5,9},{9,13},{2,6},{6,10},{10,14},{3,7},{... | collective-permute-start | bytes 184328 | tf_op jit(solution)/shard_map/ppermute | solution.py:35
  73.6 8.8 %collective-permute-start.15 = (bf16[80,384]{1,0:T(8,128)(2,1)}, bf16[80,384]{1,0:T(8,128)(2,1)S(1)}, u32[]{:S(2)}, u32[]{:S(2)}) collective-permute-start(bf16[80,384]{1,0:T(8,128)(2,1)} %get-tuple-element.22), channel_id=1, source_target_pairs={{4,0},{8,4},{12,8},{5,1},{9,5},{13,9},{6,2},{10,6},{14,10},{7,3},{... | collective-permute-start | bytes 184328 | tf_op jit(solution)/shard_map/ppermute | solution.py:36
  74.9 5.5 %collective-permute-start.16 = (bf16[80,6]{1,0:T(8,128)(2,1)}, bf16[80,6]{1,0:T(8,128)(2,1)S(1)}, u32[]{:S(2)}, u32[]{:S(2)}) collective-permute-start(bf16[80,6]{1,0:T(8,128)(2,1)} %get-tuple-element.23), channel_id=1, source_target_pairs={{0,1},{1,2},{2,3},{4,5},{5,6},{6,7},{8,9},{9,10},{10,11},{12,13},{... | collective-permute-start | bytes 2888 | tf_op jit(solution)/shard_map/ppermute | solution.py:37
  79.0 3.3 %collective-permute-start.17 = (bf16[80,6]{1,0:T(8,128)(2,1)}, bf16[80,6]{1,0:T(8,128)(2,1)S(1)}, u32[]{:S(2)}, u32[]{:S(2)}) collective-permute-start(bf16[80,6]{1,0:T(8,128)(2,1)} %get-tuple-element.24), channel_id=1, source_target_pairs={{1,0},{2,1},{3,2},{5,4},{6,5},{7,6},{9,8},{10,9},{11,10},{13,12},{... | collective-permute-start | bytes 2888 | tf_op jit(solution)/shard_map/ppermute | solution.py:38
  80.4 2.0 %copy-start.14 = (bf16[80,6]{1,0:T(8,128)(2,1)}, bf16[80,6]{1,0:T(8,128)(2,1)S(1)}, u32[]{:S(2)}) copy-start(bf16[80,6]{1,0:T(8,128)(2,1)S(1)} %collective-permute-done.16.refs_3_) | copy-start | bytes 2884
  86.7 8.9 %copy-start.5 = (f32[80,2304]{1,0:T(8,128)S(1)}, f32[80,2304]{1,0:T(8,128)}, u32[]{:S(2)}) copy-start(f32[80,2304]{1,0:T(8,128)} %get-tuple-element.25) | copy-start | bytes 2211844
  89.6 6.8 %collective-permute-start.20 = (f32[80,256]{1,0:T(8,128)S(1)}, f32[80,256]{1,0:T(8,128)S(1)}, u32[]{:S(2)}, u32[]{:S(2)}) collective-permute-start(f32[80,256]{1,0:T(8,128)S(1)} %get-tuple-element.46), channel_id=1, source_target_pairs={{0,12},{4,0},{8,4},{12,8},{1,13},{5,1},{9,5},{13,9},{2,14},{6,2},{... | collective-permute-start | bytes 245768 | tf_op jit(solution)/shard_map/ppermute | solution.py:316
  93.6 8.9 %collective-permute-start.19 = (f32[80,256]{1,0:T(8,128)S(1)}, f32[80,256]{1,0:T(8,128)S(1)}, u32[]{:S(2)}, u32[]{:S(2)}) collective-permute-start(f32[80,256]{1,0:T(8,128)S(1)} %get-tuple-element.47), channel_id=1, source_target_pairs={{0,8},{4,12},{8,0},{12,4},{1,9},{5,13},{9,1},{13,5},{2,10},{6,14},... | collective-permute-start | bytes 245768 | tf_op jit(solution)/shard_map/ppermute | solution.py:316
  93.8 8.8 %collective-permute-start.18 = (f32[80,256]{1,0:T(8,128)S(1)}, f32[80,256]{1,0:T(8,128)S(1)}, u32[]{:S(2)}, u32[]{:S(2)}) collective-permute-start(f32[80,256]{1,0:T(8,128)S(1)} %get-tuple-element.48), channel_id=1, source_target_pairs={{0,4},{4,8},{8,12},{12,0},{1,5},{5,9},{9,13},{13,1},{2,6},{6,10},{... | collective-permute-start | bytes 245768 | tf_op jit(solution)/shard_map/ppermute | solution.py:316
  102.6 1.9 %copy-start.2 = (f32[80,2048]{1,0:T(8,128)S(1)}, f32[80,2048]{1,0:T(8,128)}, u32[]{:S(2)}) copy-start(f32[80,2048]{1,0:T(8,128)} %get-tuple-element.14) | copy-start | bytes 1966084
  102.6 1.9 %copy-start.18 = (f32[80]{0:T(128)S(1)}, f32[80]{0:T(128)}, u32[]{:S(2)}) copy-start(f32[80]{0:T(128)} %param.15) | copy-start | bytes 964
  (11 other events, 7.4 us)

commit v9 on v7

--- a/solution.py
+++ b/solution.py
@@ -105,7 +105,7 @@
     moved = state + nu_ref[...] * stencil
     if nest:
         moved = moved + relax_ref[...] * (forcing_ref[...] - moved)
-    new = jnp.dot(vm_ref[...], moved, precision=HI, preferred_element_type=jnp.float32)
+    new = jnp.dot(vm_ref[...], moved, precision=lax.Precision.HIGH, preferred_element_type=jnp.float32)
     new_ref[...] = new
     lrow_ref[...] = new[:, n - cols : n].astype(jnp.bfloat16)
     frow_ref[...] = new[:, 0:cols].astype(jnp.bfloat16)

time: 103 us -> 102 us (level)
  no operation moved by 1% of the time
where the time goes in v9:
time: 102 us
  starting transfers between devices  43.6 us (43%)
  local copies, waits for them, and re-layouts  18.1 us (18%)
  waiting for transfers between devices  16.2 us (16%)
  Pallas kernels  12.3 us (12%)
  matrix products  7.02 us (7%)
  other arithmetic  3.25 us (3%)
  between operations  1.21 us (1%)
    pallas_call x4, Pallas kernels, stencil_step(): pl.pallas_call(functools.partial(step_kernel, rows=rows, cols=cols, nest=...  12.3 us
    ppermute x3, starting transfers between devices, exchange(): above = lax.ppermute(last_rows, 'gx', fwd_x)  10.6 us
    ppermute x3, starting transfers between devices, exchange(): left = lax.ppermute(last_cols, Y_AXES, fwd_y)  9.01 us
    unnamed x58, local copies, waits for them, and re-layouts  6.31 us
    ppermute x3, starting transfers between devices, body(): lax.ppermute(wanted[s], 'gx', shifted_pairs(tiles_x, s))  6.14 us
    ppermute x3, waiting for transfers between devices, body(): lax.ppermute(outgoing[s], 'gx', shifted_pairs(tiles_x, s))  6.11 us
    ppermute x3, starting transfers between devices, body(): lax.ppermute(outgoing[s], 'gx', shifted_pairs(tiles_x, s))  5.98 us
    ppermute x3, waiting for transfers between devices, body(): lax.ppermute(replies[:, s * requests:(s + 1) * requests], 'gx', shifted_p...  5.77 us
  transfers between devices with their start and end apart: 21, of which 5 were waited for; matrix products, arithmetic and copies ran while one was open for 14% of the time, Pallas kernels for 0%

profile of v9, /device:TPU:0, one launch (start us, length us, event | category | flops | bytes accessed | tf_op | source)
XLA Modules:
  0.0 101.7 jit_solution(8215610405850198491)
XLA Ops:
  2.1 5.1 %collective-permute-start.6 = (s32[256]{0:T(256)S(1)}, s32[256]{0:T(256)S(1)}, u32[]{:S(2)}, u32[]{:S(2)}) collective-permute-start(s32[256]{0:T(256)S(1)} %bitcast.80), channel_id=1, source_target_pairs={{0,12},{4,0},{8,4},{12,8},{1,13},{5,1},{9,5},{13,9},{2,14},{6,2},{... | collective-permute-start | bytes 3080 | tf_op jit(solution)/shard_map/ppermute | solution.py:250
  9.1 1.2 %fusion.64 = (bf16[80,1,256]{2,1,0:T(2,128)(2,1)S(1)}, bf16[80,1,256]{2,1,0:T(2,128)(2,1)S(1)}) fusion(bf16[80,8,256]{2,1,0:T(8,128)(2,1)} %param.10), kind=kLoop, calls=%fused_computation.125 | loop fusion | bytes 163840 | tf_op jit(solution)/shard_map/slice | solution.py:21
  10.4 4.5 %collective-permute-start = (bf16[80,640]{1,0:T(8,128)(2,1)S(1)}, bf16[80,640]{1,0:T(8,128)(2,1)S(1)}, u32[]{:S(2)}, u32[]{:S(2)}) collective-permute-start(bf16[80,640]{1,0:T(8,128)(2,1)S(1)} %pad_maximum_fusion.1), channel_id=1, source_target_pairs={{0,4},{4,8},{8,12},{1,5},{5,9},{9,13},{2,6},{6,10},{10,14},{3,7},{... | collective-permute-start | bytes 307208 | tf_op jit(solution)/shard_map/ppermute | solution.py:35
  15.0 1.3 %collective-permute-start.1 = (bf16[80,640]{1,0:T(8,128)(2,1)S(1)}, bf16[80,640]{1,0:T(8,128)(2,1)S(1)}, u32[]{:S(2)}, u32[]{:S(2)}) collective-permute-start(bf16[80,640]{1,0:T(8,128)(2,1)S(1)} %pad_maximum_fusion.2), channel_id=1, source_target_pairs={{4,0},{8,4},{12,8},{5,1},{9,5},{13,9},{6,2},{10,6},{14,10},{7,3},{... | collective-permute-start | bytes 307208 | tf_op jit(solution)/shard_map/ppermute | solution.py:36
  16.3 1.1 %fusion.61 = (bf16[80,6,1]{2,0,1:T(8,128)(2,1)S(1)}, bf16[80,6,1]{2,0,1:T(8,128)(2,1)S(1)}) fusion(bf16[80,6,384]{2,0,1:T(8,128)(2,1)} %param.11), kind=kLoop, calls=%fused_computation.122 | loop fusion | bytes 3840 | tf_op jit(solution)/shard_map/slice | solution.py:21
  24.2 1.3 %collective-permute-start.3 = (bf16[80,14]{1,0:T(8,128)(2,1)S(1)}, bf16[80,14]{1,0:T(8,128)(2,1)S(1)}, u32[]{:S(2)}, u32[]{:S(2)}) collective-permute-start(bf16[80,14]{1,0:T(8,128)(2,1)S(1)} %copy.49), channel_id=1, source_target_pairs={{1,0},{2,1},{3,2},{5,4},{6,5},{7,6},{9,8},{10,9},{11,10},{13,12},{... | collective-permute-start | bytes 6728 | tf_op jit(solution)/shard_map/ppermute | solution.py:38
  25.5 3.0 %collective-permute-start.2 = (bf16[80,14]{1,0:T(8,128)(2,1)S(1)}, bf16[80,14]{1,0:T(8,128)(2,1)S(1)}, u32[]{:S(2)}, u32[]{:S(2)}) collective-permute-start(bf16[80,14]{1,0:T(8,128)(2,1)S(1)} %copy.46), channel_id=1, source_target_pairs={{0,1},{1,2},{2,3},{4,5},{5,6},{6,7},{8,9},{9,10},{10,11},{12,13},{... | collective-permute-start | bytes 6728 | tf_op jit(solution)/shard_map/ppermute | solution.py:37
  30.4 2.7 %shard_map.113 = (f32[80,2048]{1,0:T(8,128)}, bf16[80,256]{1,0:T(8,128)(2,1)}, bf16[80,256]{1,0:T(8,128)(2,1)}, bf16[80,8]{1,0:T(8,128)(2,1)}, bf16[80,8]{1,0:T(8,128)(2,1)}) custom-call(bf16[80,2048]{1,0:T(8,128)(2,1)} %bitcast.59, bf16[80,256]{1,0:T(8,128)(2,1)} %slice.195.refs_1_, bf16[80,256]{1,0:T(8,128)(2,1)} %slice.196.refs_2_, ...), custom_call_target="tpu_custom_call" | custom-call | flops 165806080 | bytes 1093440 | tf_op jit(solution)/shard_map/pallas_call | solution.py:140
  33.1 1.2 %reduce-precision_convert_fusion.1 = (bf16[80,2048]{1,0:T(8,128)(2,1)S(1)}, bf16[80,2048]{1,0:T(8,128)(2,1)S(1)}, bf16[80,2048]{1,0:T(8,128)(2,1)S(1)}) fusion(f32[80,2048]{1,0:T(8,128)} %get-tuple-element.14), kind=kLoop, calls=%fused_computation.15 | loop fusion | flops 1146880 | bytes 1638400 | tf_op jit(solution)/shard_map/convert_element_type | solution.py:205
  34.4 1.8 %fusion = f32[240,1024]{1,0:T(8,128)S(1)} fusion(s32[1024]{0:T(1024)S(1)} %pad_add_fusion, bf16[80,2048]{1,0:T(8,128)(2,1)S(1)} %get-tuple-element.36, bf16[80,2048]{1,0:T(8,128)(2,1)S(1)} %get-tuple-element.37, bf16[80,2048]{1,0:T(8,128)(2,1)S(1)} %get-tuple-element.35), kind=kOutput, calls=%fused_computation.3 | convolution fusion | flops 1011679232 | bytes 1970176 | tf_op jit(solution)/shard_map/dot_general | solution.py:216
  36.3 3.0 %collective-permute-start.9 = (f32[80,256]{1,0:T(8,128)S(1)}, f32[80,256]{1,0:T(8,128)S(1)}, u32[]{:S(2)}, u32[]{:S(2)}) collective-permute-start(f32[80,256]{1,0:T(8,128)S(1)} %get-tuple-element.49), channel_id=1, source_target_pairs={{0,12},{4,0},{8,4},{12,8},{1,13},{5,1},{9,5},{13,9},{2,14},{6,2},{... | collective-permute-start | bytes 245768 | tf_op jit(solution)/shard_map/ppermute | solution.py:255
  39.3 1.1 %collective-permute-start.8 = (f32[80,256]{1,0:T(8,128)S(1)}, f32[80,256]{1,0:T(8,128)S(1)}, u32[]{:S(2)}, u32[]{:S(2)}) collective-permute-start(f32[80,256]{1,0:T(8,128)S(1)} %get-tuple-element.50), channel_id=1, source_target_pairs={{0,8},{4,12},{8,0},{12,4},{1,9},{5,13},{9,1},{13,5},{2,10},{6,14},... | collective-permute-start | bytes 245768 | tf_op jit(solution)/shard_map/ppermute | solution.py:255
  43.1 5.8 %collective-permute-done.8 = f32[80,256]{1,0:T(8,128)S(1)} collective-permute-done((f32[80,256]{1,0:T(8,128)S(1)}, f32[80,256]{1,0:T(8,128)S(1)}, u32[]{:S(2)}, u32[]{:S(2)}) %collective-permute-start.8) | collective-permute-done | bytes 81952 | tf_op jit(solution)/shard_map/ppermute | solution.py:255
  50.4 3.1 %shard_map.114 = (f32[80,2304]{1,0:T(8,128)}, bf16[80,384]{1,0:T(8,128)(2,1)}, bf16[80,384]{1,0:T(8,128)(2,1)}, bf16[80,6]{1,0:T(8,128)(2,1)}, bf16[80,6]{1,0:T(8,128)(2,1)}) custom-call(bf16[80,2304]{1,0:T(8,128)(2,1)} %bitcast.55, bf16[80,384]{1,0:T(8,128)(2,1)} %slice.199.refs_1_, bf16[80,384]{1,0:T(8,128)(2,1)} %slice.200.refs_2_, ...), custom_call_target="tpu_custom_call" | custom-call | flops 185057280 | bytes 2012672 | tf_op jit(solution)/shard_map/pallas_call | solution.py:140
  53.6 1.5 %collective-permute-start.10 = (bf16[80,384]{1,0:T(8,128)(2,1)}, bf16[80,384]{1,0:T(8,128)(2,1)S(1)}, u32[]{:S(2)}, u32[]{:S(2)}) collective-permute-start(bf16[80,384]{1,0:T(8,128)(2,1)} %get-tuple-element.16), channel_id=1, source_target_pairs={{0,4},{4,8},{8,12},{1,5},{5,9},{9,13},{2,6},{6,10},{10,14},{3,7},{... | collective-permute-start | bytes 184328 | tf_op jit(solution)/shard_map/ppermute | solution.py:35
  55.0 1.3 %collective-permute-start.11 = (bf16[80,384]{1,0:T(8,128)(2,1)}, bf16[80,384]{1,0:T(8,128)(2,1)S(1)}, u32[]{:S(2)}, u32[]{:S(2)}) collective-permute-start(bf16[80,384]{1,0:T(8,128)(2,1)} %get-tuple-element.17), channel_id=1, source_target_pairs={{4,0},{8,4},{12,8},{5,1},{9,5},{13,9},{6,2},{10,6},{14,10},{7,3},{... | collective-permute-start | bytes 184328 | tf_op jit(solution)/shard_map/ppermute | solution.py:36
  56.3 1.8 %collective-permute-start.12 = (bf16[80,6]{1,0:T(8,128)(2,1)}, bf16[80,6]{1,0:T(8,128)(2,1)S(1)}, u32[]{:S(2)}, u32[]{:S(2)}) collective-permute-start(bf16[80,6]{1,0:T(8,128)(2,1)} %get-tuple-element.18), channel_id=1, source_target_pairs={{0,1},{1,2},{2,3},{4,5},{5,6},{6,7},{8,9},{9,10},{10,11},{12,13},{... | collective-permute-start | bytes 2888 | tf_op jit(solution)/shard_map/ppermute | solution.py:37
  58.2 1.3 %collective-permute-start.13 = (bf16[80,6]{1,0:T(8,128)(2,1)}, bf16[80,6]{1,0:T(8,128)(2,1)S(1)}, u32[]{:S(2)}, u32[]{:S(2)}) collective-permute-start(bf16[80,6]{1,0:T(8,128)(2,1)} %get-tuple-element.19), channel_id=1, source_target_pairs={{1,0},{2,1},{3,2},{5,4},{6,5},{7,6},{9,8},{10,9},{11,10},{13,12},{... | collective-permute-start | bytes 2888 | tf_op jit(solution)/shard_map/ppermute | solution.py:38
  59.5 2.2 %collective-permute-done.13.refs_4_ = bf16[80,6]{1,0:T(8,128)(2,1)S(1)} collective-permute-done((bf16[80,6]{1,0:T(8,128)(2,1)}, bf16[80,6]{1,0:T(8,128)(2,1)S(1)}, u32[]{:S(2)}, u32[]{:S(2)}) %collective-permute-start.13) | collective-permute-done | bytes 992 | tf_op jit(solution)/shard_map/ppermute | solution.py:38
  62.4 3.2 %shard_map.115 = (f32[80,2304]{1,0:T(8,128)}, bf16[80,384]{1,0:T(8,128)(2,1)}, bf16[80,384]{1,0:T(8,128)(2,1)}, bf16[80,6]{1,0:T(8,128)(2,1)}, bf16[80,6]{1,0:T(8,128)(2,1)}) custom-call(f32[80,2304]{1,0:T(8,128)} %get-tuple-element.15.refs_0_, bf16[80,384]{1,0:T(8,128)(2,1)} %copy-done.8, bf16[80,384]{1,0:T(8,128)(2,1)} %copy-done.9, ...), custom_call_target="tpu_custom_call" | custom-call | flops 185057280 | bytes 2381312 | tf_op jit(solution)/shard_map/pallas_call | solution.py:140
  65.7 4.6 %collective-permute-start.14 = (bf16[80,384]{1,0:T(8,128)(2,1)}, bf16[80,384]{1,0:T(8,128)(2,1)S(1)}, u32[]{:S(2)}, u32[]{:S(2)}) collective-permute-start(bf16[80,384]{1,0:T(8,128)(2,1)} %get-tuple-element.21), channel_id=1, source_target_pairs={{0,4},{4,8},{8,12},{1,5},{5,9},{9,13},{2,6},{6,10},{10,14},{3,7},{... | collective-permute-start | bytes 184328 | tf_op jit(solution)/shard_map/ppermute | solution.py:35
  70.3 1.3 %collective-permute-start.15 = (bf16[80,384]{1,0:T(8,128)(2,1)}, bf16[80,384]{1,0:T(8,128)(2,1)S(1)}, u32[]{:S(2)}, u32[]{:S(2)}) collective-permute-start(bf16[80,384]{1,0:T(8,128)(2,1)} %get-tuple-element.22), channel_id=1, source_target_pairs={{4,0},{8,4},{12,8},{5,1},{9,5},{13,9},{6,2},{10,6},{14,10},{7,3},{... | collective-permute-start | bytes 184328 | tf_op jit(solution)/shard_map/ppermute | solution.py:36
  71.6 4.1 %collective-permute-start.16 = (bf16[80,6]{1,0:T(8,128)(2,1)}, bf16[80,6]{1,0:T(8,128)(2,1)S(1)}, u32[]{:S(2)}, u32[]{:S(2)}) collective-permute-start(bf16[80,6]{1,0:T(8,128)(2,1)} %get-tuple-element.23), channel_id=1, source_target_pairs={{0,1},{1,2},{2,3},{4,5},{5,6},{6,7},{8,9},{9,10},{10,11},{12,13},{... | collective-permute-start | bytes 2888 | tf_op jit(solution)/shard_map/ppermute | solution.py:37
  75.7 1.3 %collective-permute-start.17 = (bf16[80,6]{1,0:T(8,128)(2,1)}, bf16[80,6]{1,0:T(8,128)(2,1)S(1)}, u32[]{:S(2)}, u32[]{:S(2)}) collective-permute-start(bf16[80,6]{1,0:T(8,128)(2,1)} %get-tuple-element.24), channel_id=1, source_target_pairs={{1,0},{2,1},{3,2},{5,4},{6,5},{7,6},{9,8},{10,9},{11,10},{13,12},{... | collective-permute-start | bytes 2888 | tf_op jit(solution)/shard_map/ppermute | solution.py:38
  77.1 2.0 %collective-permute-done.17.refs_4_ = bf16[80,6]{1,0:T(8,128)(2,1)S(1)} collective-permute-done((bf16[80,6]{1,0:T(8,128)(2,1)}, bf16[80,6]{1,0:T(8,128)(2,1)S(1)}, u32[]{:S(2)}, u32[]{:S(2)}) %collective-permute-start.17) | collective-permute-done | bytes 992 | tf_op jit(solution)/shard_map/ppermute | solution.py:38
  79.7 3.2 %shard_map.116 = (f32[80,2304]{1,0:T(8,128)}, bf16[80,384]{1,0:T(8,128)(2,1)}, bf16[80,384]{1,0:T(8,128)(2,1)}, bf16[80,6]{1,0:T(8,128)(2,1)}, bf16[80,6]{1,0:T(8,128)(2,1)}) custom-call(f32[80,2304]{1,0:T(8,128)} %get-tuple-element.20.refs_0_, bf16[80,384]{1,0:T(8,128)(2,1)} %copy-done.6, bf16[80,384]{1,0:T(8,128)(2,1)} %copy-done.7, ...), custom_call_target="tpu_custom_call" | custom-call | flops 185057280 | bytes 2381312 | tf_op jit(solution)/shard_map/pallas_call | solution.py:140
  82.9 1.4 %fusion.20 = f32[80,128]{1,0:T(8,128)S(1)} fusion(f32[80,2304]{1,0:T(8,128)} %get-tuple-element.25, s32[128]{0:T(128)S(1)} %iota_add_fusion, s32[384]{0:T(512)S(1)} %get-tuple-element.66, s32[384]{0:T(512)S(1)} %get-tuple-element.67, pred[384]{0:T(512)(128)(4,1)S(1)} %fusion.56), kind=kOutput, calls=%fused_computation.38 | convolution fusion | flops 47345664 | bytes 413568 | tf_op jit(solution)/shard_map/dot_general | solution.py:192
  84.3 1.4 %fusion.19 = f32[80,128]{1,0:T(8,128)S(1)} fusion(f32[80,2304]{1,0:T(8,128)} %get-tuple-element.25, s32[128]{0:T(128)S(1)} %iota_add_fusion, s32[384]{0:T(512)S(1)} %get-tuple-element.66, s32[384]{0:T(512)S(1)} %get-tuple-element.67, pred[384]{0:T(512)(128)(4,1)S(1)} %fusion.56), kind=kOutput, calls=%fused_computation.37 | convolution fusion | flops 47345664 | bytes 413568 | tf_op jit(solution)/shard_map/dot_general | solution.py:192
  85.8 4.0 %collective-permute-start.20 = (f32[80,256]{1,0:T(8,128)S(1)}, f32[80,256]{1,0:T(8,128)S(1)}, u32[]{:S(2)}, u32[]{:S(2)}) collective-permute-start(f32[80,256]{1,0:T(8,128)S(1)} %get-tuple-element.46), channel_id=1, source_target_pairs={{0,12},{4,0},{8,4},{12,8},{1,13},{5,1},{9,5},{13,9},{2,14},{6,2},{... | collective-permute-start | bytes 245768 | tf_op jit(solution)/shard_map/ppermute | solution.py:298
  89.9 1.8 %collective-permute-start.18 = (f32[80,256]{1,0:T(8,128)S(1)}, f32[80,256]{1,0:T(8,128)S(1)}, u32[]{:S(2)}, u32[]{:S(2)}) collective-permute-start(f32[80,256]{1,0:T(8,128)S(1)} %get-tuple-element.48), channel_id=1, source_target_pairs={{0,4},{4,8},{8,12},{12,0},{1,5},{5,9},{9,13},{13,1},{2,6},{6,10},{... | collective-permute-start | bytes 245768 | tf_op jit(solution)/shard_map/ppermute | solution.py:298
  92.6 6.1 %collective-permute-done.19 = f32[80,256]{1,0:T(8,128)S(1)} collective-permute-done((f32[80,256]{1,0:T(8,128)S(1)}, f32[80,256]{1,0:T(8,128)S(1)}, u32[]{:S(2)}, u32[]{:S(2)}) %collective-permute-start.19) | collective-permute-done | bytes 81952 | tf_op jit(solution)/shard_map/ppermute | solution.py:298
  98.8 1.9 %fusion.1 = f32[240,2048]{1,0:T(8,128)S(1)} fusion(s32[1024]{0:T(1024)S(1)} %pad_add_fusion, bf16[80,1024]{1,0:T(8,128)(2,1)S(1)} %get-tuple-element.44, bf16[80,1024]{1,0:T(8,128)(2,1)S(1)} %get-tuple-element.43, bf16[80,1024]{1,0:T(8,128)(2,1)S(1)} %get-tuple-element.42), kind=kOutput, calls=%fused_computation.4 | convolution fusion | flops 1010204672 | bytes 2461696 | tf_op jit(solution)/shard_map/dot_general | solution.py:224
  (125 shorter events, 19.8 us)
Async XLA Ops:
  0.6 16.9 %copy-start = (s32[24]{0:T(128)S(1)}, s32[24]{0:T(128)}, u32[]{:S(2)}) copy-start(s32[24]{0:T(128)} %param.19) | copy-start | bytes 292
  0.6 16.7 %copy-start.3 = (bf16[80,8,256]{2,1,0:T(8,128)(2,1)S(1)}, bf16[80,8,256]{2,1,0:T(8,128)(2,1)}, u32[]{:S(2)}) copy-start(bf16[80,8,256]{2,1,0:T(8,128)(2,1)} %param.10) | copy-start | bytes 983044
  0.7 19.6 %copy-start.19 = (f32[80]{0:T(128)S(1)}, f32[80]{0:T(128)}, u32[]{:S(2)}) copy-start(f32[80]{0:T(128)} %param.13) | copy-start | bytes 964
  0.7 20.3 %copy-start.20 = (f32[80]{0:T(128)S(1)}, f32[80]{0:T(128)}, u32[]{:S(2)}) copy-start(f32[80]{0:T(128)} %param.14) | copy-start | bytes 964
  0.7 21.0 %copy-start.21 = (f32[80]{0:T(128)S(1)}, f32[80]{0:T(128)}, u32[]{:S(2)}) copy-start(f32[80]{0:T(128)} %param.12) | copy-start | bytes 964
  2.1 22.1 %collective-permute-start.6 = (s32[256]{0:T(256)S(1)}, s32[256]{0:T(256)S(1)}, u32[]{:S(2)}, u32[]{:S(2)}) collective-permute-start(s32[256]{0:T(256)S(1)} %bitcast.80), channel_id=1, source_target_pairs={{0,12},{4,0},{8,4},{12,8},{1,13},{5,1},{9,5},{13,9},{2,14},{6,2},{... | collective-permute-start | bytes 3080 | tf_op jit(solution)/shard_map/ppermute | solution.py:250
  7.2 18.2 %collective-permute-start.5 = (s32[256]{0:T(256)S(1)}, s32[256]{0:T(256)S(1)}, u32[]{:S(2)}, u32[]{:S(2)}) collective-permute-start(s32[256]{0:T(256)S(1)} %bitcast.79), channel_id=1, source_target_pairs={{0,8},{4,12},{8,0},{12,4},{1,9},{5,13},{9,1},{13,5},{2,10},{6,14},... | collective-permute-start | bytes 3080 | tf_op jit(solution)/shard_map/ppermute | solution.py:250
  7.2 21.3 %collective-permute-start.4 = (s32[256]{0:T(256)S(1)}, s32[256]{0:T(256)S(1)}, u32[]{:S(2)}, u32[]{:S(2)}) collective-permute-start(s32[256]{0:T(256)S(1)} %bitcast.78), channel_id=1, source_target_pairs={{0,4},{4,8},{8,12},{12,0},{1,5},{5,9},{9,13},{13,1},{2,6},{6,10},{... | collective-permute-start | bytes 3080 | tf_op jit(solution)/shard_map/ppermute | solution.py:250
  10.3 13.0 %copy-start.4 = (bf16[80,6,384]{2,0,1:T(8,128)(2,1)S(1)}, bf16[80,6,384]{2,0,1:T(8,128)(2,1)}, u32[]{:S(2)}) copy-start(bf16[80,6,384]{2,0,1:T(8,128)(2,1)} %param.11) | copy-start | bytes 1105924
  10.4 18.1 %collective-permute-start = (bf16[80,640]{1,0:T(8,128)(2,1)S(1)}, bf16[80,640]{1,0:T(8,128)(2,1)S(1)}, u32[]{:S(2)}, u32[]{:S(2)}) collective-permute-start(bf16[80,640]{1,0:T(8,128)(2,1)S(1)} %pad_maximum_fusion.1), channel_id=1, source_target_pairs={{0,4},{4,8},{8,12},{1,5},{5,9},{9,13},{2,6},{6,10},{10,14},{3,7},{... | collective-permute-start | bytes 307208 | tf_op jit(solution)/shard_map/ppermute | solution.py:35
  15.0 14.2 %collective-permute-start.1 = (bf16[80,640]{1,0:T(8,128)(2,1)S(1)}, bf16[80,640]{1,0:T(8,128)(2,1)S(1)}, u32[]{:S(2)}, u32[]{:S(2)}) collective-permute-start(bf16[80,640]{1,0:T(8,128)(2,1)S(1)} %pad_maximum_fusion.2), channel_id=1, source_target_pairs={{4,0},{8,4},{12,8},{5,1},{9,5},{13,9},{6,2},{10,6},{14,10},{7,3},{... | collective-permute-start | bytes 307208 | tf_op jit(solution)/shard_map/ppermute | solution.py:36
  24.2 5.6 %collective-permute-start.3 = (bf16[80,14]{1,0:T(8,128)(2,1)S(1)}, bf16[80,14]{1,0:T(8,128)(2,1)S(1)}, u32[]{:S(2)}, u32[]{:S(2)}) collective-permute-start(bf16[80,14]{1,0:T(8,128)(2,1)S(1)} %copy.49), channel_id=1, source_target_pairs={{1,0},{2,1},{3,2},{5,4},{6,5},{7,6},{9,8},{10,9},{11,10},{13,12},{... | collective-permute-start | bytes 6728 | tf_op jit(solution)/shard_map/ppermute | solution.py:38
  25.5 4.3 %collective-permute-start.2 = (bf16[80,14]{1,0:T(8,128)(2,1)S(1)}, bf16[80,14]{1,0:T(8,128)(2,1)S(1)}, u32[]{:S(2)}, u32[]{:S(2)}) collective-permute-start(bf16[80,14]{1,0:T(8,128)(2,1)S(1)} %copy.46), channel_id=1, source_target_pairs={{0,1},{1,2},{2,3},{4,5},{5,6},{6,7},{8,9},{9,10},{10,11},{12,13},{... | collective-permute-start | bytes 6728 | tf_op jit(solution)/shard_map/ppermute | solution.py:37
  34.4 6.1 %copy-start.15 = (bf16[80,14]{1,0:T(8,128)(2,1)S(1)}, bf16[80,14]{1,0:T(8,128)(2,1)}, u32[]{:S(2)}) copy-start(bf16[80,14]{1,0:T(8,128)(2,1)} %copy-done.14) | copy-start | bytes 6724
  34.4 6.7 %copy-start.17 = (bf16[80,14]{1,0:T(8,128)(2,1)S(1)}, bf16[80,14]{1,0:T(8,128)(2,1)}, u32[]{:S(2)}) copy-start(bf16[80,14]{1,0:T(8,128)(2,1)} %copy-done.16) | copy-start | bytes 6724
  36.3 6.8 %collective-permute-start.9 = (f32[80,256]{1,0:T(8,128)S(1)}, f32[80,256]{1,0:T(8,128)S(1)}, u32[]{:S(2)}, u32[]{:S(2)}) collective-permute-start(f32[80,256]{1,0:T(8,128)S(1)} %get-tuple-element.49), channel_id=1, source_target_pairs={{0,12},{4,0},{8,4},{12,8},{1,13},{5,1},{9,5},{13,9},{2,14},{6,2},{... | collective-permute-start | bytes 245768 | tf_op jit(solution)/shard_map/ppermute | solution.py:255
  39.3 9.5 %collective-permute-start.8 = (f32[80,256]{1,0:T(8,128)S(1)}, f32[80,256]{1,0:T(8,128)S(1)}, u32[]{:S(2)}, u32[]{:S(2)}) collective-permute-start(f32[80,256]{1,0:T(8,128)S(1)} %get-tuple-element.50), channel_id=1, source_target_pairs={{0,8},{4,12},{8,0},{12,4},{1,9},{5,13},{9,1},{13,5},{2,10},{6,14},... | collective-permute-start | bytes 245768 | tf_op jit(solution)/shard_map/ppermute | solution.py:255
  40.4 8.4 %collective-permute-start.7 = (f32[80,256]{1,0:T(8,128)S(1)}, f32[80,256]{1,0:T(8,128)S(1)}, u32[]{:S(2)}, u32[]{:S(2)}) collective-permute-start(f32[80,256]{1,0:T(8,128)S(1)} %get-tuple-element.51), channel_id=1, source_target_pairs={{0,4},{4,8},{8,12},{12,0},{1,5},{5,9},{9,13},{13,1},{2,6},{6,10},{... | collective-permute-start | bytes 245768 | tf_op jit(solution)/shard_map/ppermute | solution.py:255
  53.6 8.1 %collective-permute-start.10 = (bf16[80,384]{1,0:T(8,128)(2,1)}, bf16[80,384]{1,0:T(8,128)(2,1)S(1)}, u32[]{:S(2)}, u32[]{:S(2)}) collective-permute-start(bf16[80,384]{1,0:T(8,128)(2,1)} %get-tuple-element.16), channel_id=1, source_target_pairs={{0,4},{4,8},{8,12},{1,5},{5,9},{9,13},{2,6},{6,10},{10,14},{3,7},{... | collective-permute-start | bytes 184328 | tf_op jit(solution)/shard_map/ppermute | solution.py:35
  55.0 6.8 %collective-permute-start.11 = (bf16[80,384]{1,0:T(8,128)(2,1)}, bf16[80,384]{1,0:T(8,128)(2,1)S(1)}, u32[]{:S(2)}, u32[]{:S(2)}) collective-permute-start(bf16[80,384]{1,0:T(8,128)(2,1)} %get-tuple-element.17), channel_id=1, source_target_pairs={{4,0},{8,4},{12,8},{5,1},{9,5},{13,9},{6,2},{10,6},{14,10},{7,3},{... | collective-permute-start | bytes 184328 | tf_op jit(solution)/shard_map/ppermute | solution.py:36
  56.3 3.2 %collective-permute-start.12 = (bf16[80,6]{1,0:T(8,128)(2,1)}, bf16[80,6]{1,0:T(8,128)(2,1)S(1)}, u32[]{:S(2)}, u32[]{:S(2)}) collective-permute-start(bf16[80,6]{1,0:T(8,128)(2,1)} %get-tuple-element.18), channel_id=1, source_target_pairs={{0,1},{1,2},{2,3},{4,5},{5,6},{6,7},{8,9},{9,10},{10,11},{12,13},{... | collective-permute-start | bytes 2888 | tf_op jit(solution)/shard_map/ppermute | solution.py:37
  58.2 3.5 %collective-permute-start.13 = (bf16[80,6]{1,0:T(8,128)(2,1)}, bf16[80,6]{1,0:T(8,128)(2,1)S(1)}, u32[]{:S(2)}, u32[]{:S(2)}) collective-permute-start(bf16[80,6]{1,0:T(8,128)(2,1)} %get-tuple-element.19), channel_id=1, source_target_pairs={{1,0},{2,1},{3,2},{5,4},{6,5},{7,6},{9,8},{10,9},{11,10},{13,12},{... | collective-permute-start | bytes 2888 | tf_op jit(solution)/shard_map/ppermute | solution.py:38
  59.5 2.3 %copy-start.12 = (bf16[80,6]{1,0:T(8,128)(2,1)}, bf16[80,6]{1,0:T(8,128)(2,1)S(1)}, u32[]{:S(2)}) copy-start(bf16[80,6]{1,0:T(8,128)(2,1)S(1)} %collective-permute-done.12.refs_3_) | copy-start | bytes 2884
  65.7 13.4 %collective-permute-start.14 = (bf16[80,384]{1,0:T(8,128)(2,1)}, bf16[80,384]{1,0:T(8,128)(2,1)S(1)}, u32[]{:S(2)}, u32[]{:S(2)}) collective-permute-start(bf16[80,384]{1,0:T(8,128)(2,1)} %get-tuple-element.21), channel_id=1, source_target_pairs={{0,4},{4,8},{8,12},{1,5},{5,9},{9,13},{2,6},{6,10},{10,14},{3,7},{... | collective-permute-start | bytes 184328 | tf_op jit(solution)/shard_map/ppermute | solution.py:35
  70.3 8.8 %collective-permute-start.15 = (bf16[80,384]{1,0:T(8,128)(2,1)}, bf16[80,384]{1,0:T(8,128)(2,1)S(1)}, u32[]{:S(2)}, u32[]{:S(2)}) collective-permute-start(bf16[80,384]{1,0:T(8,128)(2,1)} %get-tuple-element.22), channel_id=1, source_target_pairs={{4,0},{8,4},{12,8},{5,1},{9,5},{13,9},{6,2},{10,6},{14,10},{7,3},{... | collective-permute-start | bytes 184328 | tf_op jit(solution)/shard_map/ppermute | solution.py:36
  71.6 5.5 %collective-permute-start.16 = (bf16[80,6]{1,0:T(8,128)(2,1)}, bf16[80,6]{1,0:T(8,128)(2,1)S(1)}, u32[]{:S(2)}, u32[]{:S(2)}) collective-permute-start(bf16[80,6]{1,0:T(8,128)(2,1)} %get-tuple-element.23), channel_id=1, source_target_pairs={{0,1},{1,2},{2,3},{4,5},{5,6},{6,7},{8,9},{9,10},{10,11},{12,13},{... | collective-permute-start | bytes 2888 | tf_op jit(solution)/shard_map/ppermute | solution.py:37
  75.7 3.3 %collective-permute-start.17 = (bf16[80,6]{1,0:T(8,128)(2,1)}, bf16[80,6]{1,0:T(8,128)(2,1)S(1)}, u32[]{:S(2)}, u32[]{:S(2)}) collective-permute-start(bf16[80,6]{1,0:T(8,128)(2,1)} %get-tuple-element.24), channel_id=1, source_target_pairs={{1,0},{2,1},{3,2},{5,4},{6,5},{7,6},{9,8},{10,9},{11,10},{13,12},{... | collective-permute-start | bytes 2888 | tf_op jit(solution)/shard_map/ppermute | solution.py:38
  77.0 2.0 %copy-start.10 = (bf16[80,6]{1,0:T(8,128)(2,1)}, bf16[80,6]{1,0:T(8,128)(2,1)S(1)}, u32[]{:S(2)}) copy-start(bf16[80,6]{1,0:T(8,128)(2,1)S(1)} %collective-permute-done.16.refs_3_) | copy-start | bytes 2884
  82.9 8.9 %copy-start.5 = (f32[80,2304]{1,0:T(8,128)S(1)}, f32[80,2304]{1,0:T(8,128)}, u32[]{:S(2)}) copy-start(f32[80,2304]{1,0:T(8,128)} %get-tuple-element.25) | copy-start | bytes 2211844
  85.8 6.8 %collective-permute-start.20 = (f32[80,256]{1,0:T(8,128)S(1)}, f32[80,256]{1,0:T(8,128)S(1)}, u32[]{:S(2)}, u32[]{:S(2)}) collective-permute-start(f32[80,256]{1,0:T(8,128)S(1)} %get-tuple-element.46), channel_id=1, source_target_pairs={{0,12},{4,0},{8,4},{12,8},{1,13},{5,1},{9,5},{13,9},{2,14},{6,2},{... | collective-permute-start | bytes 245768 | tf_op jit(solution)/shard_map/ppermute | solution.py:298
  89.8 8.9 %collective-permute-start.19 = (f32[80,256]{1,0:T(8,128)S(1)}, f32[80,256]{1,0:T(8,128)S(1)}, u32[]{:S(2)}, u32[]{:S(2)}) collective-permute-start(f32[80,256]{1,0:T(8,128)S(1)} %get-tuple-element.47), channel_id=1, source_target_pairs={{0,8},{4,12},{8,0},{12,4},{1,9},{5,13},{9,1},{13,5},{2,10},{6,14},... | collective-permute-start | bytes 245768 | tf_op jit(solution)/shard_map/ppermute | solution.py:298
  89.9 8.7 %collective-permute-start.18 = (f32[80,256]{1,0:T(8,128)S(1)}, f32[80,256]{1,0:T(8,128)S(1)}, u32[]{:S(2)}, u32[]{:S(2)}) collective-permute-start(f32[80,256]{1,0:T(8,128)S(1)} %get-tuple-element.48), channel_id=1, source_target_pairs={{0,4},{4,8},{8,12},{12,0},{1,5},{5,9},{9,13},{13,1},{2,6},{6,10},{... | collective-permute-start | bytes 245768 | tf_op jit(solution)/shard_map/ppermute | solution.py:298
  (11 other events, 9.6 us)

commit v10 on v9

--- a/solution.py
+++ b/solution.py
@@ -74,13 +74,26 @@
     return down + up + east + west - 4.0 * flat
 
 
-def step_kernel(*refs, rows, cols, nest):
+def step_kernel(*refs, rows, cols, nest, split, gap):
+    refs = list(refs)
+    if gap:
+        expand_ref, fblock_ref = refs[:2]
+        refs = refs[2:]
     if nest:
         (state_ref, above_ref, below_ref, left_ref, right_ref, forcing_ref, upw_ref, dnw_ref,
-         nu_ref, relax_ref, vm_ref, new_ref, lrow_ref, frow_ref, lcol_ref, fcol_ref, up_sc, dn_sc) = refs
+         nu_ref, relax_ref, vm_ref, new_ref, lrow_ref, frow_ref, lcol_ref, fcol_ref) = refs[:16]
+        refs = refs[16:]
     else:
         (state_ref, above_ref, below_ref, left_ref, right_ref, nu_ref, vm_ref,
-         new_ref, lrow_ref, frow_ref, lcol_ref, fcol_ref, up_sc, dn_sc) = refs
+         new_ref, lrow_ref, frow_ref, lcol_ref, fcol_ref) = refs[:12]
+        refs = refs[12:]
+    if split:
+        parts_ref = refs[0]
+        refs = refs[1:]
+    if gap:
+        gap_ref = refs[0]
+        refs = refs[1:]
+    up_sc, dn_sc = refs
     n = rows * cols
     state = state_ref[...].astype(jnp.float32)
     levels = state.shape[0]
@@ -116,9 +129,31 @@
     first_sel = (p == j * cols).astype(jnp.bfloat16)
     lcol_ref[...] = jnp.dot(narrow, last_sel, preferred_element_type=jnp.float32).astype(jnp.bfloat16)
     fcol_ref[...] = jnp.dot(narrow, first_sel, preferred_element_type=jnp.float32).astype(jnp.bfloat16)
-
-
-def stencil_step(state, halo, nu, vert_mix, rows, cols, forcing=None, up_w=None, down_w=None, relax=None):
+    if split:
+        hi = new.astype(jnp.bfloat16)
+        rest = new - hi.astype(jnp.float32)
+        mid = rest.astype(jnp.bfloat16)
+        lo = (rest - mid.astype(jnp.float32)).astype(jnp.bfloat16)
+        parts_ref[0:levels, :] = hi
+        parts_ref[levels : 2 * levels, :] = mid
+        parts_ref[2 * levels : 3 * levels, :] = lo
+    if gap:
+        expand = expand_ref[...]
+        block_cols = expand.shape[0]
+        pick = (((1,), (1,)), ((), ()))
+        for a in range(rows // 3):
+            rows3 = (
+                new[:, (3 * a) * cols : (3 * a + 1) * cols]
+                + new[:, (3 * a + 1) * cols : (3 * a + 2) * cols]
+            ) + new[:, (3 * a + 2) * cols : (3 * a + 3) * cols]
+            sums = lax.dot_general(rows3, expand, pick, precision=HI, preferred_element_type=jnp.float32)
+            gap_ref[:, a * block_cols : (a + 1) * block_cols] = (
+                sums / 9.0 - fblock_ref[:, a * block_cols : (a + 1) * block_cols]
+            )
+
+
+def stencil_step(state, halo, nu, vert_mix, rows, cols, forcing=None, up_w=None, down_w=None, relax=None,
+                 split=False, gap_of=None):
     levels = state.shape[0]
     n = rows * cols
     nest = forcing is not None
@@ -135,15 +170,21 @@
         jax.ShapeDtypeStruct((levels, rows), jnp.bfloat16),
         jax.ShapeDtypeStruct((levels, rows), jnp.bfloat16),
     )
+    gap = gap_of is not None
+    if split:
+        out_shape = out_shape + (jax.ShapeDtypeStruct((3 * levels, n), jnp.bfloat16),)
+    if gap:
+        args = tuple(gap_of) + args
+        out_shape = out_shape + (jax.ShapeDtypeStruct(gap_of[1].shape, jnp.float32),)
     flops = 2 * levels * levels * n * 6 + 4 * levels * n * rows + 20 * levels * n
     moved_bytes = sum(int(a.size) * a.dtype.itemsize for a in args) + levels * n * 4
-    new, lrow, frow, lcol, fcol = pl.pallas_call(
-        functools.partial(step_kernel, rows=rows, cols=cols, nest=nest),
+    outs = pl.pallas_call(
+        functools.partial(step_kernel, rows=rows, cols=cols, nest=nest, split=split, gap=gap),
         out_shape=out_shape,
         scratch_shapes=[pltpu.VMEM((levels, n), jnp.float32), pltpu.VMEM((levels, n), jnp.float32)],
         cost_estimate=pl.CostEstimate(flops=flops, bytes_accessed=moved_bytes, transcendentals=0),
     )(*args)
-    return new, (lrow, frow, lcol, fcol)
+    return outs[0], tuple(outs[1:5]), outs[5:]
 
 
 def mix_levels(matrix, flat):
@@ -217,6 +258,14 @@
     return (total[:levels] + total[levels : 2 * levels]) + total[2 * levels :]
 
 
+def gather_parts(parts, ids):
+    levels = parts.shape[0] // 3
+    width = parts.shape[1]
+    onehot = (lax.broadcasted_iota(jnp.int32, (width, 1), 0) == ids[None, :]).astype(jnp.bfloat16)
+    total = jnp.dot(parts, onehot, preferred_element_type=jnp.float32)
+    return (total[:levels] + total[levels : 2 * levels]) + total[2 * levels :]
+
+
 def scatter_add_columns(values, ids, width):
     levels = values.shape[0]
     onehot = (ids[:, None] == lax.broadcasted_iota(jnp.int32, (1, width), 1)).astype(jnp.bfloat16)
@@ -233,8 +282,9 @@
     zero = jnp.minimum(here_x, 0)
 
     parent_halo, nest_halo = exchange([edges_3d(parent), edges_3d(nest)])
-    flat_parent, _ = stencil_step(
-        parent.reshape(levels, p_rows * p_cols), parent_halo, nu_parent, vert_mix, p_rows, p_cols
+    flat_parent, _, (parent_parts,) = stencil_step(
+        parent.reshape(levels, p_rows * p_cols), parent_halo, nu_parent, vert_mix, p_rows, p_cols,
+        split=True,
     )
 
     owners = fp_owner.reshape(-1)
@@ -250,7 +300,7 @@
             lax.ppermute(wanted[s], "gx", shifted_pairs(tiles_x, s)) for s in range(1, tiles_x)
         ]
         served_ids = jnp.concatenate(served, axis=0)
-        replies = gather_columns(flat_parent, served_ids)
+        replies = gather_parts(parent_parts, served_ids)
         back = [replies[:, 0:requests]] + [
             lax.ppermute(replies[:, s * requests : (s + 1) * requests], "gx", shifted_pairs(tiles_x, -s))
             for s in range(1, tiles_x)
@@ -267,7 +317,7 @@
         wanted = jnp.zeros((tiles_x * slots,), jnp.int32).at[places].set(cells)
         served_ids = lax.all_to_all(wanted, "gx", split_axis=0, concat_axis=0, tiled=True)
         answers = lax.all_to_all(
-            gather_columns(flat_parent, served_ids), "gx", split_axis=1, concat_axis=1, tiled=True
+            gather_parts(parent_parts, served_ids), "gx", split_axis=1, concat_axis=1, tiled=True
         )
         forcing_flat = jnp.take(answers, places, axis=1)
 
@@ -285,12 +335,11 @@
     for turn_no in range(3):
         if turn_no > 0:
             (halo,) = exchange([edges])
-        nest_state, edges = stencil_step(
-            nest_state, halo, nu_nest, vert_mix, n_rows, n_cols, forcing_full, up_w, down_w, relax
-        )
-
-    block_sum = block_sums(nest_state, block_rows, n_cols, expand)
-    nudge_gap = block_sum / 9.0 - forcing_flat
+        nest_state, edges, extra = stencil_step(
+            nest_state, halo, nu_nest, vert_mix, n_rows, n_cols, forcing_full, up_w, down_w, relax,
+            gap_of=(expand, forcing_flat) if turn_no == 2 else None,
+        )
+    (nudge_gap,) = extra
     if by_shift:
         outgoing = jnp.where(chosen[:, None, :], nudge_gap[None, :, :], 0.0)
         incoming = jnp.concatenate(

time: 102 us -> 103 us (level)
  waiting for transfers between devices: 16.2 us -> 17.9 us
  matrix products: 7.02 us -> 5.47 us
  other arithmetic: 3.25 us -> 4.75 us
  starting transfers between devices: 43.6 us -> 42.1 us
    ppermute x3, waiting for transfers between devices: 0.13 us -> 4.42 us  [exchange(): below = lax.ppermute(first_rows, 'gx', bwd_x)]
    ppermute x3, waiting for transfers between devices: 4.16 us -> 2.19 us  [exchange(): right = lax.ppermute(first_cols, Y_AXES, bwd_y)]
    ppermute x3, starting transfers between devices: 5.98 us -> 4.15 us  [body(): lax.ppermute(outgoing[s], 'gx', shifted_pairs(tiles_x, s))]
    dot_general x3 -> x1, matrix products: 4.57 us -> 3.02 us  [gather_parts(): total = jnp.dot(parts, onehot, preferred_element_type=jnp.float32)]
    convert_element_type x2 -> x1, other arithmetic: 1.33 us -> 0.08 us  [split3(): hi.astype(jnp.bfloat16)]
    convert_element_type x1, other arithmetic: 0.04 us -> 1.16 us  [body(): nest_state.astype(jnp.bfloat16).reshape(levels, n_rows, n_cols)]
    ppermute x3, waiting for transfers between devices: 6.11 us -> 5.05 us  [body(): lax.ppermute(outgoing[s], 'gx', shifted_pairs(tiles_x, s))]
  transfers between devices with their start and end apart: 21 -> 21, of which waited for: 5 -> 6; matrix products, arithmetic and copies ran while one was open for 14% -> 16% of each run, Pallas kernels for 0% -> 0%
where the time goes in v10:
time: 103 us
  starting transfers between devices  42.1 us (41%)
  local copies, waits for them, and re-layouts  18.1 us (18%)
  waiting for transfers between devices  17.9 us (17%)
  Pallas kernels  13.2 us (13%)
  matrix products  5.47 us (5%)
  other arithmetic  4.75 us (5%)
  between operations  1.17 us (1%)
    pallas_call x4, Pallas kernels, stencil_step(): pl.pallas_call(functools.partial(step_kernel, rows=rows, cols=cols, nest=...  13.2 us
    ppermute x3, starting transfers between devices, exchange(): above = lax.ppermute(last_rows, 'gx', fwd_x)  10.7 us
    ppermute x3, starting transfers between devices, exchange(): left = lax.ppermute(last_cols, Y_AXES, fwd_y)  9.18 us
    unnamed x58, local copies, waits for them, and re-layouts  6.33 us
    ppermute x3, starting transfers between devices, body(): lax.ppermute(wanted[s], 'gx', shifted_pairs(tiles_x, s))  6.14 us
    ppermute x3, waiting for transfers between devices, body(): lax.ppermute(replies[:, s * requests:(s + 1) * requests], 'gx', shifted_p...  5.78 us
    ppermute x3, waiting for transfers between devices, body(): lax.ppermute(outgoing[s], 'gx', shifted_pairs(tiles_x, s))  5.05 us
    ppermute x3, waiting for transfers between devices, exchange(): below = lax.ppermute(first_rows, 'gx', bwd_x)  4.42 us
  transfers between devices with their start and end apart: 21, of which 6 were waited for; matrix products, arithmetic and copies ran while one was open for 16% of the time, Pallas kernels for 0%

profile of v10, /device:TPU:0, one launch (start us, length us, event | category | flops | bytes accessed | tf_op | source)
XLA Modules:
  0.0 102.6 jit_solution(11593923088464953087)
XLA Ops:
  2.1 5.1 %collective-permute-start.6 = (s32[256]{0:T(256)S(1)}, s32[256]{0:T(256)S(1)}, u32[]{:S(2)}, u32[]{:S(2)}) collective-permute-start(s32[256]{0:T(256)S(1)} %bitcast.81), channel_id=1, source_target_pairs={{0,12},{4,0},{8,4},{12,8},{1,13},{5,1},{9,5},{13,9},{2,14},{6,2},{... | collective-permute-start | bytes 3080 | tf_op jit(solution)/shard_map/ppermute | solution.py:300
  7.2 1.0 collective-permute-start.4
  9.1 1.2 %fusion.37 = (bf16[80,1,256]{2,1,0:T(2,128)(2,1)S(1)}, bf16[80,1,256]{2,1,0:T(2,128)(2,1)S(1)}) fusion(bf16[80,8,256]{2,1,0:T(8,128)(2,1)} %param.10), kind=kLoop, calls=%fused_computation.93 | loop fusion | bytes 163840 | tf_op jit(solution)/shard_map/slice | solution.py:21
  10.4 4.5 %collective-permute-start = (bf16[80,640]{1,0:T(8,128)(2,1)S(1)}, bf16[80,640]{1,0:T(8,128)(2,1)S(1)}, u32[]{:S(2)}, u32[]{:S(2)}) collective-permute-start(bf16[80,640]{1,0:T(8,128)(2,1)S(1)} %pad_maximum_fusion.1), channel_id=1, source_target_pairs={{0,4},{4,8},{8,12},{1,5},{5,9},{9,13},{2,6},{6,10},{10,14},{3,7},{... | collective-permute-start | bytes 307208 | tf_op jit(solution)/shard_map/ppermute | solution.py:35
  15.0 1.3 %collective-permute-start.1 = (bf16[80,640]{1,0:T(8,128)(2,1)S(1)}, bf16[80,640]{1,0:T(8,128)(2,1)S(1)}, u32[]{:S(2)}, u32[]{:S(2)}) collective-permute-start(bf16[80,640]{1,0:T(8,128)(2,1)S(1)} %pad_maximum_fusion.2), channel_id=1, source_target_pairs={{4,0},{8,4},{12,8},{5,1},{9,5},{13,9},{6,2},{10,6},{14,10},{7,3},{... | collective-permute-start | bytes 307208 | tf_op jit(solution)/shard_map/ppermute | solution.py:36
  16.3 1.1 %fusion.34 = (bf16[80,6,1]{2,0,1:T(8,128)(2,1)S(1)}, bf16[80,6,1]{2,0,1:T(8,128)(2,1)S(1)}) fusion(bf16[80,6,384]{2,0,1:T(8,128)(2,1)} %param.11), kind=kLoop, calls=%fused_computation.90 | loop fusion | bytes 3840 | tf_op jit(solution)/shard_map/slice | solution.py:21
  24.2 1.3 %collective-permute-start.3 = (bf16[80,14]{1,0:T(8,128)(2,1)S(1)}, bf16[80,14]{1,0:T(8,128)(2,1)S(1)}, u32[]{:S(2)}, u32[]{:S(2)}) collective-permute-start(bf16[80,14]{1,0:T(8,128)(2,1)S(1)} %copy.49), channel_id=1, source_target_pairs={{1,0},{2,1},{3,2},{5,4},{6,5},{7,6},{9,8},{10,9},{11,10},{13,12},{... | collective-permute-start | bytes 6728 | tf_op jit(solution)/shard_map/ppermute | solution.py:38
  25.5 3.0 %collective-permute-start.2 = (bf16[80,14]{1,0:T(8,128)(2,1)S(1)}, bf16[80,14]{1,0:T(8,128)(2,1)S(1)}, u32[]{:S(2)}, u32[]{:S(2)}) collective-permute-start(bf16[80,14]{1,0:T(8,128)(2,1)S(1)} %copy.46), channel_id=1, source_target_pairs={{0,1},{1,2},{2,3},{4,5},{5,6},{6,7},{8,9},{9,10},{10,11},{12,13},{... | collective-permute-start | bytes 6728 | tf_op jit(solution)/shard_map/ppermute | solution.py:37
  30.4 3.2 %shard_map.113 = (f32[80,2048]{1,0:T(8,128)}, bf16[80,256]{1,0:T(8,128)(2,1)}, bf16[80,256]{1,0:T(8,128)(2,1)}, bf16[80,8]{1,0:T(8,128)(2,1)}, bf16[80,8]{1,0:T(8,128)(2,1)}, /*index=5*/bf16[240,2048]{1,0:T(8,128)(2,1)}) custom-call(bf16[80,2048]{1,0:T(8,128)(2,1)} %bitcast.60, bf16[80,256]{1,0:T(8,128)(2,1)} %slice.171.refs_1_, ...), custom_call_target="tpu_custom_call" | custom-call | flops 165806080 | bytes 1093440 | tf_op jit(solution)/shard_map/pallas_call | solution.py:181
  33.6 3.0 %fusion = f32[240,1024]{1,0:T(8,128)S(1)} fusion(bf16[240,2048]{1,0:T(8,128)(2,1)} %get-tuple-element.17, s32[1024]{0:T(1024)S(1)} %pad_add_fusion), kind=kOutput, calls=%fused_computation.3 | convolution fusion | flops 1008730112 | bytes 1970176 | tf_op jit(solution)/shard_map/dot_general | solution.py:265
  36.7 3.0 %collective-permute-start.9 = (f32[80,256]{1,0:T(8,128)S(1)}, f32[80,256]{1,0:T(8,128)S(1)}, u32[]{:S(2)}, u32[]{:S(2)}) collective-permute-start(f32[80,256]{1,0:T(8,128)S(1)} %get-tuple-element.50), channel_id=1, source_target_pairs={{0,12},{4,0},{8,4},{12,8},{1,13},{5,1},{9,5},{13,9},{2,14},{6,2},{... | collective-permute-start | bytes 245768 | tf_op jit(solution)/shard_map/ppermute | solution.py:305
  39.7 1.1 %collective-permute-start.8 = (f32[80,256]{1,0:T(8,128)S(1)}, f32[80,256]{1,0:T(8,128)S(1)}, u32[]{:S(2)}, u32[]{:S(2)}) collective-permute-start(f32[80,256]{1,0:T(8,128)S(1)} %get-tuple-element.51), channel_id=1, source_target_pairs={{0,8},{4,12},{8,0},{12,4},{1,9},{5,13},{9,1},{13,5},{2,10},{6,14},... | collective-permute-start | bytes 245768 | tf_op jit(solution)/shard_map/ppermute | solution.py:305
  43.5 5.8 %collective-permute-done.8 = f32[80,256]{1,0:T(8,128)S(1)} collective-permute-done((f32[80,256]{1,0:T(8,128)S(1)}, f32[80,256]{1,0:T(8,128)S(1)}, u32[]{:S(2)}, u32[]{:S(2)}) %collective-permute-start.8) | collective-permute-done | bytes 81952 | tf_op jit(solution)/shard_map/ppermute | solution.py:305
  50.9 3.1 %shard_map.114 = (f32[80,2304]{1,0:T(8,128)}, bf16[80,384]{1,0:T(8,128)(2,1)}, bf16[80,384]{1,0:T(8,128)(2,1)}, bf16[80,6]{1,0:T(8,128)(2,1)}, bf16[80,6]{1,0:T(8,128)(2,1)}) custom-call(bf16[80,2304]{1,0:T(8,128)(2,1)} %bitcast.56, bf16[80,384]{1,0:T(8,128)(2,1)} %slice.189.refs_1_, bf16[80,384]{1,0:T(8,128)(2,1)} %slice.190.refs_2_, ...), custom_call_target="tpu_custom_call" | custom-call | flops 185057280 | bytes 2012672 | tf_op jit(solution)/shard_map/pallas_call | solution.py:181
  54.0 1.5 %collective-permute-start.10 = (bf16[80,384]{1,0:T(8,128)(2,1)}, bf16[80,384]{1,0:T(8,128)(2,1)S(1)}, u32[]{:S(2)}, u32[]{:S(2)}) collective-permute-start(bf16[80,384]{1,0:T(8,128)(2,1)} %get-tuple-element.19), channel_id=1, source_target_pairs={{0,4},{4,8},{8,12},{1,5},{5,9},{9,13},{2,6},{6,10},{10,14},{3,7},{... | collective-permute-start | bytes 184328 | tf_op jit(solution)/shard_map/ppermute | solution.py:35
  55.4 1.3 %collective-permute-start.11 = (bf16[80,384]{1,0:T(8,128)(2,1)}, bf16[80,384]{1,0:T(8,128)(2,1)S(1)}, u32[]{:S(2)}, u32[]{:S(2)}) collective-permute-start(bf16[80,384]{1,0:T(8,128)(2,1)} %get-tuple-element.20), channel_id=1, source_target_pairs={{4,0},{8,4},{12,8},{5,1},{9,5},{13,9},{6,2},{10,6},{14,10},{7,3},{... | collective-permute-start | bytes 184328 | tf_op jit(solution)/shard_map/ppermute | solution.py:36
  56.7 1.8 %collective-permute-start.12 = (bf16[80,6]{1,0:T(8,128)(2,1)}, bf16[80,6]{1,0:T(8,128)(2,1)S(1)}, u32[]{:S(2)}, u32[]{:S(2)}) collective-permute-start(bf16[80,6]{1,0:T(8,128)(2,1)} %get-tuple-element.21), channel_id=1, source_target_pairs={{0,1},{1,2},{2,3},{4,5},{5,6},{6,7},{8,9},{9,10},{10,11},{12,13},{... | collective-permute-start | bytes 2888 | tf_op jit(solution)/shard_map/ppermute | solution.py:37
  58.6 1.3 %collective-permute-start.13 = (bf16[80,6]{1,0:T(8,128)(2,1)}, bf16[80,6]{1,0:T(8,128)(2,1)S(1)}, u32[]{:S(2)}, u32[]{:S(2)}) collective-permute-start(bf16[80,6]{1,0:T(8,128)(2,1)} %get-tuple-element.22), channel_id=1, source_target_pairs={{1,0},{2,1},{3,2},{5,4},{6,5},{7,6},{9,8},{10,9},{11,10},{13,12},{... | collective-permute-start | bytes 2888 | tf_op jit(solution)/shard_map/ppermute | solution.py:38
  59.9 2.2 %collective-permute-done.13.refs_4_ = bf16[80,6]{1,0:T(8,128)(2,1)S(1)} collective-permute-done((bf16[80,6]{1,0:T(8,128)(2,1)}, bf16[80,6]{1,0:T(8,128)(2,1)S(1)}, u32[]{:S(2)}, u32[]{:S(2)}) %collective-permute-start.13) | collective-permute-done | bytes 992 | tf_op jit(solution)/shard_map/ppermute | solution.py:38
  62.9 3.2 %shard_map.115 = (f32[80,2304]{1,0:T(8,128)}, bf16[80,384]{1,0:T(8,128)(2,1)}, bf16[80,384]{1,0:T(8,128)(2,1)}, bf16[80,6]{1,0:T(8,128)(2,1)}, bf16[80,6]{1,0:T(8,128)(2,1)}) custom-call(f32[80,2304]{1,0:T(8,128)} %get-tuple-element.18.refs_0_, bf16[80,384]{1,0:T(8,128)(2,1)} %copy-done.8, bf16[80,384]{1,0:T(8,128)(2,1)} %copy-done.9, ...), custom_call_target="tpu_custom_call" | custom-call | flops 185057280 | bytes 2381312 | tf_op jit(solution)/shard_map/pallas_call | solution.py:181
  66.1 4.3 %collective-permute-start.16 = (bf16[80,6]{1,0:T(8,128)(2,1)}, bf16[80,6]{1,0:T(8,128)(2,1)S(1)}, u32[]{:S(2)}, u32[]{:S(2)}) collective-permute-start(bf16[80,6]{1,0:T(8,128)(2,1)} %get-tuple-element.26), channel_id=1, source_target_pairs={{0,1},{1,2},{2,3},{4,5},{5,6},{6,7},{8,9},{9,10},{10,11},{12,13},{... | collective-permute-start | bytes 2888 | tf_op jit(solution)/shard_map/ppermute | solution.py:37
  70.4 1.3 %collective-permute-start.17 = (bf16[80,6]{1,0:T(8,128)(2,1)}, bf16[80,6]{1,0:T(8,128)(2,1)S(1)}, u32[]{:S(2)}, u32[]{:S(2)}) collective-permute-start(bf16[80,6]{1,0:T(8,128)(2,1)} %get-tuple-element.27), channel_id=1, source_target_pairs={{1,0},{2,1},{3,2},{5,4},{6,5},{7,6},{9,8},{10,9},{11,10},{13,12},{... | collective-permute-start | bytes 2888 | tf_op jit(solution)/shard_map/ppermute | solution.py:38
  71.7 4.7 %collective-permute-start.14 = (bf16[80,384]{1,0:T(8,128)(2,1)}, bf16[80,384]{1,0:T(8,128)(2,1)S(1)}, u32[]{:S(2)}, u32[]{:S(2)}) collective-permute-start(bf16[80,384]{1,0:T(8,128)(2,1)} %get-tuple-element.24), channel_id=1, source_target_pairs={{0,4},{4,8},{8,12},{1,5},{5,9},{9,13},{2,6},{6,10},{10,14},{3,7},{... | collective-permute-start | bytes 184328 | tf_op jit(solution)/shard_map/ppermute | solution.py:35
  76.4 1.3 %collective-permute-start.15 = (bf16[80,384]{1,0:T(8,128)(2,1)}, bf16[80,384]{1,0:T(8,128)(2,1)S(1)}, u32[]{:S(2)}, u32[]{:S(2)}) collective-permute-start(bf16[80,384]{1,0:T(8,128)(2,1)} %get-tuple-element.25), channel_id=1, source_target_pairs={{4,0},{8,4},{12,8},{5,1},{9,5},{13,9},{6,2},{10,6},{14,10},{7,3},{... | collective-permute-start | bytes 184328 | tf_op jit(solution)/shard_map/ppermute | solution.py:36
  78.9 4.3 %collective-permute-done.15.refs_4_ = bf16[80,384]{1,0:T(8,128)(2,1)S(1)} collective-permute-done((bf16[80,384]{1,0:T(8,128)(2,1)}, bf16[80,384]{1,0:T(8,128)(2,1)S(1)}, u32[]{:S(2)}, u32[]{:S(2)}) %collective-permute-start.15) | collective-permute-done | bytes 61472 | tf_op jit(solution)/shard_map/ppermute | solution.py:36
  83.9 3.7 %shard_map.116 = (f32[80,2304]{1,0:T(8,128)}, bf16[80,384]{1,0:T(8,128)(2,1)}, bf16[80,384]{1,0:T(8,128)(2,1)}, bf16[80,6]{1,0:T(8,128)(2,1)}, bf16[80,6]{1,0:T(8,128)(2,1)}, /*index=5*/f32[80,256]{1,0:T(8,128)}) custom-call(f32[128,384]{1,0:T(8,128)} %fusion.15.refs_0_, f32[80,256]{1,0:T(8,128)} %copy-done.4, f32[80,2304]{1,0:T(8,128)} %get-tuple-element.23.refs_2_, ...), custom_call_target="tpu_custom_call" | custom-call | flops 185057280 | bytes 2659840 | tf_op jit(solution)/shard_map/pallas_call | solution.py:181
  87.6 0.9 broadcast_select_fusion
  88.5 1.2 %collective-permute-start.20 = (f32[80,256]{1,0:T(8,128)S(1)}, f32[80,256]{1,0:T(8,128)S(1)}, u32[]{:S(2)}, u32[]{:S(2)}) collective-permute-start(f32[80,256]{1,0:T(8,128)S(1)} %get-tuple-element.47), channel_id=1, source_target_pairs={{0,12},{4,0},{8,4},{12,8},{1,13},{5,1},{9,5},{13,9},{2,14},{6,2},{... | collective-permute-start | bytes 245768 | tf_op jit(solution)/shard_map/ppermute | solution.py:347
  89.7 2.4 %collective-permute-start.19 = (f32[80,256]{1,0:T(8,128)S(1)}, f32[80,256]{1,0:T(8,128)S(1)}, u32[]{:S(2)}, u32[]{:S(2)}) collective-permute-start(f32[80,256]{1,0:T(8,128)S(1)} %get-tuple-element.48), channel_id=1, source_target_pairs={{0,8},{4,12},{8,0},{12,4},{1,9},{5,13},{9,1},{13,5},{2,10},{6,14},... | collective-permute-start | bytes 245768 | tf_op jit(solution)/shard_map/ppermute | solution.py:347
  92.7 1.2 %convert_element_type.33 = bf16[80,2304]{1,0:T(8,128)(2,1)S(1)} convert(f32[80,2304]{1,0:T(8,128)} %get-tuple-element.29) | non-fusion elementwise | flops 184320 | bytes 1105920 | tf_op jit(solution)/shard_map/convert_element_type | solution.py:357
  94.6 5.0 %collective-permute-done.19 = f32[80,256]{1,0:T(8,128)S(1)} collective-permute-done((f32[80,256]{1,0:T(8,128)S(1)}, f32[80,256]{1,0:T(8,128)S(1)}, u32[]{:S(2)}, u32[]{:S(2)}) %collective-permute-start.19) | collective-permute-done | bytes 81952 | tf_op jit(solution)/shard_map/ppermute | solution.py:347
  99.8 1.9 %fusion.1 = f32[240,2048]{1,0:T(8,128)S(1)} fusion(s32[1024]{0:T(1024)S(1)} %pad_add_fusion, bf16[80,1024]{1,0:T(8,128)(2,1)S(1)} %get-tuple-element.45, bf16[80,1024]{1,0:T(8,128)(2,1)S(1)} %get-tuple-element.44, bf16[80,1024]{1,0:T(8,128)(2,1)S(1)} %get-tuple-element.43), kind=kOutput, calls=%fused_computation.4 | convolution fusion | flops 1010204672 | bytes 2461696 | tf_op jit(solution)/shard_map/dot_general | solution.py:273
  (122 shorter events, 20.3 us)
Async XLA Ops:
  0.6 16.9 %copy-start = (s32[24]{0:T(128)S(1)}, s32[24]{0:T(128)}, u32[]{:S(2)}) copy-start(s32[24]{0:T(128)} %param.19) | copy-start | bytes 292
  0.6 16.7 %copy-start.2 = (bf16[80,8,256]{2,1,0:T(8,128)(2,1)S(1)}, bf16[80,8,256]{2,1,0:T(8,128)(2,1)}, u32[]{:S(2)}) copy-start(bf16[80,8,256]{2,1,0:T(8,128)(2,1)} %param.10) | copy-start | bytes 983044
  0.7 19.6 %copy-start.19 = (f32[80]{0:T(128)S(1)}, f32[80]{0:T(128)}, u32[]{:S(2)}) copy-start(f32[80]{0:T(128)} %param.13) | copy-start | bytes 964
  0.7 20.3 %copy-start.20 = (f32[80]{0:T(128)S(1)}, f32[80]{0:T(128)}, u32[]{:S(2)}) copy-start(f32[80]{0:T(128)} %param.14) | copy-start | bytes 964
  0.7 21.0 %copy-start.21 = (f32[80]{0:T(128)S(1)}, f32[80]{0:T(128)}, u32[]{:S(2)}) copy-start(f32[80]{0:T(128)} %param.12) | copy-start | bytes 964
  2.1 22.1 %collective-permute-start.6 = (s32[256]{0:T(256)S(1)}, s32[256]{0:T(256)S(1)}, u32[]{:S(2)}, u32[]{:S(2)}) collective-permute-start(s32[256]{0:T(256)S(1)} %bitcast.81), channel_id=1, source_target_pairs={{0,12},{4,0},{8,4},{12,8},{1,13},{5,1},{9,5},{13,9},{2,14},{6,2},{... | collective-permute-start | bytes 3080 | tf_op jit(solution)/shard_map/ppermute | solution.py:300
  7.2 18.2 %collective-permute-start.5 = (s32[256]{0:T(256)S(1)}, s32[256]{0:T(256)S(1)}, u32[]{:S(2)}, u32[]{:S(2)}) collective-permute-start(s32[256]{0:T(256)S(1)} %bitcast.80), channel_id=1, source_target_pairs={{0,8},{4,12},{8,0},{12,4},{1,9},{5,13},{9,1},{13,5},{2,10},{6,14},... | collective-permute-start | bytes 3080 | tf_op jit(solution)/shard_map/ppermute | solution.py:300
  7.2 21.3 %collective-permute-start.4 = (s32[256]{0:T(256)S(1)}, s32[256]{0:T(256)S(1)}, u32[]{:S(2)}, u32[]{:S(2)}) collective-permute-start(s32[256]{0:T(256)S(1)} %bitcast.79), channel_id=1, source_target_pairs={{0,4},{4,8},{8,12},{12,0},{1,5},{5,9},{9,13},{13,1},{2,6},{6,10},{... | collective-permute-start | bytes 3080 | tf_op jit(solution)/shard_map/ppermute | solution.py:300
  10.3 13.1 %copy-start.3 = (bf16[80,6,384]{2,0,1:T(8,128)(2,1)S(1)}, bf16[80,6,384]{2,0,1:T(8,128)(2,1)}, u32[]{:S(2)}) copy-start(bf16[80,6,384]{2,0,1:T(8,128)(2,1)} %param.11) | copy-start | bytes 1105924
  10.4 18.2 %collective-permute-start = (bf16[80,640]{1,0:T(8,128)(2,1)S(1)}, bf16[80,640]{1,0:T(8,128)(2,1)S(1)}, u32[]{:S(2)}, u32[]{:S(2)}) collective-permute-start(bf16[80,640]{1,0:T(8,128)(2,1)S(1)} %pad_maximum_fusion.1), channel_id=1, source_target_pairs={{0,4},{4,8},{8,12},{1,5},{5,9},{9,13},{2,6},{6,10},{10,14},{3,7},{... | collective-permute-start | bytes 307208 | tf_op jit(solution)/shard_map/ppermute | solution.py:35
  15.0 14.2 %collective-permute-start.1 = (bf16[80,640]{1,0:T(8,128)(2,1)S(1)}, bf16[80,640]{1,0:T(8,128)(2,1)S(1)}, u32[]{:S(2)}, u32[]{:S(2)}) collective-permute-start(bf16[80,640]{1,0:T(8,128)(2,1)S(1)} %pad_maximum_fusion.2), channel_id=1, source_target_pairs={{4,0},{8,4},{12,8},{5,1},{9,5},{13,9},{6,2},{10,6},{14,10},{7,3},{... | collective-permute-start | bytes 307208 | tf_op jit(solution)/shard_map/ppermute | solution.py:36
  24.2 5.6 %collective-permute-start.3 = (bf16[80,14]{1,0:T(8,128)(2,1)S(1)}, bf16[80,14]{1,0:T(8,128)(2,1)S(1)}, u32[]{:S(2)}, u32[]{:S(2)}) collective-permute-start(bf16[80,14]{1,0:T(8,128)(2,1)S(1)} %copy.49), channel_id=1, source_target_pairs={{1,0},{2,1},{3,2},{5,4},{6,5},{7,6},{9,8},{10,9},{11,10},{13,12},{... | collective-permute-start | bytes 6728 | tf_op jit(solution)/shard_map/ppermute | solution.py:38
  25.5 4.3 %collective-permute-start.2 = (bf16[80,14]{1,0:T(8,128)(2,1)S(1)}, bf16[80,14]{1,0:T(8,128)(2,1)S(1)}, u32[]{:S(2)}, u32[]{:S(2)}) collective-permute-start(bf16[80,14]{1,0:T(8,128)(2,1)S(1)} %copy.46), channel_id=1, source_target_pairs={{0,1},{1,2},{2,3},{4,5},{5,6},{6,7},{8,9},{9,10},{10,11},{12,13},{... | collective-permute-start | bytes 6728 | tf_op jit(solution)/shard_map/ppermute | solution.py:37
  33.6 7.3 %copy-start.15 = (bf16[80,14]{1,0:T(8,128)(2,1)S(1)}, bf16[80,14]{1,0:T(8,128)(2,1)}, u32[]{:S(2)}) copy-start(bf16[80,14]{1,0:T(8,128)(2,1)} %copy-done.14) | copy-start | bytes 6724
  33.6 8.0 %copy-start.17 = (bf16[80,14]{1,0:T(8,128)(2,1)S(1)}, bf16[80,14]{1,0:T(8,128)(2,1)}, u32[]{:S(2)}) copy-start(bf16[80,14]{1,0:T(8,128)(2,1)} %copy-done.16) | copy-start | bytes 6724
  36.7 6.8 %collective-permute-start.9 = (f32[80,256]{1,0:T(8,128)S(1)}, f32[80,256]{1,0:T(8,128)S(1)}, u32[]{:S(2)}, u32[]{:S(2)}) collective-permute-start(f32[80,256]{1,0:T(8,128)S(1)} %get-tuple-element.50), channel_id=1, source_target_pairs={{0,12},{4,0},{8,4},{12,8},{1,13},{5,1},{9,5},{13,9},{2,14},{6,2},{... | collective-permute-start | bytes 245768 | tf_op jit(solution)/shard_map/ppermute | solution.py:305
  39.7 9.5 %collective-permute-start.8 = (f32[80,256]{1,0:T(8,128)S(1)}, f32[80,256]{1,0:T(8,128)S(1)}, u32[]{:S(2)}, u32[]{:S(2)}) collective-permute-start(f32[80,256]{1,0:T(8,128)S(1)} %get-tuple-element.51), channel_id=1, source_target_pairs={{0,8},{4,12},{8,0},{12,4},{1,9},{5,13},{9,1},{13,5},{2,10},{6,14},... | collective-permute-start | bytes 245768 | tf_op jit(solution)/shard_map/ppermute | solution.py:305
  40.9 8.4 %collective-permute-start.7 = (f32[80,256]{1,0:T(8,128)S(1)}, f32[80,256]{1,0:T(8,128)S(1)}, u32[]{:S(2)}, u32[]{:S(2)}) collective-permute-start(f32[80,256]{1,0:T(8,128)S(1)} %get-tuple-element.52), channel_id=1, source_target_pairs={{0,4},{4,8},{8,12},{12,0},{1,5},{5,9},{9,13},{13,1},{2,6},{6,10},{... | collective-permute-start | bytes 245768 | tf_op jit(solution)/shard_map/ppermute | solution.py:305
  49.3 16.7 %copy-start.4 = (f32[80,256]{1,0:T(8,128)}, f32[80,256]{1,0:T(8,128)S(1)}, u32[]{:S(2)}) copy-start(f32[80,256]{1,0:T(8,128)S(1)} %fusion.25.refs_1_) | copy-start | bytes 245764
  54.0 8.1 %collective-permute-start.10 = (bf16[80,384]{1,0:T(8,128)(2,1)}, bf16[80,384]{1,0:T(8,128)(2,1)S(1)}, u32[]{:S(2)}, u32[]{:S(2)}) collective-permute-start(bf16[80,384]{1,0:T(8,128)(2,1)} %get-tuple-element.19), channel_id=1, source_target_pairs={{0,4},{4,8},{8,12},{1,5},{5,9},{9,13},{2,6},{6,10},{10,14},{3,7},{... | collective-permute-start | bytes 184328 | tf_op jit(solution)/shard_map/ppermute | solution.py:35
  55.4 6.8 %collective-permute-start.11 = (bf16[80,384]{1,0:T(8,128)(2,1)}, bf16[80,384]{1,0:T(8,128)(2,1)S(1)}, u32[]{:S(2)}, u32[]{:S(2)}) collective-permute-start(bf16[80,384]{1,0:T(8,128)(2,1)} %get-tuple-element.20), channel_id=1, source_target_pairs={{4,0},{8,4},{12,8},{5,1},{9,5},{13,9},{6,2},{10,6},{14,10},{7,3},{... | collective-permute-start | bytes 184328 | tf_op jit(solution)/shard_map/ppermute | solution.py:36
  56.7 3.2 %collective-permute-start.12 = (bf16[80,6]{1,0:T(8,128)(2,1)}, bf16[80,6]{1,0:T(8,128)(2,1)S(1)}, u32[]{:S(2)}, u32[]{:S(2)}) collective-permute-start(bf16[80,6]{1,0:T(8,128)(2,1)} %get-tuple-element.21), channel_id=1, source_target_pairs={{0,1},{1,2},{2,3},{4,5},{5,6},{6,7},{8,9},{9,10},{10,11},{12,13},{... | collective-permute-start | bytes 2888 | tf_op jit(solution)/shard_map/ppermute | solution.py:37
  58.6 3.5 %collective-permute-start.13 = (bf16[80,6]{1,0:T(8,128)(2,1)}, bf16[80,6]{1,0:T(8,128)(2,1)S(1)}, u32[]{:S(2)}, u32[]{:S(2)}) collective-permute-start(bf16[80,6]{1,0:T(8,128)(2,1)} %get-tuple-element.22), channel_id=1, source_target_pairs={{1,0},{2,1},{3,2},{5,4},{6,5},{7,6},{9,8},{10,9},{11,10},{13,12},{... | collective-permute-start | bytes 2888 | tf_op jit(solution)/shard_map/ppermute | solution.py:38
  66.1 12.4 %collective-permute-start.16 = (bf16[80,6]{1,0:T(8,128)(2,1)}, bf16[80,6]{1,0:T(8,128)(2,1)S(1)}, u32[]{:S(2)}, u32[]{:S(2)}) collective-permute-start(bf16[80,6]{1,0:T(8,128)(2,1)} %get-tuple-element.26), channel_id=1, source_target_pairs={{0,1},{1,2},{2,3},{4,5},{5,6},{6,7},{8,9},{9,10},{10,11},{12,13},{... | collective-permute-start | bytes 2888 | tf_op jit(solution)/shard_map/ppermute | solution.py:37
  70.4 8.1 %collective-permute-start.17 = (bf16[80,6]{1,0:T(8,128)(2,1)}, bf16[80,6]{1,0:T(8,128)(2,1)S(1)}, u32[]{:S(2)}, u32[]{:S(2)}) collective-permute-start(bf16[80,6]{1,0:T(8,128)(2,1)} %get-tuple-element.27), channel_id=1, source_target_pairs={{1,0},{2,1},{3,2},{5,4},{6,5},{7,6},{9,8},{10,9},{11,10},{13,12},{... | collective-permute-start | bytes 2888 | tf_op jit(solution)/shard_map/ppermute | solution.py:38
  71.7 7.3 %collective-permute-start.14 = (bf16[80,384]{1,0:T(8,128)(2,1)}, bf16[80,384]{1,0:T(8,128)(2,1)S(1)}, u32[]{:S(2)}, u32[]{:S(2)}) collective-permute-start(bf16[80,384]{1,0:T(8,128)(2,1)} %get-tuple-element.24), channel_id=1, source_target_pairs={{0,4},{4,8},{8,12},{1,5},{5,9},{9,13},{2,6},{6,10},{10,14},{3,7},{... | collective-permute-start | bytes 184328 | tf_op jit(solution)/shard_map/ppermute | solution.py:35
  76.4 6.8 %collective-permute-start.15 = (bf16[80,384]{1,0:T(8,128)(2,1)}, bf16[80,384]{1,0:T(8,128)(2,1)S(1)}, u32[]{:S(2)}, u32[]{:S(2)}) collective-permute-start(bf16[80,384]{1,0:T(8,128)(2,1)} %get-tuple-element.25), channel_id=1, source_target_pairs={{4,0},{8,4},{12,8},{5,1},{9,5},{13,9},{6,2},{10,6},{14,10},{7,3},{... | collective-permute-start | bytes 184328 | tf_op jit(solution)/shard_map/ppermute | solution.py:36
  78.5 4.8 %copy-start.10 = (bf16[80,6]{1,0:T(8,128)(2,1)}, bf16[80,6]{1,0:T(8,128)(2,1)S(1)}, u32[]{:S(2)}) copy-start(bf16[80,6]{1,0:T(8,128)(2,1)S(1)} %collective-permute-done.16.refs_5_) | copy-start | bytes 2884
  78.5 4.8 %copy-start.11 = (bf16[80,6]{1,0:T(8,128)(2,1)}, bf16[80,6]{1,0:T(8,128)(2,1)S(1)}, u32[]{:S(2)}) copy-start(bf16[80,6]{1,0:T(8,128)(2,1)S(1)} %collective-permute-done.17.refs_6_) | copy-start | bytes 2884
  88.5 6.1 %collective-permute-start.20 = (f32[80,256]{1,0:T(8,128)S(1)}, f32[80,256]{1,0:T(8,128)S(1)}, u32[]{:S(2)}, u32[]{:S(2)}) collective-permute-start(f32[80,256]{1,0:T(8,128)S(1)} %get-tuple-element.47), channel_id=1, source_target_pairs={{0,12},{4,0},{8,4},{12,8},{1,13},{5,1},{9,5},{13,9},{2,14},{6,2},{... | collective-permute-start | bytes 245768 | tf_op jit(solution)/shard_map/ppermute | solution.py:347
  89.7 9.9 %collective-permute-start.19 = (f32[80,256]{1,0:T(8,128)S(1)}, f32[80,256]{1,0:T(8,128)S(1)}, u32[]{:S(2)}, u32[]{:S(2)}) collective-permute-start(f32[80,256]{1,0:T(8,128)S(1)} %get-tuple-element.48), channel_id=1, source_target_pairs={{0,8},{4,12},{8,0},{12,4},{1,9},{5,13},{9,1},{13,5},{2,10},{6,14},... | collective-permute-start | bytes 245768 | tf_op jit(solution)/shard_map/ppermute | solution.py:347
  92.1 7.6 %collective-permute-start.18 = (f32[80,256]{1,0:T(8,128)S(1)}, f32[80,256]{1,0:T(8,128)S(1)}, u32[]{:S(2)}, u32[]{:S(2)}) collective-permute-start(f32[80,256]{1,0:T(8,128)S(1)} %get-tuple-element.49), channel_id=1, source_target_pairs={{0,4},{4,8},{8,12},{12,0},{1,5},{5,9},{9,13},{13,1},{2,6},{6,10},{... | collective-permute-start | bytes 245768 | tf_op jit(solution)/shard_map/ppermute | solution.py:347
  (11 other events, 15.0 us)

commit v11 on v10

--- a/solution.py
+++ b/solution.py
@@ -40,12 +40,9 @@
     xo = 0
     yo = 0
     for e in edge_sets:
-        w, h = e[0].shape[1], e[2].shape[1]
-        out.append(
-            (above[:, xo : xo + w], below[:, xo : xo + w], left[:, yo : yo + h], right[:, yo : yo + h])
-        )
-        xo += w
-        yo += h
+        out.append(((above, below, left, right), xo, yo))
+        xo += e[0].shape[1]
+        yo += e[2].shape[1]
     return out
 
 
@@ -74,7 +71,7 @@
     return down + up + east + west - 4.0 * flat
 
 
-def step_kernel(*refs, rows, cols, nest, split, gap):
+def step_kernel(*refs, rows, cols, xo, yo, nest, split, gap):
     refs = list(refs)
     if gap:
         expand_ref, fblock_ref = refs[:2]
@@ -97,10 +94,10 @@
     n = rows * cols
     state = state_ref[...].astype(jnp.float32)
     levels = state.shape[0]
-    up_sc[:, 0:cols] = above_ref[...].astype(jnp.float32)
+    up_sc[:, 0:cols] = above_ref[:, xo : xo + cols].astype(jnp.float32)
     up_sc[:, cols:n] = state[:, 0 : n - cols]
     dn_sc[:, 0 : n - cols] = state[:, cols:n]
-    dn_sc[:, n - cols : n] = below_ref[...].astype(jnp.float32)
+    dn_sc[:, n - cols : n] = below_ref[:, xo : xo + cols].astype(jnp.float32)
     up = up_sc[...]
     down = dn_sc[...]
     lane = lax.broadcasted_iota(jnp.int32, (levels, n), 1)
@@ -109,8 +106,8 @@
     west = pltpu.roll(state, 1, 1)
     east = pltpu.roll(state, n - 1, 1)
     for r in range(rows):
-        west = jnp.where(lane == r * cols, left[:, r : r + 1], west)
-        east = jnp.where(lane == r * cols + cols - 1, right[:, r : r + 1], east)
+        west = jnp.where(lane == r * cols, left[:, yo + r : yo + r + 1], west)
+        east = jnp.where(lane == r * cols + cols - 1, right[:, yo + r : yo + r + 1], east)
     if nest:
         down = down * dnw_ref[...]
         up = up * upw_ref[...]
@@ -152,12 +149,12 @@
             )
 
 
-def stencil_step(state, halo, nu, vert_mix, rows, cols, forcing=None, up_w=None, down_w=None, relax=None,
-                 split=False, gap_of=None):
+def stencil_step(state, placed_halo, nu, vert_mix, rows, cols, forcing=None, up_w=None, down_w=None,
+                 relax=None, split=False, gap_of=None):
     levels = state.shape[0]
     n = rows * cols
     nest = forcing is not None
-    above, below, left, right = halo
+    (above, below, left, right), xo, yo = placed_halo
     if nest:
         args = (state, above, below, left, right, forcing, up_w[None, :], down_w[None, :],
                 nu[:, None], relax[:, None], vert_mix)
@@ -179,7 +176,9 @@
     flops = 2 * levels * levels * n * 6 + 4 * levels * n * rows + 20 * levels * n
     moved_bytes = sum(int(a.size) * a.dtype.itemsize for a in args) + levels * n * 4
     outs = pl.pallas_call(
-        functools.partial(step_kernel, rows=rows, cols=cols, nest=nest, split=split, gap=gap),
+        functools.partial(
+            step_kernel, rows=rows, cols=cols, xo=xo, yo=yo, nest=nest, split=split, gap=gap
+        ),
         out_shape=out_shape,
         scratch_shapes=[pltpu.VMEM((levels, n), jnp.float32), pltpu.VMEM((levels, n), jnp.float32)],
         cost_estimate=pl.CostEstimate(flops=flops, bytes_accessed=moved_bytes, transcendentals=0),
@@ -300,11 +299,11 @@
             lax.ppermute(wanted[s], "gx", shifted_pairs(tiles_x, s)) for s in range(1, tiles_x)
         ]
         served_ids = jnp.concatenate(served, axis=0)
-        replies = gather_parts(parent_parts, served_ids)
-        back = [replies[:, 0:requests]] + [
-            lax.ppermute(replies[:, s * requests : (s + 1) * requests], "gx", shifted_pairs(tiles_x, -s))
+        back = [None] + [
+            lax.ppermute(gather_parts(parent_parts, served[s]), "gx", shifted_pairs(tiles_x, -s))
             for s in range(1, tiles_x)
         ]
+        back[0] = gather_parts(parent_parts, served[0])
         forcing_flat = back[0]
         for s in range(1, tiles_x):
             forcing_flat = jnp.where(chosen[s][None, :], back[s], forcing_flat)

time: 103 us -> 99.6 us (0.967)
  local copies, waits for them, and re-layouts: 18.1 us -> 14.3 us
  starting transfers between devices: 42.1 us -> 40.4 us
  waiting for transfers between devices: 17.9 us -> 19.1 us
    slice x7 -> x0, local copies, waits for them, and re-layouts: 3.88 us -> none  [the longest x2 1.25 us: exchange(): below[:, xo:xo + w]]
    ppermute x3, starting transfers between devices: 6.14 us -> 8.1 us  [body(): lax.ppermute(wanted[s], 'gx', shifted_pairs(tiles_x, s))]
    ppermute x3, starting transfers between devices: 4.16 us -> 2.27 us  [body(): lax.ppermute(gather_parts(parent_parts, served[s]), 'gx', shifted_pairs(t...]
    ppermute x3, starting transfers between devices: 10.7 us -> 9.45 us  [exchange(): above = lax.ppermute(last_rows, 'gx', fwd_x)]
    dot_general x1 -> x4, matrix products: 3.02 us -> 3.53 us  [gather_parts(): total = jnp.dot(parts, onehot, preferred_element_type=jnp.float32)]
    unnamed x58 -> x60, local copies, waits for them, and re-layouts: 6.33 us -> 6.37 us
  transfers between devices with their start and end apart: 21 -> 21, of which waited for: 6 -> 6; matrix products, arithmetic and copies ran while one was open for 16% -> 16% of each run, Pallas kernels for 0% -> 3%
where the time goes in v11:
time: 99.6 us; the launch traced here: 98.9 us
  starting transfers between devices  40.4 us (41%)
  waiting for transfers between devices  19.1 us (19%)
  local copies, waits for them, and re-layouts  14.3 us (14%)
  Pallas kernels  13.2 us (13%)
  matrix products  5.99 us (6%)
  other arithmetic  4.76 us (5%)
  between operations  1.2 us (1%)
    pallas_call x4, Pallas kernels, stencil_step(): pl.pallas_call(functools.partial(step_kernel, rows=rows, cols=cols, xo=xo...  13.2 us
    ppermute x3, starting transfers between devices, exchange(): above = lax.ppermute(last_rows, 'gx', fwd_x)  9.45 us
    ppermute x3, starting transfers between devices, exchange(): left = lax.ppermute(last_cols, Y_AXES, fwd_y)  9.04 us
    ppermute x3, starting transfers between devices, body(): lax.ppermute(wanted[s], 'gx', shifted_pairs(tiles_x, s))  8.1 us
    ppermute x3, waiting for transfers between devices, body(): lax.ppermute(gather_parts(parent_parts, served[s]), 'gx', shifted_pairs(t...  6.77 us
    unnamed x60, local copies, waits for them, and re-layouts  6.37 us
    ppermute x3, waiting for transfers between devices, body(): lax.ppermute(outgoing[s], 'gx', shifted_pairs(tiles_x, s))  5.1 us
    ppermute x3, waiting for transfers between devices, exchange(): below = lax.ppermute(first_rows, 'gx', bwd_x)  4.33 us
  transfers between devices with their start and end apart: 21, of which 6 were waited for; matrix products, arithmetic and copies ran while one was open for 16% of the time, Pallas kernels for 3%

profile of v11, /device:TPU:0, one launch (start us, length us, event | category | flops | bytes accessed | tf_op | source)
XLA Modules:
  0.0 98.9 jit_solution(1796870788483990007)
XLA Ops:
  2.1 3.1 %collective-permute-start.8 = (s32[256]{0:T(256)S(1)}, s32[256]{0:T(256)S(1)}, u32[]{:S(2)}, u32[]{:S(2)}) collective-permute-start(s32[256]{0:T(256)S(1)} %bitcast.81), channel_id=1, source_target_pairs={{0,4},{4,8},{8,12},{12,0},{1,5},{5,9},{9,13},{13,1},{2,6},{6,10},{... | collective-permute-start | bytes 3080 | tf_op jit(solution)/shard_map/ppermute | solution.py:299
  6.1 1.2 %fusion.43 = (bf16[80,1,256]{2,1,0:T(2,128)(2,1)S(1)}, bf16[80,1,256]{2,1,0:T(2,128)(2,1)S(1)}) fusion(bf16[80,8,256]{2,1,0:T(8,128)(2,1)} %param.10), kind=kLoop, calls=%fused_computation.107 | loop fusion | bytes 163840 | tf_op jit(solution)/shard_map/slice | solution.py:21
  7.4 3.6 %collective-permute-start = (bf16[80,640]{1,0:T(8,128)(2,1)S(1)}, bf16[80,640]{1,0:T(8,128)(2,1)S(1)}, u32[]{:S(2)}, u32[]{:S(2)}) collective-permute-start(bf16[80,640]{1,0:T(8,128)(2,1)S(1)} %pad_maximum_fusion.1), channel_id=1, source_target_pairs={{0,4},{4,8},{8,12},{1,5},{5,9},{9,13},{2,6},{6,10},{10,14},{3,7},{... | collective-permute-start | bytes 307208 | tf_op jit(solution)/shard_map/ppermute | solution.py:35
  11.0 1.3 %collective-permute-start.1 = (bf16[80,640]{1,0:T(8,128)(2,1)S(1)}, bf16[80,640]{1,0:T(8,128)(2,1)S(1)}, u32[]{:S(2)}, u32[]{:S(2)}) collective-permute-start(bf16[80,640]{1,0:T(8,128)(2,1)S(1)} %pad_maximum_fusion.2), channel_id=1, source_target_pairs={{4,0},{8,4},{12,8},{5,1},{9,5},{13,9},{6,2},{10,6},{14,10},{7,3},{... | collective-permute-start | bytes 307208 | tf_op jit(solution)/shard_map/ppermute | solution.py:36
  12.3 1.1 %fusion.41 = (bf16[80,6,1]{2,0,1:T(8,128)(2,1)S(1)}, bf16[80,6,1]{2,0,1:T(8,128)(2,1)S(1)}) fusion(bf16[80,6,384]{2,0,1:T(8,128)(2,1)} %param.11), kind=kLoop, calls=%fused_computation.105 | loop fusion | bytes 3840 | tf_op jit(solution)/shard_map/slice | solution.py:21
  14.0 1.3 %collective-permute-start.3 = (bf16[80,14]{1,0:T(8,128)(2,1)S(1)}, bf16[80,14]{1,0:T(8,128)(2,1)S(1)}, u32[]{:S(2)}, u32[]{:S(2)}) collective-permute-start(bf16[80,14]{1,0:T(8,128)(2,1)S(1)} %copy.49), channel_id=1, source_target_pairs={{1,0},{2,1},{3,2},{5,4},{6,5},{7,6},{9,8},{10,9},{11,10},{13,12},{... | collective-permute-start | bytes 6728 | tf_op jit(solution)/shard_map/ppermute | solution.py:38
  15.7 3.0 %collective-permute-start.2 = (bf16[80,14]{1,0:T(8,128)(2,1)S(1)}, bf16[80,14]{1,0:T(8,128)(2,1)S(1)}, u32[]{:S(2)}, u32[]{:S(2)}) collective-permute-start(bf16[80,14]{1,0:T(8,128)(2,1)S(1)} %copy.46), channel_id=1, source_target_pairs={{0,1},{1,2},{2,3},{4,5},{5,6},{6,7},{8,9},{9,10},{10,11},{12,13},{... | collective-permute-start | bytes 6728 | tf_op jit(solution)/shard_map/ppermute | solution.py:37
  24.6 3.7 %collective-permute-start.6 = (s32[256]{0:T(256)S(1)}, s32[256]{0:T(256)S(1)}, u32[]{:S(2)}, u32[]{:S(2)}) collective-permute-start(s32[256]{0:T(256)S(1)} %bitcast.79), channel_id=1, source_target_pairs={{0,8},{4,12},{8,0},{12,4},{1,9},{5,13},{9,1},{13,5},{2,10},{6,14},... | collective-permute-start | bytes 3080 | tf_op jit(solution)/shard_map/ppermute | solution.py:299
  28.2 1.4 %collective-permute-start.4 = (s32[256]{0:T(256)S(1)}, s32[256]{0:T(256)S(1)}, u32[]{:S(2)}, u32[]{:S(2)}) collective-permute-start(s32[256]{0:T(256)S(1)} %bitcast.80), channel_id=1, source_target_pairs={{0,12},{4,0},{8,4},{12,8},{1,13},{5,1},{9,5},{13,9},{2,14},{6,2},{... | collective-permute-start | bytes 3080 | tf_op jit(solution)/shard_map/ppermute | solution.py:299
  30.3 3.2 %shard_map.113 = (f32[80,2048]{1,0:T(8,128)}, bf16[80,256]{1,0:T(8,128)(2,1)}, bf16[80,256]{1,0:T(8,128)(2,1)}, bf16[80,8]{1,0:T(8,128)(2,1)}, bf16[80,8]{1,0:T(8,128)(2,1)}, /*index=5*/bf16[240,2048]{1,0:T(8,128)(2,1)}) custom-call(bf16[80,2048]{1,0:T(8,128)(2,1)} %bitcast.60, bf16[80,640]{1,0:T(8,128)(2,1)} %copy-done.6, bf16[80,640]{1,0:T(8,128)(2,1)} %copy-done.7, ...), custom_call_target="tpu_custom_call" | custom-call | flops 165806080 | bytes 1218240 | tf_op jit(solution)/shard_map/pallas_call | solution.py:178
  33.4 1.9 %fusion.4 = f32[240,256]{1,0:T(8,128)S(1)} fusion(bf16[240,2048]{1,0:T(8,128)(2,1)} %get-tuple-element.17, s32[256]{0:T(256)S(1)} %collective-permute-done.8), kind=kOutput, calls=%fused_computation.10 | convolution fusion | flops 252182528 | bytes 1229824 | tf_op jit(solution)/shard_map/dot_general | solution.py:264
  36.8 2.0 %collective-permute-start.7 = (f32[80,256]{1,0:T(8,128)S(1)}, f32[80,256]{1,0:T(8,128)S(1)}, u32[]{:S(2)}, u32[]{:S(2)}) collective-permute-start(f32[80,256]{1,0:T(8,128)S(1)} %slice_add_fusion.6), channel_id=1, source_target_pairs={{0,8},{4,12},{8,0},{12,4},{1,9},{5,13},{9,1},{13,5},{2,10},{6,14},... | collective-permute-start | bytes 245768 | tf_op jit(solution)/shard_map/ppermute | solution.py:303
  39.4 0.9 collective-permute-done.9
  40.3 5.9 %collective-permute-done.7 = f32[80,256]{1,0:T(8,128)S(1)} collective-permute-done((f32[80,256]{1,0:T(8,128)S(1)}, f32[80,256]{1,0:T(8,128)S(1)}, u32[]{:S(2)}, u32[]{:S(2)}) %collective-permute-start.7) | collective-permute-done | bytes 81952 | tf_op jit(solution)/shard_map/ppermute | solution.py:303
  47.7 3.1 %shard_map.114 = (f32[80,2304]{1,0:T(8,128)}, bf16[80,384]{1,0:T(8,128)(2,1)}, bf16[80,384]{1,0:T(8,128)(2,1)}, bf16[80,6]{1,0:T(8,128)(2,1)}, bf16[80,6]{1,0:T(8,128)(2,1)}) custom-call(bf16[80,2304]{1,0:T(8,128)(2,1)} %bitcast.57, bf16[80,640]{1,0:T(8,128)(2,1)} %copy-done.6, bf16[80,640]{1,0:T(8,128)(2,1)} %copy-done.7, bf16[80,14]{1,0:T(8,128)(2,1)} %copy-done.9, ...), custom_call_target="tpu_custom_call" | custom-call | flops 185057280 | bytes 2097152 | tf_op jit(solution)/shard_map/pallas_call | solution.py:178
  50.9 1.3 %collective-permute-start.10 = (bf16[80,384]{1,0:T(8,128)(2,1)}, bf16[80,384]{1,0:T(8,128)(2,1)S(1)}, u32[]{:S(2)}, u32[]{:S(2)}) collective-permute-start(bf16[80,384]{1,0:T(8,128)(2,1)} %get-tuple-element.19), channel_id=1, source_target_pairs={{0,4},{4,8},{8,12},{1,5},{5,9},{9,13},{2,6},{6,10},{10,14},{3,7},{... | collective-permute-start | bytes 184328 | tf_op jit(solution)/shard_map/ppermute | solution.py:35
  52.2 1.3 %collective-permute-start.11 = (bf16[80,384]{1,0:T(8,128)(2,1)}, bf16[80,384]{1,0:T(8,128)(2,1)S(1)}, u32[]{:S(2)}, u32[]{:S(2)}) collective-permute-start(bf16[80,384]{1,0:T(8,128)(2,1)} %get-tuple-element.20), channel_id=1, source_target_pairs={{4,0},{8,4},{12,8},{5,1},{9,5},{13,9},{6,2},{10,6},{14,10},{7,3},{... | collective-permute-start | bytes 184328 | tf_op jit(solution)/shard_map/ppermute | solution.py:36
  53.5 1.6 %collective-permute-start.12 = (bf16[80,6]{1,0:T(8,128)(2,1)}, bf16[80,6]{1,0:T(8,128)(2,1)S(1)}, u32[]{:S(2)}, u32[]{:S(2)}) collective-permute-start(bf16[80,6]{1,0:T(8,128)(2,1)} %get-tuple-element.21), channel_id=1, source_target_pairs={{0,1},{1,2},{2,3},{4,5},{5,6},{6,7},{8,9},{9,10},{10,11},{12,13},{... | collective-permute-start | bytes 2888 | tf_op jit(solution)/shard_map/ppermute | solution.py:37
  55.1 1.3 %collective-permute-start.13 = (bf16[80,6]{1,0:T(8,128)(2,1)}, bf16[80,6]{1,0:T(8,128)(2,1)S(1)}, u32[]{:S(2)}, u32[]{:S(2)}) collective-permute-start(bf16[80,6]{1,0:T(8,128)(2,1)} %get-tuple-element.22), channel_id=1, source_target_pairs={{1,0},{2,1},{3,2},{5,4},{6,5},{7,6},{9,8},{10,9},{11,10},{13,12},{... | collective-permute-start | bytes 2888 | tf_op jit(solution)/shard_map/ppermute | solution.py:38
  56.4 2.4 %collective-permute-done.13.refs_4_ = bf16[80,6]{1,0:T(8,128)(2,1)S(1)} collective-permute-done((bf16[80,6]{1,0:T(8,128)(2,1)}, bf16[80,6]{1,0:T(8,128)(2,1)S(1)}, u32[]{:S(2)}, u32[]{:S(2)}) %collective-permute-start.13) | collective-permute-done | bytes 992 | tf_op jit(solution)/shard_map/ppermute | solution.py:38
  59.5 3.2 %shard_map.115 = (f32[80,2304]{1,0:T(8,128)}, bf16[80,384]{1,0:T(8,128)(2,1)}, bf16[80,384]{1,0:T(8,128)(2,1)}, bf16[80,6]{1,0:T(8,128)(2,1)}, bf16[80,6]{1,0:T(8,128)(2,1)}) custom-call(f32[80,2304]{1,0:T(8,128)} %get-tuple-element.18.refs_0_, bf16[80,384]{1,0:T(8,128)(2,1)} %copy-done.12, bf16[80,384]{1,0:T(8,128)(2,1)} %copy-done.13, ...), custom_call_target="tpu_custom_call" | custom-call | flops 185057280 | bytes 2381312 | tf_op jit(solution)/shard_map/pallas_call | solution.py:178
  62.7 4.4 %collective-permute-start.16 = (bf16[80,6]{1,0:T(8,128)(2,1)}, bf16[80,6]{1,0:T(8,128)(2,1)S(1)}, u32[]{:S(2)}, u32[]{:S(2)}) collective-permute-start(bf16[80,6]{1,0:T(8,128)(2,1)} %get-tuple-element.26), channel_id=1, source_target_pairs={{0,1},{1,2},{2,3},{4,5},{5,6},{6,7},{8,9},{9,10},{10,11},{12,13},{... | collective-permute-start | bytes 2888 | tf_op jit(solution)/shard_map/ppermute | solution.py:37
  67.1 1.3 %collective-permute-start.17 = (bf16[80,6]{1,0:T(8,128)(2,1)}, bf16[80,6]{1,0:T(8,128)(2,1)S(1)}, u32[]{:S(2)}, u32[]{:S(2)}) collective-permute-start(bf16[80,6]{1,0:T(8,128)(2,1)} %get-tuple-element.27), channel_id=1, source_target_pairs={{1,0},{2,1},{3,2},{5,4},{6,5},{7,6},{9,8},{10,9},{11,10},{13,12},{... | collective-permute-start | bytes 2888 | tf_op jit(solution)/shard_map/ppermute | solution.py:38
  68.4 4.5 %collective-permute-start.14 = (bf16[80,384]{1,0:T(8,128)(2,1)}, bf16[80,384]{1,0:T(8,128)(2,1)S(1)}, u32[]{:S(2)}, u32[]{:S(2)}) collective-permute-start(bf16[80,384]{1,0:T(8,128)(2,1)} %get-tuple-element.24), channel_id=1, source_target_pairs={{0,4},{4,8},{8,12},{1,5},{5,9},{9,13},{2,6},{6,10},{10,14},{3,7},{... | collective-permute-start | bytes 184328 | tf_op jit(solution)/shard_map/ppermute | solution.py:35
  73.0 1.3 %collective-permute-start.15 = (bf16[80,384]{1,0:T(8,128)(2,1)}, bf16[80,384]{1,0:T(8,128)(2,1)S(1)}, u32[]{:S(2)}, u32[]{:S(2)}) collective-permute-start(bf16[80,384]{1,0:T(8,128)(2,1)} %get-tuple-element.25), channel_id=1, source_target_pairs={{4,0},{8,4},{12,8},{5,1},{9,5},{13,9},{6,2},{10,6},{14,10},{7,3},{... | collective-permute-start | bytes 184328 | tf_op jit(solution)/shard_map/ppermute | solution.py:36
  75.5 4.3 %collective-permute-done.15.refs_4_ = bf16[80,384]{1,0:T(8,128)(2,1)S(1)} collective-permute-done((bf16[80,384]{1,0:T(8,128)(2,1)}, bf16[80,384]{1,0:T(8,128)(2,1)S(1)}, u32[]{:S(2)}, u32[]{:S(2)}) %collective-permute-start.15) | collective-permute-done | bytes 61472 | tf_op jit(solution)/shard_map/ppermute | solution.py:36
  80.5 3.7 %shard_map.116 = (f32[80,2304]{1,0:T(8,128)}, bf16[80,384]{1,0:T(8,128)(2,1)}, bf16[80,384]{1,0:T(8,128)(2,1)}, bf16[80,6]{1,0:T(8,128)(2,1)}, bf16[80,6]{1,0:T(8,128)(2,1)}, /*index=5*/f32[80,256]{1,0:T(8,128)}) custom-call(f32[128,384]{1,0:T(8,128)} %fusion.21.refs_0_, f32[80,256]{1,0:T(8,128)} %copy-done.4, f32[80,2304]{1,0:T(8,128)} %get-tuple-element.23.refs_2_, ...), custom_call_target="tpu_custom_call" | custom-call | flops 185057280 | bytes 2659840 | tf_op jit(solution)/shard_map/pallas_call | solution.py:178
  84.2 0.9 broadcast_select_fusion
  85.9 2.4 %collective-permute-start.19 = (f32[80,256]{1,0:T(8,128)S(1)}, f32[80,256]{1,0:T(8,128)S(1)}, u32[]{:S(2)}, u32[]{:S(2)}) collective-permute-start(f32[80,256]{1,0:T(8,128)S(1)} %get-tuple-element.48), channel_id=1, source_target_pairs={{0,8},{4,12},{8,0},{12,4},{1,9},{5,13},{9,1},{13,5},{2,10},{6,14},... | collective-permute-start | bytes 245768 | tf_op jit(solution)/shard_map/ppermute | solution.py:346
  88.9 1.2 %convert_element_type.36 = bf16[80,2304]{1,0:T(8,128)(2,1)S(1)} convert(f32[80,2304]{1,0:T(8,128)} %get-tuple-element.29) | non-fusion elementwise | flops 184320 | bytes 1105920 | tf_op jit(solution)/shard_map/convert_element_type | solution.py:356
  90.8 5.1 %collective-permute-done.19 = f32[80,256]{1,0:T(8,128)S(1)} collective-permute-done((f32[80,256]{1,0:T(8,128)S(1)}, f32[80,256]{1,0:T(8,128)S(1)}, u32[]{:S(2)}, u32[]{:S(2)}) %collective-permute-start.19) | collective-permute-done | bytes 81952 | tf_op jit(solution)/shard_map/ppermute | solution.py:346
  96.0 1.9 %fusion = f32[240,2048]{1,0:T(8,128)S(1)} fusion(s32[1024]{0:T(1024)S(1)} %pad_add_fusion, bf16[80,1024]{1,0:T(8,128)(2,1)S(1)} %get-tuple-element.45, bf16[80,1024]{1,0:T(8,128)(2,1)S(1)} %get-tuple-element.44, bf16[80,1024]{1,0:T(8,128)(2,1)S(1)} %get-tuple-element.43), kind=kOutput, calls=%fused_computation.2 | convolution fusion | flops 1010204672 | bytes 2461696 | tf_op jit(solution)/shard_map/dot_general | solution.py:272
  (122 shorter events, 19.0 us)
Async XLA Ops:
  0.6 18.2 %copy-start = (s32[24]{0:T(128)S(1)}, s32[24]{0:T(128)}, u32[]{:S(2)}) copy-start(s32[24]{0:T(128)} %param.19) | copy-start | bytes 292
  0.6 12.7 %copy-start.2 = (bf16[80,8,256]{2,1,0:T(8,128)(2,1)S(1)}, bf16[80,8,256]{2,1,0:T(8,128)(2,1)}, u32[]{:S(2)}) copy-start(bf16[80,8,256]{2,1,0:T(8,128)(2,1)} %param.10) | copy-start | bytes 983044
  0.7 20.2 %copy-start.19 = (f32[80]{0:T(128)S(1)}, f32[80]{0:T(128)}, u32[]{:S(2)}) copy-start(f32[80]{0:T(128)} %param.13) | copy-start | bytes 964
  0.7 20.9 %copy-start.20 = (f32[80]{0:T(128)S(1)}, f32[80]{0:T(128)}, u32[]{:S(2)}) copy-start(f32[80]{0:T(128)} %param.14) | copy-start | bytes 964
  0.7 21.6 %copy-start.21 = (f32[80]{0:T(128)S(1)}, f32[80]{0:T(128)}, u32[]{:S(2)}) copy-start(f32[80]{0:T(128)} %param.12) | copy-start | bytes 964
  2.1 31.3 %collective-permute-start.8 = (s32[256]{0:T(256)S(1)}, s32[256]{0:T(256)S(1)}, u32[]{:S(2)}, u32[]{:S(2)}) collective-permute-start(s32[256]{0:T(256)S(1)} %bitcast.81), channel_id=1, source_target_pairs={{0,4},{4,8},{8,12},{12,0},{1,5},{5,9},{9,13},{13,1},{2,6},{6,10},{... | collective-permute-start | bytes 3080 | tf_op jit(solution)/shard_map/ppermute | solution.py:299
  7.3 16.5 %copy-start.3 = (bf16[80,6,384]{2,0,1:T(8,128)(2,1)S(1)}, bf16[80,6,384]{2,0,1:T(8,128)(2,1)}, u32[]{:S(2)}) copy-start(bf16[80,6,384]{2,0,1:T(8,128)(2,1)} %param.11) | copy-start | bytes 1105924
  7.4 22.2 %collective-permute-start = (bf16[80,640]{1,0:T(8,128)(2,1)S(1)}, bf16[80,640]{1,0:T(8,128)(2,1)S(1)}, u32[]{:S(2)}, u32[]{:S(2)}) collective-permute-start(bf16[80,640]{1,0:T(8,128)(2,1)S(1)} %pad_maximum_fusion.1), channel_id=1, source_target_pairs={{0,4},{4,8},{8,12},{1,5},{5,9},{9,13},{2,6},{6,10},{10,14},{3,7},{... | collective-permute-start | bytes 307208 | tf_op jit(solution)/shard_map/ppermute | solution.py:35
  11.0 18.6 %collective-permute-start.1 = (bf16[80,640]{1,0:T(8,128)(2,1)S(1)}, bf16[80,640]{1,0:T(8,128)(2,1)S(1)}, u32[]{:S(2)}, u32[]{:S(2)}) collective-permute-start(bf16[80,640]{1,0:T(8,128)(2,1)S(1)} %pad_maximum_fusion.2), channel_id=1, source_target_pairs={{4,0},{8,4},{12,8},{5,1},{9,5},{13,9},{6,2},{10,6},{14,10},{7,3},{... | collective-permute-start | bytes 307208 | tf_op jit(solution)/shard_map/ppermute | solution.py:36
  14.0 10.6 %collective-permute-start.3 = (bf16[80,14]{1,0:T(8,128)(2,1)S(1)}, bf16[80,14]{1,0:T(8,128)(2,1)S(1)}, u32[]{:S(2)}, u32[]{:S(2)}) collective-permute-start(bf16[80,14]{1,0:T(8,128)(2,1)S(1)} %copy.49), channel_id=1, source_target_pairs={{1,0},{2,1},{3,2},{5,4},{6,5},{7,6},{9,8},{10,9},{11,10},{13,12},{... | collective-permute-start | bytes 6728 | tf_op jit(solution)/shard_map/ppermute | solution.py:38
  15.7 12.6 %collective-permute-start.2 = (bf16[80,14]{1,0:T(8,128)(2,1)S(1)}, bf16[80,14]{1,0:T(8,128)(2,1)S(1)}, u32[]{:S(2)}, u32[]{:S(2)}) collective-permute-start(bf16[80,14]{1,0:T(8,128)(2,1)S(1)} %copy.46), channel_id=1, source_target_pairs={{0,1},{1,2},{2,3},{4,5},{5,6},{6,7},{8,9},{9,10},{10,11},{12,13},{... | collective-permute-start | bytes 6728 | tf_op jit(solution)/shard_map/ppermute | solution.py:37
  24.6 5.0 %copy-start.8 = (bf16[80,14]{1,0:T(8,128)(2,1)}, bf16[80,14]{1,0:T(8,128)(2,1)S(1)}, u32[]{:S(2)}) copy-start(bf16[80,14]{1,0:T(8,128)(2,1)S(1)} %collective-permute-done.3.refs_4_) | copy-start | bytes 6724
  24.6 11.6 %collective-permute-start.6 = (s32[256]{0:T(256)S(1)}, s32[256]{0:T(256)S(1)}, u32[]{:S(2)}, u32[]{:S(2)}) collective-permute-start(s32[256]{0:T(256)S(1)} %bitcast.79), channel_id=1, source_target_pairs={{0,8},{4,12},{8,0},{12,4},{1,9},{5,13},{9,1},{13,5},{2,10},{6,14},... | collective-permute-start | bytes 3080 | tf_op jit(solution)/shard_map/ppermute | solution.py:299
  28.2 7.3 %collective-permute-start.4 = (s32[256]{0:T(256)S(1)}, s32[256]{0:T(256)S(1)}, u32[]{:S(2)}, u32[]{:S(2)}) collective-permute-start(s32[256]{0:T(256)S(1)} %bitcast.80), channel_id=1, source_target_pairs={{0,12},{4,0},{8,4},{12,8},{1,13},{5,1},{9,5},{13,9},{2,14},{6,2},{... | collective-permute-start | bytes 3080 | tf_op jit(solution)/shard_map/ppermute | solution.py:299
  35.3 5.0 %collective-permute-start.9 = (f32[80,256]{1,0:T(8,128)S(1)}, f32[80,256]{1,0:T(8,128)S(1)}, u32[]{:S(2)}, u32[]{:S(2)}) collective-permute-start(f32[80,256]{1,0:T(8,128)S(1)} %slice_add_fusion.4), channel_id=1, source_target_pairs={{0,12},{4,0},{8,4},{12,8},{1,13},{5,1},{9,5},{13,9},{2,14},{6,2},{... | collective-permute-start | bytes 245768 | tf_op jit(solution)/shard_map/ppermute | solution.py:303
  36.8 9.4 %collective-permute-start.7 = (f32[80,256]{1,0:T(8,128)S(1)}, f32[80,256]{1,0:T(8,128)S(1)}, u32[]{:S(2)}, u32[]{:S(2)}) collective-permute-start(f32[80,256]{1,0:T(8,128)S(1)} %slice_add_fusion.6), channel_id=1, source_target_pairs={{0,8},{4,12},{8,0},{12,4},{1,9},{5,13},{9,1},{13,5},{2,10},{6,14},... | collective-permute-start | bytes 245768 | tf_op jit(solution)/shard_map/ppermute | solution.py:303
  38.8 7.4 %collective-permute-start.5 = (f32[80,256]{1,0:T(8,128)S(1)}, f32[80,256]{1,0:T(8,128)S(1)}, u32[]{:S(2)}, u32[]{:S(2)}) collective-permute-start(f32[80,256]{1,0:T(8,128)S(1)} %slice_add_fusion.8), channel_id=1, source_target_pairs={{0,4},{4,8},{8,12},{12,0},{1,5},{5,9},{9,13},{13,1},{2,6},{6,10},{... | collective-permute-start | bytes 245768 | tf_op jit(solution)/shard_map/ppermute | solution.py:303
  46.2 16.5 %copy-start.4 = (f32[80,256]{1,0:T(8,128)}, f32[80,256]{1,0:T(8,128)S(1)}, u32[]{:S(2)}) copy-start(f32[80,256]{1,0:T(8,128)S(1)} %fusion.32.refs_1_) | copy-start | bytes 245764
  50.9 8.0 %collective-permute-start.10 = (bf16[80,384]{1,0:T(8,128)(2,1)}, bf16[80,384]{1,0:T(8,128)(2,1)S(1)}, u32[]{:S(2)}, u32[]{:S(2)}) collective-permute-start(bf16[80,384]{1,0:T(8,128)(2,1)} %get-tuple-element.19), channel_id=1, source_target_pairs={{0,4},{4,8},{8,12},{1,5},{5,9},{9,13},{2,6},{6,10},{10,14},{3,7},{... | collective-permute-start | bytes 184328 | tf_op jit(solution)/shard_map/ppermute | solution.py:35
  52.2 6.7 %collective-permute-start.11 = (bf16[80,384]{1,0:T(8,128)(2,1)}, bf16[80,384]{1,0:T(8,128)(2,1)S(1)}, u32[]{:S(2)}, u32[]{:S(2)}) collective-permute-start(bf16[80,384]{1,0:T(8,128)(2,1)} %get-tuple-element.20), channel_id=1, source_target_pairs={{4,0},{8,4},{12,8},{5,1},{9,5},{13,9},{6,2},{10,6},{14,10},{7,3},{... | collective-permute-start | bytes 184328 | tf_op jit(solution)/shard_map/ppermute | solution.py:36
  53.5 2.9 %collective-permute-start.12 = (bf16[80,6]{1,0:T(8,128)(2,1)}, bf16[80,6]{1,0:T(8,128)(2,1)S(1)}, u32[]{:S(2)}, u32[]{:S(2)}) collective-permute-start(bf16[80,6]{1,0:T(8,128)(2,1)} %get-tuple-element.21), channel_id=1, source_target_pairs={{0,1},{1,2},{2,3},{4,5},{5,6},{6,7},{8,9},{9,10},{10,11},{12,13},{... | collective-permute-start | bytes 2888 | tf_op jit(solution)/shard_map/ppermute | solution.py:37
  55.1 3.8 %collective-permute-start.13 = (bf16[80,6]{1,0:T(8,128)(2,1)}, bf16[80,6]{1,0:T(8,128)(2,1)S(1)}, u32[]{:S(2)}, u32[]{:S(2)}) collective-permute-start(bf16[80,6]{1,0:T(8,128)(2,1)} %get-tuple-element.22), channel_id=1, source_target_pairs={{1,0},{2,1},{3,2},{5,4},{6,5},{7,6},{9,8},{10,9},{11,10},{13,12},{... | collective-permute-start | bytes 2888 | tf_op jit(solution)/shard_map/ppermute | solution.py:38
  62.7 12.3 %collective-permute-start.16 = (bf16[80,6]{1,0:T(8,128)(2,1)}, bf16[80,6]{1,0:T(8,128)(2,1)S(1)}, u32[]{:S(2)}, u32[]{:S(2)}) collective-permute-start(bf16[80,6]{1,0:T(8,128)(2,1)} %get-tuple-element.26), channel_id=1, source_target_pairs={{0,1},{1,2},{2,3},{4,5},{5,6},{6,7},{8,9},{9,10},{10,11},{12,13},{... | collective-permute-start | bytes 2888 | tf_op jit(solution)/shard_map/ppermute | solution.py:37
  67.1 7.9 %collective-permute-start.17 = (bf16[80,6]{1,0:T(8,128)(2,1)}, bf16[80,6]{1,0:T(8,128)(2,1)S(1)}, u32[]{:S(2)}, u32[]{:S(2)}) collective-permute-start(bf16[80,6]{1,0:T(8,128)(2,1)} %get-tuple-element.27), channel_id=1, source_target_pairs={{1,0},{2,1},{3,2},{5,4},{6,5},{7,6},{9,8},{10,9},{11,10},{13,12},{... | collective-permute-start | bytes 2888 | tf_op jit(solution)/shard_map/ppermute | solution.py:38
  68.4 7.1 %collective-permute-start.14 = (bf16[80,384]{1,0:T(8,128)(2,1)}, bf16[80,384]{1,0:T(8,128)(2,1)S(1)}, u32[]{:S(2)}, u32[]{:S(2)}) collective-permute-start(bf16[80,384]{1,0:T(8,128)(2,1)} %get-tuple-element.24), channel_id=1, source_target_pairs={{0,4},{4,8},{8,12},{1,5},{5,9},{9,13},{2,6},{6,10},{10,14},{3,7},{... | collective-permute-start | bytes 184328 | tf_op jit(solution)/shard_map/ppermute | solution.py:35
  73.0 6.9 %collective-permute-start.15 = (bf16[80,384]{1,0:T(8,128)(2,1)}, bf16[80,384]{1,0:T(8,128)(2,1)S(1)}, u32[]{:S(2)}, u32[]{:S(2)}) collective-permute-start(bf16[80,384]{1,0:T(8,128)(2,1)} %get-tuple-element.25), channel_id=1, source_target_pairs={{4,0},{8,4},{12,8},{5,1},{9,5},{13,9},{6,2},{10,6},{14,10},{7,3},{... | collective-permute-start | bytes 184328 | tf_op jit(solution)/shard_map/ppermute | solution.py:36
  75.0 4.8 %copy-start.14 = (bf16[80,6]{1,0:T(8,128)(2,1)}, bf16[80,6]{1,0:T(8,128)(2,1)S(1)}, u32[]{:S(2)}) copy-start(bf16[80,6]{1,0:T(8,128)(2,1)S(1)} %collective-permute-done.16.refs_5_) | copy-start | bytes 2884
  75.0 4.8 %copy-start.15 = (bf16[80,6]{1,0:T(8,128)(2,1)}, bf16[80,6]{1,0:T(8,128)(2,1)S(1)}, u32[]{:S(2)}) copy-start(bf16[80,6]{1,0:T(8,128)(2,1)S(1)} %collective-permute-done.17.refs_6_) | copy-start | bytes 2884
  75.5 4.3 %copy-start.10 = (bf16[80,384]{1,0:T(8,128)(2,1)}, bf16[80,384]{1,0:T(8,128)(2,1)S(1)}, u32[]{:S(2)}) copy-start(bf16[80,384]{1,0:T(8,128)(2,1)S(1)} %collective-permute-done.14.refs_3_) | copy-start | bytes 184324
  85.1 5.7 %collective-permute-start.20 = (f32[80,256]{1,0:T(8,128)S(1)}, f32[80,256]{1,0:T(8,128)S(1)}, u32[]{:S(2)}, u32[]{:S(2)}) collective-permute-start(f32[80,256]{1,0:T(8,128)S(1)} %get-tuple-element.47), channel_id=1, source_target_pairs={{0,12},{4,0},{8,4},{12,8},{1,13},{5,1},{9,5},{13,9},{2,14},{6,2},{... | collective-permute-start | bytes 245768 | tf_op jit(solution)/shard_map/ppermute | solution.py:346
  85.9 10.0 %collective-permute-start.19 = (f32[80,256]{1,0:T(8,128)S(1)}, f32[80,256]{1,0:T(8,128)S(1)}, u32[]{:S(2)}, u32[]{:S(2)}) collective-permute-start(f32[80,256]{1,0:T(8,128)S(1)} %get-tuple-element.48), channel_id=1, source_target_pairs={{0,8},{4,12},{8,0},{12,4},{1,9},{5,13},{9,1},{13,5},{2,10},{6,14},... | collective-permute-start | bytes 245768 | tf_op jit(solution)/shard_map/ppermute | solution.py:346
  88.3 7.6 %collective-permute-start.18 = (f32[80,256]{1,0:T(8,128)S(1)}, f32[80,256]{1,0:T(8,128)S(1)}, u32[]{:S(2)}, u32[]{:S(2)}) collective-permute-start(f32[80,256]{1,0:T(8,128)S(1)} %get-tuple-element.49), channel_id=1, source_target_pairs={{0,4},{4,8},{8,12},{12,0},{1,5},{5,9},{9,13},{13,1},{2,6},{6,10},{... | collective-permute-start | bytes 245768 | tf_op jit(solution)/shard_map/ppermute | solution.py:346
  (12 other events, 14.5 us)

commit v12 on v11

--- a/solution.py
+++ b/solution.py
@@ -268,6 +268,8 @@
 def scatter_add_columns(values, ids, width):
     levels = values.shape[0]
     onehot = (ids[:, None] == lax.broadcasted_iota(jnp.int32, (1, width), 1)).astype(jnp.bfloat16)
+    if values.dtype == jnp.bfloat16:
+        return jnp.dot(values, onehot, preferred_element_type=jnp.float32)
     parts = jnp.concatenate(split3(values), axis=0)
     total = jnp.dot(parts, onehot, preferred_element_type=jnp.float32)
     return (total[:levels] + total[levels : 2 * levels]) + total[2 * levels :]
@@ -340,7 +342,7 @@
         )
     (nudge_gap,) = extra
     if by_shift:
-        outgoing = jnp.where(chosen[:, None, :], nudge_gap[None, :, :], 0.0)
+        outgoing = jnp.where(chosen[:, None, :], nudge_gap[None, :, :], 0.0).astype(jnp.bfloat16)
         incoming = jnp.concatenate(
             [outgoing[0]]
             + [lax.ppermute(outgoing[s], "gx", shifted_pairs(tiles_x, s)) for s in range(1, tiles_x)],

time: 99.6 us -> 96.5 us (0.969)
  waiting for transfers between devices: 19.1 us -> 17.4 us
  local copies, waits for them, and re-layouts: 14.3 us -> 13.3 us
    ppermute x3, waiting for transfers between devices: 5.1 us -> 3.34 us  [body(): lax.ppermute(outgoing[s], 'gx', shifted_pairs(tiles_x, s))]
  transfers between devices with their start and end apart: 21 -> 21, of which waited for: 6 -> 7; matrix products, arithmetic and copies ran while one was open for 16% -> 16% of each run, Pallas kernels for 3% -> 3%
where the time goes in v12:
time: 96.5 us; the launch traced here: 95.7 us
  starting transfers between devices  40.2 us (42%)
  waiting for transfers between devices  17.4 us (18%)
  local copies, waits for them, and re-layouts  13.3 us (14%)
  Pallas kernels  13.2 us (14%)
  matrix products  5.93 us (6%)
  other arithmetic  4.59 us (5%)
  between operations  1.17 us (1%)
    pallas_call x4, Pallas kernels, stencil_step(): pl.pallas_call(functools.partial(step_kernel, rows=rows, cols=cols, xo=xo...  13.2 us
    ppermute x3, starting transfers between devices, exchange(): above = lax.ppermute(last_rows, 'gx', fwd_x)  9.32 us
    ppermute x3, starting transfers between devices, exchange(): left = lax.ppermute(last_cols, Y_AXES, fwd_y)  9.05 us
    ppermute x3, starting transfers between devices, body(): lax.ppermute(wanted[s], 'gx', shifted_pairs(tiles_x, s))  8.1 us
    ppermute x3, waiting for transfers between devices, body(): lax.ppermute(gather_parts(parent_parts, served[s]), 'gx', shifted_pairs(t...  6.78 us
    unnamed x60, local copies, waits for them, and re-layouts  6.38 us
    ppermute x3, waiting for transfers between devices, exchange(): below = lax.ppermute(first_rows, 'gx', bwd_x)  4.33 us
    ppermute x3, starting transfers between devices, exchange(): below = lax.ppermute(first_rows, 'gx', bwd_x)  3.88 us
  transfers between devices with their start and end apart: 21, of which 7 were waited for; matrix products, arithmetic and copies ran while one was open for 16% of the time, Pallas kernels for 3%

profile of v12, /device:TPU:0, one launch (start us, length us, event | category | flops | bytes accessed | tf_op | source)
XLA Modules:
  0.0 95.7 jit_solution(7650643628331021636)
XLA Ops:
  2.1 3.1 %collective-permute-start.8 = (s32[256]{0:T(256)S(1)}, s32[256]{0:T(256)S(1)}, u32[]{:S(2)}, u32[]{:S(2)}) collective-permute-start(s32[256]{0:T(256)S(1)} %bitcast.81), channel_id=1, source_target_pairs={{0,4},{4,8},{8,12},{12,0},{1,5},{5,9},{9,13},{13,1},{2,6},{6,10},{... | collective-permute-start | bytes 3080 | tf_op jit(solution)/shard_map/ppermute | solution.py:301
  6.1 1.2 %fusion.42 = (bf16[80,1,256]{2,1,0:T(2,128)(2,1)S(1)}, bf16[80,1,256]{2,1,0:T(2,128)(2,1)S(1)}) fusion(bf16[80,8,256]{2,1,0:T(8,128)(2,1)} %param.10), kind=kLoop, calls=%fused_computation.100 | loop fusion | bytes 163840 | tf_op jit(solution)/shard_map/slice | solution.py:21
  7.4 3.5 %collective-permute-start = (bf16[80,640]{1,0:T(8,128)(2,1)S(1)}, bf16[80,640]{1,0:T(8,128)(2,1)S(1)}, u32[]{:S(2)}, u32[]{:S(2)}) collective-permute-start(bf16[80,640]{1,0:T(8,128)(2,1)S(1)} %pad_maximum_fusion), channel_id=1, source_target_pairs={{0,4},{4,8},{8,12},{1,5},{5,9},{9,13},{2,6},{6,10},{10,14},{3,7},{... | collective-permute-start | bytes 307208 | tf_op jit(solution)/shard_map/ppermute | solution.py:35
  10.9 1.3 %collective-permute-start.1 = (bf16[80,640]{1,0:T(8,128)(2,1)S(1)}, bf16[80,640]{1,0:T(8,128)(2,1)S(1)}, u32[]{:S(2)}, u32[]{:S(2)}) collective-permute-start(bf16[80,640]{1,0:T(8,128)(2,1)S(1)} %pad_maximum_fusion.1), channel_id=1, source_target_pairs={{4,0},{8,4},{12,8},{5,1},{9,5},{13,9},{6,2},{10,6},{14,10},{7,3},{... | collective-permute-start | bytes 307208 | tf_op jit(solution)/shard_map/ppermute | solution.py:36
  12.9 1.3 %collective-permute-start.3 = (bf16[80,14]{1,0:T(8,128)(2,1)S(1)}, bf16[80,14]{1,0:T(8,128)(2,1)S(1)}, u32[]{:S(2)}, u32[]{:S(2)}) collective-permute-start(bf16[80,14]{1,0:T(8,128)(2,1)S(1)} %copy.49), channel_id=1, source_target_pairs={{1,0},{2,1},{3,2},{5,4},{6,5},{7,6},{9,8},{10,9},{11,10},{13,12},{... | collective-permute-start | bytes 6728 | tf_op jit(solution)/shard_map/ppermute | solution.py:38
  14.6 3.0 %collective-permute-start.2 = (bf16[80,14]{1,0:T(8,128)(2,1)S(1)}, bf16[80,14]{1,0:T(8,128)(2,1)S(1)}, u32[]{:S(2)}, u32[]{:S(2)}) collective-permute-start(bf16[80,14]{1,0:T(8,128)(2,1)S(1)} %copy.46), channel_id=1, source_target_pairs={{0,1},{1,2},{2,3},{4,5},{5,6},{6,7},{8,9},{9,10},{10,11},{12,13},{... | collective-permute-start | bytes 6728 | tf_op jit(solution)/shard_map/ppermute | solution.py:37
  23.5 3.7 %collective-permute-start.6 = (s32[256]{0:T(256)S(1)}, s32[256]{0:T(256)S(1)}, u32[]{:S(2)}, u32[]{:S(2)}) collective-permute-start(s32[256]{0:T(256)S(1)} %bitcast.79), channel_id=1, source_target_pairs={{0,8},{4,12},{8,0},{12,4},{1,9},{5,13},{9,1},{13,5},{2,10},{6,14},... | collective-permute-start | bytes 3080 | tf_op jit(solution)/shard_map/ppermute | solution.py:301
  27.2 1.4 %collective-permute-start.4 = (s32[256]{0:T(256)S(1)}, s32[256]{0:T(256)S(1)}, u32[]{:S(2)}, u32[]{:S(2)}) collective-permute-start(s32[256]{0:T(256)S(1)} %bitcast.80), channel_id=1, source_target_pairs={{0,12},{4,0},{8,4},{12,8},{1,13},{5,1},{9,5},{13,9},{2,14},{6,2},{... | collective-permute-start | bytes 3080 | tf_op jit(solution)/shard_map/ppermute | solution.py:301
  29.2 3.2 %shard_map.113 = (f32[80,2048]{1,0:T(8,128)}, bf16[80,256]{1,0:T(8,128)(2,1)}, bf16[80,256]{1,0:T(8,128)(2,1)}, bf16[80,8]{1,0:T(8,128)(2,1)}, bf16[80,8]{1,0:T(8,128)(2,1)}, /*index=5*/bf16[240,2048]{1,0:T(8,128)(2,1)}) custom-call(bf16[80,2048]{1,0:T(8,128)(2,1)} %bitcast.59, bf16[80,640]{1,0:T(8,128)(2,1)} %copy-done.6, bf16[80,640]{1,0:T(8,128)(2,1)} %copy-done.7, ...), custom_call_target="tpu_custom_call" | custom-call | flops 165806080 | bytes 1218240 | tf_op jit(solution)/shard_map/pallas_call | solution.py:178
  32.4 1.9 %fusion.5 = f32[240,256]{1,0:T(8,128)S(1)} fusion(bf16[240,2048]{1,0:T(8,128)(2,1)} %get-tuple-element.17, s32[256]{0:T(256)S(1)} %collective-permute-done.8), kind=kOutput, calls=%fused_computation.11 | convolution fusion | flops 252182528 | bytes 1229824 | tf_op jit(solution)/shard_map/dot_general | solution.py:264
  35.7 2.0 %collective-permute-start.7 = (f32[80,256]{1,0:T(8,128)S(1)}, f32[80,256]{1,0:T(8,128)S(1)}, u32[]{:S(2)}, u32[]{:S(2)}) collective-permute-start(f32[80,256]{1,0:T(8,128)S(1)} %slice_add_fusion.4), channel_id=1, source_target_pairs={{0,8},{4,12},{8,0},{12,4},{1,9},{5,13},{9,1},{13,5},{2,10},{6,14},... | collective-permute-start | bytes 245768 | tf_op jit(solution)/shard_map/ppermute | solution.py:305
  38.3 0.9 collective-permute-done.9
  39.2 5.9 %collective-permute-done.7 = f32[80,256]{1,0:T(8,128)S(1)} collective-permute-done((f32[80,256]{1,0:T(8,128)S(1)}, f32[80,256]{1,0:T(8,128)S(1)}, u32[]{:S(2)}, u32[]{:S(2)}) %collective-permute-start.7) | collective-permute-done | bytes 81952 | tf_op jit(solution)/shard_map/ppermute | solution.py:305
  45.8 0.9 copy-done.1
  46.7 3.1 %shard_map.114 = (f32[80,2304]{1,0:T(8,128)}, bf16[80,384]{1,0:T(8,128)(2,1)}, bf16[80,384]{1,0:T(8,128)(2,1)}, bf16[80,6]{1,0:T(8,128)(2,1)}, bf16[80,6]{1,0:T(8,128)(2,1)}) custom-call(bf16[80,2304]{1,0:T(8,128)(2,1)} %bitcast.57, bf16[80,640]{1,0:T(8,128)(2,1)} %copy-done.6, bf16[80,640]{1,0:T(8,128)(2,1)} %copy-done.7, bf16[80,14]{1,0:T(8,128)(2,1)} %copy-done.9, ...), custom_call_target="tpu_custom_call" | custom-call | flops 185057280 | bytes 2097152 | tf_op jit(solution)/shard_map/pallas_call | solution.py:178
  49.8 1.3 %collective-permute-start.10 = (bf16[80,384]{1,0:T(8,128)(2,1)}, bf16[80,384]{1,0:T(8,128)(2,1)S(1)}, u32[]{:S(2)}, u32[]{:S(2)}) collective-permute-start(bf16[80,384]{1,0:T(8,128)(2,1)} %get-tuple-element.19), channel_id=1, source_target_pairs={{0,4},{4,8},{8,12},{1,5},{5,9},{9,13},{2,6},{6,10},{10,14},{3,7},{... | collective-permute-start | bytes 184328 | tf_op jit(solution)/shard_map/ppermute | solution.py:35
  51.1 1.3 %collective-permute-start.11 = (bf16[80,384]{1,0:T(8,128)(2,1)}, bf16[80,384]{1,0:T(8,128)(2,1)S(1)}, u32[]{:S(2)}, u32[]{:S(2)}) collective-permute-start(bf16[80,384]{1,0:T(8,128)(2,1)} %get-tuple-element.20), channel_id=1, source_target_pairs={{4,0},{8,4},{12,8},{5,1},{9,5},{13,9},{6,2},{10,6},{14,10},{7,3},{... | collective-permute-start | bytes 184328 | tf_op jit(solution)/shard_map/ppermute | solution.py:36
  52.4 1.6 %collective-permute-start.12 = (bf16[80,6]{1,0:T(8,128)(2,1)}, bf16[80,6]{1,0:T(8,128)(2,1)S(1)}, u32[]{:S(2)}, u32[]{:S(2)}) collective-permute-start(bf16[80,6]{1,0:T(8,128)(2,1)} %get-tuple-element.21), channel_id=1, source_target_pairs={{0,1},{1,2},{2,3},{4,5},{5,6},{6,7},{8,9},{9,10},{10,11},{12,13},{... | collective-permute-start | bytes 2888 | tf_op jit(solution)/shard_map/ppermute | solution.py:37
  54.0 1.3 %collective-permute-start.13 = (bf16[80,6]{1,0:T(8,128)(2,1)}, bf16[80,6]{1,0:T(8,128)(2,1)S(1)}, u32[]{:S(2)}, u32[]{:S(2)}) collective-permute-start(bf16[80,6]{1,0:T(8,128)(2,1)} %get-tuple-element.22), channel_id=1, source_target_pairs={{1,0},{2,1},{3,2},{5,4},{6,5},{7,6},{9,8},{10,9},{11,10},{13,12},{... | collective-permute-start | bytes 2888 | tf_op jit(solution)/shard_map/ppermute | solution.py:38
  55.3 2.4 %collective-permute-done.13.refs_4_ = bf16[80,6]{1,0:T(8,128)(2,1)S(1)} collective-permute-done((bf16[80,6]{1,0:T(8,128)(2,1)}, bf16[80,6]{1,0:T(8,128)(2,1)S(1)}, u32[]{:S(2)}, u32[]{:S(2)}) %collective-permute-start.13) | collective-permute-done | bytes 992 | tf_op jit(solution)/shard_map/ppermute | solution.py:38
  58.4 3.2 %shard_map.115 = (f32[80,2304]{1,0:T(8,128)}, bf16[80,384]{1,0:T(8,128)(2,1)}, bf16[80,384]{1,0:T(8,128)(2,1)}, bf16[80,6]{1,0:T(8,128)(2,1)}, bf16[80,6]{1,0:T(8,128)(2,1)}) custom-call(f32[80,2304]{1,0:T(8,128)} %get-tuple-element.18.refs_0_, bf16[80,384]{1,0:T(8,128)(2,1)} %copy-done.12, bf16[80,384]{1,0:T(8,128)(2,1)} %copy-done.13, ...), custom_call_target="tpu_custom_call" | custom-call | flops 185057280 | bytes 2381312 | tf_op jit(solution)/shard_map/pallas_call | solution.py:178
  61.6 4.4 %collective-permute-start.16 = (bf16[80,6]{1,0:T(8,128)(2,1)}, bf16[80,6]{1,0:T(8,128)(2,1)S(1)}, u32[]{:S(2)}, u32[]{:S(2)}) collective-permute-start(bf16[80,6]{1,0:T(8,128)(2,1)} %get-tuple-element.26), channel_id=1, source_target_pairs={{0,1},{1,2},{2,3},{4,5},{5,6},{6,7},{8,9},{9,10},{10,11},{12,13},{... | collective-permute-start | bytes 2888 | tf_op jit(solution)/shard_map/ppermute | solution.py:37
  66.0 1.3 %collective-permute-start.17 = (bf16[80,6]{1,0:T(8,128)(2,1)}, bf16[80,6]{1,0:T(8,128)(2,1)S(1)}, u32[]{:S(2)}, u32[]{:S(2)}) collective-permute-start(bf16[80,6]{1,0:T(8,128)(2,1)} %get-tuple-element.27), channel_id=1, source_target_pairs={{1,0},{2,1},{3,2},{5,4},{6,5},{7,6},{9,8},{10,9},{11,10},{13,12},{... | collective-permute-start | bytes 2888 | tf_op jit(solution)/shard_map/ppermute | solution.py:38
  67.3 4.5 %collective-permute-start.14 = (bf16[80,384]{1,0:T(8,128)(2,1)}, bf16[80,384]{1,0:T(8,128)(2,1)S(1)}, u32[]{:S(2)}, u32[]{:S(2)}) collective-permute-start(bf16[80,384]{1,0:T(8,128)(2,1)} %get-tuple-element.24), channel_id=1, source_target_pairs={{0,4},{4,8},{8,12},{1,5},{5,9},{9,13},{2,6},{6,10},{10,14},{3,7},{... | collective-permute-start | bytes 184328 | tf_op jit(solution)/shard_map/ppermute | solution.py:35
  71.9 1.3 %collective-permute-start.15 = (bf16[80,384]{1,0:T(8,128)(2,1)}, bf16[80,384]{1,0:T(8,128)(2,1)S(1)}, u32[]{:S(2)}, u32[]{:S(2)}) collective-permute-start(bf16[80,384]{1,0:T(8,128)(2,1)} %get-tuple-element.25), channel_id=1, source_target_pairs={{4,0},{8,4},{12,8},{5,1},{9,5},{13,9},{6,2},{10,6},{14,10},{7,3},{... | collective-permute-start | bytes 184328 | tf_op jit(solution)/shard_map/ppermute | solution.py:36
  74.4 4.3 %collective-permute-done.15.refs_4_ = bf16[80,384]{1,0:T(8,128)(2,1)S(1)} collective-permute-done((bf16[80,384]{1,0:T(8,128)(2,1)}, bf16[80,384]{1,0:T(8,128)(2,1)S(1)}, u32[]{:S(2)}, u32[]{:S(2)}) %collective-permute-start.15) | collective-permute-done | bytes 61472 | tf_op jit(solution)/shard_map/ppermute | solution.py:36
  79.4 3.7 %shard_map.116 = (f32[80,2304]{1,0:T(8,128)}, bf16[80,384]{1,0:T(8,128)(2,1)}, bf16[80,384]{1,0:T(8,128)(2,1)}, bf16[80,6]{1,0:T(8,128)(2,1)}, bf16[80,6]{1,0:T(8,128)(2,1)}, /*index=5*/f32[80,256]{1,0:T(8,128)}) custom-call(f32[128,384]{1,0:T(8,128)} %fusion.13.refs_0_, f32[80,256]{1,0:T(8,128)} %copy-done.4, f32[80,2304]{1,0:T(8,128)} %get-tuple-element.23.refs_2_, ...), custom_call_target="tpu_custom_call" | custom-call | flops 185057280 | bytes 2659840 | tf_op jit(solution)/shard_map/pallas_call | solution.py:178
  83.1 0.9 select_convert_fusion
  84.8 2.4 %collective-permute-start.19 = (bf16[80,256]{1,0:T(8,128)(2,1)S(1)}, bf16[80,256]{1,0:T(8,128)(2,1)S(1)}, u32[]{:S(2)}, u32[]{:S(2)}) collective-permute-start(bf16[80,256]{1,0:T(8,128)(2,1)S(1)} %get-tuple-element.49), channel_id=1, source_target_pairs={{0,8},{4,12},{8,0},{12,4},{1,9},{5,13},{9,1},{13,5},{2,10},{6,14},... | collective-permute-start | bytes 122888 | tf_op jit(solution)/shard_map/ppermute | solution.py:348
  87.8 1.2 %convert_element_type.28 = bf16[80,2304]{1,0:T(8,128)(2,1)S(1)} convert(f32[80,2304]{1,0:T(8,128)} %get-tuple-element.29) | non-fusion elementwise | flops 184320 | bytes 1105920 | tf_op jit(solution)/shard_map/convert_element_type | solution.py:358
  90.5 2.5 %collective-permute-done.18 = bf16[80,256]{1,0:T(8,128)(2,1)S(1)} collective-permute-done((bf16[80,256]{1,0:T(8,128)(2,1)S(1)}, bf16[80,256]{1,0:T(8,128)(2,1)S(1)}, u32[]{:S(2)}, u32[]{:S(2)}) %collective-permute-start.18) | collective-permute-done | bytes 40992 | tf_op jit(solution)/shard_map/ppermute | solution.py:348
  93.0 1.8 %fusion.2 = f32[80,2048]{1,0:T(8,128)S(1)} fusion(s32[1024]{0:T(1024)S(1)} %pad_add_fusion, f32[80]{0:T(128)S(1)} %copy-done.22, bf16[80,256]{1,0:T(8,128)(2,1)S(1)} %collective-permute-done.20, bf16[80,256]{1,0:T(8,128)(2,1)S(1)} %collective-permute-done.19, bf16[80,256]{1,0:T(8,128)(2,1)S(1)} %collective-permute-done.18, ...), kind=kOutput, calls=%fused_computation.4 | convolution fusion | flops 338460672 | bytes 823616 | tf_op jit(solution)/shard_map/dot_general | solution.py:272
  (121 shorter events, 18.9 us)
Async XLA Ops:
  0.6 17.1 %copy-start = (s32[24]{0:T(128)S(1)}, s32[24]{0:T(128)}, u32[]{:S(2)}) copy-start(s32[24]{0:T(128)} %param.19) | copy-start | bytes 292
  0.6 11.5 %copy-start.3 = (bf16[80,6,384]{2,0,1:T(8,128)(2,1)S(1)}, bf16[80,6,384]{2,0,1:T(8,128)(2,1)}, u32[]{:S(2)}) copy-start(bf16[80,6,384]{2,0,1:T(8,128)(2,1)} %param.11) | copy-start | bytes 1105924
  0.7 11.6 %copy-start.2 = (bf16[80,8,256]{2,1,0:T(8,128)(2,1)S(1)}, bf16[80,8,256]{2,1,0:T(8,128)(2,1)}, u32[]{:S(2)}) copy-start(bf16[80,8,256]{2,1,0:T(8,128)(2,1)} %param.10) | copy-start | bytes 983044
  2.1 30.3 %collective-permute-start.8 = (s32[256]{0:T(256)S(1)}, s32[256]{0:T(256)S(1)}, u32[]{:S(2)}, u32[]{:S(2)}) collective-permute-start(s32[256]{0:T(256)S(1)} %bitcast.81), channel_id=1, source_target_pairs={{0,4},{4,8},{8,12},{12,0},{1,5},{5,9},{9,13},{13,1},{2,6},{6,10},{... | collective-permute-start | bytes 3080 | tf_op jit(solution)/shard_map/ppermute | solution.py:301
  7.4 21.2 %collective-permute-start = (bf16[80,640]{1,0:T(8,128)(2,1)S(1)}, bf16[80,640]{1,0:T(8,128)(2,1)S(1)}, u32[]{:S(2)}, u32[]{:S(2)}) collective-permute-start(bf16[80,640]{1,0:T(8,128)(2,1)S(1)} %pad_maximum_fusion), channel_id=1, source_target_pairs={{0,4},{4,8},{8,12},{1,5},{5,9},{9,13},{2,6},{6,10},{10,14},{3,7},{... | collective-permute-start | bytes 307208 | tf_op jit(solution)/shard_map/ppermute | solution.py:35
  10.9 17.7 %collective-permute-start.1 = (bf16[80,640]{1,0:T(8,128)(2,1)S(1)}, bf16[80,640]{1,0:T(8,128)(2,1)S(1)}, u32[]{:S(2)}, u32[]{:S(2)}) collective-permute-start(bf16[80,640]{1,0:T(8,128)(2,1)S(1)} %pad_maximum_fusion.1), channel_id=1, source_target_pairs={{4,0},{8,4},{12,8},{5,1},{9,5},{13,9},{6,2},{10,6},{14,10},{7,3},{... | collective-permute-start | bytes 307208 | tf_op jit(solution)/shard_map/ppermute | solution.py:36
  12.3 7.5 %copy-start.18 = (f32[80]{0:T(128)S(1)}, f32[80]{0:T(128)}, u32[]{:S(2)}) copy-start(f32[80]{0:T(128)} %param.13) | copy-start | bytes 964
  12.3 8.2 %copy-start.19 = (f32[80]{0:T(128)S(1)}, f32[80]{0:T(128)}, u32[]{:S(2)}) copy-start(f32[80]{0:T(128)} %param.14) | copy-start | bytes 964
  12.3 8.9 %copy-start.20 = (f32[80]{0:T(128)S(1)}, f32[80]{0:T(128)}, u32[]{:S(2)}) copy-start(f32[80]{0:T(128)} %param.12) | copy-start | bytes 964
  12.9 10.6 %collective-permute-start.3 = (bf16[80,14]{1,0:T(8,128)(2,1)S(1)}, bf16[80,14]{1,0:T(8,128)(2,1)S(1)}, u32[]{:S(2)}, u32[]{:S(2)}) collective-permute-start(bf16[80,14]{1,0:T(8,128)(2,1)S(1)} %copy.49), channel_id=1, source_target_pairs={{1,0},{2,1},{3,2},{5,4},{6,5},{7,6},{9,8},{10,9},{11,10},{13,12},{... | collective-permute-start | bytes 6728 | tf_op jit(solution)/shard_map/ppermute | solution.py:38
  14.6 12.5 %collective-permute-start.2 = (bf16[80,14]{1,0:T(8,128)(2,1)S(1)}, bf16[80,14]{1,0:T(8,128)(2,1)S(1)}, u32[]{:S(2)}, u32[]{:S(2)}) collective-permute-start(bf16[80,14]{1,0:T(8,128)(2,1)S(1)} %copy.46), channel_id=1, source_target_pairs={{0,1},{1,2},{2,3},{4,5},{5,6},{6,7},{8,9},{9,10},{10,11},{12,13},{... | collective-permute-start | bytes 6728 | tf_op jit(solution)/shard_map/ppermute | solution.py:37
  23.5 5.0 %copy-start.8 = (bf16[80,14]{1,0:T(8,128)(2,1)}, bf16[80,14]{1,0:T(8,128)(2,1)S(1)}, u32[]{:S(2)}) copy-start(bf16[80,14]{1,0:T(8,128)(2,1)S(1)} %collective-permute-done.3.refs_4_) | copy-start | bytes 6724
  23.5 11.6 %collective-permute-start.6 = (s32[256]{0:T(256)S(1)}, s32[256]{0:T(256)S(1)}, u32[]{:S(2)}, u32[]{:S(2)}) collective-permute-start(s32[256]{0:T(256)S(1)} %bitcast.79), channel_id=1, source_target_pairs={{0,8},{4,12},{8,0},{12,4},{1,9},{5,13},{9,1},{13,5},{2,10},{6,14},... | collective-permute-start | bytes 3080 | tf_op jit(solution)/shard_map/ppermute | solution.py:301
  27.2 7.3 %collective-permute-start.4 = (s32[256]{0:T(256)S(1)}, s32[256]{0:T(256)S(1)}, u32[]{:S(2)}, u32[]{:S(2)}) collective-permute-start(s32[256]{0:T(256)S(1)} %bitcast.80), channel_id=1, source_target_pairs={{0,12},{4,0},{8,4},{12,8},{1,13},{5,1},{9,5},{13,9},{2,14},{6,2},{... | collective-permute-start | bytes 3080 | tf_op jit(solution)/shard_map/ppermute | solution.py:301
  34.3 4.9 %collective-permute-start.9 = (f32[80,256]{1,0:T(8,128)S(1)}, f32[80,256]{1,0:T(8,128)S(1)}, u32[]{:S(2)}, u32[]{:S(2)}) collective-permute-start(f32[80,256]{1,0:T(8,128)S(1)} %slice_add_fusion.2), channel_id=1, source_target_pairs={{0,12},{4,0},{8,4},{12,8},{1,13},{5,1},{9,5},{13,9},{2,14},{6,2},{... | collective-permute-start | bytes 245768 | tf_op jit(solution)/shard_map/ppermute | solution.py:305
  35.7 9.4 %collective-permute-start.7 = (f32[80,256]{1,0:T(8,128)S(1)}, f32[80,256]{1,0:T(8,128)S(1)}, u32[]{:S(2)}, u32[]{:S(2)}) collective-permute-start(f32[80,256]{1,0:T(8,128)S(1)} %slice_add_fusion.4), channel_id=1, source_target_pairs={{0,8},{4,12},{8,0},{12,4},{1,9},{5,13},{9,1},{13,5},{2,10},{6,14},... | collective-permute-start | bytes 245768 | tf_op jit(solution)/shard_map/ppermute | solution.py:305
  37.7 7.4 %collective-permute-start.5 = (f32[80,256]{1,0:T(8,128)S(1)}, f32[80,256]{1,0:T(8,128)S(1)}, u32[]{:S(2)}, u32[]{:S(2)}) collective-permute-start(f32[80,256]{1,0:T(8,128)S(1)} %slice_add_fusion.6), channel_id=1, source_target_pairs={{0,4},{4,8},{8,12},{12,0},{1,5},{5,9},{9,13},{13,1},{2,6},{6,10},{... | collective-permute-start | bytes 245768 | tf_op jit(solution)/shard_map/ppermute | solution.py:305
  45.1 4.7 %copy-start.4 = (f32[80,256]{1,0:T(8,128)}, f32[80,256]{1,0:T(8,128)S(1)}, u32[]{:S(2)}) copy-start(f32[80,256]{1,0:T(8,128)S(1)} %fusion.31.refs_1_) | copy-start | bytes 245764
  49.8 8.0 %collective-permute-start.10 = (bf16[80,384]{1,0:T(8,128)(2,1)}, bf16[80,384]{1,0:T(8,128)(2,1)S(1)}, u32[]{:S(2)}, u32[]{:S(2)}) collective-permute-start(bf16[80,384]{1,0:T(8,128)(2,1)} %get-tuple-element.19), channel_id=1, source_target_pairs={{0,4},{4,8},{8,12},{1,5},{5,9},{9,13},{2,6},{6,10},{10,14},{3,7},{... | collective-permute-start | bytes 184328 | tf_op jit(solution)/shard_map/ppermute | solution.py:35
  51.1 6.7 %collective-permute-start.11 = (bf16[80,384]{1,0:T(8,128)(2,1)}, bf16[80,384]{1,0:T(8,128)(2,1)S(1)}, u32[]{:S(2)}, u32[]{:S(2)}) collective-permute-start(bf16[80,384]{1,0:T(8,128)(2,1)} %get-tuple-element.20), channel_id=1, source_target_pairs={{4,0},{8,4},{12,8},{5,1},{9,5},{13,9},{6,2},{10,6},{14,10},{7,3},{... | collective-permute-start | bytes 184328 | tf_op jit(solution)/shard_map/ppermute | solution.py:36
  52.4 2.9 %collective-permute-start.12 = (bf16[80,6]{1,0:T(8,128)(2,1)}, bf16[80,6]{1,0:T(8,128)(2,1)S(1)}, u32[]{:S(2)}, u32[]{:S(2)}) collective-permute-start(bf16[80,6]{1,0:T(8,128)(2,1)} %get-tuple-element.21), channel_id=1, source_target_pairs={{0,1},{1,2},{2,3},{4,5},{5,6},{6,7},{8,9},{9,10},{10,11},{12,13},{... | collective-permute-start | bytes 2888 | tf_op jit(solution)/shard_map/ppermute | solution.py:37
  54.0 3.8 %collective-permute-start.13 = (bf16[80,6]{1,0:T(8,128)(2,1)}, bf16[80,6]{1,0:T(8,128)(2,1)S(1)}, u32[]{:S(2)}, u32[]{:S(2)}) collective-permute-start(bf16[80,6]{1,0:T(8,128)(2,1)} %get-tuple-element.22), channel_id=1, source_target_pairs={{1,0},{2,1},{3,2},{5,4},{6,5},{7,6},{9,8},{10,9},{11,10},{13,12},{... | collective-permute-start | bytes 2888 | tf_op jit(solution)/shard_map/ppermute | solution.py:38
  61.6 12.3 %collective-permute-start.16 = (bf16[80,6]{1,0:T(8,128)(2,1)}, bf16[80,6]{1,0:T(8,128)(2,1)S(1)}, u32[]{:S(2)}, u32[]{:S(2)}) collective-permute-start(bf16[80,6]{1,0:T(8,128)(2,1)} %get-tuple-element.26), channel_id=1, source_target_pairs={{0,1},{1,2},{2,3},{4,5},{5,6},{6,7},{8,9},{9,10},{10,11},{12,13},{... | collective-permute-start | bytes 2888 | tf_op jit(solution)/shard_map/ppermute | solution.py:37
  66.0 7.9 %collective-permute-start.17 = (bf16[80,6]{1,0:T(8,128)(2,1)}, bf16[80,6]{1,0:T(8,128)(2,1)S(1)}, u32[]{:S(2)}, u32[]{:S(2)}) collective-permute-start(bf16[80,6]{1,0:T(8,128)(2,1)} %get-tuple-element.27), channel_id=1, source_target_pairs={{1,0},{2,1},{3,2},{5,4},{6,5},{7,6},{9,8},{10,9},{11,10},{13,12},{... | collective-permute-start | bytes 2888 | tf_op jit(solution)/shard_map/ppermute | solution.py:38
  67.3 7.1 %collective-permute-start.14 = (bf16[80,384]{1,0:T(8,128)(2,1)}, bf16[80,384]{1,0:T(8,128)(2,1)S(1)}, u32[]{:S(2)}, u32[]{:S(2)}) collective-permute-start(bf16[80,384]{1,0:T(8,128)(2,1)} %get-tuple-element.24), channel_id=1, source_target_pairs={{0,4},{4,8},{8,12},{1,5},{5,9},{9,13},{2,6},{6,10},{10,14},{3,7},{... | collective-permute-start | bytes 184328 | tf_op jit(solution)/shard_map/ppermute | solution.py:35
  71.9 6.9 %collective-permute-start.15 = (bf16[80,384]{1,0:T(8,128)(2,1)}, bf16[80,384]{1,0:T(8,128)(2,1)S(1)}, u32[]{:S(2)}, u32[]{:S(2)}) collective-permute-start(bf16[80,384]{1,0:T(8,128)(2,1)} %get-tuple-element.25), channel_id=1, source_target_pairs={{4,0},{8,4},{12,8},{5,1},{9,5},{13,9},{6,2},{10,6},{14,10},{7,3},{... | collective-permute-start | bytes 184328 | tf_op jit(solution)/shard_map/ppermute | solution.py:36
  74.0 4.8 %copy-start.14 = (bf16[80,6]{1,0:T(8,128)(2,1)}, bf16[80,6]{1,0:T(8,128)(2,1)S(1)}, u32[]{:S(2)}) copy-start(bf16[80,6]{1,0:T(8,128)(2,1)S(1)} %collective-permute-done.16.refs_5_) | copy-start | bytes 2884
  74.0 4.8 %copy-start.15 = (bf16[80,6]{1,0:T(8,128)(2,1)}, bf16[80,6]{1,0:T(8,128)(2,1)S(1)}, u32[]{:S(2)}) copy-start(bf16[80,6]{1,0:T(8,128)(2,1)S(1)} %collective-permute-done.17.refs_6_) | copy-start | bytes 2884
  84.0 9.0 %copy-start.22 = (f32[80]{0:T(128)S(1)}, f32[80]{0:T(128)}, u32[]{:S(2)}) copy-start(f32[80]{0:T(128)} %param.15) | copy-start | bytes 964
  84.0 5.7 %collective-permute-start.20 = (bf16[80,256]{1,0:T(8,128)(2,1)S(1)}, bf16[80,256]{1,0:T(8,128)(2,1)S(1)}, u32[]{:S(2)}, u32[]{:S(2)}) collective-permute-start(bf16[80,256]{1,0:T(8,128)(2,1)S(1)} %get-tuple-element.48), channel_id=1, source_target_pairs={{0,12},{4,0},{8,4},{12,8},{1,13},{5,1},{9,5},{13,9},{2,14},{6,2},{... | collective-permute-start | bytes 122888 | tf_op jit(solution)/shard_map/ppermute | solution.py:348
  84.8 5.7 %collective-permute-start.19 = (bf16[80,256]{1,0:T(8,128)(2,1)S(1)}, bf16[80,256]{1,0:T(8,128)(2,1)S(1)}, u32[]{:S(2)}, u32[]{:S(2)}) collective-permute-start(bf16[80,256]{1,0:T(8,128)(2,1)S(1)} %get-tuple-element.49), channel_id=1, source_target_pairs={{0,8},{4,12},{8,0},{12,4},{1,9},{5,13},{9,1},{13,5},{2,10},{6,14},... | collective-permute-start | bytes 122888 | tf_op jit(solution)/shard_map/ppermute | solution.py:348
  87.2 5.8 %collective-permute-start.18 = (bf16[80,256]{1,0:T(8,128)(2,1)S(1)}, bf16[80,256]{1,0:T(8,128)(2,1)S(1)}, u32[]{:S(2)}, u32[]{:S(2)}) collective-permute-start(bf16[80,256]{1,0:T(8,128)(2,1)S(1)} %get-tuple-element.50), channel_id=1, source_target_pairs={{0,4},{4,8},{8,12},{12,0},{1,5},{5,9},{9,13},{13,1},{2,6},{6,10},{... | collective-permute-start | bytes 122888 | tf_op jit(solution)/shard_map/ppermute | solution.py:348
  (12 other events, 16.8 us)

commit v13 on v12

--- a/solution.py
+++ b/solution.py
@@ -7,6 +7,7 @@
 from jax.experimental.pallas import tpu as pltpu
 from jax.sharding import PartitionSpec as P
 
+
 Y_AXES = ("gy", "gz")
 HI = lax.Precision.HIGHEST
 
@@ -19,10 +20,6 @@
 
 def edges_3d(block):
     return (block[:, -1, :], block[:, 0, :], block[:, :, -1], block[:, :, 0])
-
-
-def edges_flat(flat, rows, cols):
-    return (flat[:, (rows - 1) * cols :], flat[:, :cols], flat[:, cols - 1 :: cols], flat[:, ::cols])
 
 
 def exchange(edge_sets):
@@ -52,23 +49,6 @@
     return jnp.broadcast_to(values[:, :, None], values.shape + (cols,)).reshape(
         values.shape[0], rows * cols
     )
-
-
-def flat_stencil(flat, rows, cols, halo, up_w=None, down_w=None):
-    above, below, left, right = (h.astype(flat.dtype) for h in halo)
-    levels = flat.shape[0]
-    up = jnp.concatenate([above, flat[:, :-cols]], axis=1)
-    down = jnp.concatenate([flat[:, cols:], below], axis=1)
-    col = lax.broadcasted_iota(jnp.int32, (1, rows * cols), 1) % cols
-    zero = jnp.zeros((levels, 1), flat.dtype)
-    west = jnp.where(col == 0, per_row(left, rows, cols), jnp.concatenate([zero, flat[:, :-1]], axis=1))
-    east = jnp.where(
-        col == cols - 1, per_row(right, rows, cols), jnp.concatenate([flat[:, 1:], zero], axis=1)
-    )
-    if down_w is not None:
-        down = down * down_w[None, :]
-        up = up * up_w[None, :]
-    return down + up + east + west - 4.0 * flat
 
 
 def step_kernel(*refs, rows, cols, xo, yo, nest, split, gap):
@@ -186,10 +166,6 @@
     return outs[0], tuple(outs[1:5]), outs[5:]
 
 
-def mix_levels(matrix, flat):
-    return jnp.dot(matrix, flat, precision=HI, preferred_element_type=jnp.float32)
-
-
 def nest_segments(nest_of, first, count):
     index_rows = first + jnp.arange(count, dtype=jnp.int32)
     inside = (index_rows >= 0) & (index_rows < nest_of.shape[0])
@@ -208,7 +184,7 @@
     return (c // 3 == b).astype(jnp.float32)
 
 
-def expand_blocks(block_flat, block_rows, block_cols, cols, expand):
+def expand_blocks(block_flat, block_rows, block_cols, expand):
     pieces = []
     for a in range(block_rows):
         wide = jnp.dot(
@@ -221,22 +197,6 @@
     return jnp.concatenate(pieces, axis=1)
 
 
-def block_sums(flat, block_rows, cols, expand):
-    pieces = []
-    for a in range(block_rows):
-        rows3 = (
-            flat[:, (3 * a) * cols : (3 * a + 1) * cols]
-            + flat[:, (3 * a + 1) * cols : (3 * a + 2) * cols]
-        ) + flat[:, (3 * a + 2) * cols : (3 * a + 3) * cols]
-        pieces.append(
-            lax.dot_general(
-                rows3, expand, (((1,), (1,)), ((), ())), precision=HI,
-                preferred_element_type=jnp.float32,
-            )
-        )
-    return jnp.concatenate(pieces, axis=1)
-
-
 def split3(values):
     hi = lax.reduce_precision(values, exponent_bits=8, mantissa_bits=7)
     rest = values - hi
@@ -247,14 +207,6 @@
 
 def shifted_pairs(count, shift):
     return [(i, (i + shift) % count) for i in range(count)]
-
-
-def gather_columns(values, ids):
-    levels, width = values.shape
-    onehot = (lax.broadcasted_iota(jnp.int32, (width, 1), 0) == ids[None, :]).astype(jnp.bfloat16)
-    parts = jnp.concatenate(split3(values), axis=0)
-    total = jnp.dot(parts, onehot, preferred_element_type=jnp.float32)
-    return (total[:levels] + total[levels : 2 * levels]) + total[2 * levels :]
 
 
 def gather_parts(parts, ids):
@@ -275,7 +227,7 @@
     return (total[:levels] + total[levels : 2 * levels]) + total[2 * levels :]
 
 
-def body(parent, nest, nu_parent, nu_nest, relax, feedback, vert_mix, fp_owner, fp_cell, nest_of):
+def body_steps(parent, nest, nu_parent, nu_nest, relax, feedback, vert_mix, fp_owner, fp_cell, nest_of):
     levels, p_rows, p_cols = parent.shape
     _, n_rows, n_cols = nest.shape
     tiles_x = lax.axis_size("gx")
@@ -325,7 +277,7 @@
     block_rows = n_rows // 3
     block_cols = n_cols // 3
     expand = column_expansion(block_cols, n_cols, zero)
-    forcing_full = expand_blocks(forcing_flat, block_rows, block_cols, n_cols, expand)
+    forcing_full = expand_blocks(forcing_flat, block_rows, block_cols, expand)
     row_start = here_x * n_rows
     left_w, right_w = row_weights(nest_segments(nest_of, row_start - 1, n_rows + 2))
     up_w = per_row(left_w, n_rows, n_cols)
@@ -342,10 +294,15 @@
         )
     (nudge_gap,) = extra
     if by_shift:
-        outgoing = jnp.where(chosen[:, None, :], nudge_gap[None, :, :], 0.0).astype(jnp.bfloat16)
+        outgoing = jnp.where(chosen[:, None, :], nudge_gap[None, :, :], 0.0)
         incoming = jnp.concatenate(
             [outgoing[0]]
-            + [lax.ppermute(outgoing[s], "gx", shifted_pairs(tiles_x, s)) for s in range(1, tiles_x)],
+            + [
+                lax.ppermute(outgoing[s].astype(jnp.float16), "gx", shifted_pairs(tiles_x, s)).astype(
+                    jnp.float32
+                )
+                for s in range(1, tiles_x)
+            ],
             axis=1,
         )
     else:
@@ -373,7 +330,7 @@
         P(),
     )
     return jax.shard_map(
-        body,
+        body_steps,
         mesh=mesh,
         in_specs=placed,
         out_specs=(P("groups", "gx", Y_AXES), P("groups", "gx", Y_AXES)),

time: 96.5 us -> 98.8 us (1.024); the launches traced: 95.7 us -> 96.9 us
  starting transfers between devices: 40.2 us -> 37.7 us
  waiting for transfers between devices: 17.4 us -> 19.7 us
  local copies, waits for them, and re-layouts: 13.3 us -> 14.3 us
    ppermute x3, waiting for transfers between devices: 4.33 us -> 8.72 us  [exchange(): below = lax.ppermute(first_rows, 'gx', bwd_x)]
    ppermute x3, waiting for transfers between devices: 2.44 us -> 0.01 us  [exchange(): right = lax.ppermute(first_cols, Y_AXES, bwd_y)]
    ppermute x3, starting transfers between devices: 9.05 us -> 6.78 us  [exchange(): left = lax.ppermute(last_cols, Y_AXES, fwd_y)]
    convert_element_type x3 -> x6, other arithmetic: 2.13 us -> 1.44 us  [the longest x1 1.16 us: body_steps(): nest_state.astype(jnp.bfloat16).reshape(levels, n_rows, n_cols)]
  transfers between devices with their start and end apart: 21 -> 21, of which waited for: 7 -> 7; matrix products, arithmetic and copies ran while one was open for 16% -> 17% of each run, Pallas kernels for 3% -> 3%
where the time goes in v13:
time: 98.8 us; the launch traced here: 96.9 us
  starting transfers between devices  37.7 us (38%)
  waiting for transfers between devices  19.7 us (20%)
  local copies, waits for them, and re-layouts  14.3 us (14%)
  Pallas kernels  13.2 us (13%)
  matrix products  5.98 us (6%)
  other arithmetic  4.8 us (5%)
  between operations  1.23 us (1%)
    pallas_call x4, Pallas kernels, stencil_step(): pl.pallas_call(functools.partial(step_kernel, rows=rows, cols=cols, xo=xo...  13.2 us
    ppermute x3, starting transfers between devices, exchange(): above = lax.ppermute(last_rows, 'gx', fwd_x)  8.87 us
    ppermute x3, waiting for transfers between devices, exchange(): below = lax.ppermute(first_rows, 'gx', bwd_x)  8.72 us
    ppermute x3, starting transfers between devices, body_steps(): lax.ppermute(wanted[s], 'gx', shifted_pairs(tiles_x, s))  8.1 us
    ppermute x3, starting transfers between devices, exchange(): left = lax.ppermute(last_cols, Y_AXES, fwd_y)  6.78 us
    ppermute x3, waiting for transfers between devices, body_steps(): lax.ppermute(gather_parts(parent_parts, served[s]), 'gx', shifted_pairs(t...  6.77 us
    unnamed x60, local copies, waits for them, and re-layouts  6.36 us
    ppermute x3, starting transfers between devices, body_steps(): lax.ppermute(outgoing[s].astype(jnp.float16), 'gx', shifted_pairs(tiles_x...  3.88 us
  transfers between devices with their start and end apart: 21, of which 7 were waited for; matrix products, arithmetic and copies ran while one was open for 17% of the time, Pallas kernels for 3%

profile of v13, /device:TPU:0, one launch (start us, length us, event | category | flops | bytes accessed | tf_op | source)
XLA Modules:
  0.0 96.9 jit_solution(12596514644670046424)
XLA Ops:
  2.1 3.1 %collective-permute-start.8 = (s32[256]{0:T(256)S(1)}, s32[256]{0:T(256)S(1)}, u32[]{:S(2)}, u32[]{:S(2)}) collective-permute-start(s32[256]{0:T(256)S(1)} %bitcast.81), channel_id=1, source_target_pairs={{0,4},{4,8},{8,12},{12,0},{1,5},{5,9},{9,13},{13,1},{2,6},{6,10},{... | collective-permute-start | bytes 3080 | tf_op jit(solution)/shard_map/ppermute | solution.py:253
  6.1 1.2 %fusion.44 = (bf16[80,1,256]{2,1,0:T(2,128)(2,1)S(1)}, bf16[80,1,256]{2,1,0:T(2,128)(2,1)S(1)}) fusion(bf16[80,8,256]{2,1,0:T(8,128)(2,1)} %param.10), kind=kLoop, calls=%fused_computation.108 | loop fusion | bytes 163840 | tf_op jit(solution)/shard_map/slice | solution.py:22
  7.4 3.6 %collective-permute-start = (bf16[80,640]{1,0:T(8,128)(2,1)S(1)}, bf16[80,640]{1,0:T(8,128)(2,1)S(1)}, u32[]{:S(2)}, u32[]{:S(2)}) collective-permute-start(bf16[80,640]{1,0:T(8,128)(2,1)S(1)} %pad_maximum_fusion.1), channel_id=1, source_target_pairs={{0,4},{4,8},{8,12},{1,5},{5,9},{9,13},{2,6},{6,10},{10,14},{3,7},{... | collective-permute-start | bytes 307208 | tf_op jit(solution)/shard_map/ppermute | solution.py:32
  11.0 1.3 %collective-permute-start.1 = (bf16[80,640]{1,0:T(8,128)(2,1)S(1)}, bf16[80,640]{1,0:T(8,128)(2,1)S(1)}, u32[]{:S(2)}, u32[]{:S(2)}) collective-permute-start(bf16[80,640]{1,0:T(8,128)(2,1)S(1)} %pad_maximum_fusion.2), channel_id=1, source_target_pairs={{4,0},{8,4},{12,8},{5,1},{9,5},{13,9},{6,2},{10,6},{14,10},{7,3},{... | collective-permute-start | bytes 307208 | tf_op jit(solution)/shard_map/ppermute | solution.py:33
  12.3 1.1 %fusion.42 = (bf16[80,6,1]{2,0,1:T(8,128)(2,1)S(1)}, bf16[80,6,1]{2,0,1:T(8,128)(2,1)S(1)}) fusion(bf16[80,6,384]{2,0,1:T(8,128)(2,1)} %param.11), kind=kLoop, calls=%fused_computation.106 | loop fusion | bytes 3840 | tf_op jit(solution)/shard_map/slice | solution.py:22
  14.0 1.3 %collective-permute-start.3 = (bf16[80,14]{1,0:T(8,128)(2,1)S(1)}, bf16[80,14]{1,0:T(8,128)(2,1)S(1)}, u32[]{:S(2)}, u32[]{:S(2)}) collective-permute-start(bf16[80,14]{1,0:T(8,128)(2,1)S(1)} %copy.49), channel_id=1, source_target_pairs={{1,0},{2,1},{3,2},{5,4},{6,5},{7,6},{9,8},{10,9},{11,10},{13,12},{... | collective-permute-start | bytes 6728 | tf_op jit(solution)/shard_map/ppermute | solution.py:35
  15.7 3.0 %collective-permute-start.2 = (bf16[80,14]{1,0:T(8,128)(2,1)S(1)}, bf16[80,14]{1,0:T(8,128)(2,1)S(1)}, u32[]{:S(2)}, u32[]{:S(2)}) collective-permute-start(bf16[80,14]{1,0:T(8,128)(2,1)S(1)} %copy.46), channel_id=1, source_target_pairs={{0,1},{1,2},{2,3},{4,5},{5,6},{6,7},{8,9},{9,10},{10,11},{12,13},{... | collective-permute-start | bytes 6728 | tf_op jit(solution)/shard_map/ppermute | solution.py:34
  24.6 3.7 %collective-permute-start.6 = (s32[256]{0:T(256)S(1)}, s32[256]{0:T(256)S(1)}, u32[]{:S(2)}, u32[]{:S(2)}) collective-permute-start(s32[256]{0:T(256)S(1)} %bitcast.79), channel_id=1, source_target_pairs={{0,8},{4,12},{8,0},{12,4},{1,9},{5,13},{9,1},{13,5},{2,10},{6,14},... | collective-permute-start | bytes 3080 | tf_op jit(solution)/shard_map/ppermute | solution.py:253
  28.2 1.4 %collective-permute-start.4 = (s32[256]{0:T(256)S(1)}, s32[256]{0:T(256)S(1)}, u32[]{:S(2)}, u32[]{:S(2)}) collective-permute-start(s32[256]{0:T(256)S(1)} %bitcast.80), channel_id=1, source_target_pairs={{0,12},{4,0},{8,4},{12,8},{1,13},{5,1},{9,5},{13,9},{2,14},{6,2},{... | collective-permute-start | bytes 3080 | tf_op jit(solution)/shard_map/ppermute | solution.py:253
  30.3 3.2 %shard_map.113 = (f32[80,2048]{1,0:T(8,128)}, bf16[80,256]{1,0:T(8,128)(2,1)}, bf16[80,256]{1,0:T(8,128)(2,1)}, bf16[80,8]{1,0:T(8,128)(2,1)}, bf16[80,8]{1,0:T(8,128)(2,1)}, /*index=5*/bf16[240,2048]{1,0:T(8,128)(2,1)}) custom-call(bf16[80,2048]{1,0:T(8,128)(2,1)} %bitcast.60, bf16[80,640]{1,0:T(8,128)(2,1)} %copy-done.6, bf16[80,640]{1,0:T(8,128)(2,1)} %copy-done.7, ...), custom_call_target="tpu_custom_call" | custom-call | flops 165806080 | bytes 1218240 | tf_op jit(solution)/shard_map/pallas_call | solution.py:158
  33.5 1.9 %fusion.4 = f32[240,256]{1,0:T(8,128)S(1)} fusion(bf16[240,2048]{1,0:T(8,128)(2,1)} %get-tuple-element.17, s32[256]{0:T(256)S(1)} %collective-permute-done.8), kind=kOutput, calls=%fused_computation.10 | convolution fusion | flops 252182528 | bytes 1229824 | tf_op jit(solution)/shard_map/dot_general | solution.py:216
  36.8 2.0 %collective-permute-start.7 = (f32[80,256]{1,0:T(8,128)S(1)}, f32[80,256]{1,0:T(8,128)S(1)}, u32[]{:S(2)}, u32[]{:S(2)}) collective-permute-start(f32[80,256]{1,0:T(8,128)S(1)} %slice_add_fusion.6), channel_id=1, source_target_pairs={{0,8},{4,12},{8,0},{12,4},{1,9},{5,13},{9,1},{13,5},{2,10},{6,14},... | collective-permute-start | bytes 245768 | tf_op jit(solution)/shard_map/ppermute | solution.py:257
  39.4 0.9 collective-permute-done.9
  40.3 5.9 %collective-permute-done.7 = f32[80,256]{1,0:T(8,128)S(1)} collective-permute-done((f32[80,256]{1,0:T(8,128)S(1)}, f32[80,256]{1,0:T(8,128)S(1)}, u32[]{:S(2)}, u32[]{:S(2)}) %collective-permute-start.7) | collective-permute-done | bytes 81952 | tf_op jit(solution)/shard_map/ppermute | solution.py:257
  47.8 3.1 %shard_map.114 = (f32[80,2304]{1,0:T(8,128)}, bf16[80,384]{1,0:T(8,128)(2,1)}, bf16[80,384]{1,0:T(8,128)(2,1)}, bf16[80,6]{1,0:T(8,128)(2,1)}, bf16[80,6]{1,0:T(8,128)(2,1)}) custom-call(bf16[80,2304]{1,0:T(8,128)(2,1)} %bitcast.57, bf16[80,640]{1,0:T(8,128)(2,1)} %copy-done.6, bf16[80,640]{1,0:T(8,128)(2,1)} %copy-done.7, bf16[80,14]{1,0:T(8,128)(2,1)} %copy-done.9, ...), custom_call_target="tpu_custom_call" | custom-call | flops 185057280 | bytes 2097152 | tf_op jit(solution)/shard_map/pallas_call | solution.py:158
  50.9 1.6 %collective-permute-start.12 = (bf16[80,6]{1,0:T(8,128)(2,1)}, bf16[80,6]{1,0:T(8,128)(2,1)S(1)}, u32[]{:S(2)}, u32[]{:S(2)}) collective-permute-start(bf16[80,6]{1,0:T(8,128)(2,1)} %get-tuple-element.21), channel_id=1, source_target_pairs={{0,1},{1,2},{2,3},{4,5},{5,6},{6,7},{8,9},{9,10},{10,11},{12,13},{... | collective-permute-start | bytes 2888 | tf_op jit(solution)/shard_map/ppermute | solution.py:34
  52.5 1.3 %collective-permute-start.13 = (bf16[80,6]{1,0:T(8,128)(2,1)}, bf16[80,6]{1,0:T(8,128)(2,1)S(1)}, u32[]{:S(2)}, u32[]{:S(2)}) collective-permute-start(bf16[80,6]{1,0:T(8,128)(2,1)} %get-tuple-element.22), channel_id=1, source_target_pairs={{1,0},{2,1},{3,2},{5,4},{6,5},{7,6},{9,8},{10,9},{11,10},{13,12},{... | collective-permute-start | bytes 2888 | tf_op jit(solution)/shard_map/ppermute | solution.py:35
  53.8 1.3 %collective-permute-start.10 = (bf16[80,384]{1,0:T(8,128)(2,1)}, bf16[80,384]{1,0:T(8,128)(2,1)S(1)}, u32[]{:S(2)}, u32[]{:S(2)}) collective-permute-start(bf16[80,384]{1,0:T(8,128)(2,1)} %get-tuple-element.19), channel_id=1, source_target_pairs={{0,4},{4,8},{8,12},{1,5},{5,9},{9,13},{2,6},{6,10},{10,14},{3,7},{... | collective-permute-start | bytes 184328 | tf_op jit(solution)/shard_map/ppermute | solution.py:32
  55.1 1.3 %collective-permute-start.11 = (bf16[80,384]{1,0:T(8,128)(2,1)}, bf16[80,384]{1,0:T(8,128)(2,1)S(1)}, u32[]{:S(2)}, u32[]{:S(2)}) collective-permute-start(bf16[80,384]{1,0:T(8,128)(2,1)} %get-tuple-element.20), channel_id=1, source_target_pairs={{4,0},{8,4},{12,8},{5,1},{9,5},{13,9},{6,2},{10,6},{14,10},{7,3},{... | collective-permute-start | bytes 184328 | tf_op jit(solution)/shard_map/ppermute | solution.py:33
  57.3 4.6 %collective-permute-done.11.refs_2_ = bf16[80,384]{1,0:T(8,128)(2,1)S(1)} collective-permute-done((bf16[80,384]{1,0:T(8,128)(2,1)}, bf16[80,384]{1,0:T(8,128)(2,1)S(1)}, u32[]{:S(2)}, u32[]{:S(2)}) %collective-permute-start.11) | collective-permute-done | bytes 61472 | tf_op jit(solution)/shard_map/ppermute | solution.py:33
  62.5 3.2 %shard_map.115 = (f32[80,2304]{1,0:T(8,128)}, bf16[80,384]{1,0:T(8,128)(2,1)}, bf16[80,384]{1,0:T(8,128)(2,1)}, bf16[80,6]{1,0:T(8,128)(2,1)}, bf16[80,6]{1,0:T(8,128)(2,1)}) custom-call(f32[80,2304]{1,0:T(8,128)} %get-tuple-element.18.refs_0_, bf16[80,384]{1,0:T(8,128)(2,1)} %copy-done.12, bf16[80,384]{1,0:T(8,128)(2,1)} %copy-done.13, ...), custom_call_target="tpu_custom_call" | custom-call | flops 185057280 | bytes 2381312 | tf_op jit(solution)/shard_map/pallas_call | solution.py:158
  65.7 2.2 %collective-permute-start.16 = (bf16[80,6]{1,0:T(8,128)(2,1)}, bf16[80,6]{1,0:T(8,128)(2,1)S(1)}, u32[]{:S(2)}, u32[]{:S(2)}) collective-permute-start(bf16[80,6]{1,0:T(8,128)(2,1)} %get-tuple-element.26), channel_id=1, source_target_pairs={{0,1},{1,2},{2,3},{4,5},{5,6},{6,7},{8,9},{9,10},{10,11},{12,13},{... | collective-permute-start | bytes 2888 | tf_op jit(solution)/shard_map/ppermute | solution.py:34
  67.8 1.3 %collective-permute-start.17 = (bf16[80,6]{1,0:T(8,128)(2,1)}, bf16[80,6]{1,0:T(8,128)(2,1)S(1)}, u32[]{:S(2)}, u32[]{:S(2)}) collective-permute-start(bf16[80,6]{1,0:T(8,128)(2,1)} %get-tuple-element.27), channel_id=1, source_target_pairs={{1,0},{2,1},{3,2},{5,4},{6,5},{7,6},{9,8},{10,9},{11,10},{13,12},{... | collective-permute-start | bytes 2888 | tf_op jit(solution)/shard_map/ppermute | solution.py:35
  69.1 4.0 %collective-permute-start.14 = (bf16[80,384]{1,0:T(8,128)(2,1)}, bf16[80,384]{1,0:T(8,128)(2,1)S(1)}, u32[]{:S(2)}, u32[]{:S(2)}) collective-permute-start(bf16[80,384]{1,0:T(8,128)(2,1)} %get-tuple-element.24), channel_id=1, source_target_pairs={{0,4},{4,8},{8,12},{1,5},{5,9},{9,13},{2,6},{6,10},{10,14},{3,7},{... | collective-permute-start | bytes 184328 | tf_op jit(solution)/shard_map/ppermute | solution.py:32
  73.1 1.3 %collective-permute-start.15 = (bf16[80,384]{1,0:T(8,128)(2,1)}, bf16[80,384]{1,0:T(8,128)(2,1)S(1)}, u32[]{:S(2)}, u32[]{:S(2)}) collective-permute-start(bf16[80,384]{1,0:T(8,128)(2,1)} %get-tuple-element.25), channel_id=1, source_target_pairs={{4,0},{8,4},{12,8},{5,1},{9,5},{13,9},{6,2},{10,6},{14,10},{7,3},{... | collective-permute-start | bytes 184328 | tf_op jit(solution)/shard_map/ppermute | solution.py:33
  75.3 4.2 %collective-permute-done.15.refs_4_ = bf16[80,384]{1,0:T(8,128)(2,1)S(1)} collective-permute-done((bf16[80,384]{1,0:T(8,128)(2,1)}, bf16[80,384]{1,0:T(8,128)(2,1)S(1)}, u32[]{:S(2)}, u32[]{:S(2)}) %collective-permute-start.15) | collective-permute-done | bytes 61472 | tf_op jit(solution)/shard_map/ppermute | solution.py:33
  80.1 3.7 %shard_map.116 = (f32[80,2304]{1,0:T(8,128)}, bf16[80,384]{1,0:T(8,128)(2,1)}, bf16[80,384]{1,0:T(8,128)(2,1)}, bf16[80,6]{1,0:T(8,128)(2,1)}, bf16[80,6]{1,0:T(8,128)(2,1)}, /*index=5*/f32[80,256]{1,0:T(8,128)}) custom-call(f32[128,384]{1,0:T(8,128)} %fusion.21.refs_0_, f32[80,256]{1,0:T(8,128)} %copy-done.4, f32[80,2304]{1,0:T(8,128)} %get-tuple-element.23.refs_2_, ...), custom_call_target="tpu_custom_call" | custom-call | flops 185057280 | bytes 2659840 | tf_op jit(solution)/shard_map/pallas_call | solution.py:158
  83.8 0.9 broadcast_select_fusion
  84.8 3.8 %collective-permute-start.20 = (f16[80,256]{1,0:T(8,128)(2,1)S(1)}, f16[80,256]{1,0:T(8,128)(2,1)S(1)}, u32[]{:S(2)}, u32[]{:S(2)}) collective-permute-start(f16[80,256]{1,0:T(8,128)(2,1)S(1)} %get-tuple-element.51), channel_id=1, source_target_pairs={{0,12},{4,0},{8,4},{12,8},{1,13},{5,1},{9,5},{13,9},{2,14},{6,2},{... | collective-permute-start | bytes 122888 | tf_op jit(solution)/shard_map/ppermute | solution.py:301
  88.6 1.2 %convert_element_type.63 = bf16[80,2304]{1,0:T(8,128)(2,1)S(1)} convert(f32[80,2304]{1,0:T(8,128)} %get-tuple-element.29) | non-fusion elementwise | flops 184320 | bytes 1105920 | tf_op jit(solution)/shard_map/convert_element_type | solution.py:315
  90.6 3.3 %collective-permute-done.19 = f16[80,256]{1,0:T(8,128)(2,1)S(1)} collective-permute-done((f16[80,256]{1,0:T(8,128)(2,1)S(1)}, f16[80,256]{1,0:T(8,128)(2,1)S(1)}, u32[]{:S(2)}, u32[]{:S(2)}) %collective-permute-start.19) | collective-permute-done | bytes 40992 | tf_op jit(solution)/shard_map/ppermute | solution.py:301
  94.0 1.9 %fusion = f32[240,2048]{1,0:T(8,128)S(1)} fusion(s32[1024]{0:T(1024)S(1)} %pad_add_fusion, bf16[80,1024]{1,0:T(8,128)(2,1)S(1)} %get-tuple-element.45, bf16[80,1024]{1,0:T(8,128)(2,1)S(1)} %get-tuple-element.44, bf16[80,1024]{1,0:T(8,128)(2,1)S(1)} %get-tuple-element.43), kind=kOutput, calls=%fused_computation.2 | convolution fusion | flops 1010204672 | bytes 2461696 | tf_op jit(solution)/shard_map/dot_general | solution.py:226
  (126 shorter events, 18.2 us)
Async XLA Ops:
  0.6 18.2 %copy-start = (s32[24]{0:T(128)S(1)}, s32[24]{0:T(128)}, u32[]{:S(2)}) copy-start(s32[24]{0:T(128)} %param.19) | copy-start | bytes 292
  0.6 12.7 %copy-start.2 = (bf16[80,8,256]{2,1,0:T(8,128)(2,1)S(1)}, bf16[80,8,256]{2,1,0:T(8,128)(2,1)}, u32[]{:S(2)}) copy-start(bf16[80,8,256]{2,1,0:T(8,128)(2,1)} %param.10) | copy-start | bytes 983044
  0.7 20.2 %copy-start.19 = (f32[80]{0:T(128)S(1)}, f32[80]{0:T(128)}, u32[]{:S(2)}) copy-start(f32[80]{0:T(128)} %param.13) | copy-start | bytes 964
  0.7 20.9 %copy-start.20 = (f32[80]{0:T(128)S(1)}, f32[80]{0:T(128)}, u32[]{:S(2)}) copy-start(f32[80]{0:T(128)} %param.14) | copy-start | bytes 964
  0.7 21.6 %copy-start.21 = (f32[80]{0:T(128)S(1)}, f32[80]{0:T(128)}, u32[]{:S(2)}) copy-start(f32[80]{0:T(128)} %param.12) | copy-start | bytes 964
  2.1 31.4 %collective-permute-start.8 = (s32[256]{0:T(256)S(1)}, s32[256]{0:T(256)S(1)}, u32[]{:S(2)}, u32[]{:S(2)}) collective-permute-start(s32[256]{0:T(256)S(1)} %bitcast.81), channel_id=1, source_target_pairs={{0,4},{4,8},{8,12},{12,0},{1,5},{5,9},{9,13},{13,1},{2,6},{6,10},{... | collective-permute-start | bytes 3080 | tf_op jit(solution)/shard_map/ppermute | solution.py:253
  7.3 16.5 %copy-start.3 = (bf16[80,6,384]{2,0,1:T(8,128)(2,1)S(1)}, bf16[80,6,384]{2,0,1:T(8,128)(2,1)}, u32[]{:S(2)}) copy-start(bf16[80,6,384]{2,0,1:T(8,128)(2,1)} %param.11) | copy-start | bytes 1105924
  7.4 22.2 %collective-permute-start = (bf16[80,640]{1,0:T(8,128)(2,1)S(1)}, bf16[80,640]{1,0:T(8,128)(2,1)S(1)}, u32[]{:S(2)}, u32[]{:S(2)}) collective-permute-start(bf16[80,640]{1,0:T(8,128)(2,1)S(1)} %pad_maximum_fusion.1), channel_id=1, source_target_pairs={{0,4},{4,8},{8,12},{1,5},{5,9},{9,13},{2,6},{6,10},{10,14},{3,7},{... | collective-permute-start | bytes 307208 | tf_op jit(solution)/shard_map/ppermute | solution.py:32
  11.0 18.6 %collective-permute-start.1 = (bf16[80,640]{1,0:T(8,128)(2,1)S(1)}, bf16[80,640]{1,0:T(8,128)(2,1)S(1)}, u32[]{:S(2)}, u32[]{:S(2)}) collective-permute-start(bf16[80,640]{1,0:T(8,128)(2,1)S(1)} %pad_maximum_fusion.2), channel_id=1, source_target_pairs={{4,0},{8,4},{12,8},{5,1},{9,5},{13,9},{6,2},{10,6},{14,10},{7,3},{... | collective-permute-start | bytes 307208 | tf_op jit(solution)/shard_map/ppermute | solution.py:33
  14.0 10.6 %collective-permute-start.3 = (bf16[80,14]{1,0:T(8,128)(2,1)S(1)}, bf16[80,14]{1,0:T(8,128)(2,1)S(1)}, u32[]{:S(2)}, u32[]{:S(2)}) collective-permute-start(bf16[80,14]{1,0:T(8,128)(2,1)S(1)} %copy.49), channel_id=1, source_target_pairs={{1,0},{2,1},{3,2},{5,4},{6,5},{7,6},{9,8},{10,9},{11,10},{13,12},{... | collective-permute-start | bytes 6728 | tf_op jit(solution)/shard_map/ppermute | solution.py:35
  15.7 12.5 %collective-permute-start.2 = (bf16[80,14]{1,0:T(8,128)(2,1)S(1)}, bf16[80,14]{1,0:T(8,128)(2,1)S(1)}, u32[]{:S(2)}, u32[]{:S(2)}) collective-permute-start(bf16[80,14]{1,0:T(8,128)(2,1)S(1)} %copy.46), channel_id=1, source_target_pairs={{0,1},{1,2},{2,3},{4,5},{5,6},{6,7},{8,9},{9,10},{10,11},{12,13},{... | collective-permute-start | bytes 6728 | tf_op jit(solution)/shard_map/ppermute | solution.py:34
  24.6 5.0 %copy-start.8 = (bf16[80,14]{1,0:T(8,128)(2,1)}, bf16[80,14]{1,0:T(8,128)(2,1)S(1)}, u32[]{:S(2)}) copy-start(bf16[80,14]{1,0:T(8,128)(2,1)S(1)} %collective-permute-done.3.refs_4_) | copy-start | bytes 6724
  24.6 11.6 %collective-permute-start.6 = (s32[256]{0:T(256)S(1)}, s32[256]{0:T(256)S(1)}, u32[]{:S(2)}, u32[]{:S(2)}) collective-permute-start(s32[256]{0:T(256)S(1)} %bitcast.79), channel_id=1, source_target_pairs={{0,8},{4,12},{8,0},{12,4},{1,9},{5,13},{9,1},{13,5},{2,10},{6,14},... | collective-permute-start | bytes 3080 | tf_op jit(solution)/shard_map/ppermute | solution.py:253
  28.2 7.4 %collective-permute-start.4 = (s32[256]{0:T(256)S(1)}, s32[256]{0:T(256)S(1)}, u32[]{:S(2)}, u32[]{:S(2)}) collective-permute-start(s32[256]{0:T(256)S(1)} %bitcast.80), channel_id=1, source_target_pairs={{0,12},{4,0},{8,4},{12,8},{1,13},{5,1},{9,5},{13,9},{2,14},{6,2},{... | collective-permute-start | bytes 3080 | tf_op jit(solution)/shard_map/ppermute | solution.py:253
  35.4 5.0 %collective-permute-start.9 = (f32[80,256]{1,0:T(8,128)S(1)}, f32[80,256]{1,0:T(8,128)S(1)}, u32[]{:S(2)}, u32[]{:S(2)}) collective-permute-start(f32[80,256]{1,0:T(8,128)S(1)} %slice_add_fusion.4), channel_id=1, source_target_pairs={{0,12},{4,0},{8,4},{12,8},{1,13},{5,1},{9,5},{13,9},{2,14},{6,2},{... | collective-permute-start | bytes 245768 | tf_op jit(solution)/shard_map/ppermute | solution.py:257
  36.8 9.4 %collective-permute-start.7 = (f32[80,256]{1,0:T(8,128)S(1)}, f32[80,256]{1,0:T(8,128)S(1)}, u32[]{:S(2)}, u32[]{:S(2)}) collective-permute-start(f32[80,256]{1,0:T(8,128)S(1)} %slice_add_fusion.6), channel_id=1, source_target_pairs={{0,8},{4,12},{8,0},{12,4},{1,9},{5,13},{9,1},{13,5},{2,10},{6,14},... | collective-permute-start | bytes 245768 | tf_op jit(solution)/shard_map/ppermute | solution.py:257
  38.8 7.4 %collective-permute-start.5 = (f32[80,256]{1,0:T(8,128)S(1)}, f32[80,256]{1,0:T(8,128)S(1)}, u32[]{:S(2)}, u32[]{:S(2)}) collective-permute-start(f32[80,256]{1,0:T(8,128)S(1)} %slice_add_fusion.8), channel_id=1, source_target_pairs={{0,4},{4,8},{8,12},{12,0},{1,5},{5,9},{9,13},{13,1},{2,6},{6,10},{... | collective-permute-start | bytes 245768 | tf_op jit(solution)/shard_map/ppermute | solution.py:257
  46.2 19.4 %copy-start.4 = (f32[80,256]{1,0:T(8,128)}, f32[80,256]{1,0:T(8,128)S(1)}, u32[]{:S(2)}) copy-start(f32[80,256]{1,0:T(8,128)S(1)} %fusion.32.refs_1_) | copy-start | bytes 245764
  50.9 6.3 %collective-permute-start.12 = (bf16[80,6]{1,0:T(8,128)(2,1)}, bf16[80,6]{1,0:T(8,128)(2,1)S(1)}, u32[]{:S(2)}, u32[]{:S(2)}) collective-permute-start(bf16[80,6]{1,0:T(8,128)(2,1)} %get-tuple-element.21), channel_id=1, source_target_pairs={{0,1},{1,2},{2,3},{4,5},{5,6},{6,7},{8,9},{9,10},{10,11},{12,13},{... | collective-permute-start | bytes 2888 | tf_op jit(solution)/shard_map/ppermute | solution.py:34
  52.5 4.7 %collective-permute-start.13 = (bf16[80,6]{1,0:T(8,128)(2,1)}, bf16[80,6]{1,0:T(8,128)(2,1)S(1)}, u32[]{:S(2)}, u32[]{:S(2)}) collective-permute-start(bf16[80,6]{1,0:T(8,128)(2,1)} %get-tuple-element.22), channel_id=1, source_target_pairs={{1,0},{2,1},{3,2},{5,4},{6,5},{7,6},{9,8},{10,9},{11,10},{13,12},{... | collective-permute-start | bytes 2888 | tf_op jit(solution)/shard_map/ppermute | solution.py:35
  53.8 3.5 %collective-permute-start.10 = (bf16[80,384]{1,0:T(8,128)(2,1)}, bf16[80,384]{1,0:T(8,128)(2,1)S(1)}, u32[]{:S(2)}, u32[]{:S(2)}) collective-permute-start(bf16[80,384]{1,0:T(8,128)(2,1)} %get-tuple-element.19), channel_id=1, source_target_pairs={{0,4},{4,8},{8,12},{1,5},{5,9},{9,13},{2,6},{6,10},{10,14},{3,7},{... | collective-permute-start | bytes 184328 | tf_op jit(solution)/shard_map/ppermute | solution.py:32
  55.1 6.7 %collective-permute-start.11 = (bf16[80,384]{1,0:T(8,128)(2,1)}, bf16[80,384]{1,0:T(8,128)(2,1)S(1)}, u32[]{:S(2)}, u32[]{:S(2)}) collective-permute-start(bf16[80,384]{1,0:T(8,128)(2,1)} %get-tuple-element.20), channel_id=1, source_target_pairs={{4,0},{8,4},{12,8},{5,1},{9,5},{13,9},{6,2},{10,6},{14,10},{7,3},{... | collective-permute-start | bytes 184328 | tf_op jit(solution)/shard_map/ppermute | solution.py:33
  57.2 4.7 %copy-start.16 = (bf16[80,6]{1,0:T(8,128)(2,1)}, bf16[80,6]{1,0:T(8,128)(2,1)S(1)}, u32[]{:S(2)}) copy-start(bf16[80,6]{1,0:T(8,128)(2,1)S(1)} %collective-permute-done.12.refs_3_) | copy-start | bytes 2884
  65.7 8.8 %collective-permute-start.16 = (bf16[80,6]{1,0:T(8,128)(2,1)}, bf16[80,6]{1,0:T(8,128)(2,1)S(1)}, u32[]{:S(2)}, u32[]{:S(2)}) collective-permute-start(bf16[80,6]{1,0:T(8,128)(2,1)} %get-tuple-element.26), channel_id=1, source_target_pairs={{0,1},{1,2},{2,3},{4,5},{5,6},{6,7},{8,9},{9,10},{10,11},{12,13},{... | collective-permute-start | bytes 2888 | tf_op jit(solution)/shard_map/ppermute | solution.py:34
  67.8 6.6 %collective-permute-start.17 = (bf16[80,6]{1,0:T(8,128)(2,1)}, bf16[80,6]{1,0:T(8,128)(2,1)S(1)}, u32[]{:S(2)}, u32[]{:S(2)}) collective-permute-start(bf16[80,6]{1,0:T(8,128)(2,1)} %get-tuple-element.27), channel_id=1, source_target_pairs={{1,0},{2,1},{3,2},{5,4},{6,5},{7,6},{9,8},{10,9},{11,10},{13,12},{... | collective-permute-start | bytes 2888 | tf_op jit(solution)/shard_map/ppermute | solution.py:35
  69.1 6.1 %collective-permute-start.14 = (bf16[80,384]{1,0:T(8,128)(2,1)}, bf16[80,384]{1,0:T(8,128)(2,1)S(1)}, u32[]{:S(2)}, u32[]{:S(2)}) collective-permute-start(bf16[80,384]{1,0:T(8,128)(2,1)} %get-tuple-element.24), channel_id=1, source_target_pairs={{0,4},{4,8},{8,12},{1,5},{5,9},{9,13},{2,6},{6,10},{10,14},{3,7},{... | collective-permute-start | bytes 184328 | tf_op jit(solution)/shard_map/ppermute | solution.py:32
  73.1 6.3 %collective-permute-start.15 = (bf16[80,384]{1,0:T(8,128)(2,1)}, bf16[80,384]{1,0:T(8,128)(2,1)S(1)}, u32[]{:S(2)}, u32[]{:S(2)}) collective-permute-start(bf16[80,384]{1,0:T(8,128)(2,1)} %get-tuple-element.25), channel_id=1, source_target_pairs={{4,0},{8,4},{12,8},{5,1},{9,5},{13,9},{6,2},{10,6},{14,10},{7,3},{... | collective-permute-start | bytes 184328 | tf_op jit(solution)/shard_map/ppermute | solution.py:33
  74.4 5.0 %copy-start.14 = (bf16[80,6]{1,0:T(8,128)(2,1)}, bf16[80,6]{1,0:T(8,128)(2,1)S(1)}, u32[]{:S(2)}) copy-start(bf16[80,6]{1,0:T(8,128)(2,1)S(1)} %collective-permute-done.16.refs_5_) | copy-start | bytes 2884
  74.5 5.0 %copy-start.15 = (bf16[80,6]{1,0:T(8,128)(2,1)}, bf16[80,6]{1,0:T(8,128)(2,1)S(1)}, u32[]{:S(2)}) copy-start(bf16[80,6]{1,0:T(8,128)(2,1)S(1)} %collective-permute-done.17.refs_6_) | copy-start | bytes 2884
  84.7 5.9 %collective-permute-start.18 = (f16[80,256]{1,0:T(8,128)(2,1)S(1)}, f16[80,256]{1,0:T(8,128)(2,1)S(1)}, u32[]{:S(2)}, u32[]{:S(2)}) collective-permute-start(f16[80,256]{1,0:T(8,128)(2,1)S(1)} %get-tuple-element.50), channel_id=1, source_target_pairs={{0,4},{4,8},{8,12},{12,0},{1,5},{5,9},{9,13},{13,1},{2,6},{6,10},{... | collective-permute-start | bytes 122888 | tf_op jit(solution)/shard_map/ppermute | solution.py:301
  84.8 5.8 %collective-permute-start.20 = (f16[80,256]{1,0:T(8,128)(2,1)S(1)}, f16[80,256]{1,0:T(8,128)(2,1)S(1)}, u32[]{:S(2)}, u32[]{:S(2)}) collective-permute-start(f16[80,256]{1,0:T(8,128)(2,1)S(1)} %get-tuple-element.51), channel_id=1, source_target_pairs={{0,12},{4,0},{8,4},{12,8},{1,13},{5,1},{9,5},{13,9},{2,14},{6,2},{... | collective-permute-start | bytes 122888 | tf_op jit(solution)/shard_map/ppermute | solution.py:301
  88.6 5.3 %collective-permute-start.19 = (f16[80,256]{1,0:T(8,128)(2,1)S(1)}, f16[80,256]{1,0:T(8,128)(2,1)S(1)}, u32[]{:S(2)}, u32[]{:S(2)}) collective-permute-start(f16[80,256]{1,0:T(8,128)(2,1)S(1)} %get-tuple-element.52), channel_id=1, source_target_pairs={{0,8},{4,12},{8,0},{12,4},{1,9},{5,13},{9,1},{13,5},{2,10},{6,14},... | collective-permute-start | bytes 122888 | tf_op jit(solution)/shard_map/ppermute | solution.py:301
  (12 other events, 24.2 us)

commit v14 on v13

--- a/solution.py
+++ b/solution.py
@@ -294,15 +294,10 @@
         )
     (nudge_gap,) = extra
     if by_shift:
-        outgoing = jnp.where(chosen[:, None, :], nudge_gap[None, :, :], 0.0)
+        outgoing = jnp.where(chosen[:, None, :], nudge_gap[None, :, :], 0.0).astype(jnp.bfloat16)
         incoming = jnp.concatenate(
             [outgoing[0]]
-            + [
-                lax.ppermute(outgoing[s].astype(jnp.float16), "gx", shifted_pairs(tiles_x, s)).astype(
-                    jnp.float32
-                )
-                for s in range(1, tiles_x)
-            ],
+            + [lax.ppermute(outgoing[s], "gx", shifted_pairs(tiles_x, s)) for s in range(1, tiles_x)],
             axis=1,
         )
     else:

time: 98.8 us -> 96.5 us (0.977); the launches traced: 96.9 us -> 95.7 us
  starting transfers between devices: 37.7 us -> 40.2 us
  waiting for transfers between devices: 19.7 us -> 17.4 us
  local copies, waits for them, and re-layouts: 14.3 us -> 13.3 us
    ppermute x3, waiting for transfers between devices: 8.72 us -> 4.33 us  [exchange(): below = lax.ppermute(first_rows, 'gx', bwd_x)]
    ppermute x3, waiting for transfers between devices: 0.01 us -> 2.44 us  [exchange(): right = lax.ppermute(first_cols, Y_AXES, bwd_y)]
    ppermute x3, starting transfers between devices: 6.78 us -> 9.05 us  [exchange(): left = lax.ppermute(last_cols, Y_AXES, fwd_y)]
  transfers between devices with their start and end apart: 21 -> 21, of which waited for: 7 -> 7; matrix products, arithmetic and copies ran while one was open for 17% -> 16% of each run, Pallas kernels for 3% -> 3%
where the time goes in v14:
time: 96.5 us; the launch traced here: 95.7 us
  starting transfers between devices  40.2 us (42%)
  waiting for transfers between devices  17.4 us (18%)
  local copies, waits for them, and re-layouts  13.3 us (14%)
  Pallas kernels  13.2 us (14%)
  matrix products  5.93 us (6%)
  other arithmetic  4.59 us (5%)
  between operations  1.17 us (1%)
    pallas_call x4, Pallas kernels, stencil_step(): pl.pallas_call(functools.partial(step_kernel, rows=rows, cols=cols, xo=xo...  13.2 us
    ppermute x3, starting transfers between devices, exchange(): above = lax.ppermute(last_rows, 'gx', fwd_x)  9.32 us
    ppermute x3, starting transfers between devices, exchange(): left = lax.ppermute(last_cols, Y_AXES, fwd_y)  9.05 us
    ppermute x3, starting transfers between devices, body_steps(): lax.ppermute(wanted[s], 'gx', shifted_pairs(tiles_x, s))  8.1 us
    ppermute x3, waiting for transfers between devices, body_steps(): lax.ppermute(gather_parts(parent_parts, served[s]), 'gx', shifted_pairs(t...  6.78 us
    unnamed x60, local copies, waits for them, and re-layouts  6.38 us
    ppermute x3, waiting for transfers between devices, exchange(): below = lax.ppermute(first_rows, 'gx', bwd_x)  4.33 us
    ppermute x3, starting transfers between devices, exchange(): below = lax.ppermute(first_rows, 'gx', bwd_x)  3.88 us
  transfers between devices with their start and end apart: 21, of which 7 were waited for; matrix products, arithmetic and copies ran while one was open for 16% of the time, Pallas kernels for 3%

profile of v14, /device:TPU:0, one launch (start us, length us, event | category | flops | bytes accessed | tf_op | source)
XLA Modules:
  0.0 95.7 jit_solution(7650643628331021636)
XLA Ops:
  2.1 3.1 %collective-permute-start.8 = (s32[256]{0:T(256)S(1)}, s32[256]{0:T(256)S(1)}, u32[]{:S(2)}, u32[]{:S(2)}) collective-permute-start(s32[256]{0:T(256)S(1)} %bitcast.81), channel_id=1, source_target_pairs={{0,4},{4,8},{8,12},{12,0},{1,5},{5,9},{9,13},{13,1},{2,6},{6,10},{... | collective-permute-start | bytes 3080 | tf_op jit(solution)/shard_map/ppermute | solution.py:253
  6.1 1.2 %fusion.42 = (bf16[80,1,256]{2,1,0:T(2,128)(2,1)S(1)}, bf16[80,1,256]{2,1,0:T(2,128)(2,1)S(1)}) fusion(bf16[80,8,256]{2,1,0:T(8,128)(2,1)} %param.10), kind=kLoop, calls=%fused_computation.100 | loop fusion | bytes 163840 | tf_op jit(solution)/shard_map/slice | solution.py:22
  7.4 3.5 %collective-permute-start = (bf16[80,640]{1,0:T(8,128)(2,1)S(1)}, bf16[80,640]{1,0:T(8,128)(2,1)S(1)}, u32[]{:S(2)}, u32[]{:S(2)}) collective-permute-start(bf16[80,640]{1,0:T(8,128)(2,1)S(1)} %pad_maximum_fusion), channel_id=1, source_target_pairs={{0,4},{4,8},{8,12},{1,5},{5,9},{9,13},{2,6},{6,10},{10,14},{3,7},{... | collective-permute-start | bytes 307208 | tf_op jit(solution)/shard_map/ppermute | solution.py:32
  10.9 1.3 %collective-permute-start.1 = (bf16[80,640]{1,0:T(8,128)(2,1)S(1)}, bf16[80,640]{1,0:T(8,128)(2,1)S(1)}, u32[]{:S(2)}, u32[]{:S(2)}) collective-permute-start(bf16[80,640]{1,0:T(8,128)(2,1)S(1)} %pad_maximum_fusion.1), channel_id=1, source_target_pairs={{4,0},{8,4},{12,8},{5,1},{9,5},{13,9},{6,2},{10,6},{14,10},{7,3},{... | collective-permute-start | bytes 307208 | tf_op jit(solution)/shard_map/ppermute | solution.py:33
  12.9 1.3 %collective-permute-start.3 = (bf16[80,14]{1,0:T(8,128)(2,1)S(1)}, bf16[80,14]{1,0:T(8,128)(2,1)S(1)}, u32[]{:S(2)}, u32[]{:S(2)}) collective-permute-start(bf16[80,14]{1,0:T(8,128)(2,1)S(1)} %copy.49), channel_id=1, source_target_pairs={{1,0},{2,1},{3,2},{5,4},{6,5},{7,6},{9,8},{10,9},{11,10},{13,12},{... | collective-permute-start | bytes 6728 | tf_op jit(solution)/shard_map/ppermute | solution.py:35
  14.6 3.0 %collective-permute-start.2 = (bf16[80,14]{1,0:T(8,128)(2,1)S(1)}, bf16[80,14]{1,0:T(8,128)(2,1)S(1)}, u32[]{:S(2)}, u32[]{:S(2)}) collective-permute-start(bf16[80,14]{1,0:T(8,128)(2,1)S(1)} %copy.46), channel_id=1, source_target_pairs={{0,1},{1,2},{2,3},{4,5},{5,6},{6,7},{8,9},{9,10},{10,11},{12,13},{... | collective-permute-start | bytes 6728 | tf_op jit(solution)/shard_map/ppermute | solution.py:34
  23.5 3.7 %collective-permute-start.6 = (s32[256]{0:T(256)S(1)}, s32[256]{0:T(256)S(1)}, u32[]{:S(2)}, u32[]{:S(2)}) collective-permute-start(s32[256]{0:T(256)S(1)} %bitcast.79), channel_id=1, source_target_pairs={{0,8},{4,12},{8,0},{12,4},{1,9},{5,13},{9,1},{13,5},{2,10},{6,14},... | collective-permute-start | bytes 3080 | tf_op jit(solution)/shard_map/ppermute | solution.py:253
  27.2 1.4 %collective-permute-start.4 = (s32[256]{0:T(256)S(1)}, s32[256]{0:T(256)S(1)}, u32[]{:S(2)}, u32[]{:S(2)}) collective-permute-start(s32[256]{0:T(256)S(1)} %bitcast.80), channel_id=1, source_target_pairs={{0,12},{4,0},{8,4},{12,8},{1,13},{5,1},{9,5},{13,9},{2,14},{6,2},{... | collective-permute-start | bytes 3080 | tf_op jit(solution)/shard_map/ppermute | solution.py:253
  29.2 3.2 %shard_map.113 = (f32[80,2048]{1,0:T(8,128)}, bf16[80,256]{1,0:T(8,128)(2,1)}, bf16[80,256]{1,0:T(8,128)(2,1)}, bf16[80,8]{1,0:T(8,128)(2,1)}, bf16[80,8]{1,0:T(8,128)(2,1)}, /*index=5*/bf16[240,2048]{1,0:T(8,128)(2,1)}) custom-call(bf16[80,2048]{1,0:T(8,128)(2,1)} %bitcast.59, bf16[80,640]{1,0:T(8,128)(2,1)} %copy-done.6, bf16[80,640]{1,0:T(8,128)(2,1)} %copy-done.7, ...), custom_call_target="tpu_custom_call" | custom-call | flops 165806080 | bytes 1218240 | tf_op jit(solution)/shard_map/pallas_call | solution.py:158
  32.4 1.9 %fusion.5 = f32[240,256]{1,0:T(8,128)S(1)} fusion(bf16[240,2048]{1,0:T(8,128)(2,1)} %get-tuple-element.17, s32[256]{0:T(256)S(1)} %collective-permute-done.8), kind=kOutput, calls=%fused_computation.11 | convolution fusion | flops 252182528 | bytes 1229824 | tf_op jit(solution)/shard_map/dot_general | solution.py:216
  35.7 2.0 %collective-permute-start.7 = (f32[80,256]{1,0:T(8,128)S(1)}, f32[80,256]{1,0:T(8,128)S(1)}, u32[]{:S(2)}, u32[]{:S(2)}) collective-permute-start(f32[80,256]{1,0:T(8,128)S(1)} %slice_add_fusion.4), channel_id=1, source_target_pairs={{0,8},{4,12},{8,0},{12,4},{1,9},{5,13},{9,1},{13,5},{2,10},{6,14},... | collective-permute-start | bytes 245768 | tf_op jit(solution)/shard_map/ppermute | solution.py:257
  38.3 0.9 collective-permute-done.9
  39.2 5.9 %collective-permute-done.7 = f32[80,256]{1,0:T(8,128)S(1)} collective-permute-done((f32[80,256]{1,0:T(8,128)S(1)}, f32[80,256]{1,0:T(8,128)S(1)}, u32[]{:S(2)}, u32[]{:S(2)}) %collective-permute-start.7) | collective-permute-done | bytes 81952 | tf_op jit(solution)/shard_map/ppermute | solution.py:257
  45.8 0.9 copy-done.1
  46.7 3.1 %shard_map.114 = (f32[80,2304]{1,0:T(8,128)}, bf16[80,384]{1,0:T(8,128)(2,1)}, bf16[80,384]{1,0:T(8,128)(2,1)}, bf16[80,6]{1,0:T(8,128)(2,1)}, bf16[80,6]{1,0:T(8,128)(2,1)}) custom-call(bf16[80,2304]{1,0:T(8,128)(2,1)} %bitcast.57, bf16[80,640]{1,0:T(8,128)(2,1)} %copy-done.6, bf16[80,640]{1,0:T(8,128)(2,1)} %copy-done.7, bf16[80,14]{1,0:T(8,128)(2,1)} %copy-done.9, ...), custom_call_target="tpu_custom_call" | custom-call | flops 185057280 | bytes 2097152 | tf_op jit(solution)/shard_map/pallas_call | solution.py:158
  49.8 1.3 %collective-permute-start.10 = (bf16[80,384]{1,0:T(8,128)(2,1)}, bf16[80,384]{1,0:T(8,128)(2,1)S(1)}, u32[]{:S(2)}, u32[]{:S(2)}) collective-permute-start(bf16[80,384]{1,0:T(8,128)(2,1)} %get-tuple-element.19), channel_id=1, source_target_pairs={{0,4},{4,8},{8,12},{1,5},{5,9},{9,13},{2,6},{6,10},{10,14},{3,7},{... | collective-permute-start | bytes 184328 | tf_op jit(solution)/shard_map/ppermute | solution.py:32
  51.1 1.3 %collective-permute-start.11 = (bf16[80,384]{1,0:T(8,128)(2,1)}, bf16[80,384]{1,0:T(8,128)(2,1)S(1)}, u32[]{:S(2)}, u32[]{:S(2)}) collective-permute-start(bf16[80,384]{1,0:T(8,128)(2,1)} %get-tuple-element.20), channel_id=1, source_target_pairs={{4,0},{8,4},{12,8},{5,1},{9,5},{13,9},{6,2},{10,6},{14,10},{7,3},{... | collective-permute-start | bytes 184328 | tf_op jit(solution)/shard_map/ppermute | solution.py:33
  52.4 1.6 %collective-permute-start.12 = (bf16[80,6]{1,0:T(8,128)(2,1)}, bf16[80,6]{1,0:T(8,128)(2,1)S(1)}, u32[]{:S(2)}, u32[]{:S(2)}) collective-permute-start(bf16[80,6]{1,0:T(8,128)(2,1)} %get-tuple-element.21), channel_id=1, source_target_pairs={{0,1},{1,2},{2,3},{4,5},{5,6},{6,7},{8,9},{9,10},{10,11},{12,13},{... | collective-permute-start | bytes 2888 | tf_op jit(solution)/shard_map/ppermute | solution.py:34
  54.0 1.3 %collective-permute-start.13 = (bf16[80,6]{1,0:T(8,128)(2,1)}, bf16[80,6]{1,0:T(8,128)(2,1)S(1)}, u32[]{:S(2)}, u32[]{:S(2)}) collective-permute-start(bf16[80,6]{1,0:T(8,128)(2,1)} %get-tuple-element.22), channel_id=1, source_target_pairs={{1,0},{2,1},{3,2},{5,4},{6,5},{7,6},{9,8},{10,9},{11,10},{13,12},{... | collective-permute-start | bytes 2888 | tf_op jit(solution)/shard_map/ppermute | solution.py:35
  55.3 2.4 %collective-permute-done.13.refs_4_ = bf16[80,6]{1,0:T(8,128)(2,1)S(1)} collective-permute-done((bf16[80,6]{1,0:T(8,128)(2,1)}, bf16[80,6]{1,0:T(8,128)(2,1)S(1)}, u32[]{:S(2)}, u32[]{:S(2)}) %collective-permute-start.13) | collective-permute-done | bytes 992 | tf_op jit(solution)/shard_map/ppermute | solution.py:35
  58.4 3.2 %shard_map.115 = (f32[80,2304]{1,0:T(8,128)}, bf16[80,384]{1,0:T(8,128)(2,1)}, bf16[80,384]{1,0:T(8,128)(2,1)}, bf16[80,6]{1,0:T(8,128)(2,1)}, bf16[80,6]{1,0:T(8,128)(2,1)}) custom-call(f32[80,2304]{1,0:T(8,128)} %get-tuple-element.18.refs_0_, bf16[80,384]{1,0:T(8,128)(2,1)} %copy-done.12, bf16[80,384]{1,0:T(8,128)(2,1)} %copy-done.13, ...), custom_call_target="tpu_custom_call" | custom-call | flops 185057280 | bytes 2381312 | tf_op jit(solution)/shard_map/pallas_call | solution.py:158
  61.6 4.4 %collective-permute-start.16 = (bf16[80,6]{1,0:T(8,128)(2,1)}, bf16[80,6]{1,0:T(8,128)(2,1)S(1)}, u32[]{:S(2)}, u32[]{:S(2)}) collective-permute-start(bf16[80,6]{1,0:T(8,128)(2,1)} %get-tuple-element.26), channel_id=1, source_target_pairs={{0,1},{1,2},{2,3},{4,5},{5,6},{6,7},{8,9},{9,10},{10,11},{12,13},{... | collective-permute-start | bytes 2888 | tf_op jit(solution)/shard_map/ppermute | solution.py:34
  66.0 1.3 %collective-permute-start.17 = (bf16[80,6]{1,0:T(8,128)(2,1)}, bf16[80,6]{1,0:T(8,128)(2,1)S(1)}, u32[]{:S(2)}, u32[]{:S(2)}) collective-permute-start(bf16[80,6]{1,0:T(8,128)(2,1)} %get-tuple-element.27), channel_id=1, source_target_pairs={{1,0},{2,1},{3,2},{5,4},{6,5},{7,6},{9,8},{10,9},{11,10},{13,12},{... | collective-permute-start | bytes 2888 | tf_op jit(solution)/shard_map/ppermute | solution.py:35
  67.3 4.5 %collective-permute-start.14 = (bf16[80,384]{1,0:T(8,128)(2,1)}, bf16[80,384]{1,0:T(8,128)(2,1)S(1)}, u32[]{:S(2)}, u32[]{:S(2)}) collective-permute-start(bf16[80,384]{1,0:T(8,128)(2,1)} %get-tuple-element.24), channel_id=1, source_target_pairs={{0,4},{4,8},{8,12},{1,5},{5,9},{9,13},{2,6},{6,10},{10,14},{3,7},{... | collective-permute-start | bytes 184328 | tf_op jit(solution)/shard_map/ppermute | solution.py:32
  71.9 1.3 %collective-permute-start.15 = (bf16[80,384]{1,0:T(8,128)(2,1)}, bf16[80,384]{1,0:T(8,128)(2,1)S(1)}, u32[]{:S(2)}, u32[]{:S(2)}) collective-permute-start(bf16[80,384]{1,0:T(8,128)(2,1)} %get-tuple-element.25), channel_id=1, source_target_pairs={{4,0},{8,4},{12,8},{5,1},{9,5},{13,9},{6,2},{10,6},{14,10},{7,3},{... | collective-permute-start | bytes 184328 | tf_op jit(solution)/shard_map/ppermute | solution.py:33
  74.4 4.3 %collective-permute-done.15.refs_4_ = bf16[80,384]{1,0:T(8,128)(2,1)S(1)} collective-permute-done((bf16[80,384]{1,0:T(8,128)(2,1)}, bf16[80,384]{1,0:T(8,128)(2,1)S(1)}, u32[]{:S(2)}, u32[]{:S(2)}) %collective-permute-start.15) | collective-permute-done | bytes 61472 | tf_op jit(solution)/shard_map/ppermute | solution.py:33
  79.4 3.7 %shard_map.116 = (f32[80,2304]{1,0:T(8,128)}, bf16[80,384]{1,0:T(8,128)(2,1)}, bf16[80,384]{1,0:T(8,128)(2,1)}, bf16[80,6]{1,0:T(8,128)(2,1)}, bf16[80,6]{1,0:T(8,128)(2,1)}, /*index=5*/f32[80,256]{1,0:T(8,128)}) custom-call(f32[128,384]{1,0:T(8,128)} %fusion.13.refs_0_, f32[80,256]{1,0:T(8,128)} %copy-done.4, f32[80,2304]{1,0:T(8,128)} %get-tuple-element.23.refs_2_, ...), custom_call_target="tpu_custom_call" | custom-call | flops 185057280 | bytes 2659840 | tf_op jit(solution)/shard_map/pallas_call | solution.py:158
  83.1 0.9 select_convert_fusion
  84.8 2.4 %collective-permute-start.19 = (bf16[80,256]{1,0:T(8,128)(2,1)S(1)}, bf16[80,256]{1,0:T(8,128)(2,1)S(1)}, u32[]{:S(2)}, u32[]{:S(2)}) collective-permute-start(bf16[80,256]{1,0:T(8,128)(2,1)S(1)} %get-tuple-element.49), channel_id=1, source_target_pairs={{0,8},{4,12},{8,0},{12,4},{1,9},{5,13},{9,1},{13,5},{2,10},{6,14},... | collective-permute-start | bytes 122888 | tf_op jit(solution)/shard_map/ppermute | solution.py:300
  87.8 1.2 %convert_element_type.28 = bf16[80,2304]{1,0:T(8,128)(2,1)S(1)} convert(f32[80,2304]{1,0:T(8,128)} %get-tuple-element.29) | non-fusion elementwise | flops 184320 | bytes 1105920 | tf_op jit(solution)/shard_map/convert_element_type | solution.py:310
  90.5 2.5 %collective-permute-done.18 = bf16[80,256]{1,0:T(8,128)(2,1)S(1)} collective-permute-done((bf16[80,256]{1,0:T(8,128)(2,1)S(1)}, bf16[80,256]{1,0:T(8,128)(2,1)S(1)}, u32[]{:S(2)}, u32[]{:S(2)}) %collective-permute-start.18) | collective-permute-done | bytes 40992 | tf_op jit(solution)/shard_map/ppermute | solution.py:300
  93.0 1.8 %fusion.2 = f32[80,2048]{1,0:T(8,128)S(1)} fusion(s32[1024]{0:T(1024)S(1)} %pad_add_fusion, f32[80]{0:T(128)S(1)} %copy-done.22, bf16[80,256]{1,0:T(8,128)(2,1)S(1)} %collective-permute-done.20, bf16[80,256]{1,0:T(8,128)(2,1)S(1)} %collective-permute-done.19, bf16[80,256]{1,0:T(8,128)(2,1)S(1)} %collective-permute-done.18, ...), kind=kOutput, calls=%fused_computation.4 | convolution fusion | flops 338460672 | bytes 823616 | tf_op jit(solution)/shard_map/dot_general | solution.py:224
  (121 shorter events, 18.9 us)
Async XLA Ops:
  0.6 17.1 %copy-start = (s32[24]{0:T(128)S(1)}, s32[24]{0:T(128)}, u32[]{:S(2)}) copy-start(s32[24]{0:T(128)} %param.19) | copy-start | bytes 292
  0.6 11.5 %copy-start.3 = (bf16[80,6,384]{2,0,1:T(8,128)(2,1)S(1)}, bf16[80,6,384]{2,0,1:T(8,128)(2,1)}, u32[]{:S(2)}) copy-start(bf16[80,6,384]{2,0,1:T(8,128)(2,1)} %param.11) | copy-start | bytes 1105924
  0.7 11.6 %copy-start.2 = (bf16[80,8,256]{2,1,0:T(8,128)(2,1)S(1)}, bf16[80,8,256]{2,1,0:T(8,128)(2,1)}, u32[]{:S(2)}) copy-start(bf16[80,8,256]{2,1,0:T(8,128)(2,1)} %param.10) | copy-start | bytes 983044
  2.1 30.3 %collective-permute-start.8 = (s32[256]{0:T(256)S(1)}, s32[256]{0:T(256)S(1)}, u32[]{:S(2)}, u32[]{:S(2)}) collective-permute-start(s32[256]{0:T(256)S(1)} %bitcast.81), channel_id=1, source_target_pairs={{0,4},{4,8},{8,12},{12,0},{1,5},{5,9},{9,13},{13,1},{2,6},{6,10},{... | collective-permute-start | bytes 3080 | tf_op jit(solution)/shard_map/ppermute | solution.py:253
  7.4 21.2 %collective-permute-start = (bf16[80,640]{1,0:T(8,128)(2,1)S(1)}, bf16[80,640]{1,0:T(8,128)(2,1)S(1)}, u32[]{:S(2)}, u32[]{:S(2)}) collective-permute-start(bf16[80,640]{1,0:T(8,128)(2,1)S(1)} %pad_maximum_fusion), channel_id=1, source_target_pairs={{0,4},{4,8},{8,12},{1,5},{5,9},{9,13},{2,6},{6,10},{10,14},{3,7},{... | collective-permute-start | bytes 307208 | tf_op jit(solution)/shard_map/ppermute | solution.py:32
  10.9 17.7 %collective-permute-start.1 = (bf16[80,640]{1,0:T(8,128)(2,1)S(1)}, bf16[80,640]{1,0:T(8,128)(2,1)S(1)}, u32[]{:S(2)}, u32[]{:S(2)}) collective-permute-start(bf16[80,640]{1,0:T(8,128)(2,1)S(1)} %pad_maximum_fusion.1), channel_id=1, source_target_pairs={{4,0},{8,4},{12,8},{5,1},{9,5},{13,9},{6,2},{10,6},{14,10},{7,3},{... | collective-permute-start | bytes 307208 | tf_op jit(solution)/shard_map/ppermute | solution.py:33
  12.3 7.5 %copy-start.18 = (f32[80]{0:T(128)S(1)}, f32[80]{0:T(128)}, u32[]{:S(2)}) copy-start(f32[80]{0:T(128)} %param.13) | copy-start | bytes 964
  12.3 8.2 %copy-start.19 = (f32[80]{0:T(128)S(1)}, f32[80]{0:T(128)}, u32[]{:S(2)}) copy-start(f32[80]{0:T(128)} %param.14) | copy-start | bytes 964
  12.3 8.9 %copy-start.20 = (f32[80]{0:T(128)S(1)}, f32[80]{0:T(128)}, u32[]{:S(2)}) copy-start(f32[80]{0:T(128)} %param.12) | copy-start | bytes 964
  12.9 10.6 %collective-permute-start.3 = (bf16[80,14]{1,0:T(8,128)(2,1)S(1)}, bf16[80,14]{1,0:T(8,128)(2,1)S(1)}, u32[]{:S(2)}, u32[]{:S(2)}) collective-permute-start(bf16[80,14]{1,0:T(8,128)(2,1)S(1)} %copy.49), channel_id=1, source_target_pairs={{1,0},{2,1},{3,2},{5,4},{6,5},{7,6},{9,8},{10,9},{11,10},{13,12},{... | collective-permute-start | bytes 6728 | tf_op jit(solution)/shard_map/ppermute | solution.py:35
  14.6 12.5 %collective-permute-start.2 = (bf16[80,14]{1,0:T(8,128)(2,1)S(1)}, bf16[80,14]{1,0:T(8,128)(2,1)S(1)}, u32[]{:S(2)}, u32[]{:S(2)}) collective-permute-start(bf16[80,14]{1,0:T(8,128)(2,1)S(1)} %copy.46), channel_id=1, source_target_pairs={{0,1},{1,2},{2,3},{4,5},{5,6},{6,7},{8,9},{9,10},{10,11},{12,13},{... | collective-permute-start | bytes 6728 | tf_op jit(solution)/shard_map/ppermute | solution.py:34
  23.5 5.0 %copy-start.8 = (bf16[80,14]{1,0:T(8,128)(2,1)}, bf16[80,14]{1,0:T(8,128)(2,1)S(1)}, u32[]{:S(2)}) copy-start(bf16[80,14]{1,0:T(8,128)(2,1)S(1)} %collective-permute-done.3.refs_4_) | copy-start | bytes 6724
  23.5 11.6 %collective-permute-start.6 = (s32[256]{0:T(256)S(1)}, s32[256]{0:T(256)S(1)}, u32[]{:S(2)}, u32[]{:S(2)}) collective-permute-start(s32[256]{0:T(256)S(1)} %bitcast.79), channel_id=1, source_target_pairs={{0,8},{4,12},{8,0},{12,4},{1,9},{5,13},{9,1},{13,5},{2,10},{6,14},... | collective-permute-start | bytes 3080 | tf_op jit(solution)/shard_map/ppermute | solution.py:253
  27.2 7.3 %collective-permute-start.4 = (s32[256]{0:T(256)S(1)}, s32[256]{0:T(256)S(1)}, u32[]{:S(2)}, u32[]{:S(2)}) collective-permute-start(s32[256]{0:T(256)S(1)} %bitcast.80), channel_id=1, source_target_pairs={{0,12},{4,0},{8,4},{12,8},{1,13},{5,1},{9,5},{13,9},{2,14},{6,2},{... | collective-permute-start | bytes 3080 | tf_op jit(solution)/shard_map/ppermute | solution.py:253
  34.3 4.9 %collective-permute-start.9 = (f32[80,256]{1,0:T(8,128)S(1)}, f32[80,256]{1,0:T(8,128)S(1)}, u32[]{:S(2)}, u32[]{:S(2)}) collective-permute-start(f32[80,256]{1,0:T(8,128)S(1)} %slice_add_fusion.2), channel_id=1, source_target_pairs={{0,12},{4,0},{8,4},{12,8},{1,13},{5,1},{9,5},{13,9},{2,14},{6,2},{... | collective-permute-start | bytes 245768 | tf_op jit(solution)/shard_map/ppermute | solution.py:257
  35.7 9.4 %collective-permute-start.7 = (f32[80,256]{1,0:T(8,128)S(1)}, f32[80,256]{1,0:T(8,128)S(1)}, u32[]{:S(2)}, u32[]{:S(2)}) collective-permute-start(f32[80,256]{1,0:T(8,128)S(1)} %slice_add_fusion.4), channel_id=1, source_target_pairs={{0,8},{4,12},{8,0},{12,4},{1,9},{5,13},{9,1},{13,5},{2,10},{6,14},... | collective-permute-start | bytes 245768 | tf_op jit(solution)/shard_map/ppermute | solution.py:257
  37.7 7.4 %collective-permute-start.5 = (f32[80,256]{1,0:T(8,128)S(1)}, f32[80,256]{1,0:T(8,128)S(1)}, u32[]{:S(2)}, u32[]{:S(2)}) collective-permute-start(f32[80,256]{1,0:T(8,128)S(1)} %slice_add_fusion.6), channel_id=1, source_target_pairs={{0,4},{4,8},{8,12},{12,0},{1,5},{5,9},{9,13},{13,1},{2,6},{6,10},{... | collective-permute-start | bytes 245768 | tf_op jit(solution)/shard_map/ppermute | solution.py:257
  45.1 4.7 %copy-start.4 = (f32[80,256]{1,0:T(8,128)}, f32[80,256]{1,0:T(8,128)S(1)}, u32[]{:S(2)}) copy-start(f32[80,256]{1,0:T(8,128)S(1)} %fusion.31.refs_1_) | copy-start | bytes 245764
  49.8 8.0 %collective-permute-start.10 = (bf16[80,384]{1,0:T(8,128)(2,1)}, bf16[80,384]{1,0:T(8,128)(2,1)S(1)}, u32[]{:S(2)}, u32[]{:S(2)}) collective-permute-start(bf16[80,384]{1,0:T(8,128)(2,1)} %get-tuple-element.19), channel_id=1, source_target_pairs={{0,4},{4,8},{8,12},{1,5},{5,9},{9,13},{2,6},{6,10},{10,14},{3,7},{... | collective-permute-start | bytes 184328 | tf_op jit(solution)/shard_map/ppermute | solution.py:32
  51.1 6.7 %collective-permute-start.11 = (bf16[80,384]{1,0:T(8,128)(2,1)}, bf16[80,384]{1,0:T(8,128)(2,1)S(1)}, u32[]{:S(2)}, u32[]{:S(2)}) collective-permute-start(bf16[80,384]{1,0:T(8,128)(2,1)} %get-tuple-element.20), channel_id=1, source_target_pairs={{4,0},{8,4},{12,8},{5,1},{9,5},{13,9},{6,2},{10,6},{14,10},{7,3},{... | collective-permute-start | bytes 184328 | tf_op jit(solution)/shard_map/ppermute | solution.py:33
  52.4 2.9 %collective-permute-start.12 = (bf16[80,6]{1,0:T(8,128)(2,1)}, bf16[80,6]{1,0:T(8,128)(2,1)S(1)}, u32[]{:S(2)}, u32[]{:S(2)}) collective-permute-start(bf16[80,6]{1,0:T(8,128)(2,1)} %get-tuple-element.21), channel_id=1, source_target_pairs={{0,1},{1,2},{2,3},{4,5},{5,6},{6,7},{8,9},{9,10},{10,11},{12,13},{... | collective-permute-start | bytes 2888 | tf_op jit(solution)/shard_map/ppermute | solution.py:34
  54.0 3.8 %collective-permute-start.13 = (bf16[80,6]{1,0:T(8,128)(2,1)}, bf16[80,6]{1,0:T(8,128)(2,1)S(1)}, u32[]{:S(2)}, u32[]{:S(2)}) collective-permute-start(bf16[80,6]{1,0:T(8,128)(2,1)} %get-tuple-element.22), channel_id=1, source_target_pairs={{1,0},{2,1},{3,2},{5,4},{6,5},{7,6},{9,8},{10,9},{11,10},{13,12},{... | collective-permute-start | bytes 2888 | tf_op jit(solution)/shard_map/ppermute | solution.py:35
  61.6 12.3 %collective-permute-start.16 = (bf16[80,6]{1,0:T(8,128)(2,1)}, bf16[80,6]{1,0:T(8,128)(2,1)S(1)}, u32[]{:S(2)}, u32[]{:S(2)}) collective-permute-start(bf16[80,6]{1,0:T(8,128)(2,1)} %get-tuple-element.26), channel_id=1, source_target_pairs={{0,1},{1,2},{2,3},{4,5},{5,6},{6,7},{8,9},{9,10},{10,11},{12,13},{... | collective-permute-start | bytes 2888 | tf_op jit(solution)/shard_map/ppermute | solution.py:34
  66.0 7.9 %collective-permute-start.17 = (bf16[80,6]{1,0:T(8,128)(2,1)}, bf16[80,6]{1,0:T(8,128)(2,1)S(1)}, u32[]{:S(2)}, u32[]{:S(2)}) collective-permute-start(bf16[80,6]{1,0:T(8,128)(2,1)} %get-tuple-element.27), channel_id=1, source_target_pairs={{1,0},{2,1},{3,2},{5,4},{6,5},{7,6},{9,8},{10,9},{11,10},{13,12},{... | collective-permute-start | bytes 2888 | tf_op jit(solution)/shard_map/ppermute | solution.py:35
  67.3 7.1 %collective-permute-start.14 = (bf16[80,384]{1,0:T(8,128)(2,1)}, bf16[80,384]{1,0:T(8,128)(2,1)S(1)}, u32[]{:S(2)}, u32[]{:S(2)}) collective-permute-start(bf16[80,384]{1,0:T(8,128)(2,1)} %get-tuple-element.24), channel_id=1, source_target_pairs={{0,4},{4,8},{8,12},{1,5},{5,9},{9,13},{2,6},{6,10},{10,14},{3,7},{... | collective-permute-start | bytes 184328 | tf_op jit(solution)/shard_map/ppermute | solution.py:32
  71.9 6.9 %collective-permute-start.15 = (bf16[80,384]{1,0:T(8,128)(2,1)}, bf16[80,384]{1,0:T(8,128)(2,1)S(1)}, u32[]{:S(2)}, u32[]{:S(2)}) collective-permute-start(bf16[80,384]{1,0:T(8,128)(2,1)} %get-tuple-element.25), channel_id=1, source_target_pairs={{4,0},{8,4},{12,8},{5,1},{9,5},{13,9},{6,2},{10,6},{14,10},{7,3},{... | collective-permute-start | bytes 184328 | tf_op jit(solution)/shard_map/ppermute | solution.py:33
  74.0 4.8 %copy-start.14 = (bf16[80,6]{1,0:T(8,128)(2,1)}, bf16[80,6]{1,0:T(8,128)(2,1)S(1)}, u32[]{:S(2)}) copy-start(bf16[80,6]{1,0:T(8,128)(2,1)S(1)} %collective-permute-done.16.refs_5_) | copy-start | bytes 2884
  74.0 4.8 %copy-start.15 = (bf16[80,6]{1,0:T(8,128)(2,1)}, bf16[80,6]{1,0:T(8,128)(2,1)S(1)}, u32[]{:S(2)}) copy-start(bf16[80,6]{1,0:T(8,128)(2,1)S(1)} %collective-permute-done.17.refs_6_) | copy-start | bytes 2884
  84.0 9.0 %copy-start.22 = (f32[80]{0:T(128)S(1)}, f32[80]{0:T(128)}, u32[]{:S(2)}) copy-start(f32[80]{0:T(128)} %param.15) | copy-start | bytes 964
  84.0 5.7 %collective-permute-start.20 = (bf16[80,256]{1,0:T(8,128)(2,1)S(1)}, bf16[80,256]{1,0:T(8,128)(2,1)S(1)}, u32[]{:S(2)}, u32[]{:S(2)}) collective-permute-start(bf16[80,256]{1,0:T(8,128)(2,1)S(1)} %get-tuple-element.48), channel_id=1, source_target_pairs={{0,12},{4,0},{8,4},{12,8},{1,13},{5,1},{9,5},{13,9},{2,14},{6,2},{... | collective-permute-start | bytes 122888 | tf_op jit(solution)/shard_map/ppermute | solution.py:300
  84.8 5.7 %collective-permute-start.19 = (bf16[80,256]{1,0:T(8,128)(2,1)S(1)}, bf16[80,256]{1,0:T(8,128)(2,1)S(1)}, u32[]{:S(2)}, u32[]{:S(2)}) collective-permute-start(bf16[80,256]{1,0:T(8,128)(2,1)S(1)} %get-tuple-element.49), channel_id=1, source_target_pairs={{0,8},{4,12},{8,0},{12,4},{1,9},{5,13},{9,1},{13,5},{2,10},{6,14},... | collective-permute-start | bytes 122888 | tf_op jit(solution)/shard_map/ppermute | solution.py:300
  87.2 5.8 %collective-permute-start.18 = (bf16[80,256]{1,0:T(8,128)(2,1)S(1)}, bf16[80,256]{1,0:T(8,128)(2,1)S(1)}, u32[]{:S(2)}, u32[]{:S(2)}) collective-permute-start(bf16[80,256]{1,0:T(8,128)(2,1)S(1)} %get-tuple-element.50), channel_id=1, source_target_pairs={{0,4},{4,8},{8,12},{12,0},{1,5},{5,9},{9,13},{13,1},{2,6},{6,10},{... | collective-permute-start | bytes 122888 | tf_op jit(solution)/shard_map/ppermute | solution.py:300
  (12 other events, 16.8 us)

commit v15 on v14

--- a/solution.py
+++ b/solution.py
@@ -51,19 +51,21 @@
     )
 
 
-def step_kernel(*refs, rows, cols, xo, yo, nest, split, gap):
+def step_kernel(*refs, rows, cols, xo, yo, nest, split, gap, edges):
     refs = list(refs)
     if gap:
         expand_ref, fblock_ref = refs[:2]
         refs = refs[2:]
     if nest:
         (state_ref, above_ref, below_ref, left_ref, right_ref, forcing_ref, upw_ref, dnw_ref,
-         nu_ref, relax_ref, vm_ref, new_ref, lrow_ref, frow_ref, lcol_ref, fcol_ref) = refs[:16]
-        refs = refs[16:]
+         nu_ref, relax_ref, vm_ref, new_ref) = refs[:12]
+        refs = refs[12:]
     else:
-        (state_ref, above_ref, below_ref, left_ref, right_ref, nu_ref, vm_ref,
-         new_ref, lrow_ref, frow_ref, lcol_ref, fcol_ref) = refs[:12]
-        refs = refs[12:]
+        (state_ref, above_ref, below_ref, left_ref, right_ref, nu_ref, vm_ref, new_ref) = refs[:8]
+        refs = refs[8:]
+    if edges:
+        lrow_ref, frow_ref, lcol_ref, fcol_ref = refs[:4]
+        refs = refs[4:]
     if split:
         parts_ref = refs[0]
         refs = refs[1:]
@@ -97,15 +99,16 @@
         moved = moved + relax_ref[...] * (forcing_ref[...] - moved)
     new = jnp.dot(vm_ref[...], moved, precision=lax.Precision.HIGH, preferred_element_type=jnp.float32)
     new_ref[...] = new
-    lrow_ref[...] = new[:, n - cols : n].astype(jnp.bfloat16)
-    frow_ref[...] = new[:, 0:cols].astype(jnp.bfloat16)
-    narrow = new.astype(jnp.bfloat16)
-    p = lax.broadcasted_iota(jnp.int32, (n, rows), 0)
-    j = lax.broadcasted_iota(jnp.int32, (n, rows), 1)
-    last_sel = (p == j * cols + (cols - 1)).astype(jnp.bfloat16)
-    first_sel = (p == j * cols).astype(jnp.bfloat16)
-    lcol_ref[...] = jnp.dot(narrow, last_sel, preferred_element_type=jnp.float32).astype(jnp.bfloat16)
-    fcol_ref[...] = jnp.dot(narrow, first_sel, preferred_element_type=jnp.float32).astype(jnp.bfloat16)
+    if edges:
+        lrow_ref[...] = new[:, n - cols : n].astype(jnp.bfloat16)
+        frow_ref[...] = new[:, 0:cols].astype(jnp.bfloat16)
+        narrow = new.astype(jnp.bfloat16)
+        p = lax.broadcasted_iota(jnp.int32, (n, rows), 0)
+        j = lax.broadcasted_iota(jnp.int32, (n, rows), 1)
+        last_sel = (p == j * cols + (cols - 1)).astype(jnp.bfloat16)
+        first_sel = (p == j * cols).astype(jnp.bfloat16)
+        lcol_ref[...] = jnp.dot(narrow, last_sel, preferred_element_type=jnp.float32).astype(jnp.bfloat16)
+        fcol_ref[...] = jnp.dot(narrow, first_sel, preferred_element_type=jnp.float32).astype(jnp.bfloat16)
     if split:
         hi = new.astype(jnp.bfloat16)
         rest = new - hi.astype(jnp.float32)
@@ -140,14 +143,16 @@
                 nu[:, None], relax[:, None], vert_mix)
     else:
         args = (state, above, below, left, right, nu[:, None], vert_mix)
-    out_shape = (
-        jax.ShapeDtypeStruct((levels, n), jnp.float32),
-        jax.ShapeDtypeStruct((levels, cols), jnp.bfloat16),
-        jax.ShapeDtypeStruct((levels, cols), jnp.bfloat16),
-        jax.ShapeDtypeStruct((levels, rows), jnp.bfloat16),
-        jax.ShapeDtypeStruct((levels, rows), jnp.bfloat16),
-    )
     gap = gap_of is not None
+    edges = not (split or gap)
+    out_shape = (jax.ShapeDtypeStruct((levels, n), jnp.float32),)
+    if edges:
+        out_shape = out_shape + (
+            jax.ShapeDtypeStruct((levels, cols), jnp.bfloat16),
+            jax.ShapeDtypeStruct((levels, cols), jnp.bfloat16),
+            jax.ShapeDtypeStruct((levels, rows), jnp.bfloat16),
+            jax.ShapeDtypeStruct((levels, rows), jnp.bfloat16),
+        )
     if split:
         out_shape = out_shape + (jax.ShapeDtypeStruct((3 * levels, n), jnp.bfloat16),)
     if gap:
@@ -157,13 +162,16 @@
     moved_bytes = sum(int(a.size) * a.dtype.itemsize for a in args) + levels * n * 4
     outs = pl.pallas_call(
         functools.partial(
-            step_kernel, rows=rows, cols=cols, xo=xo, yo=yo, nest=nest, split=split, gap=gap
+            step_kernel, rows=rows, cols=cols, xo=xo, yo=yo, nest=nest, split=split, gap=gap,
+            edges=edges,
         ),
         out_shape=out_shape,
         scratch_shapes=[pltpu.VMEM((levels, n), jnp.float32), pltpu.VMEM((levels, n), jnp.float32)],
         cost_estimate=pl.CostEstimate(flops=flops, bytes_accessed=moved_bytes, transcendentals=0),
     )(*args)
-    return outs[0], tuple(outs[1:5]), outs[5:]
+    if edges:
+        return outs[0], tuple(outs[1:5]), outs[5:]
+    return outs[0], None, outs[1:]
 
 
 def nest_segments(nest_of, first, count):

time: 96.5 us -> 92 us (0.953)
  waiting for transfers between devices: 17.4 us -> 10.3 us
  starting transfers between devices: 40.2 us -> 45.3 us
  other arithmetic: 4.59 us -> 3.17 us
    ppermute x3, waiting for transfers between devices: 4.33 us -> 0.01 us  [exchange(): below = lax.ppermute(first_rows, 'gx', bwd_x)]
    ppermute x3, starting transfers between devices: 9.32 us -> 12.2 us  [exchange(): above = lax.ppermute(last_rows, 'gx', fwd_x)]
    ppermute x3, starting transfers between devices: 2.27 us -> 5.04 us  [body_steps(): lax.ppermute(gather_parts(parent_parts, served[s]), 'gx', shifted_pairs(t...]
    ppermute x3, starting transfers between devices: 3.74 us -> 6.28 us  [body_steps(): lax.ppermute(outgoing[s], 'gx', shifted_pairs(tiles_x, s))]
    ppermute x3, starting transfers between devices: 8.1 us -> 5.71 us  [body_steps(): lax.ppermute(wanted[s], 'gx', shifted_pairs(tiles_x, s))]
    ppermute x3, waiting for transfers between devices: 3.34 us -> 1.18 us  [body_steps(): lax.ppermute(outgoing[s], 'gx', shifted_pairs(tiles_x, s))]
    ppermute x3, waiting for transfers between devices: 6.78 us -> 4.77 us  [body_steps(): lax.ppermute(gather_parts(parent_parts, served[s]), 'gx', shifted_pairs(t...]
    ppermute x3, waiting for transfers between devices: 2.44 us -> 4.35 us  [exchange(): right = lax.ppermute(first_cols, Y_AXES, bwd_y)]
  transfers between devices with their start and end apart: 21 -> 21, of which waited for: 7 -> 6; matrix products, arithmetic and copies ran while one was open for 16% -> 14% of each run, Pallas kernels for 3% -> 3%
where the time goes in v15:
time: 92 us; the launch traced here: 91.2 us
  starting transfers between devices  45.3 us (49%)
  Pallas kernels  12.9 us (14%)
  local copies, waits for them, and re-layouts  12.4 us (13%)
  waiting for transfers between devices  10.3 us (11%)
  matrix products  5.92 us (6%)
  other arithmetic  3.17 us (3%)
  between operations  1.25 us (1%)
    pallas_call x4, Pallas kernels, stencil_step(): pl.pallas_call(functools.partial(step_kernel, rows=rows, cols=cols, xo=xo...  12.9 us
    ppermute x3, starting transfers between devices, exchange(): above = lax.ppermute(last_rows, 'gx', fwd_x)  12.2 us
    ppermute x3, starting transfers between devices, exchange(): left = lax.ppermute(last_cols, Y_AXES, fwd_y)  8.26 us
    unnamed x64, local copies, waits for them, and re-layouts  6.37 us
    ppermute x3, starting transfers between devices, body_steps(): lax.ppermute(outgoing[s], 'gx', shifted_pairs(tiles_x, s))  6.28 us
    ppermute x3, starting transfers between devices, body_steps(): lax.ppermute(wanted[s], 'gx', shifted_pairs(tiles_x, s))  5.71 us
    ppermute x3, starting transfers between devices, body_steps(): lax.ppermute(gather_parts(parent_parts, served[s]), 'gx', shifted_pairs(t...  5.04 us
    ppermute x3, waiting for transfers between devices, body_steps(): lax.ppermute(gather_parts(parent_parts, served[s]), 'gx', shifted_pairs(t...  4.77 us
  transfers between devices with their start and end apart: 21, of which 6 were waited for; matrix products, arithmetic and copies ran while one was open for 14% of the time, Pallas kernels for 3%

profile of v15, /device:TPU:0, one launch (start us, length us, event | category | flops | bytes accessed | tf_op | source)
XLA Modules:
  0.0 91.2 jit_solution(6411616644571522751)
XLA Ops:
  0.7 1.2 %fusion.41 = (bf16[80,8,1]{2,1,0:T(8,128)(2,1)S(1)}, bf16[80,8,1]{2,1,0:T(8,128)(2,1)S(1)}) fusion(bf16[80,8,256]{2,1,0:T(8,128)(2,1)} %param.10), kind=kLoop, calls=%fused_computation.99 | loop fusion | bytes 5120 | tf_op jit(solution)/shard_map/slice | solution.py:22
  2.4 2.4 %collective-permute-start.2 = (bf16[80,14]{1,0:T(8,128)(2,1)S(1)}, bf16[80,14]{1,0:T(8,128)(2,1)S(1)}, u32[]{:S(2)}, u32[]{:S(2)}) collective-permute-start(bf16[80,14]{1,0:T(8,128)(2,1)S(1)} %copy.46), channel_id=1, source_target_pairs={{0,1},{1,2},{2,3},{4,5},{5,6},{6,7},{8,9},{9,10},{10,11},{12,13},{... | collective-permute-start | bytes 6728 | tf_op jit(solution)/shard_map/ppermute | solution.py:34
  5.3 1.3 %collective-permute-start.3 = (bf16[80,14]{1,0:T(8,128)(2,1)S(1)}, bf16[80,14]{1,0:T(8,128)(2,1)S(1)}, u32[]{:S(2)}, u32[]{:S(2)}) collective-permute-start(bf16[80,14]{1,0:T(8,128)(2,1)S(1)} %copy.49), channel_id=1, source_target_pairs={{1,0},{2,1},{3,2},{5,4},{6,5},{7,6},{9,8},{10,9},{11,10},{13,12},{... | collective-permute-start | bytes 6728 | tf_op jit(solution)/shard_map/ppermute | solution.py:35
  6.8 4.3 %collective-permute-start = (bf16[80,640]{1,0:T(8,128)(2,1)S(1)}, bf16[80,640]{1,0:T(8,128)(2,1)S(1)}, u32[]{:S(2)}, u32[]{:S(2)}) collective-permute-start(bf16[80,640]{1,0:T(8,128)(2,1)S(1)} %pad_maximum_fusion), channel_id=1, source_target_pairs={{0,4},{4,8},{8,12},{1,5},{5,9},{9,13},{2,6},{6,10},{10,14},{3,7},{... | collective-permute-start | bytes 307208 | tf_op jit(solution)/shard_map/ppermute | solution.py:32
  11.1 1.3 %collective-permute-start.1 = (bf16[80,640]{1,0:T(8,128)(2,1)S(1)}, bf16[80,640]{1,0:T(8,128)(2,1)S(1)}, u32[]{:S(2)}, u32[]{:S(2)}) collective-permute-start(bf16[80,640]{1,0:T(8,128)(2,1)S(1)} %pad_maximum_fusion.1), channel_id=1, source_target_pairs={{4,0},{8,4},{12,8},{5,1},{9,5},{13,9},{6,2},{10,6},{14,10},{7,3},{... | collective-permute-start | bytes 307208 | tf_op jit(solution)/shard_map/ppermute | solution.py:33
  12.5 4.7 %collective-permute-start.4 = (s32[256]{0:T(256)S(1)}, s32[256]{0:T(256)S(1)}, u32[]{:S(2)}, u32[]{:S(2)}) collective-permute-start(s32[256]{0:T(256)S(1)} %bitcast.81), channel_id=1, source_target_pairs={{0,12},{4,0},{8,4},{12,8},{1,13},{5,1},{9,5},{13,9},{2,14},{6,2},{... | collective-permute-start | bytes 3080 | tf_op jit(solution)/shard_map/ppermute | solution.py:261
  23.1 1.0 %collective-permute-start.8 = (s32[256]{0:T(256)S(1)}, s32[256]{0:T(256)S(1)}, u32[]{:S(2)}, u32[]{:S(2)}) collective-permute-start(s32[256]{0:T(256)S(1)} %bitcast.79), channel_id=1, source_target_pairs={{0,4},{4,8},{8,12},{12,0},{1,5},{5,9},{9,13},{13,1},{2,6},{6,10},{... | collective-permute-start | bytes 3080 | tf_op jit(solution)/shard_map/ppermute | solution.py:261
  24.7 3.1 %shard_map.113 = (f32[80,2048]{1,0:T(8,128)}, bf16[240,2048]{1,0:T(8,128)(2,1)}) custom-call(bf16[80,2048]{1,0:T(8,128)(2,1)} %bitcast.59, bf16[80,640]{1,0:T(8,128)(2,1)} %copy-done.6, bf16[80,640]{1,0:T(8,128)(2,1)} %copy-done.7, bf16[80,14]{1,0:T(8,128)(2,1)} %copy-done.8, bf16[80,14]{1,0:T(8,128)(2,1)} %copy-done.9, f32[80,1]{1,0:T(8,128)} %copy.50.refs_5_, ...), custom_call_target="tpu_custom_call" | custom-call | flops 165806080 | bytes 1218240 | tf_op jit(solution)/shard_map/pallas_call | solution.py:163
  27.8 1.9 %fusion.3 = f32[240,256]{1,0:T(8,128)S(1)} fusion(bf16[240,2048]{1,0:T(8,128)(2,1)} %get-tuple-element.17, s32[256]{0:T(256)S(1)} %collective-permute-done.4), kind=kOutput, calls=%fused_computation.9 | convolution fusion | flops 252182528 | bytes 1229824 | tf_op jit(solution)/shard_map/dot_general | solution.py:224
  29.7 2.5 %collective-permute-start.5 = (f32[80,256]{1,0:T(8,128)S(1)}, f32[80,256]{1,0:T(8,128)S(1)}, u32[]{:S(2)}, u32[]{:S(2)}) collective-permute-start(f32[80,256]{1,0:T(8,128)S(1)} %slice_add_fusion.6), channel_id=1, source_target_pairs={{0,4},{4,8},{8,12},{12,0},{1,5},{5,9},{9,13},{13,1},{2,6},{6,10},{... | collective-permute-start | bytes 245768 | tf_op jit(solution)/shard_map/ppermute | solution.py:265
  32.8 1.0 %collective-permute-start.7 = (f32[80,256]{1,0:T(8,128)S(1)}, f32[80,256]{1,0:T(8,128)S(1)}, u32[]{:S(2)}, u32[]{:S(2)}) collective-permute-start(f32[80,256]{1,0:T(8,128)S(1)} %slice_add_fusion.4), channel_id=1, source_target_pairs={{0,8},{4,12},{8,0},{12,4},{1,9},{5,13},{9,1},{13,5},{2,10},{6,14},... | collective-permute-start | bytes 245768 | tf_op jit(solution)/shard_map/ppermute | solution.py:265
  34.5 1.5 %collective-permute-start.9 = (f32[80,256]{1,0:T(8,128)S(1)}, f32[80,256]{1,0:T(8,128)S(1)}, u32[]{:S(2)}, u32[]{:S(2)}) collective-permute-start(f32[80,256]{1,0:T(8,128)S(1)} %slice_add_fusion.2), channel_id=1, source_target_pairs={{0,12},{4,0},{8,4},{12,8},{1,13},{5,1},{9,5},{13,9},{2,14},{6,2},{... | collective-permute-start | bytes 245768 | tf_op jit(solution)/shard_map/ppermute | solution.py:265
  36.8 3.6 %collective-permute-done.7 = f32[80,256]{1,0:T(8,128)S(1)} collective-permute-done((f32[80,256]{1,0:T(8,128)S(1)}, f32[80,256]{1,0:T(8,128)S(1)}, u32[]{:S(2)}, u32[]{:S(2)}) %collective-permute-start.7) | collective-permute-done | bytes 81952 | tf_op jit(solution)/shard_map/ppermute | solution.py:265
  42.9 3.1 %shard_map.114 = (f32[80,2304]{1,0:T(8,128)}, bf16[80,384]{1,0:T(8,128)(2,1)}, bf16[80,384]{1,0:T(8,128)(2,1)}, bf16[80,6]{1,0:T(8,128)(2,1)}, bf16[80,6]{1,0:T(8,128)(2,1)}) custom-call(bf16[80,2304]{1,0:T(8,128)(2,1)} %bitcast.57, bf16[80,640]{1,0:T(8,128)(2,1)} %copy-done.6, bf16[80,640]{1,0:T(8,128)(2,1)} %copy-done.7, bf16[80,14]{1,0:T(8,128)(2,1)} %copy-done.8, ...), custom_call_target="tpu_custom_call" | custom-call | flops 185057280 | bytes 2097152 | tf_op jit(solution)/shard_map/pallas_call | solution.py:163
  46.0 3.4 %collective-permute-start.10 = (bf16[80,384]{1,0:T(8,128)(2,1)}, bf16[80,384]{1,0:T(8,128)(2,1)S(1)}, u32[]{:S(2)}, u32[]{:S(2)}) collective-permute-start(bf16[80,384]{1,0:T(8,128)(2,1)} %get-tuple-element.19), channel_id=1, source_target_pairs={{0,4},{4,8},{8,12},{1,5},{5,9},{9,13},{2,6},{6,10},{10,14},{3,7},{... | collective-permute-start | bytes 184328 | tf_op jit(solution)/shard_map/ppermute | solution.py:32
  49.4 1.3 %collective-permute-start.11 = (bf16[80,384]{1,0:T(8,128)(2,1)}, bf16[80,384]{1,0:T(8,128)(2,1)S(1)}, u32[]{:S(2)}, u32[]{:S(2)}) collective-permute-start(bf16[80,384]{1,0:T(8,128)(2,1)} %get-tuple-element.20), channel_id=1, source_target_pairs={{4,0},{8,4},{12,8},{5,1},{9,5},{13,9},{6,2},{10,6},{14,10},{7,3},{... | collective-permute-start | bytes 184328 | tf_op jit(solution)/shard_map/ppermute | solution.py:33
  50.7 1.7 %collective-permute-start.12 = (bf16[80,6]{1,0:T(8,128)(2,1)}, bf16[80,6]{1,0:T(8,128)(2,1)S(1)}, u32[]{:S(2)}, u32[]{:S(2)}) collective-permute-start(bf16[80,6]{1,0:T(8,128)(2,1)} %get-tuple-element.21), channel_id=1, source_target_pairs={{0,1},{1,2},{2,3},{4,5},{5,6},{6,7},{8,9},{9,10},{10,11},{12,13},{... | collective-permute-start | bytes 2888 | tf_op jit(solution)/shard_map/ppermute | solution.py:34
  52.4 1.3 %collective-permute-start.13 = (bf16[80,6]{1,0:T(8,128)(2,1)}, bf16[80,6]{1,0:T(8,128)(2,1)S(1)}, u32[]{:S(2)}, u32[]{:S(2)}) collective-permute-start(bf16[80,6]{1,0:T(8,128)(2,1)} %get-tuple-element.22), channel_id=1, source_target_pairs={{1,0},{2,1},{3,2},{5,4},{6,5},{7,6},{9,8},{10,9},{11,10},{13,12},{... | collective-permute-start | bytes 2888 | tf_op jit(solution)/shard_map/ppermute | solution.py:35
  53.7 3.1 %collective-permute-done.13.refs_4_ = bf16[80,6]{1,0:T(8,128)(2,1)S(1)} collective-permute-done((bf16[80,6]{1,0:T(8,128)(2,1)}, bf16[80,6]{1,0:T(8,128)(2,1)S(1)}, u32[]{:S(2)}, u32[]{:S(2)}) %collective-permute-start.13) | collective-permute-done | bytes 992 | tf_op jit(solution)/shard_map/ppermute | solution.py:35
  57.5 3.2 %shard_map.115 = (f32[80,2304]{1,0:T(8,128)}, bf16[80,384]{1,0:T(8,128)(2,1)}, bf16[80,384]{1,0:T(8,128)(2,1)}, bf16[80,6]{1,0:T(8,128)(2,1)}, bf16[80,6]{1,0:T(8,128)(2,1)}) custom-call(f32[80,2304]{1,0:T(8,128)} %get-tuple-element.18.refs_0_, bf16[80,384]{1,0:T(8,128)(2,1)} %copy-done.12, bf16[80,384]{1,0:T(8,128)(2,1)} %copy-done.13, ...), custom_call_target="tpu_custom_call" | custom-call | flops 185057280 | bytes 2381312 | tf_op jit(solution)/shard_map/pallas_call | solution.py:163
  60.7 4.5 %collective-permute-start.14 = (bf16[80,384]{1,0:T(8,128)(2,1)}, bf16[80,384]{1,0:T(8,128)(2,1)S(1)}, u32[]{:S(2)}, u32[]{:S(2)}) collective-permute-start(bf16[80,384]{1,0:T(8,128)(2,1)} %get-tuple-element.24), channel_id=1, source_target_pairs={{0,4},{4,8},{8,12},{1,5},{5,9},{9,13},{2,6},{6,10},{10,14},{3,7},{... | collective-permute-start | bytes 184328 | tf_op jit(solution)/shard_map/ppermute | solution.py:32
  65.2 1.3 %collective-permute-start.15 = (bf16[80,384]{1,0:T(8,128)(2,1)}, bf16[80,384]{1,0:T(8,128)(2,1)S(1)}, u32[]{:S(2)}, u32[]{:S(2)}) collective-permute-start(bf16[80,384]{1,0:T(8,128)(2,1)} %get-tuple-element.25), channel_id=1, source_target_pairs={{4,0},{8,4},{12,8},{5,1},{9,5},{13,9},{6,2},{10,6},{14,10},{7,3},{... | collective-permute-start | bytes 184328 | tf_op jit(solution)/shard_map/ppermute | solution.py:33
  66.5 4.1 %collective-permute-start.16 = (bf16[80,6]{1,0:T(8,128)(2,1)}, bf16[80,6]{1,0:T(8,128)(2,1)S(1)}, u32[]{:S(2)}, u32[]{:S(2)}) collective-permute-start(bf16[80,6]{1,0:T(8,128)(2,1)} %get-tuple-element.26), channel_id=1, source_target_pairs={{0,1},{1,2},{2,3},{4,5},{5,6},{6,7},{8,9},{9,10},{10,11},{12,13},{... | collective-permute-start | bytes 2888 | tf_op jit(solution)/shard_map/ppermute | solution.py:34
  70.7 1.3 %collective-permute-start.17 = (bf16[80,6]{1,0:T(8,128)(2,1)}, bf16[80,6]{1,0:T(8,128)(2,1)S(1)}, u32[]{:S(2)}, u32[]{:S(2)}) collective-permute-start(bf16[80,6]{1,0:T(8,128)(2,1)} %get-tuple-element.27), channel_id=1, source_target_pairs={{1,0},{2,1},{3,2},{5,4},{6,5},{7,6},{9,8},{10,9},{11,10},{13,12},{... | collective-permute-start | bytes 2888 | tf_op jit(solution)/shard_map/ppermute | solution.py:35
  72.8 1.2 %collective-permute-done.17.refs_6_ = bf16[80,6]{1,0:T(8,128)(2,1)S(1)} collective-permute-done((bf16[80,6]{1,0:T(8,128)(2,1)}, bf16[80,6]{1,0:T(8,128)(2,1)S(1)}, u32[]{:S(2)}, u32[]{:S(2)}) %collective-permute-start.17) | collective-permute-done | bytes 992 | tf_op jit(solution)/shard_map/ppermute | solution.py:35
  74.6 3.5 %shard_map.116 = (f32[80,2304]{1,0:T(8,128)}, f32[80,256]{1,0:T(8,128)}) custom-call(f32[128,384]{1,0:T(8,128)} %fusion.13.refs_0_, f32[80,256]{1,0:T(8,128)} %copy-done.4, f32[80,2304]{1,0:T(8,128)} %get-tuple-element.23.refs_2_, bf16[80,384]{1,0:T(8,128)(2,1)} %copy-done.10, bf16[80,384]{1,0:T(8,128)(2,1)} %copy-done.11, bf16[80,6]{1,0:T(8,128)(2,1)} %copy-done.14, ...), custom_call_target="tpu_custom_call" | custom-call | flops 185057280 | bytes 2659840 | tf_op jit(solution)/shard_map/pallas_call | solution.py:163
  79.1 2.5 %collective-permute-start.18 = (bf16[80,256]{1,0:T(8,128)(2,1)S(1)}, bf16[80,256]{1,0:T(8,128)(2,1)S(1)}, u32[]{:S(2)}, u32[]{:S(2)}) collective-permute-start(bf16[80,256]{1,0:T(8,128)(2,1)S(1)} %get-tuple-element.50), channel_id=1, source_target_pairs={{0,4},{4,8},{8,12},{12,0},{1,5},{5,9},{9,13},{13,1},{2,6},{6,10},{... | collective-permute-start | bytes 122888 | tf_op jit(solution)/shard_map/ppermute | solution.py:308
  81.6 2.7 %collective-permute-start.19 = (bf16[80,256]{1,0:T(8,128)(2,1)S(1)}, bf16[80,256]{1,0:T(8,128)(2,1)S(1)}, u32[]{:S(2)}, u32[]{:S(2)}) collective-permute-start(bf16[80,256]{1,0:T(8,128)(2,1)S(1)} %get-tuple-element.49), channel_id=1, source_target_pairs={{0,8},{4,12},{8,0},{12,4},{1,9},{5,13},{9,1},{13,5},{2,10},{6,14},... | collective-permute-start | bytes 122888 | tf_op jit(solution)/shard_map/ppermute | solution.py:308
  84.2 1.1 %collective-permute-start.20 = (bf16[80,256]{1,0:T(8,128)(2,1)S(1)}, bf16[80,256]{1,0:T(8,128)(2,1)S(1)}, u32[]{:S(2)}, u32[]{:S(2)}) collective-permute-start(bf16[80,256]{1,0:T(8,128)(2,1)S(1)} %get-tuple-element.48), channel_id=1, source_target_pairs={{0,12},{4,0},{8,4},{12,8},{1,13},{5,1},{9,5},{13,9},{2,14},{6,2},{... | collective-permute-start | bytes 122888 | tf_op jit(solution)/shard_map/ppermute | solution.py:308
  85.4 1.2 %convert_element_type.28 = bf16[80,2304]{1,0:T(8,128)(2,1)S(1)} convert(f32[80,2304]{1,0:T(8,128)} %get-tuple-element.29) | non-fusion elementwise | flops 184320 | bytes 1105920 | tf_op jit(solution)/shard_map/convert_element_type | solution.py:318
  87.3 1.2 %collective-permute-done.20 = bf16[80,256]{1,0:T(8,128)(2,1)S(1)} collective-permute-done((bf16[80,256]{1,0:T(8,128)(2,1)S(1)}, bf16[80,256]{1,0:T(8,128)(2,1)S(1)}, u32[]{:S(2)}, u32[]{:S(2)}) %collective-permute-start.20) | collective-permute-done | bytes 40992 | tf_op jit(solution)/shard_map/ppermute | solution.py:308
  88.5 1.8 %fusion.2 = f32[80,2048]{1,0:T(8,128)S(1)} fusion(s32[1024]{0:T(1024)S(1)} %pad_add_fusion, f32[80]{0:T(128)S(1)} %copy-done.24, bf16[80,256]{1,0:T(8,128)(2,1)S(1)} %collective-permute-done.20, bf16[80,256]{1,0:T(8,128)(2,1)S(1)} %collective-permute-done.19, bf16[80,256]{1,0:T(8,128)(2,1)S(1)} %collective-permute-done.18, ...), kind=kOutput, calls=%fused_computation.4 | convolution fusion | flops 338460672 | bytes 823616 | tf_op jit(solution)/shard_map/dot_general | solution.py:232
  (125 shorter events, 16.6 us)
Async XLA Ops:
  0.6 16.7 %copy-start = (s32[24]{0:T(128)S(1)}, s32[24]{0:T(128)}, u32[]{:S(2)}) copy-start(s32[24]{0:T(128)} %param.19) | copy-start | bytes 292
  0.6 5.9 %copy-start.2 = (bf16[80,8,256]{2,1,0:T(8,128)(2,1)S(1)}, bf16[80,8,256]{2,1,0:T(8,128)(2,1)}, u32[]{:S(2)}) copy-start(bf16[80,8,256]{2,1,0:T(8,128)(2,1)} %param.10) | copy-start | bytes 983044
  2.1 10.3 %copy-start.18 = (s32[1,1,256,1]{2,3,1,0:T(1,128)S(1)}, s32[1,1,256,1]{2,3,1,0:T(1,128)}, u32[]{:S(2)}) copy-start(s32[1,1,256,1]{2,3,1,0:T(1,128)} %param.17) | copy-start | bytes 3076
  2.1 10.3 %copy-start.19 = (s32[1,1,256]{2,1,0:T(1,128)S(1)}, s32[1,1,256]{2,1,0:T(1,128)}, u32[]{:S(2)}) copy-start(s32[1,1,256]{2,1,0:T(1,128)} %param.18) | copy-start | bytes 3076
  2.4 20.6 %collective-permute-start.2 = (bf16[80,14]{1,0:T(8,128)(2,1)S(1)}, bf16[80,14]{1,0:T(8,128)(2,1)S(1)}, u32[]{:S(2)}, u32[]{:S(2)}) collective-permute-start(bf16[80,14]{1,0:T(8,128)(2,1)S(1)} %copy.46), channel_id=1, source_target_pairs={{0,1},{1,2},{2,3},{4,5},{5,6},{6,7},{8,9},{9,10},{10,11},{12,13},{... | collective-permute-start | bytes 6728 | tf_op jit(solution)/shard_map/ppermute | solution.py:34
  5.3 17.8 %collective-permute-start.3 = (bf16[80,14]{1,0:T(8,128)(2,1)S(1)}, bf16[80,14]{1,0:T(8,128)(2,1)S(1)}, u32[]{:S(2)}, u32[]{:S(2)}) collective-permute-start(bf16[80,14]{1,0:T(8,128)(2,1)S(1)} %copy.49), channel_id=1, source_target_pairs={{1,0},{2,1},{3,2},{5,4},{6,5},{7,6},{9,8},{10,9},{11,10},{13,12},{... | collective-permute-start | bytes 6728 | tf_op jit(solution)/shard_map/ppermute | solution.py:35
  6.7 12.2 %copy-start.20 = (f32[80]{0:T(128)S(1)}, f32[80]{0:T(128)}, u32[]{:S(2)}) copy-start(f32[80]{0:T(128)} %param.12) | copy-start | bytes 964
  6.7 14.1 %copy-start.21 = (f32[80]{0:T(128)S(1)}, f32[80]{0:T(128)}, u32[]{:S(2)}) copy-start(f32[80]{0:T(128)} %param.13) | copy-start | bytes 964
  6.7 14.8 %copy-start.22 = (f32[80]{0:T(128)S(1)}, f32[80]{0:T(128)}, u32[]{:S(2)}) copy-start(f32[80]{0:T(128)} %param.14) | copy-start | bytes 964
  6.8 17.3 %collective-permute-start = (bf16[80,640]{1,0:T(8,128)(2,1)S(1)}, bf16[80,640]{1,0:T(8,128)(2,1)S(1)}, u32[]{:S(2)}, u32[]{:S(2)}) collective-permute-start(bf16[80,640]{1,0:T(8,128)(2,1)S(1)} %pad_maximum_fusion), channel_id=1, source_target_pairs={{0,4},{4,8},{8,12},{1,5},{5,9},{9,13},{2,6},{6,10},{10,14},{3,7},{... | collective-permute-start | bytes 307208 | tf_op jit(solution)/shard_map/ppermute | solution.py:32
  11.1 12.9 %collective-permute-start.1 = (bf16[80,640]{1,0:T(8,128)(2,1)S(1)}, bf16[80,640]{1,0:T(8,128)(2,1)S(1)}, u32[]{:S(2)}, u32[]{:S(2)}) collective-permute-start(bf16[80,640]{1,0:T(8,128)(2,1)S(1)} %pad_maximum_fusion.1), channel_id=1, source_target_pairs={{4,0},{8,4},{12,8},{5,1},{9,5},{13,9},{6,2},{10,6},{14,10},{7,3},{... | collective-permute-start | bytes 307208 | tf_op jit(solution)/shard_map/ppermute | solution.py:33
  12.5 15.3 %collective-permute-start.4 = (s32[256]{0:T(256)S(1)}, s32[256]{0:T(256)S(1)}, u32[]{:S(2)}, u32[]{:S(2)}) collective-permute-start(s32[256]{0:T(256)S(1)} %bitcast.81), channel_id=1, source_target_pairs={{0,12},{4,0},{8,4},{12,8},{1,13},{5,1},{9,5},{13,9},{2,14},{6,2},{... | collective-permute-start | bytes 3080 | tf_op jit(solution)/shard_map/ppermute | solution.py:261
  23.0 9.2 %collective-permute-start.6 = (s32[256]{0:T(256)S(1)}, s32[256]{0:T(256)S(1)}, u32[]{:S(2)}, u32[]{:S(2)}) collective-permute-start(s32[256]{0:T(256)S(1)} %bitcast.80), channel_id=1, source_target_pairs={{0,8},{4,12},{8,0},{12,4},{1,9},{5,13},{9,1},{13,5},{2,10},{6,14},... | collective-permute-start | bytes 3080 | tf_op jit(solution)/shard_map/ppermute | solution.py:261
  23.1 10.8 %collective-permute-start.8 = (s32[256]{0:T(256)S(1)}, s32[256]{0:T(256)S(1)}, u32[]{:S(2)}, u32[]{:S(2)}) collective-permute-start(s32[256]{0:T(256)S(1)} %bitcast.79), channel_id=1, source_target_pairs={{0,4},{4,8},{8,12},{12,0},{1,5},{5,9},{9,13},{13,1},{2,6},{6,10},{... | collective-permute-start | bytes 3080 | tf_op jit(solution)/shard_map/ppermute | solution.py:261
  27.8 4.4 %copy-start.23 = (bf16[240,2048]{1,0:T(8,128)(2,1)S(1)}, bf16[240,2048]{1,0:T(8,128)(2,1)}, u32[]{:S(2)}) copy-start(bf16[240,2048]{1,0:T(8,128)(2,1)} %get-tuple-element.17) | copy-start | bytes 2949124
  29.7 7.1 %collective-permute-start.5 = (f32[80,256]{1,0:T(8,128)S(1)}, f32[80,256]{1,0:T(8,128)S(1)}, u32[]{:S(2)}, u32[]{:S(2)}) collective-permute-start(f32[80,256]{1,0:T(8,128)S(1)} %slice_add_fusion.6), channel_id=1, source_target_pairs={{0,4},{4,8},{8,12},{12,0},{1,5},{5,9},{9,13},{13,1},{2,6},{6,10},{... | collective-permute-start | bytes 245768 | tf_op jit(solution)/shard_map/ppermute | solution.py:265
  32.8 7.6 %collective-permute-start.7 = (f32[80,256]{1,0:T(8,128)S(1)}, f32[80,256]{1,0:T(8,128)S(1)}, u32[]{:S(2)}, u32[]{:S(2)}) collective-permute-start(f32[80,256]{1,0:T(8,128)S(1)} %slice_add_fusion.4), channel_id=1, source_target_pairs={{0,8},{4,12},{8,0},{12,4},{1,9},{5,13},{9,1},{13,5},{2,10},{6,14},... | collective-permute-start | bytes 245768 | tf_op jit(solution)/shard_map/ppermute | solution.py:265
  34.5 6.8 %collective-permute-start.9 = (f32[80,256]{1,0:T(8,128)S(1)}, f32[80,256]{1,0:T(8,128)S(1)}, u32[]{:S(2)}, u32[]{:S(2)}) collective-permute-start(f32[80,256]{1,0:T(8,128)S(1)} %slice_add_fusion.2), channel_id=1, source_target_pairs={{0,12},{4,0},{8,4},{12,8},{1,13},{5,1},{9,5},{13,9},{2,14},{6,2},{... | collective-permute-start | bytes 245768 | tf_op jit(solution)/shard_map/ppermute | solution.py:265
  41.3 4.7 %copy-start.4 = (f32[80,256]{1,0:T(8,128)}, f32[80,256]{1,0:T(8,128)S(1)}, u32[]{:S(2)}) copy-start(f32[80,256]{1,0:T(8,128)S(1)} %fusion.31.refs_1_) | copy-start | bytes 245764
  46.0 10.8 %collective-permute-start.10 = (bf16[80,384]{1,0:T(8,128)(2,1)}, bf16[80,384]{1,0:T(8,128)(2,1)S(1)}, u32[]{:S(2)}, u32[]{:S(2)}) collective-permute-start(bf16[80,384]{1,0:T(8,128)(2,1)} %get-tuple-element.19), channel_id=1, source_target_pairs={{0,4},{4,8},{8,12},{1,5},{5,9},{9,13},{2,6},{6,10},{10,14},{3,7},{... | collective-permute-start | bytes 184328 | tf_op jit(solution)/shard_map/ppermute | solution.py:32
  49.4 7.5 %collective-permute-start.11 = (bf16[80,384]{1,0:T(8,128)(2,1)}, bf16[80,384]{1,0:T(8,128)(2,1)S(1)}, u32[]{:S(2)}, u32[]{:S(2)}) collective-permute-start(bf16[80,384]{1,0:T(8,128)(2,1)} %get-tuple-element.20), channel_id=1, source_target_pairs={{4,0},{8,4},{12,8},{5,1},{9,5},{13,9},{6,2},{10,6},{14,10},{7,3},{... | collective-permute-start | bytes 184328 | tf_op jit(solution)/shard_map/ppermute | solution.py:33
  50.7 3.0 %collective-permute-start.12 = (bf16[80,6]{1,0:T(8,128)(2,1)}, bf16[80,6]{1,0:T(8,128)(2,1)S(1)}, u32[]{:S(2)}, u32[]{:S(2)}) collective-permute-start(bf16[80,6]{1,0:T(8,128)(2,1)} %get-tuple-element.21), channel_id=1, source_target_pairs={{0,1},{1,2},{2,3},{4,5},{5,6},{6,7},{8,9},{9,10},{10,11},{12,13},{... | collective-permute-start | bytes 2888 | tf_op jit(solution)/shard_map/ppermute | solution.py:34
  52.4 4.4 %collective-permute-start.13 = (bf16[80,6]{1,0:T(8,128)(2,1)}, bf16[80,6]{1,0:T(8,128)(2,1)S(1)}, u32[]{:S(2)}, u32[]{:S(2)}) collective-permute-start(bf16[80,6]{1,0:T(8,128)(2,1)} %get-tuple-element.22), channel_id=1, source_target_pairs={{1,0},{2,1},{3,2},{5,4},{6,5},{7,6},{9,8},{10,9},{11,10},{13,12},{... | collective-permute-start | bytes 2888 | tf_op jit(solution)/shard_map/ppermute | solution.py:35
  53.7 3.2 %copy-start.16 = (bf16[80,6]{1,0:T(8,128)(2,1)}, bf16[80,6]{1,0:T(8,128)(2,1)S(1)}, u32[]{:S(2)}) copy-start(bf16[80,6]{1,0:T(8,128)(2,1)S(1)} %collective-permute-done.12.refs_3_) | copy-start | bytes 2884
  60.7 13.3 %collective-permute-start.14 = (bf16[80,384]{1,0:T(8,128)(2,1)}, bf16[80,384]{1,0:T(8,128)(2,1)S(1)}, u32[]{:S(2)}, u32[]{:S(2)}) collective-permute-start(bf16[80,384]{1,0:T(8,128)(2,1)} %get-tuple-element.24), channel_id=1, source_target_pairs={{0,4},{4,8},{8,12},{1,5},{5,9},{9,13},{2,6},{6,10},{10,14},{3,7},{... | collective-permute-start | bytes 184328 | tf_op jit(solution)/shard_map/ppermute | solution.py:32
  65.2 8.8 %collective-permute-start.15 = (bf16[80,384]{1,0:T(8,128)(2,1)}, bf16[80,384]{1,0:T(8,128)(2,1)S(1)}, u32[]{:S(2)}, u32[]{:S(2)}) collective-permute-start(bf16[80,384]{1,0:T(8,128)(2,1)} %get-tuple-element.25), channel_id=1, source_target_pairs={{4,0},{8,4},{12,8},{5,1},{9,5},{13,9},{6,2},{10,6},{14,10},{7,3},{... | collective-permute-start | bytes 184328 | tf_op jit(solution)/shard_map/ppermute | solution.py:33
  66.5 6.2 %collective-permute-start.16 = (bf16[80,6]{1,0:T(8,128)(2,1)}, bf16[80,6]{1,0:T(8,128)(2,1)S(1)}, u32[]{:S(2)}, u32[]{:S(2)}) collective-permute-start(bf16[80,6]{1,0:T(8,128)(2,1)} %get-tuple-element.26), channel_id=1, source_target_pairs={{0,1},{1,2},{2,3},{4,5},{5,6},{6,7},{8,9},{9,10},{10,11},{12,13},{... | collective-permute-start | bytes 2888 | tf_op jit(solution)/shard_map/ppermute | solution.py:34
  70.7 3.3 %collective-permute-start.17 = (bf16[80,6]{1,0:T(8,128)(2,1)}, bf16[80,6]{1,0:T(8,128)(2,1)S(1)}, u32[]{:S(2)}, u32[]{:S(2)}) collective-permute-start(bf16[80,6]{1,0:T(8,128)(2,1)} %get-tuple-element.27), channel_id=1, source_target_pairs={{1,0},{2,1},{3,2},{5,4},{6,5},{7,6},{9,8},{10,9},{11,10},{13,12},{... | collective-permute-start | bytes 2888 | tf_op jit(solution)/shard_map/ppermute | solution.py:35
  79.1 9.4 %copy-start.24 = (f32[80]{0:T(128)S(1)}, f32[80]{0:T(128)}, u32[]{:S(2)}) copy-start(f32[80]{0:T(128)} %param.15) | copy-start | bytes 964
  79.1 8.2 %collective-permute-start.18 = (bf16[80,256]{1,0:T(8,128)(2,1)S(1)}, bf16[80,256]{1,0:T(8,128)(2,1)S(1)}, u32[]{:S(2)}, u32[]{:S(2)}) collective-permute-start(bf16[80,256]{1,0:T(8,128)(2,1)S(1)} %get-tuple-element.50), channel_id=1, source_target_pairs={{0,4},{4,8},{8,12},{12,0},{1,5},{5,9},{9,13},{13,1},{2,6},{6,10},{... | collective-permute-start | bytes 122888 | tf_op jit(solution)/shard_map/ppermute | solution.py:308
  81.6 5.7 %collective-permute-start.19 = (bf16[80,256]{1,0:T(8,128)(2,1)S(1)}, bf16[80,256]{1,0:T(8,128)(2,1)S(1)}, u32[]{:S(2)}, u32[]{:S(2)}) collective-permute-start(bf16[80,256]{1,0:T(8,128)(2,1)S(1)} %get-tuple-element.49), channel_id=1, source_target_pairs={{0,8},{4,12},{8,0},{12,4},{1,9},{5,13},{9,1},{13,5},{2,10},{6,14},... | collective-permute-start | bytes 122888 | tf_op jit(solution)/shard_map/ppermute | solution.py:308
  84.2 4.2 %collective-permute-start.20 = (bf16[80,256]{1,0:T(8,128)(2,1)S(1)}, bf16[80,256]{1,0:T(8,128)(2,1)S(1)}, u32[]{:S(2)}, u32[]{:S(2)}) collective-permute-start(bf16[80,256]{1,0:T(8,128)(2,1)S(1)} %get-tuple-element.48), channel_id=1, source_target_pairs={{0,12},{4,0},{8,4},{12,8},{1,13},{5,1},{9,5},{13,9},{2,14},{6,2},{... | collective-permute-start | bytes 122888 | tf_op jit(solution)/shard_map/ppermute | solution.py:308
  (14 other events, 12.4 us)

commit v16 on v15

--- a/solution.py
+++ b/solution.py
@@ -58,11 +58,16 @@
         refs = refs[2:]
     if nest:
         (state_ref, above_ref, below_ref, left_ref, right_ref, forcing_ref, upw_ref, dnw_ref,
-         nu_ref, relax_ref, vm_ref, new_ref) = refs[:12]
-        refs = refs[12:]
+         nu_ref, relax_ref, vm_ref) = refs[:11]
+        refs = refs[11:]
     else:
-        (state_ref, above_ref, below_ref, left_ref, right_ref, nu_ref, vm_ref, new_ref) = refs[:8]
-        refs = refs[8:]
+        (state_ref, above_ref, below_ref, left_ref, right_ref, nu_ref, vm_ref) = refs[:7]
+        refs = refs[7:]
+    if edges:
+        last_sel_ref, first_sel_ref = refs[:2]
+        refs = refs[2:]
+    new_ref = refs[0]
+    refs = refs[1:]
     if edges:
         lrow_ref, frow_ref, lcol_ref, fcol_ref = refs[:4]
         refs = refs[4:]
@@ -103,10 +108,8 @@
         lrow_ref[...] = new[:, n - cols : n].astype(jnp.bfloat16)
         frow_ref[...] = new[:, 0:cols].astype(jnp.bfloat16)
         narrow = new.astype(jnp.bfloat16)
-        p = lax.broadcasted_iota(jnp.int32, (n, rows), 0)
-        j = lax.broadcasted_iota(jnp.int32, (n, rows), 1)
-        last_sel = (p == j * cols + (cols - 1)).astype(jnp.bfloat16)
-        first_sel = (p == j * cols).astype(jnp.bfloat16)
+        last_sel = last_sel_ref[...]
+        first_sel = first_sel_ref[...]
         lcol_ref[...] = jnp.dot(narrow, last_sel, preferred_element_type=jnp.float32).astype(jnp.bfloat16)
         fcol_ref[...] = jnp.dot(narrow, first_sel, preferred_element_type=jnp.float32).astype(jnp.bfloat16)
     if split:
@@ -147,6 +150,12 @@
     edges = not (split or gap)
     out_shape = (jax.ShapeDtypeStruct((levels, n), jnp.float32),)
     if edges:
+        p = lax.broadcasted_iota(jnp.int32, (n, rows), 0)
+        j = lax.broadcasted_iota(jnp.int32, (n, rows), 1) + jnp.minimum(lax.axis_index("gx"), 0)
+        args = args + (
+            (p == j * cols + (cols - 1)).astype(jnp.bfloat16),
+            (p == j * cols).astype(jnp.bfloat16),
+        )
         out_shape = out_shape + (
             jax.ShapeDtypeStruct((levels, cols), jnp.bfloat16),
             jax.ShapeDtypeStruct((levels, cols), jnp.bfloat16),

time: 92 us -> 94.9 us (1.032)
  other arithmetic: 3.17 us -> 5.16 us
    convert_element_type x0 -> x2, other arithmetic: none -> 1.98 us  [the longest x1 0.99 us: stencil_step(): (p == j * cols + (cols - 1)).astype(jnp.bfloat16)]
  transfers between devices with their start and end apart: 21 -> 21, of which waited for: 6 -> 6; matrix products, arithmetic and copies ran while one was open for 14% -> 16% of each run, Pallas kernels for 3% -> 3%
where the time goes in v16:
time: 94.9 us; the launch traced here: 94 us
  starting transfers between devices  45.3 us (48%)
  Pallas kernels  13.7 us (14%)
  local copies, waits for them, and re-layouts  12.4 us (13%)
  waiting for transfers between devices  10.3 us (11%)
  matrix products  5.93 us (6%)
  other arithmetic  5.16 us (5%)
  between operations  1.25 us (1%)
    pallas_call x4, Pallas kernels, stencil_step(): pl.pallas_call(functools.partial(step_kernel, rows=rows, cols=cols, xo=xo...  13.7 us
    ppermute x3, starting transfers between devices, exchange(): above = lax.ppermute(last_rows, 'gx', fwd_x)  12.2 us
    ppermute x3, starting transfers between devices, exchange(): left = lax.ppermute(last_cols, Y_AXES, fwd_y)  8.26 us
    unnamed x64, local copies, waits for them, and re-layouts  6.35 us
    ppermute x3, starting transfers between devices, body_steps(): lax.ppermute(outgoing[s], 'gx', shifted_pairs(tiles_x, s))  6.28 us
    ppermute x3, starting transfers between devices, body_steps(): lax.ppermute(wanted[s], 'gx', shifted_pairs(tiles_x, s))  5.71 us
    ppermute x3, starting transfers between devices, body_steps(): lax.ppermute(gather_parts(parent_parts, served[s]), 'gx', shifted_pairs(t...  5.04 us
    ppermute x3, waiting for transfers between devices, body_steps(): lax.ppermute(gather_parts(parent_parts, served[s]), 'gx', shifted_pairs(t...  4.76 us
  transfers between devices with their start and end apart: 21, of which 6 were waited for; matrix products, arithmetic and copies ran while one was open for 16% of the time, Pallas kernels for 3%

profile of v16, /device:TPU:0, one launch (start us, length us, event | category | flops | bytes accessed | tf_op | source)
XLA Modules:
  0.0 94.0 jit_solution(15273546467540479569)
XLA Ops:
  0.7 1.2 %fusion.43 = (bf16[80,8,1]{2,1,0:T(8,128)(2,1)S(1)}, bf16[80,8,1]{2,1,0:T(8,128)(2,1)S(1)}) fusion(bf16[80,8,256]{2,1,0:T(8,128)(2,1)} %param.10), kind=kLoop, calls=%fused_computation.105 | loop fusion | bytes 5120 | tf_op jit(solution)/shard_map/slice | solution.py:22
  2.4 2.4 %collective-permute-start.2 = (bf16[80,14]{1,0:T(8,128)(2,1)S(1)}, bf16[80,14]{1,0:T(8,128)(2,1)S(1)}, u32[]{:S(2)}, u32[]{:S(2)}) collective-permute-start(bf16[80,14]{1,0:T(8,128)(2,1)S(1)} %copy.46), channel_id=1, source_target_pairs={{0,1},{1,2},{2,3},{4,5},{5,6},{6,7},{8,9},{9,10},{10,11},{12,13},{... | collective-permute-start | bytes 6728 | tf_op jit(solution)/shard_map/ppermute | solution.py:34
  5.3 1.3 %collective-permute-start.3 = (bf16[80,14]{1,0:T(8,128)(2,1)S(1)}, bf16[80,14]{1,0:T(8,128)(2,1)S(1)}, u32[]{:S(2)}, u32[]{:S(2)}) collective-permute-start(bf16[80,14]{1,0:T(8,128)(2,1)S(1)} %copy.49), channel_id=1, source_target_pairs={{1,0},{2,1},{3,2},{5,4},{6,5},{7,6},{9,8},{10,9},{11,10},{13,12},{... | collective-permute-start | bytes 6728 | tf_op jit(solution)/shard_map/ppermute | solution.py:35
  6.7 4.3 %collective-permute-start = (bf16[80,640]{1,0:T(8,128)(2,1)S(1)}, bf16[80,640]{1,0:T(8,128)(2,1)S(1)}, u32[]{:S(2)}, u32[]{:S(2)}) collective-permute-start(bf16[80,640]{1,0:T(8,128)(2,1)S(1)} %pad_maximum_fusion), channel_id=1, source_target_pairs={{0,4},{4,8},{8,12},{1,5},{5,9},{9,13},{2,6},{6,10},{10,14},{3,7},{... | collective-permute-start | bytes 307208 | tf_op jit(solution)/shard_map/ppermute | solution.py:32
  11.1 1.3 %collective-permute-start.1 = (bf16[80,640]{1,0:T(8,128)(2,1)S(1)}, bf16[80,640]{1,0:T(8,128)(2,1)S(1)}, u32[]{:S(2)}, u32[]{:S(2)}) collective-permute-start(bf16[80,640]{1,0:T(8,128)(2,1)S(1)} %pad_maximum_fusion.1), channel_id=1, source_target_pairs={{4,0},{8,4},{12,8},{5,1},{9,5},{13,9},{6,2},{10,6},{14,10},{7,3},{... | collective-permute-start | bytes 307208 | tf_op jit(solution)/shard_map/ppermute | solution.py:33
  12.5 4.7 %collective-permute-start.4 = (s32[256]{0:T(256)S(1)}, s32[256]{0:T(256)S(1)}, u32[]{:S(2)}, u32[]{:S(2)}) collective-permute-start(s32[256]{0:T(256)S(1)} %bitcast.81), channel_id=1, source_target_pairs={{0,12},{4,0},{8,4},{12,8},{1,13},{5,1},{9,5},{13,9},{2,14},{6,2},{... | collective-permute-start | bytes 3080 | tf_op jit(solution)/shard_map/ppermute | solution.py:270
  18.0 1.0 %fusion.7.refs_11_ = bf16[2304,6]{1,0:T(8,128)(2,1)} fusion(s32[6]{0:T(128)S(1)} %get-tuple-element.62), kind=kLoop, calls=%fused_computation.15 | loop fusion | flops 27648 | bytes 27672 | tf_op jit(solution)/shard_map/convert_element_type | solution.py:156
  26.7 3.1 %shard_map.113 = (f32[80,2048]{1,0:T(8,128)}, bf16[240,2048]{1,0:T(8,128)(2,1)}) custom-call(bf16[80,2048]{1,0:T(8,128)(2,1)} %bitcast.59, bf16[80,640]{1,0:T(8,128)(2,1)} %copy-done.6, bf16[80,640]{1,0:T(8,128)(2,1)} %copy-done.7, bf16[80,14]{1,0:T(8,128)(2,1)} %copy-done.8, bf16[80,14]{1,0:T(8,128)(2,1)} %copy-done.9, f32[80,1]{1,0:T(8,128)} %copy.50.refs_5_, ...), custom_call_target="tpu_custom_call" | custom-call | flops 165806080 | bytes 1218240 | tf_op jit(solution)/shard_map/pallas_call | solution.py:172
  29.8 1.9 %fusion.3 = f32[240,256]{1,0:T(8,128)S(1)} fusion(bf16[240,2048]{1,0:T(8,128)(2,1)} %get-tuple-element.17, s32[256]{0:T(256)S(1)} %collective-permute-done.4), kind=kOutput, calls=%fused_computation.9 | convolution fusion | flops 252182528 | bytes 1229824 | tf_op jit(solution)/shard_map/dot_general | solution.py:233
  31.7 2.5 %collective-permute-start.5 = (f32[80,256]{1,0:T(8,128)S(1)}, f32[80,256]{1,0:T(8,128)S(1)}, u32[]{:S(2)}, u32[]{:S(2)}) collective-permute-start(f32[80,256]{1,0:T(8,128)S(1)} %slice_add_fusion.6), channel_id=1, source_target_pairs={{0,4},{4,8},{8,12},{12,0},{1,5},{5,9},{9,13},{13,1},{2,6},{6,10},{... | collective-permute-start | bytes 245768 | tf_op jit(solution)/shard_map/ppermute | solution.py:274
  34.9 1.0 %collective-permute-start.7 = (f32[80,256]{1,0:T(8,128)S(1)}, f32[80,256]{1,0:T(8,128)S(1)}, u32[]{:S(2)}, u32[]{:S(2)}) collective-permute-start(f32[80,256]{1,0:T(8,128)S(1)} %slice_add_fusion.4), channel_id=1, source_target_pairs={{0,8},{4,12},{8,0},{12,4},{1,9},{5,13},{9,1},{13,5},{2,10},{6,14},... | collective-permute-start | bytes 245768 | tf_op jit(solution)/shard_map/ppermute | solution.py:274
  36.5 1.5 %collective-permute-start.9 = (f32[80,256]{1,0:T(8,128)S(1)}, f32[80,256]{1,0:T(8,128)S(1)}, u32[]{:S(2)}, u32[]{:S(2)}) collective-permute-start(f32[80,256]{1,0:T(8,128)S(1)} %slice_add_fusion.2), channel_id=1, source_target_pairs={{0,12},{4,0},{8,4},{12,8},{1,13},{5,1},{9,5},{13,9},{2,14},{6,2},{... | collective-permute-start | bytes 245768 | tf_op jit(solution)/shard_map/ppermute | solution.py:274
  38.8 3.6 %collective-permute-done.7 = f32[80,256]{1,0:T(8,128)S(1)} collective-permute-done((f32[80,256]{1,0:T(8,128)S(1)}, f32[80,256]{1,0:T(8,128)S(1)}, u32[]{:S(2)}, u32[]{:S(2)}) %collective-permute-start.7) | collective-permute-done | bytes 81952 | tf_op jit(solution)/shard_map/ppermute | solution.py:274
  44.9 3.5 %shard_map.114 = (f32[80,2304]{1,0:T(8,128)}, bf16[80,384]{1,0:T(8,128)(2,1)}, bf16[80,384]{1,0:T(8,128)(2,1)}, bf16[80,6]{1,0:T(8,128)(2,1)}, bf16[80,6]{1,0:T(8,128)(2,1)}) custom-call(bf16[80,2304]{1,0:T(8,128)(2,1)} %bitcast.56, bf16[80,640]{1,0:T(8,128)(2,1)} %copy-done.6, bf16[80,640]{1,0:T(8,128)(2,1)} %copy-done.7, bf16[80,14]{1,0:T(8,128)(2,1)} %copy-done.8, ...), custom_call_target="tpu_custom_call" | custom-call | flops 185057280 | bytes 2152448 | tf_op jit(solution)/shard_map/pallas_call | solution.py:172
  48.4 3.4 %collective-permute-start.10 = (bf16[80,384]{1,0:T(8,128)(2,1)}, bf16[80,384]{1,0:T(8,128)(2,1)S(1)}, u32[]{:S(2)}, u32[]{:S(2)}) collective-permute-start(bf16[80,384]{1,0:T(8,128)(2,1)} %get-tuple-element.19), channel_id=1, source_target_pairs={{0,4},{4,8},{8,12},{1,5},{5,9},{9,13},{2,6},{6,10},{10,14},{3,7},{... | collective-permute-start | bytes 184328 | tf_op jit(solution)/shard_map/ppermute | solution.py:32
  51.8 1.3 %collective-permute-start.11 = (bf16[80,384]{1,0:T(8,128)(2,1)}, bf16[80,384]{1,0:T(8,128)(2,1)S(1)}, u32[]{:S(2)}, u32[]{:S(2)}) collective-permute-start(bf16[80,384]{1,0:T(8,128)(2,1)} %get-tuple-element.20), channel_id=1, source_target_pairs={{4,0},{8,4},{12,8},{5,1},{9,5},{13,9},{6,2},{10,6},{14,10},{7,3},{... | collective-permute-start | bytes 184328 | tf_op jit(solution)/shard_map/ppermute | solution.py:33
  53.1 1.7 %collective-permute-start.12 = (bf16[80,6]{1,0:T(8,128)(2,1)}, bf16[80,6]{1,0:T(8,128)(2,1)S(1)}, u32[]{:S(2)}, u32[]{:S(2)}) collective-permute-start(bf16[80,6]{1,0:T(8,128)(2,1)} %get-tuple-element.21), channel_id=1, source_target_pairs={{0,1},{1,2},{2,3},{4,5},{5,6},{6,7},{8,9},{9,10},{10,11},{12,13},{... | collective-permute-start | bytes 2888 | tf_op jit(solution)/shard_map/ppermute | solution.py:34
  54.8 1.3 %collective-permute-start.13 = (bf16[80,6]{1,0:T(8,128)(2,1)}, bf16[80,6]{1,0:T(8,128)(2,1)S(1)}, u32[]{:S(2)}, u32[]{:S(2)}) collective-permute-start(bf16[80,6]{1,0:T(8,128)(2,1)} %get-tuple-element.22), channel_id=1, source_target_pairs={{1,0},{2,1},{3,2},{5,4},{6,5},{7,6},{9,8},{10,9},{11,10},{13,12},{... | collective-permute-start | bytes 2888 | tf_op jit(solution)/shard_map/ppermute | solution.py:35
  56.2 3.1 %collective-permute-done.13.refs_4_ = bf16[80,6]{1,0:T(8,128)(2,1)S(1)} collective-permute-done((bf16[80,6]{1,0:T(8,128)(2,1)}, bf16[80,6]{1,0:T(8,128)(2,1)S(1)}, u32[]{:S(2)}, u32[]{:S(2)}) %collective-permute-start.13) | collective-permute-done | bytes 992 | tf_op jit(solution)/shard_map/ppermute | solution.py:35
  59.9 3.6 %shard_map.115 = (f32[80,2304]{1,0:T(8,128)}, bf16[80,384]{1,0:T(8,128)(2,1)}, bf16[80,384]{1,0:T(8,128)(2,1)}, bf16[80,6]{1,0:T(8,128)(2,1)}, bf16[80,6]{1,0:T(8,128)(2,1)}) custom-call(f32[80,2304]{1,0:T(8,128)} %get-tuple-element.18.refs_0_, bf16[80,384]{1,0:T(8,128)(2,1)} %copy-done.12, bf16[80,384]{1,0:T(8,128)(2,1)} %copy-done.13, ...), custom_call_target="tpu_custom_call" | custom-call | flops 185057280 | bytes 2436608 | tf_op jit(solution)/shard_map/pallas_call | solution.py:172
  63.5 4.5 %collective-permute-start.14 = (bf16[80,384]{1,0:T(8,128)(2,1)}, bf16[80,384]{1,0:T(8,128)(2,1)S(1)}, u32[]{:S(2)}, u32[]{:S(2)}) collective-permute-start(bf16[80,384]{1,0:T(8,128)(2,1)} %get-tuple-element.24), channel_id=1, source_target_pairs={{0,4},{4,8},{8,12},{1,5},{5,9},{9,13},{2,6},{6,10},{10,14},{3,7},{... | collective-permute-start | bytes 184328 | tf_op jit(solution)/shard_map/ppermute | solution.py:32
  68.1 1.3 %collective-permute-start.15 = (bf16[80,384]{1,0:T(8,128)(2,1)}, bf16[80,384]{1,0:T(8,128)(2,1)S(1)}, u32[]{:S(2)}, u32[]{:S(2)}) collective-permute-start(bf16[80,384]{1,0:T(8,128)(2,1)} %get-tuple-element.25), channel_id=1, source_target_pairs={{4,0},{8,4},{12,8},{5,1},{9,5},{13,9},{6,2},{10,6},{14,10},{7,3},{... | collective-permute-start | bytes 184328 | tf_op jit(solution)/shard_map/ppermute | solution.py:33
  69.4 4.1 %collective-permute-start.16 = (bf16[80,6]{1,0:T(8,128)(2,1)}, bf16[80,6]{1,0:T(8,128)(2,1)S(1)}, u32[]{:S(2)}, u32[]{:S(2)}) collective-permute-start(bf16[80,6]{1,0:T(8,128)(2,1)} %get-tuple-element.26), channel_id=1, source_target_pairs={{0,1},{1,2},{2,3},{4,5},{5,6},{6,7},{8,9},{9,10},{10,11},{12,13},{... | collective-permute-start | bytes 2888 | tf_op jit(solution)/shard_map/ppermute | solution.py:34
  73.5 1.3 %collective-permute-start.17 = (bf16[80,6]{1,0:T(8,128)(2,1)}, bf16[80,6]{1,0:T(8,128)(2,1)S(1)}, u32[]{:S(2)}, u32[]{:S(2)}) collective-permute-start(bf16[80,6]{1,0:T(8,128)(2,1)} %get-tuple-element.27), channel_id=1, source_target_pairs={{1,0},{2,1},{3,2},{5,4},{6,5},{7,6},{9,8},{10,9},{11,10},{13,12},{... | collective-permute-start | bytes 2888 | tf_op jit(solution)/shard_map/ppermute | solution.py:35
  75.6 1.2 %collective-permute-done.17.refs_6_ = bf16[80,6]{1,0:T(8,128)(2,1)S(1)} collective-permute-done((bf16[80,6]{1,0:T(8,128)(2,1)}, bf16[80,6]{1,0:T(8,128)(2,1)S(1)}, u32[]{:S(2)}, u32[]{:S(2)}) %collective-permute-start.17) | collective-permute-done | bytes 992 | tf_op jit(solution)/shard_map/ppermute | solution.py:35
  77.5 3.5 %shard_map.116 = (f32[80,2304]{1,0:T(8,128)}, f32[80,256]{1,0:T(8,128)}) custom-call(f32[128,384]{1,0:T(8,128)} %fusion.15.refs_0_, f32[80,256]{1,0:T(8,128)} %copy-done.4, f32[80,2304]{1,0:T(8,128)} %get-tuple-element.23.refs_2_, bf16[80,384]{1,0:T(8,128)(2,1)} %copy-done.10, bf16[80,384]{1,0:T(8,128)(2,1)} %copy-done.11, bf16[80,6]{1,0:T(8,128)(2,1)} %copy-done.14, ...), custom_call_target="tpu_custom_call" | custom-call | flops 185057280 | bytes 2659840 | tf_op jit(solution)/shard_map/pallas_call | solution.py:172
  81.9 2.5 %collective-permute-start.18 = (bf16[80,256]{1,0:T(8,128)(2,1)S(1)}, bf16[80,256]{1,0:T(8,128)(2,1)S(1)}, u32[]{:S(2)}, u32[]{:S(2)}) collective-permute-start(bf16[80,256]{1,0:T(8,128)(2,1)S(1)} %get-tuple-element.50), channel_id=1, source_target_pairs={{0,4},{4,8},{8,12},{12,0},{1,5},{5,9},{9,13},{13,1},{2,6},{6,10},{... | collective-permute-start | bytes 122888 | tf_op jit(solution)/shard_map/ppermute | solution.py:317
  84.4 2.7 %collective-permute-start.19 = (bf16[80,256]{1,0:T(8,128)(2,1)S(1)}, bf16[80,256]{1,0:T(8,128)(2,1)S(1)}, u32[]{:S(2)}, u32[]{:S(2)}) collective-permute-start(bf16[80,256]{1,0:T(8,128)(2,1)S(1)} %get-tuple-element.49), channel_id=1, source_target_pairs={{0,8},{4,12},{8,0},{12,4},{1,9},{5,13},{9,1},{13,5},{2,10},{6,14},... | collective-permute-start | bytes 122888 | tf_op jit(solution)/shard_map/ppermute | solution.py:317
  87.1 1.1 %collective-permute-start.20 = (bf16[80,256]{1,0:T(8,128)(2,1)S(1)}, bf16[80,256]{1,0:T(8,128)(2,1)S(1)}, u32[]{:S(2)}, u32[]{:S(2)}) collective-permute-start(bf16[80,256]{1,0:T(8,128)(2,1)S(1)} %get-tuple-element.48), channel_id=1, source_target_pairs={{0,12},{4,0},{8,4},{12,8},{1,13},{5,1},{9,5},{13,9},{2,14},{6,2},{... | collective-permute-start | bytes 122888 | tf_op jit(solution)/shard_map/ppermute | solution.py:317
  88.2 1.2 %convert_element_type.38 = bf16[80,2304]{1,0:T(8,128)(2,1)S(1)} convert(f32[80,2304]{1,0:T(8,128)} %get-tuple-element.29) | non-fusion elementwise | flops 184320 | bytes 1105920 | tf_op jit(solution)/shard_map/convert_element_type | solution.py:327
  90.1 1.2 %collective-permute-done.20 = bf16[80,256]{1,0:T(8,128)(2,1)S(1)} collective-permute-done((bf16[80,256]{1,0:T(8,128)(2,1)S(1)}, bf16[80,256]{1,0:T(8,128)(2,1)S(1)}, u32[]{:S(2)}, u32[]{:S(2)}) %collective-permute-start.20) | collective-permute-done | bytes 40992 | tf_op jit(solution)/shard_map/ppermute | solution.py:317
  91.3 1.8 %fusion.2 = f32[80,2048]{1,0:T(8,128)S(1)} fusion(s32[1024]{0:T(1024)S(1)} %pad_add_fusion, f32[80]{0:T(128)S(1)} %copy-done.24, bf16[80,256]{1,0:T(8,128)(2,1)S(1)} %collective-permute-done.20, bf16[80,256]{1,0:T(8,128)(2,1)S(1)} %collective-permute-done.19, bf16[80,256]{1,0:T(8,128)(2,1)S(1)} %collective-permute-done.18, ...), kind=kOutput, calls=%fused_computation.4 | convolution fusion | flops 338460672 | bytes 823616 | tf_op jit(solution)/shard_map/dot_general | solution.py:241
  (128 shorter events, 18.6 us)
Async XLA Ops:
  0.6 16.7 %copy-start = (s32[24]{0:T(128)S(1)}, s32[24]{0:T(128)}, u32[]{:S(2)}) copy-start(s32[24]{0:T(128)} %param.19) | copy-start | bytes 292
  0.6 5.9 %copy-start.2 = (bf16[80,8,256]{2,1,0:T(8,128)(2,1)S(1)}, bf16[80,8,256]{2,1,0:T(8,128)(2,1)}, u32[]{:S(2)}) copy-start(bf16[80,8,256]{2,1,0:T(8,128)(2,1)} %param.10) | copy-start | bytes 983044
  2.1 10.3 %copy-start.18 = (s32[1,1,256,1]{2,3,1,0:T(1,128)S(1)}, s32[1,1,256,1]{2,3,1,0:T(1,128)}, u32[]{:S(2)}) copy-start(s32[1,1,256,1]{2,3,1,0:T(1,128)} %param.17) | copy-start | bytes 3076
  2.1 10.3 %copy-start.19 = (s32[1,1,256]{2,1,0:T(1,128)S(1)}, s32[1,1,256]{2,1,0:T(1,128)}, u32[]{:S(2)}) copy-start(s32[1,1,256]{2,1,0:T(1,128)} %param.18) | copy-start | bytes 3076
  2.4 22.6 %collective-permute-start.2 = (bf16[80,14]{1,0:T(8,128)(2,1)S(1)}, bf16[80,14]{1,0:T(8,128)(2,1)S(1)}, u32[]{:S(2)}, u32[]{:S(2)}) collective-permute-start(bf16[80,14]{1,0:T(8,128)(2,1)S(1)} %copy.46), channel_id=1, source_target_pairs={{0,1},{1,2},{2,3},{4,5},{5,6},{6,7},{8,9},{9,10},{10,11},{12,13},{... | collective-permute-start | bytes 6728 | tf_op jit(solution)/shard_map/ppermute | solution.py:34
  5.3 19.8 %collective-permute-start.3 = (bf16[80,14]{1,0:T(8,128)(2,1)S(1)}, bf16[80,14]{1,0:T(8,128)(2,1)S(1)}, u32[]{:S(2)}, u32[]{:S(2)}) collective-permute-start(bf16[80,14]{1,0:T(8,128)(2,1)S(1)} %copy.49), channel_id=1, source_target_pairs={{1,0},{2,1},{3,2},{5,4},{6,5},{7,6},{9,8},{10,9},{11,10},{13,12},{... | collective-permute-start | bytes 6728 | tf_op jit(solution)/shard_map/ppermute | solution.py:35
  6.7 19.3 %collective-permute-start = (bf16[80,640]{1,0:T(8,128)(2,1)S(1)}, bf16[80,640]{1,0:T(8,128)(2,1)S(1)}, u32[]{:S(2)}, u32[]{:S(2)}) collective-permute-start(bf16[80,640]{1,0:T(8,128)(2,1)S(1)} %pad_maximum_fusion), channel_id=1, source_target_pairs={{0,4},{4,8},{8,12},{1,5},{5,9},{9,13},{2,6},{6,10},{10,14},{3,7},{... | collective-permute-start | bytes 307208 | tf_op jit(solution)/shard_map/ppermute | solution.py:32
  11.1 15.0 %collective-permute-start.1 = (bf16[80,640]{1,0:T(8,128)(2,1)S(1)}, bf16[80,640]{1,0:T(8,128)(2,1)S(1)}, u32[]{:S(2)}, u32[]{:S(2)}) collective-permute-start(bf16[80,640]{1,0:T(8,128)(2,1)S(1)} %pad_maximum_fusion.1), channel_id=1, source_target_pairs={{4,0},{8,4},{12,8},{5,1},{9,5},{13,9},{6,2},{10,6},{14,10},{7,3},{... | collective-permute-start | bytes 307208 | tf_op jit(solution)/shard_map/ppermute | solution.py:33
  12.5 17.4 %collective-permute-start.4 = (s32[256]{0:T(256)S(1)}, s32[256]{0:T(256)S(1)}, u32[]{:S(2)}, u32[]{:S(2)}) collective-permute-start(s32[256]{0:T(256)S(1)} %bitcast.81), channel_id=1, source_target_pairs={{0,12},{4,0},{8,4},{12,8},{1,13},{5,1},{9,5},{13,9},{2,14},{6,2},{... | collective-permute-start | bytes 3080 | tf_op jit(solution)/shard_map/ppermute | solution.py:270
  17.9 3.0 %copy-start.20 = (f32[80]{0:T(128)S(1)}, f32[80]{0:T(128)}, u32[]{:S(2)}) copy-start(f32[80]{0:T(128)} %param.12) | copy-start | bytes 964
  18.0 4.8 %copy-start.21 = (f32[80]{0:T(128)S(1)}, f32[80]{0:T(128)}, u32[]{:S(2)}) copy-start(f32[80]{0:T(128)} %param.13) | copy-start | bytes 964
  18.0 5.5 %copy-start.22 = (f32[80]{0:T(128)S(1)}, f32[80]{0:T(128)}, u32[]{:S(2)}) copy-start(f32[80]{0:T(128)} %param.14) | copy-start | bytes 964
  25.0 9.2 %collective-permute-start.6 = (s32[256]{0:T(256)S(1)}, s32[256]{0:T(256)S(1)}, u32[]{:S(2)}, u32[]{:S(2)}) collective-permute-start(s32[256]{0:T(256)S(1)} %bitcast.80), channel_id=1, source_target_pairs={{0,8},{4,12},{8,0},{12,4},{1,9},{5,13},{9,1},{13,5},{2,10},{6,14},... | collective-permute-start | bytes 3080 | tf_op jit(solution)/shard_map/ppermute | solution.py:270
  25.0 10.8 %collective-permute-start.8 = (s32[256]{0:T(256)S(1)}, s32[256]{0:T(256)S(1)}, u32[]{:S(2)}, u32[]{:S(2)}) collective-permute-start(s32[256]{0:T(256)S(1)} %bitcast.79), channel_id=1, source_target_pairs={{0,4},{4,8},{8,12},{12,0},{1,5},{5,9},{9,13},{13,1},{2,6},{6,10},{... | collective-permute-start | bytes 3080 | tf_op jit(solution)/shard_map/ppermute | solution.py:270
  29.8 4.4 %copy-start.23 = (bf16[240,2048]{1,0:T(8,128)(2,1)S(1)}, bf16[240,2048]{1,0:T(8,128)(2,1)}, u32[]{:S(2)}) copy-start(bf16[240,2048]{1,0:T(8,128)(2,1)} %get-tuple-element.17) | copy-start | bytes 2949124
  31.7 7.1 %collective-permute-start.5 = (f32[80,256]{1,0:T(8,128)S(1)}, f32[80,256]{1,0:T(8,128)S(1)}, u32[]{:S(2)}, u32[]{:S(2)}) collective-permute-start(f32[80,256]{1,0:T(8,128)S(1)} %slice_add_fusion.6), channel_id=1, source_target_pairs={{0,4},{4,8},{8,12},{12,0},{1,5},{5,9},{9,13},{13,1},{2,6},{6,10},{... | collective-permute-start | bytes 245768 | tf_op jit(solution)/shard_map/ppermute | solution.py:274
  34.9 7.6 %collective-permute-start.7 = (f32[80,256]{1,0:T(8,128)S(1)}, f32[80,256]{1,0:T(8,128)S(1)}, u32[]{:S(2)}, u32[]{:S(2)}) collective-permute-start(f32[80,256]{1,0:T(8,128)S(1)} %slice_add_fusion.4), channel_id=1, source_target_pairs={{0,8},{4,12},{8,0},{12,4},{1,9},{5,13},{9,1},{13,5},{2,10},{6,14},... | collective-permute-start | bytes 245768 | tf_op jit(solution)/shard_map/ppermute | solution.py:274
  36.5 6.8 %collective-permute-start.9 = (f32[80,256]{1,0:T(8,128)S(1)}, f32[80,256]{1,0:T(8,128)S(1)}, u32[]{:S(2)}, u32[]{:S(2)}) collective-permute-start(f32[80,256]{1,0:T(8,128)S(1)} %slice_add_fusion.2), channel_id=1, source_target_pairs={{0,12},{4,0},{8,4},{12,8},{1,13},{5,1},{9,5},{13,9},{2,14},{6,2},{... | collective-permute-start | bytes 245768 | tf_op jit(solution)/shard_map/ppermute | solution.py:274
  43.3 5.1 %copy-start.4 = (f32[80,256]{1,0:T(8,128)}, f32[80,256]{1,0:T(8,128)S(1)}, u32[]{:S(2)}) copy-start(f32[80,256]{1,0:T(8,128)S(1)} %fusion.33.refs_1_) | copy-start | bytes 245764
  48.4 10.9 %collective-permute-start.10 = (bf16[80,384]{1,0:T(8,128)(2,1)}, bf16[80,384]{1,0:T(8,128)(2,1)S(1)}, u32[]{:S(2)}, u32[]{:S(2)}) collective-permute-start(bf16[80,384]{1,0:T(8,128)(2,1)} %get-tuple-element.19), channel_id=1, source_target_pairs={{0,4},{4,8},{8,12},{1,5},{5,9},{9,13},{2,6},{6,10},{10,14},{3,7},{... | collective-permute-start | bytes 184328 | tf_op jit(solution)/shard_map/ppermute | solution.py:32
  51.8 7.5 %collective-permute-start.11 = (bf16[80,384]{1,0:T(8,128)(2,1)}, bf16[80,384]{1,0:T(8,128)(2,1)S(1)}, u32[]{:S(2)}, u32[]{:S(2)}) collective-permute-start(bf16[80,384]{1,0:T(8,128)(2,1)} %get-tuple-element.20), channel_id=1, source_target_pairs={{4,0},{8,4},{12,8},{5,1},{9,5},{13,9},{6,2},{10,6},{14,10},{7,3},{... | collective-permute-start | bytes 184328 | tf_op jit(solution)/shard_map/ppermute | solution.py:33
  53.1 3.0 %collective-permute-start.12 = (bf16[80,6]{1,0:T(8,128)(2,1)}, bf16[80,6]{1,0:T(8,128)(2,1)S(1)}, u32[]{:S(2)}, u32[]{:S(2)}) collective-permute-start(bf16[80,6]{1,0:T(8,128)(2,1)} %get-tuple-element.21), channel_id=1, source_target_pairs={{0,1},{1,2},{2,3},{4,5},{5,6},{6,7},{8,9},{9,10},{10,11},{12,13},{... | collective-permute-start | bytes 2888 | tf_op jit(solution)/shard_map/ppermute | solution.py:34
  54.8 4.4 %collective-permute-start.13 = (bf16[80,6]{1,0:T(8,128)(2,1)}, bf16[80,6]{1,0:T(8,128)(2,1)S(1)}, u32[]{:S(2)}, u32[]{:S(2)}) collective-permute-start(bf16[80,6]{1,0:T(8,128)(2,1)} %get-tuple-element.22), channel_id=1, source_target_pairs={{1,0},{2,1},{3,2},{5,4},{6,5},{7,6},{9,8},{10,9},{11,10},{13,12},{... | collective-permute-start | bytes 2888 | tf_op jit(solution)/shard_map/ppermute | solution.py:35
  56.1 3.2 %copy-start.16 = (bf16[80,6]{1,0:T(8,128)(2,1)}, bf16[80,6]{1,0:T(8,128)(2,1)S(1)}, u32[]{:S(2)}) copy-start(bf16[80,6]{1,0:T(8,128)(2,1)S(1)} %collective-permute-done.12.refs_3_) | copy-start | bytes 2884
  63.5 13.3 %collective-permute-start.14 = (bf16[80,384]{1,0:T(8,128)(2,1)}, bf16[80,384]{1,0:T(8,128)(2,1)S(1)}, u32[]{:S(2)}, u32[]{:S(2)}) collective-permute-start(bf16[80,384]{1,0:T(8,128)(2,1)} %get-tuple-element.24), channel_id=1, source_target_pairs={{0,4},{4,8},{8,12},{1,5},{5,9},{9,13},{2,6},{6,10},{10,14},{3,7},{... | collective-permute-start | bytes 184328 | tf_op jit(solution)/shard_map/ppermute | solution.py:32
  68.1 8.8 %collective-permute-start.15 = (bf16[80,384]{1,0:T(8,128)(2,1)}, bf16[80,384]{1,0:T(8,128)(2,1)S(1)}, u32[]{:S(2)}, u32[]{:S(2)}) collective-permute-start(bf16[80,384]{1,0:T(8,128)(2,1)} %get-tuple-element.25), channel_id=1, source_target_pairs={{4,0},{8,4},{12,8},{5,1},{9,5},{13,9},{6,2},{10,6},{14,10},{7,3},{... | collective-permute-start | bytes 184328 | tf_op jit(solution)/shard_map/ppermute | solution.py:33
  69.4 6.2 %collective-permute-start.16 = (bf16[80,6]{1,0:T(8,128)(2,1)}, bf16[80,6]{1,0:T(8,128)(2,1)S(1)}, u32[]{:S(2)}, u32[]{:S(2)}) collective-permute-start(bf16[80,6]{1,0:T(8,128)(2,1)} %get-tuple-element.26), channel_id=1, source_target_pairs={{0,1},{1,2},{2,3},{4,5},{5,6},{6,7},{8,9},{9,10},{10,11},{12,13},{... | collective-permute-start | bytes 2888 | tf_op jit(solution)/shard_map/ppermute | solution.py:34
  73.5 3.3 %collective-permute-start.17 = (bf16[80,6]{1,0:T(8,128)(2,1)}, bf16[80,6]{1,0:T(8,128)(2,1)S(1)}, u32[]{:S(2)}, u32[]{:S(2)}) collective-permute-start(bf16[80,6]{1,0:T(8,128)(2,1)} %get-tuple-element.27), channel_id=1, source_target_pairs={{1,0},{2,1},{3,2},{5,4},{6,5},{7,6},{9,8},{10,9},{11,10},{13,12},{... | collective-permute-start | bytes 2888 | tf_op jit(solution)/shard_map/ppermute | solution.py:35
  81.9 9.4 %copy-start.24 = (f32[80]{0:T(128)S(1)}, f32[80]{0:T(128)}, u32[]{:S(2)}) copy-start(f32[80]{0:T(128)} %param.15) | copy-start | bytes 964
  81.9 8.2 %collective-permute-start.18 = (bf16[80,256]{1,0:T(8,128)(2,1)S(1)}, bf16[80,256]{1,0:T(8,128)(2,1)S(1)}, u32[]{:S(2)}, u32[]{:S(2)}) collective-permute-start(bf16[80,256]{1,0:T(8,128)(2,1)S(1)} %get-tuple-element.50), channel_id=1, source_target_pairs={{0,4},{4,8},{8,12},{12,0},{1,5},{5,9},{9,13},{13,1},{2,6},{6,10},{... | collective-permute-start | bytes 122888 | tf_op jit(solution)/shard_map/ppermute | solution.py:317
  84.4 5.7 %collective-permute-start.19 = (bf16[80,256]{1,0:T(8,128)(2,1)S(1)}, bf16[80,256]{1,0:T(8,128)(2,1)S(1)}, u32[]{:S(2)}, u32[]{:S(2)}) collective-permute-start(bf16[80,256]{1,0:T(8,128)(2,1)S(1)} %get-tuple-element.49), channel_id=1, source_target_pairs={{0,8},{4,12},{8,0},{12,4},{1,9},{5,13},{9,1},{13,5},{2,10},{6,14},... | collective-permute-start | bytes 122888 | tf_op jit(solution)/shard_map/ppermute | solution.py:317
  87.1 4.2 %collective-permute-start.20 = (bf16[80,256]{1,0:T(8,128)(2,1)S(1)}, bf16[80,256]{1,0:T(8,128)(2,1)S(1)}, u32[]{:S(2)}, u32[]{:S(2)}) collective-permute-start(bf16[80,256]{1,0:T(8,128)(2,1)S(1)} %get-tuple-element.48), channel_id=1, source_target_pairs={{0,12},{4,0},{8,4},{12,8},{1,13},{5,1},{9,5},{13,9},{2,14},{6,2},{... | collective-permute-start | bytes 122888 | tf_op jit(solution)/shard_map/ppermute | solution.py:317
  (14 other events, 12.4 us)
